TPU v7x, 32 devices: a whole 2x2x4 slice. The times are simulated.
32 devices in a mesh: groups: 2 (over x), sy: 16 (over z, y, core).
Axes of the slice: x: 2, y: 2, z: 4, core: 2. Of those that a mesh axis runs over, the one named last changes fastest.
Arguments:
- queries: bfloat16 [64, 64, 2, 1536], P('sy', 'groups'), parts along dimension 1, may hold values from -6 to 6
- key_vecs: bfloat16 [64, 64, 2, 1536], P('sy', 'groups'), parts along dimension 1, may hold values from -6 to 6
- value_vecs: bfloat16 [64, 64, 2, 1536], P('sy', 'groups'), parts along dimension 1, may hold values from -6 to 6
- outputs_fwd: bfloat16 [64, 64, 2, 1536], P('sy', 'groups'), parts along dimension 1, may hold values from -1.5 to 1.5
- grad_out: bfloat16 [64, 64, 2, 1536], P('sy', 'groups'), parts along dimension 1, may hold values from -96 to 96
- log_norm: float32 [64, 64, 2, 12], P('sy', 'groups'), parts along dimension 1, may hold values from 6.5 to 8.5
Outputs:
- grad_queries: bfloat16 [64, 64, 2, 1536], P('sy', 'groups'), parts along dimension 1
- grad_keys: bfloat16 [64, 64, 2, 1536], P('sy', 'groups'), parts along dimension 1
- grad_values: bfloat16 [64, 64, 2, 1536], P('sy', 'groups'), parts along dimension 1
There are 2 independent parts, one for each index of `groups`. A program takes and returns all parts, laid end to end along the dimension named above; each array names one. Nothing has to cross between parts.
All inputs are finite; a program needn't handle non-finite values.
Results may differ from a plain program's by a relative error of at most 0.0057.
Values may be sent and summed in bfloat16 or wider, within the bound.
No kernel may reach another device: no remote copies, remote signals or barrier semaphores. Data moves between devices by JAX's collectives and lax.ppermute only.
A program may use at most 128 MiB of HBM per device.

v0:
```python
import jax
import jax.numpy as jnp
from jax import lax
from jax.sharding import PartitionSpec as P


def shifted(block, axis, distance):
    devices = range(lax.axis_size(axis))
    route = [((i - distance) % len(devices), i) for i in devices]
    return lax.ppermute(block, axis, route)


def join_pieces(pieces, reach_rows):
    order = list(range(-reach_rows, reach_rows + 1))
    return (
        jnp.concatenate([pieces[offset][0] for offset in order], axis=0),
        jnp.concatenate([pieces[offset][1] for offset in order], axis=0),
    )


def side_offsets(reach_rows):
    return [offset for offset in range(-reach_rows, reach_rows + 1) if offset != 0]


def near_keys(members, reach_rows):
    pieces = {0: members}
    for offset in side_offsets(reach_rows):
        pieces[offset] = shifted((members[0], members[1]), "sy", -offset)
    return join_pieces(pieces, reach_rows)


def return_rows(totals, reach_rows, rows_dev):
    slabs = {}
    for offset in range(-reach_rows, reach_rows + 1):
        row_start = (reach_rows + offset) * rows_dev
        slabs[offset] = (
            totals[0][row_start : row_start + rows_dev],
            totals[1][row_start : row_start + rows_dev],
        )
    result_keys = slabs[0][0]
    result_values = slabs[0][1]
    for offset in side_offsets(reach_rows):
        arrived = shifted(slabs[offset], "sy", offset)
        result_keys = result_keys + arrived[0]
        result_values = result_values + arrived[1]
    return (result_keys, result_values)


def column_blocks(array, margin):
    width_cells = array.shape[1]
    padded = jnp.concatenate([array[:, width_cells - margin :], array, array[:, :margin]], axis=1)
    return padded.reshape((array.shape[0], (width_cells + 2 * margin) // 8, 8) + array.shape[2:])


def key_windows(extended, row_starts, tiles_w):
    row_slabs = jnp.concatenate(
        [lax.dynamic_slice_in_dim(extended, row_start, 16, 0) for row_start in row_starts], axis=0
    )
    blocks = column_blocks(row_slabs, 4)
    windows = jnp.concatenate([blocks[:, :-1], blocks[:, 1:]], axis=2)
    windows = windows.reshape((len(row_starts), 16) + windows.shape[1:])
    windows = jnp.swapaxes(windows, 1, 2)
    return windows.reshape(len(row_starts) * tiles_w, -1, windows.shape[-1])


def query_tiles(array, groups, quarter, tiles_w):
    tiled_rows = array.reshape(groups, quarter, tiles_w, 8, array.shape[2], array.shape[3])
    tiled_rows = jnp.swapaxes(tiled_rows, 1, 2)
    return tiled_rows.reshape(groups * tiles_w, quarter * 8 * array.shape[2], array.shape[3])


def untile_queries(tiles, groups, quarter, tiles_w, frames):
    tiled_rows = tiles.reshape(groups, tiles_w, quarter, 8, frames, tiles.shape[-1])
    return jnp.swapaxes(tiled_rows, 1, 2).reshape(
        groups * quarter, tiles_w * 8, frames, tiles.shape[-1]
    )


def fold_windows(window_terms, row_starts, rows_ext, tiles_w):
    groups = len(row_starts)
    frames = window_terms.shape[1] // 256
    trailing = window_terms.shape[2]
    width_cells = tiles_w * 8
    split_cols = window_terms.reshape(groups, tiles_w, 16, 16, frames, trailing)
    split_cols = jnp.swapaxes(split_cols, 1, 2)
    first_half = split_cols[:, :, :, :8]
    second_half = split_cols[:, :, :, 8:]
    zero_block = jnp.zeros_like(first_half[:, :, :1])
    padded = jnp.concatenate([first_half, zero_block], axis=2) + jnp.concatenate(
        [zero_block, second_half], axis=2
    )
    padded = padded.reshape(groups, 16, width_cells + 8, frames, trailing)
    middle = jnp.zeros((groups, 16, width_cells - 8, frames, trailing), jnp.float32)
    core_cols = padded[:, :, 4 : width_cells + 4] + jnp.concatenate(
        [padded[:, :, width_cells + 4 :], middle, padded[:, :, :4]], axis=2
    )
    total_rows = jnp.zeros((rows_ext, width_cells, frames, trailing), jnp.float32)
    row_start = row_starts[0]
    total_rows = lax.dynamic_update_slice_in_dim(total_rows, core_cols[0], row_start, 0)
    return total_rows


def merge_heads(stacked):
    moved = jnp.moveaxis(stacked, 0, 2)
    return moved.reshape(moved.shape[0], moved.shape[1], moved.shape[2] * moved.shape[3])


def query_pass(query_t, dout_t, norm_t, delta_t, key_window, value_window, head_dim):
    scaling = head_dim ** (-0.5)
    head_count = norm_t.shape[-1]

    def head_step(head):
        column = head * head_dim
        query_head = lax.dynamic_slice_in_dim(query_t, column, head_dim, 2)
        dout_head = lax.dynamic_slice_in_dim(dout_t, column, head_dim, 2)
        key_head = lax.dynamic_slice_in_dim(key_window, column, head_dim, 2)
        value_head = lax.dynamic_slice_in_dim(value_window, column, head_dim, 2)
        norm_head = lax.dynamic_index_in_dim(norm_t, head, 2, keepdims=False)
        delta_head = lax.dynamic_index_in_dim(delta_t, head, 2, keepdims=False)
        scores = (
            jnp.einsum("tqd,tkd->tqk", query_head, key_head, preferred_element_type=jnp.float32)
            * scaling
        )
        attention = jnp.exp(scores - norm_head[:, :, None])
        grad_attention = jnp.einsum(
            "tqd,tkd->tqk", dout_head, value_head, preferred_element_type=jnp.float32
        )
        grad_scores = (attention * (grad_attention - delta_head[:, :, None])).astype(jnp.bfloat16)
        grad_q = (
            jnp.einsum("tqk,tkd->tqd", grad_scores, key_head, preferred_element_type=jnp.float32)
            * scaling
        )
        result = (grad_q,)
        grad_k = (
            jnp.einsum("tqk,tqd->tkd", grad_scores, query_head, preferred_element_type=jnp.float32)
            * scaling
        )
        grad_v = jnp.einsum(
            "tqk,tqd->tkd",
            attention.astype(jnp.bfloat16),
            dout_head,
            preferred_element_type=jnp.float32,
        )
        result = result + (grad_k, grad_v)
        return result

    stacked = lax.map(head_step, jnp.arange(head_count, dtype=jnp.int32))
    return tuple((merge_heads(member) for member in stacked))


def on_device(queries, key_vecs, value_vecs, outputs_fwd, grad_out, log_norm):
    rows_dev, width_cells, frames, channels = queries.shape
    head_count = log_norm.shape[3]
    head_dim = channels // head_count
    tiles_w = width_cells // 8
    reach_rows = 1 + 8 // rows_dev // 2
    quarter = min(rows_dev, 8)
    groups = rows_dev // quarter
    device_pos = lax.axis_index("sy")
    base_row = device_pos * rows_dev
    row_delta = jnp.einsum(
        "rwfhd,rwfhd->rwfh",
        grad_out.reshape(rows_dev, width_cells, frames, head_count, head_dim),
        outputs_fwd.reshape(rows_dev, width_cells, frames, head_count, head_dim),
        preferred_element_type=jnp.float32,
    )
    key_ext, value_ext = near_keys((key_vecs, value_vecs), reach_rows)
    first_row = base_row + 0
    row_starts = [first_row - first_row % 8 - 4 - base_row + reach_rows * rows_dev]
    key_window = key_windows(key_ext, row_starts, tiles_w)
    value_window = key_windows(value_ext, row_starts, tiles_w)
    query_t = query_tiles(queries, groups, quarter, tiles_w)
    dout_t = query_tiles(grad_out, groups, quarter, tiles_w)
    norm_t = query_tiles(log_norm, groups, quarter, tiles_w)
    delta_t = query_tiles(row_delta, groups, quarter, tiles_w)
    grad_q, grad_k, grad_v = query_pass(
        query_t, dout_t, norm_t, delta_t, key_window, value_window, head_dim
    )
    rows_ext = key_ext.shape[0]
    total_keys = fold_windows(grad_k, row_starts, rows_ext, tiles_w)
    total_values = fold_windows(grad_v, row_starts, rows_ext, tiles_w)
    result_keys, result_values = return_rows((total_keys, total_values), reach_rows, rows_dev)
    grad_keys = result_keys.astype(jnp.bfloat16)
    grad_values = result_values.astype(jnp.bfloat16)
    grad_queries = untile_queries(grad_q.astype(jnp.bfloat16), groups, quarter, tiles_w, frames)
    return (grad_queries, grad_keys, grad_values)


def solution(mesh):
    return jax.shard_map(
        on_device,
        mesh=mesh,
        in_specs=(
            P("sy", "groups", None, None),
            P("sy", "groups", None, None),
            P("sy", "groups", None, None),
            P("sy", "groups", None, None),
            P("sy", "groups", None, None),
            P("sy", "groups", None, None),
        ),
        out_specs=(
            P("sy", "groups", None, None),
            P("sy", "groups", None, None),
            P("sy", "groups", None, None),
        ),
        check_vma=False,
    )
```

profile of v0, /device:TPU:1, one launch (start us, length us, event | category | flops | bytes accessed | tf_op | source)
XLA Modules:
  0.0 687.7 jit_solution(1270664246547671306)
XLA Ops:
  4.8 3.0 collective-permute-start.3
  17.3 27.2 %collective-permute-done = bf16[4,32,2,1536]{3,2,1,0:T(2,128)(2,1)} collective-permute-done((bf16[4,32,2,1536]{3,2,1,0:T(2,128)(2,1)}, bf16[4,32,2,1536]{3,2,1,0:T(2,128)(2,1)}, u32[]{:S(2)}, u32[]{:S(2)}) %collective-permute-start) | collective-permute-done | bytes 786464 | tf_op jit(solution)/shard_map/ppermute | solution.py:10
  44.6 4.8 collective-permute-start.5
  51.0 18.8 %collective-permute-done.1 = bf16[4,32,2,1536]{3,2,1,0:T(2,128)(2,1)} collective-permute-done((bf16[4,32,2,1536]{3,2,1,0:T(2,128)(2,1)}, bf16[4,32,2,1536]{3,2,1,0:T(2,128)(2,1)}, u32[]{:S(2)}, u32[]{:S(2)}) %collective-permute-start.1) | collective-permute-done | bytes 786464 | tf_op jit(solution)/shard_map/ppermute | solution.py:10
  72.2 15.6 %collective-permute-done.4 = bf16[4,32,2,1536]{3,2,1,0:T(2,128)(2,1)} collective-permute-done((bf16[4,32,2,1536]{3,2,1,0:T(2,128)(2,1)}, bf16[4,32,2,1536]{3,2,1,0:T(2,128)(2,1)}, u32[]{:S(2)}, u32[]{:S(2)}) %collective-permute-start.4) | collective-permute-done | bytes 786464 | tf_op jit(solution)/shard_map/ppermute | solution.py:10
  87.9 5.1 collective-permute-start.7
  93.0 2.6 constant_dynamic-update-slice_fusion.9
  95.6 9.1 %collective-permute-done.5 = bf16[4,32,2,1536]{3,2,1,0:T(2,128)(2,1)S(1)} collective-permute-done((bf16[4,32,2,1536]{3,2,1,0:T(2,128)(2,1)}, bf16[4,32,2,1536]{3,2,1,0:T(2,128)(2,1)S(1)}, u32[]{:S(2)}, u32[]{:S(2)}) %collective-permute-start.5) | collective-permute-done | bytes 786464 | tf_op jit(solution)/shard_map/ppermute | solution.py:10
  114.7 7.2 %constant_dynamic-slice_fusion.6 = (bf16[16,32,2,1536]{3,2,1,0:T(2,128)(2,1)S(1)}, bf16[16,32,2,1536]{3,2,1,0:T(2,128)(2,1)S(1)}) fusion(bf16[20,32,2,1536]{3,2,1,0:T(2,128)(2,1)} %constant_dynamic-update-slice_fusion.5, s32[]{:T(128)S(6)} %select_n.25, bf16[20,32,2,1536]{3,2,1,0:T(2,128)(2,1)} %copy-done.1), kind=kLoop, calls=%fused_computation.77 | loop fusion | bytes 12582916 | tf_op jit(solution)/shard_map/dynamic_slice | solution.py:57
  121.9 3.2 constant_dynamic-slice_fusion.2
  125.1 5.9 pad_maximum_fusion.3
  131.0 7.2 %fusion.41 = (bf16[16,4,8,2,1536]{4,3,2,1,0:T(2,128)(2,1)S(1)}, bf16[16,4,8,2,1536]{4,3,2,1,0:T(2,128)(2,1)S(1)}) fusion(bf16[16,5,8,2,1536]{4,3,2,1,0:T(2,128)(2,1)S(1)} %bitcast.92), kind=kLoop, calls=%fused_computation.85 | loop fusion | bytes 12582912 | tf_op jit(solution)/shard_map/slice | solution.py:60
  138.2 8.1 %copy_bitcast_fusion.2 = bf16[1,4,16,16,2,1536]{5,4,3,2,1,0:T(2,128)(2,1)} fusion(bf16[16,4,8,2,1536]{4,3,2,1,0:T(2,128)(2,1)S(1)} %get-tuple-element.131, bf16[16,4,8,2,1536]{4,3,2,1,0:T(2,128)(2,1)S(1)} %get-tuple-element.130), kind=kLoop, calls=%fused_computation.41 | loop fusion | flops 3145728 | bytes 12582912 | tf_op jit(solution)/shard_map/transpose | solution.py:62
  146.3 13.6 %reshape.87 = bf16[4,512,1536]{2,1,0:T(8,128)(2,1)} reshape(bf16[1,4,16,16,2,1536]{5,4,3,2,1,0:T(2,128)(2,1)} %copy_bitcast_fusion.2) | data formatting | bytes 12582912 | tf_op jit(solution)/shard_map/reshape | solution.py:63
  159.9 6.7 pad_maximum_fusion.2
  166.7 7.2 %fusion.42 = (bf16[16,4,8,2,1536]{4,3,2,1,0:T(2,128)(2,1)S(1)}, bf16[16,4,8,2,1536]{4,3,2,1,0:T(2,128)(2,1)S(1)}) fusion(bf16[16,5,8,2,1536]{4,3,2,1,0:T(2,128)(2,1)S(1)} %bitcast.93), kind=kLoop, calls=%fused_computation.86 | loop fusion | bytes 12582912 | tf_op jit(solution)/shard_map/slice | solution.py:60
  173.9 8.1 %copy_bitcast_fusion.3 = bf16[1,4,16,16,2,1536]{5,4,3,2,1,0:T(2,128)(2,1)} fusion(bf16[16,4,8,2,1536]{4,3,2,1,0:T(2,128)(2,1)S(1)} %get-tuple-element.135, bf16[16,4,8,2,1536]{4,3,2,1,0:T(2,128)(2,1)S(1)} %get-tuple-element.134), kind=kLoop, calls=%fused_computation.42 | loop fusion | flops 3145728 | bytes 12582912 | tf_op jit(solution)/shard_map/transpose | solution.py:62
  182.0 13.6 %reshape.80 = bf16[4,512,1536]{2,1,0:T(8,128)(2,1)} reshape(bf16[1,4,16,16,2,1536]{5,4,3,2,1,0:T(2,128)(2,1)} %copy_bitcast_fusion.3) | data formatting | bytes 12582912 | tf_op jit(solution)/shard_map/reshape | solution.py:63
  195.6 150.4 %while.14 = (s32[]{:T(128)}, bf16[12,4,64,128]{3,2,1,0:T(8,128)(2,1)}, f32[12,4,512,128]{3,2,1,0:T(8,128)}, f32[12,4,512,128]{3,2,1,0:T(8,128)}, s32[12]{0:T(128...) while((s32[]{:T(128)}, ...), condition=%wide.region_1.2_spmd, body=%wide.region_0.1_spmd.sunk | while | flops 168853504 | bytes 6432513 | solution.py:147
  201.8 2.2 fusion.75
  204.0 2.2 fusion.76
  214.2 2.2 fusion.75
  226.7 2.2 fusion.75
  228.9 2.2 fusion.76
  239.1 2.2 fusion.75
  241.3 2.2 fusion.76
  251.6 2.2 fusion.75
  253.8 2.2 fusion.76
  264.1 2.2 fusion.75
  266.3 2.2 fusion.76
  276.6 2.2 fusion.75
  289.1 2.2 fusion.75
  291.3 2.3 fusion.76
  301.7 2.2 fusion.75
  303.9 2.2 fusion.76
  314.2 2.2 fusion.75
  316.4 2.2 fusion.76
  326.7 2.2 fusion.75
  339.1 2.3 fusion.75
  341.4 2.2 fusion.76
  346.0 17.8 %copy.47 = f32[4,512,12,128]{3,2,1,0:T(8,128)} copy(f32[4,512,12,128]{3,1,0,2:T(8,128)} %bitcast.96) | data formatting | bytes 25165824 | tf_op jit(solution)/shard_map/transpose | solution.py:104
  363.7 17.8 %reshape_reshape.6 = f32[1,4,16,16,2,1536]{5,4,3,2,1,0:T(2,128)} reshape(f32[4,512,12,128]{3,2,1,0:T(8,128)} %copy.47) | data formatting | bytes 25165824 | tf_op jit(solution)/shard_map/reshape;reshape | solution.py:84
  381.6 8.6 %fusion.36 = (f32[1,16,4,8,2,1536]{5,4,3,1,2,0:T(2,128)S(1)}, f32[1,16,4,8,2,1536]{5,4,3,1,2,0:T(2,128)S(1)}) fusion(f32[1,16,4,16,2,1536]{5,4,3,1,2,0:T(2,128)} %bitcast.84), kind=kLoop, calls=%fused_computation.80 | loop fusion | bytes 25165824 | tf_op jit(solution)/shard_map/slice | solution.py:86
  390.2 3.3 pad_add_fusion.1
  395.0 3.0 copy-done
  398.4 17.8 %copy.50 = f32[4,512,12,128]{3,2,1,0:T(8,128)} copy(f32[4,512,12,128]{3,1,0,2:T(8,128)} %bitcast.97) | data formatting | bytes 25165824 | tf_op jit(solution)/shard_map/transpose | solution.py:104
  416.2 17.8 %reshape_reshape.7 = f32[1,4,16,16,2,1536]{5,4,3,2,1,0:T(2,128)} reshape(f32[4,512,12,128]{3,2,1,0:T(8,128)} %copy.50) | data formatting | bytes 25165824 | tf_op jit(solution)/shard_map/reshape;reshape | solution.py:84
  434.1 8.6 %fusion.35 = (f32[1,16,4,8,2,1536]{5,4,3,1,2,0:T(2,128)S(1)}, f32[1,16,4,8,2,1536]{5,4,3,1,2,0:T(2,128)S(1)}) fusion(f32[1,16,4,16,2,1536]{5,4,3,1,2,0:T(2,128)} %bitcast.85), kind=kLoop, calls=%fused_computation.79 | loop fusion | bytes 25165824 | tf_op jit(solution)/shard_map/slice | solution.py:86
  442.7 3.3 pad_add_fusion
  447.9 5.9 fusion.24
  453.8 6.5 broadcast.29.clone.1
  460.3 10.5 %copy_dynamic-update-slice_fusion = f32[20,32,2,1536]{3,2,1,0:T(2,128)} fusion(f32[20,32,2,1536]{3,2,1,0:T(2,128)} %broadcast.29.clone.1, s32[]{:T(128)S(6)} %select_n.25, f32[16,32,2,1536]{3,1,2,0:T(8,128)} %get-tuple-element.138), kind=kLoop, calls=%fused_computation.43 | loop fusion | bytes 12582916 | tf_op jit(solution)/shard_map/dynamic_update_slice | solution.py:99
  470.8 5.3 fusion.37
  476.0 5.8 collective-permute-start.13
  482.0 6.5 broadcast.29.clone
  488.6 7.6 %copy_dynamic-update-slice_fusion.1 = f32[20,32,2,1536]{3,2,1,0:T(2,128)} fusion(f32[20,32,2,1536]{3,2,1,0:T(2,128)} %broadcast.29.clone, s32[]{:T(128)S(6)} %select_n.25, f32[16,32,2,1536]{3,1,2,0:T(8,128)S(1)} %bitcast.95), kind=kLoop, calls=%fused_computation.44 | loop fusion | bytes 12582916 | tf_op jit(solution)/shard_map/dynamic_update_slice | solution.py:99
  496.2 4.9 fusion.39
  501.0 77.9 %collective-permute-done.12 = f32[4,32,2,1536]{3,2,1,0:T(2,128)} collective-permute-done((f32[4,32,2,1536]{3,2,1,0:T(2,128)}, f32[4,32,2,1536]{3,2,1,0:T(2,128)}, u32[]{:S(2)}, u32[]{:S(2)}) %collective-permute-start.12) | collective-permute-done | bytes 1572896 | tf_op jit(solution)/shard_map/ppermute | solution.py:10
  578.9 51.5 %collective-permute-done.13 = f32[4,32,2,1536]{3,2,1,0:T(2,128)} collective-permute-done((f32[4,32,2,1536]{3,2,1,0:T(2,128)}, f32[4,32,2,1536]{3,2,1,0:T(2,128)}, u32[]{:S(2)}, u32[]{:S(2)}) %collective-permute-start.13) | collective-permute-done | bytes 1572896 | tf_op jit(solution)/shard_map/ppermute | solution.py:10
  630.4 3.6 collective-permute-start.9
  636.7 4.8 fusion.34
  641.5 25.4 %collective-permute-done.8 = f32[4,32,2,1536]{3,2,1,0:T(2,128)} collective-permute-done((f32[4,32,2,1536]{3,2,1,0:T(2,128)}, f32[4,32,2,1536]{3,2,1,0:T(2,128)}, u32[]{:S(2)}, u32[]{:S(2)}) %collective-permute-start.8) | collective-permute-done | bytes 1572896 | tf_op jit(solution)/shard_map/ppermute | solution.py:10
  666.9 15.5 %collective-permute-done.9 = f32[4,32,2,1536]{3,2,1,0:T(2,128)} collective-permute-done((f32[4,32,2,1536]{3,2,1,0:T(2,128)S(1)}, f32[4,32,2,1536]{3,2,1,0:T(2,128)}, u32[]{:S(2)}, u32[]{:S(2)}) %collective-permute-start.9) | collective-permute-done | bytes 1572896 | tf_op jit(solution)/shard_map/ppermute | solution.py:10
  682.4 4.8 fusion.33
  (141 shorter events, 111.6 us)
Async XLA Ops:
  0.6 9.0 %copy-start.2 = (bf16[4,32,2,1536]{3,2,1,0:T(2,128)(2,1)S(1)}, bf16[4,32,2,1536]{3,2,1,0:T(2,128)(2,1)}, u32[]{:S(2)}) copy-start(bf16[4,32,2,1536]{3,2,1,0:T(2,128)(2,1)} %param.12) | copy-start | bytes 2359300
  0.6 43.9 %collective-permute-start = (bf16[4,32,2,1536]{3,2,1,0:T(2,128)(2,1)}, bf16[4,32,2,1536]{3,2,1,0:T(2,128)(2,1)}, u32[]{:S(2)}, u32[]{:S(2)}) collective-permute-start(bf16[4,32,2,1536]{3,2,1,0:T(2,128)(2,1)} %param.9), channel_id=1, source_target_pairs={{14,0},{15,1},{0,2},{1,3},{2,4},{3,5},{4,6},{5,7},{6,8},{7,9},{8,1... | collective-permute-start | bytes 2359304 | tf_op jit(solution)/shard_map/ppermute | solution.py:10
  2.8 67.1 %collective-permute-start.1 = (bf16[4,32,2,1536]{3,2,1,0:T(2,128)(2,1)}, bf16[4,32,2,1536]{3,2,1,0:T(2,128)(2,1)}, u32[]{:S(2)}, u32[]{:S(2)}) collective-permute-start(bf16[4,32,2,1536]{3,2,1,0:T(2,128)(2,1)} %param.9), channel_id=1, source_target_pairs={{15,0},{0,1},{1,2},{2,3},{3,4},{4,5},{5,6},{6,7},{7,8},{8,9},{9,10... | collective-permute-start | bytes 2359304 | tf_op jit(solution)/shard_map/ppermute | solution.py:10
  4.8 102.7 %collective-permute-start.2 = (bf16[4,32,2,1536]{3,2,1,0:T(2,128)(2,1)}, bf16[4,32,2,1536]{3,2,1,0:T(2,128)(2,1)}, u32[]{:S(2)}, u32[]{:S(2)}) collective-permute-start(bf16[4,32,2,1536]{3,2,1,0:T(2,128)(2,1)} %param.9), channel_id=1, source_target_pairs={{1,0},{2,1},{3,2},{4,3},{5,4},{6,5},{7,6},{8,7},{9,8},{10,9},{11,1... | collective-permute-start | bytes 2359304 | tf_op jit(solution)/shard_map/ppermute | solution.py:10
  4.8 104.5 %collective-permute-start.3 = (bf16[4,32,2,1536]{3,2,1,0:T(2,128)(2,1)}, bf16[4,32,2,1536]{3,2,1,0:T(2,128)(2,1)}, u32[]{:S(2)}, u32[]{:S(2)}) collective-permute-start(bf16[4,32,2,1536]{3,2,1,0:T(2,128)(2,1)} %param.9), channel_id=1, source_target_pairs={{2,0},{3,1},{4,2},{5,3},{6,4},{7,5},{8,6},{9,7},{10,8},{11,9},{12,... | collective-permute-start | bytes 2359304 | tf_op jit(solution)/shard_map/ppermute | solution.py:10
  7.8 80.1 %collective-permute-start.4 = (bf16[4,32,2,1536]{3,2,1,0:T(2,128)(2,1)}, bf16[4,32,2,1536]{3,2,1,0:T(2,128)(2,1)}, u32[]{:S(2)}, u32[]{:S(2)}) collective-permute-start(bf16[4,32,2,1536]{3,2,1,0:T(2,128)(2,1)} %param.10), channel_id=1, source_target_pairs={{14,0},{15,1},{0,2},{1,3},{2,4},{3,5},{4,6},{5,7},{6,8},{7,9},{8,1... | collective-permute-start | bytes 2359304 | tf_op jit(solution)/shard_map/ppermute | solution.py:10
  10.8 5.6 copy-start.6
  13.4 58.2 %copy-start.4 = (bf16[4,32,2,1536]{3,2,1,0:T(2,128)(2,1)S(1)}, bf16[4,32,2,1536]{3,2,1,0:T(2,128)(2,1)}, u32[]{:S(2)}) copy-start(bf16[4,32,2,1536]{3,2,1,0:T(2,128)(2,1)} %param.9) | copy-start | bytes 2359300
  15.1 72.7 %copy-start.5 = (bf16[4,32,2,1536]{3,2,1,0:T(2,128)(2,1)S(1)}, bf16[4,32,2,1536]{3,2,1,0:T(2,128)(2,1)}, u32[]{:S(2)}) copy-start(bf16[4,32,2,1536]{3,2,1,0:T(2,128)(2,1)} %param.10) | copy-start | bytes 2359300
  44.6 60.1 %collective-permute-start.5 = (bf16[4,32,2,1536]{3,2,1,0:T(2,128)(2,1)}, bf16[4,32,2,1536]{3,2,1,0:T(2,128)(2,1)S(1)}, u32[]{:S(2)}, u32[]{:S(2)}) collective-permute-start(bf16[4,32,2,1536]{3,2,1,0:T(2,128)(2,1)} %param.10), channel_id=1, source_target_pairs={{15,0},{0,1},{1,2},{2,3},{3,4},{4,5},{5,6},{6,7},{7,8},{8,9},{9,10... | collective-permute-start | bytes 2359304 | tf_op jit(solution)/shard_map/ppermute | solution.py:10
  69.8 41.3 %collective-permute-start.6 = (bf16[4,32,2,1536]{3,2,1,0:T(2,128)(2,1)}, bf16[4,32,2,1536]{3,2,1,0:T(2,128)(2,1)S(1)}, u32[]{:S(2)}, u32[]{:S(2)}) collective-permute-start(bf16[4,32,2,1536]{3,2,1,0:T(2,128)(2,1)} %param.10), channel_id=1, source_target_pairs={{1,0},{2,1},{3,2},{4,3},{5,4},{6,5},{7,6},{8,7},{9,8},{10,9},{11,1... | collective-permute-start | bytes 2359304 | tf_op jit(solution)/shard_map/ppermute | solution.py:10
  87.9 25.1 %collective-permute-start.7 = (bf16[4,32,2,1536]{3,2,1,0:T(2,128)(2,1)S(1)}, bf16[4,32,2,1536]{3,2,1,0:T(2,128)(2,1)S(1)}, u32[]{:S(2)}, u32[]{:S(2)}) collective-permute-start(bf16[4,32,2,1536]{3,2,1,0:T(2,128)(2,1)S(1)} %copy-done.5), channel_id=1, source_target_pairs={{2,0},{3,1},{4,2},{5,3},{6,4},{7,5},{8,6},{9,7},{10,8},{11,9},{12,... | collective-permute-start | bytes 2359304 | tf_op jit(solution)/shard_map/ppermute | solution.py:10
  111.1 2.2 copy-start.1
  395.0 3.0 copy-start
  442.7 5.2 slice-start
  442.7 5.2 slice-start.1
  460.3 28.3 %slice-start.2 = ((s8[6291456]{0:T(1024)(128)(4,1)}), s8[4194304]{0:T(1024)(128)(4,1)S(1)}, s32[]{:S(2)}) async-start(s8[6291456]{0:T(1024)(128)(4,1)} %bitcast.94), calls=%async_computation.2 | async-start | bytes 8388608
  470.8 17.8 %slice-start.3 = ((s8[6291456]{0:T(1024)(128)(4,1)}), s8[2097152]{0:T(1024)(128)(4,1)S(1)}, s32[]{:S(2)}) async-start(s8[6291456]{0:T(1024)(128)(4,1)} %bitcast.94), calls=%async_computation.3 | async-start | bytes 4194304
  476.0 102.9 %collective-permute-start.12 = (f32[4,32,2,1536]{3,2,1,0:T(2,128)}, f32[4,32,2,1536]{3,2,1,0:T(2,128)}, u32[]{:S(2)}, u32[]{:S(2)}) collective-permute-start(f32[4,32,2,1536]{3,2,1,0:T(2,128)} %get-tuple-element.118), channel_id=1, source_target_pairs={{2,0},{3,1},{4,2},{5,3},{6,4},{7,5},{8,6},{9,7},{10,8},{11,9},{12,... | collective-permute-start | bytes 4718600 | tf_op jit(solution)/shard_map/ppermute | solution.py:10
  476.0 154.4 %collective-permute-start.13 = (f32[4,32,2,1536]{3,2,1,0:T(2,128)}, f32[4,32,2,1536]{3,2,1,0:T(2,128)}, u32[]{:S(2)}, u32[]{:S(2)}) collective-permute-start(f32[4,32,2,1536]{3,2,1,0:T(2,128)} %get-tuple-element.121), channel_id=1, source_target_pairs={{1,0},{2,1},{3,2},{4,3},{5,4},{6,5},{7,6},{8,7},{9,8},{10,9},{11,1... | collective-permute-start | bytes 4718600 | tf_op jit(solution)/shard_map/ppermute | solution.py:10
  481.8 148.6 %collective-permute-start.14 = (f32[4,32,2,1536]{3,2,1,0:T(2,128)}, f32[4,32,2,1536]{3,2,1,0:T(2,128)}, u32[]{:S(2)}, u32[]{:S(2)}) collective-permute-start(f32[4,32,2,1536]{3,2,1,0:T(2,128)} %get-tuple-element.120), channel_id=1, source_target_pairs={{15,0},{0,1},{1,2},{2,3},{3,4},{4,5},{5,6},{6,7},{7,8},{8,9},{9,10... | collective-permute-start | bytes 4718600 | tf_op jit(solution)/shard_map/ppermute | solution.py:10
  481.8 154.9 %collective-permute-start.15 = (f32[4,32,2,1536]{3,2,1,0:T(2,128)}, f32[4,32,2,1536]{3,2,1,0:T(2,128)}, u32[]{:S(2)}, u32[]{:S(2)}) collective-permute-start(f32[4,32,2,1536]{3,2,1,0:T(2,128)} %get-tuple-element.119), channel_id=1, source_target_pairs={{14,0},{15,1},{0,2},{1,3},{2,4},{3,5},{4,6},{5,7},{6,8},{7,9},{8,1... | collective-permute-start | bytes 4718600 | tf_op jit(solution)/shard_map/ppermute | solution.py:10
  496.1 137.8 %copy-start.3 = (bf16[12,4,64,128]{3,2,1,0:T(8,128)(2,1)S(1)}, bf16[12,4,64,128]{3,2,1,0:T(8,128)(2,1)}, u32[]{:S(2)}) copy-start(bf16[12,4,64,128]{3,2,1,0:T(8,128)(2,1)} %get-tuple-element.62) | copy-start | bytes 2359300
  501.0 140.5 %collective-permute-start.10 = (f32[4,32,2,1536]{3,2,1,0:T(2,128)}, f32[4,32,2,1536]{3,2,1,0:T(2,128)}, u32[]{:S(2)}, u32[]{:S(2)}) collective-permute-start(f32[4,32,2,1536]{3,2,1,0:T(2,128)} %get-tuple-element.126), channel_id=1, source_target_pairs={{15,0},{0,1},{1,2},{2,3},{3,4},{4,5},{5,6},{6,7},{7,8},{8,9},{9,10... | collective-permute-start | bytes 4718600 | tf_op jit(solution)/shard_map/ppermute | solution.py:10
  578.9 62.6 %collective-permute-start.11 = (f32[4,32,2,1536]{3,2,1,0:T(2,128)}, f32[4,32,2,1536]{3,2,1,0:T(2,128)}, u32[]{:S(2)}, u32[]{:S(2)}) collective-permute-start(f32[4,32,2,1536]{3,2,1,0:T(2,128)} %get-tuple-element.125), channel_id=1, source_target_pairs={{14,0},{15,1},{0,2},{1,3},{2,4},{3,5},{4,6},{5,7},{6,8},{7,9},{8,1... | collective-permute-start | bytes 4718600 | tf_op jit(solution)/shard_map/ppermute | solution.py:10
  630.4 36.5 %collective-permute-start.8 = (f32[4,32,2,1536]{3,2,1,0:T(2,128)}, f32[4,32,2,1536]{3,2,1,0:T(2,128)}, u32[]{:S(2)}, u32[]{:S(2)}) collective-permute-start(f32[4,32,2,1536]{3,2,1,0:T(2,128)} %get-tuple-element.124), channel_id=1, source_target_pairs={{2,0},{3,1},{4,2},{5,3},{6,4},{7,5},{8,6},{9,7},{10,8},{11,9},{12,... | collective-permute-start | bytes 4718600 | tf_op jit(solution)/shard_map/ppermute | solution.py:10
  630.4 52.0 %collective-permute-start.9 = (f32[4,32,2,1536]{3,2,1,0:T(2,128)S(1)}, f32[4,32,2,1536]{3,2,1,0:T(2,128)}, u32[]{:S(2)}, u32[]{:S(2)}) collective-permute-start(f32[4,32,2,1536]{3,2,1,0:T(2,128)S(1)} %get-tuple-element.127), channel_id=1, source_target_pairs={{1,0},{2,1},{3,2},{4,3},{5,4},{6,5},{7,6},{8,7},{9,8},{10,9},{11,1... | collective-permute-start | bytes 4718600 | tf_op jit(solution)/shard_map/ppermute | solution.py:10
where the time goes:
time: 698 us; the launch traced here: 688 us
  waiting for transfers between devices  241 us (35%)
  local copies, waits for them, and re-layouts  231 us (33%)
  matrix products  109 us (16%)
  other arithmetic  51.6 us (7%)
  loops' own time  27 us (4%)
  starting transfers between devices  26.7 us (4%)
    ppermute x16, waiting for transfers between devices, shifted(): return lax.ppermute(block, axis, route)  241 us
    another operation x2, local copies, waits for them, and re-layouts, fold_windows(): split_cols = window_terms.reshape(groups, tiles_w, 16, 16, frames, trailing)  35.7 us
    transpose x2, local copies, waits for them, and re-layouts, merge_heads(): moved = jnp.moveaxis(stacked, 0, 2)  35.6 us
    reshape x2, local copies, waits for them, and re-layouts, key_windows(): return windows.reshape(len(row_starts) * tiles_w, -1, windows.shape[-1])  27.2 us
    another operation x1, loops' own time, query_pass(): stacked = lax.map(head_step, jnp.arange(head_count, dtype=jnp.int32))  27 us
    ppermute x16, starting transfers between devices, shifted(): return lax.ppermute(block, axis, route)  26.7 us
    dot_general x12, matrix products, head_step(): jnp.einsum('tqk,tqd->tkd', grad_scores, query_head, preferred_element_typ...  26.3 us
    dot_general x12, matrix products, head_step(): jnp.einsum('tqk,tqd->tkd', attention.astype(jnp.bfloat16), dout_head, pre...  26.2 us
  transfers between devices with their start and end apart: 16, of which 8 were waited for; matrix products, arithmetic and copies ran while one was open for 7% of the time, Pallas kernels for 0%

commit v1 on v0

v1 whole, which is shorter than its diff:
```python
import functools

import jax
import jax.numpy as jnp
from jax import lax
from jax.experimental import pallas as pl
from jax.experimental.pallas import tpu as pltpu
from jax.sharding import PartitionSpec as P

HEAD_DIM = 128
TILE = 8
MARGIN = 4


def swap(block, pairs_of):
    n = lax.axis_size("sy")
    route = []
    for i in range(n):
        route.append((i, pairs_of(i, n)))
    return lax.ppermute(block, "sy", route)


def core_partner(i, n):
    return i ^ 1


def chip_neighbour(i, n):
    return (i + 1) % n if i % 2 else (i - 1) % n


def window_kernel(q_ref, do_ref, lse_ref, delta_ref, k_ref, v_ref, dq_ref, dk_ref, dv_ref, *, tiles, tf, mf):
    scaling = HEAD_DIM ** (-0.5)
    rows = q_ref.shape[0]
    krows = k_ref.shape[0]
    width = dk_ref.shape[1]
    span = tf + 2 * mf
    dk_ref[...] = jnp.zeros_like(dk_ref)
    dv_ref[...] = jnp.zeros_like(dv_ref)
    for b in range(tiles):
        kw = k_ref[:, b * tf : b * tf + span, :].reshape(krows * span, HEAD_DIM)
        vw = v_ref[:, b * tf : b * tf + span, :].reshape(krows * span, HEAD_DIM)
        qb = q_ref[:, b * tf : (b + 1) * tf, :].reshape(rows * tf, HEAD_DIM)
        dob = do_ref[:, b * tf : (b + 1) * tf, :].reshape(rows * tf, HEAD_DIM)
        nt = (((1,), (1,)), ((), ()))
        scores = lax.dot_general(kw, qb, nt, preferred_element_type=jnp.float32) * scaling
        attention = jnp.exp(scores - lse_ref[b])
        grad_attention = lax.dot_general(vw, dob, nt, preferred_element_type=jnp.float32)
        grad_scores = (attention * (grad_attention - delta_ref[b])).astype(jnp.bfloat16)
        grad_v = jnp.dot(attention.astype(jnp.bfloat16), dob, preferred_element_type=jnp.float32)
        grad_k = jnp.dot(grad_scores, qb, preferred_element_type=jnp.float32) * scaling
        grad_q = (
            jnp.dot(grad_scores.T, kw, preferred_element_type=jnp.float32) * scaling
        )
        dq_ref[:, b * tf : (b + 1) * tf, :] = grad_q.reshape(rows, tf, HEAD_DIM).astype(dq_ref.dtype)
        grad_k = grad_k.reshape(krows, span, HEAD_DIM)
        grad_v = grad_v.reshape(krows, span, HEAD_DIM)
        start = b * tf - mf
        pieces = []
        if start < 0:
            pieces.append((0, width + start, -start))
            pieces.append((-start, 0, span + start))
        elif start + span > width:
            pieces.append((0, start, width - start))
            pieces.append((width - start, 0, start + span - width))
        else:
            pieces.append((0, start, span))
        for src, dst, size in pieces:
            dk_ref[:, dst : dst + size, :] += grad_k[:, src : src + size, :]
            dv_ref[:, dst : dst + size, :] += grad_v[:, src : src + size, :]


def window_pass(q, do, lse_t, delta_t, k_ext, v_ext, tiles, tf, mf):
    rows, width, channels = q.shape
    krows = k_ext.shape[0]
    ext = k_ext.shape[1]
    heads = channels // HEAD_DIM
    kernel = functools.partial(window_kernel, tiles=tiles, tf=tf, mf=mf)
    qspec = pl.BlockSpec((rows, width, HEAD_DIM), lambda h: (0, 0, h))
    kspec = pl.BlockSpec((krows, ext, HEAD_DIM), lambda h: (0, 0, h))
    sspec = pl.BlockSpec((None, tiles, 1, rows * tf), lambda h: (h, 0, 0, 0))
    ospec = pl.BlockSpec((krows, width, HEAD_DIM), lambda h: (0, 0, h))
    pairs = tiles * rows * tf * krows * (tf + 2 * mf) * heads
    cost = pl.CostEstimate(
        flops=10 * pairs * HEAD_DIM,
        transcendentals=pairs,
        bytes_accessed=2 * (2 * q.size + 2 * k_ext.size + q.size) + 8 * krows * width * channels,
    )
    return pl.pallas_call(
        kernel,
        grid=(heads,),
        in_specs=[qspec, qspec, sspec, sspec, kspec, kspec],
        out_specs=[qspec, ospec, ospec],
        out_shape=[
            jax.ShapeDtypeStruct((rows, width, channels), jnp.bfloat16),
            jax.ShapeDtypeStruct((krows, width, channels), jnp.float32),
            jax.ShapeDtypeStruct((krows, width, channels), jnp.float32),
        ],
        cost_estimate=cost,
    )(q, do, lse_t, delta_t, k_ext, v_ext)


def stats_tiles(stats, tiles, tf):
    rows, width, heads = stats.shape
    tiled = stats.reshape(rows, tiles, tf, heads)
    tiled = jnp.transpose(tiled, (3, 1, 0, 2))
    return tiled.reshape(heads, tiles, 1, rows * tf)


def on_device(queries, key_vecs, value_vecs, outputs_fwd, grad_out, log_norm):
    rows, width_cells, frames, channels = queries.shape
    heads = log_norm.shape[3]
    width = width_cells * frames
    tiles = width_cells // TILE
    tf = TILE * frames
    mf = MARGIN * frames

    q = queries.reshape(rows, width, channels)
    do = grad_out.reshape(rows, width, channels)
    row_delta = jnp.einsum(
        "rwhd,rwhd->rwh",
        grad_out.reshape(rows, width, heads, HEAD_DIM),
        outputs_fwd.reshape(rows, width, heads, HEAD_DIM),
        preferred_element_type=jnp.float32,
    )
    lse_t = stats_tiles(log_norm.reshape(rows, width, heads), tiles, tf)
    delta_t = stats_tiles(row_delta, tiles, tf)

    kv_own = jnp.stack([key_vecs.reshape(rows, width, channels), value_vecs.reshape(rows, width, channels)])
    kv_partner = swap(kv_own, core_partner)
    kv_cross = swap(kv_own, chip_neighbour)
    kv_forward = swap(kv_cross, core_partner)
    kv_rows = jnp.concatenate([kv_own, kv_partner, kv_cross, kv_forward], axis=1)
    kv_ext = jnp.concatenate([kv_rows[:, :, width - mf :], kv_rows, kv_rows[:, :, :mf]], axis=2)

    dq, dk, dv = window_pass(q, do, lse_t, delta_t, kv_ext[0], kv_ext[1], tiles, tf, mf)

    parts = jnp.stack([dk, dv]).reshape(2, 4, rows, width, channels)
    back = swap(parts[:, 1:4:2], core_partner)
    own_total = parts[:, 0] + back[:, 0]
    cross_total = parts[:, 2] + back[:, 1]
    arrived = swap(cross_total, chip_neighbour)
    total = own_total + arrived
    grad_keys = total[0].astype(jnp.bfloat16).reshape(rows, width_cells, frames, channels)
    grad_values = total[1].astype(jnp.bfloat16).reshape(rows, width_cells, frames, channels)
    grad_queries = dq.reshape(rows, width_cells, frames, channels)
    return (grad_queries, grad_keys, grad_values)


def solution(mesh):
    spec = P("sy", "groups", None, None)
    return jax.shard_map(
        on_device,
        mesh=mesh,
        in_specs=(spec,) * 6,
        out_specs=(spec,) * 3,
        check_vma=False,
    )
```

time: 698 us -> 187 us (0.27); the launches traced: 688 us -> 186 us
  local copies, waits for them, and re-layouts: 231 us -> 27.5 us
  waiting for transfers between devices: 241 us -> 108 us
  matrix products: 109 us -> 0 us
  other arithmetic: 51.6 us -> 23 us
  loops' own time: 27 us -> 0 us
  starting transfers between devices: 26.7 us -> 7.84 us
  Pallas kernels: 0 us -> 18.6 us
    ppermute x16 -> x5, waiting for transfers between devices: 241 us -> 108 us  [swap(): return lax.ppermute(block, 'sy', route)]
    dot_general x60 -> x0, matrix products: 109 us -> none  [the longest x12 26.3 us: head_step(): jnp.einsum('tqk,tqd->tkd', grad_scores, query_head, preferred_element_typ...]
    another operation x5 -> x3, local copies, waits for them, and re-layouts: 48.7 us -> 5.6 us  [on_device(): jnp.stack([key_vecs.reshape(rows, width, channels), value_vecs.reshape(ro...]
    slice x9 -> x2, local copies, waits for them, and re-layouts: 45.7 us -> 3.54 us  [the longest x1 3.39 us: on_device(): back = swap(parts[:, 1:4:2], core_partner)]
    transpose x5 -> x2, local copies, waits for them, and re-layouts: 35.9 us -> 0.35 us  [stats_tiles(): tiled = jnp.transpose(tiled, (3, 1, 0, 2))]
    another operation x1 -> x0, loops' own time: 27 us -> none  [query_pass(): stacked = lax.map(head_step, jnp.arange(head_count, dtype=jnp.int32))]
    reshape x8 -> x7, local copies, waits for them, and re-layouts: 32.9 us -> 9.49 us  [the longest x1 2.95 us: on_device(): q = queries.reshape(rows, width, channels)]
    ppermute x16 -> x5, starting transfers between devices: 26.7 us -> 7.84 us  [swap(): return lax.ppermute(block, 'sy', route)]
  transfers between devices with their start and end apart: 16 -> 5, of which waited for: 8 -> 3; matrix products, arithmetic and copies ran while one was open for 7% -> 6% of each run, Pallas kernels for 0% -> 0%
where the time goes in v1:
time: 187 us; the launch traced here: 186 us
  waiting for transfers between devices  108 us (58%)
  local copies, waits for them, and re-layouts  27.5 us (15%)
  other arithmetic  23 us (12%)
  Pallas kernels  18.6 us (10%)
  starting transfers between devices  7.84 us (4%)
    ppermute x5, waiting for transfers between devices, swap(): return lax.ppermute(block, 'sy', route)  108 us
    pallas_call x1, Pallas kernels, window_pass(): pl.pallas_call(kernel, grid=(heads,), in_specs=[qspec, qspec, sspec, sspe...  18.6 us
    another operation x1, other arithmetic, on_device(): parts = jnp.stack([dk, dv]).reshape(2, 4, rows, width, channels)  11.2 us
    ppermute x5, starting transfers between devices, swap(): return lax.ppermute(block, 'sy', route)  7.84 us
    another operation x3, local copies, waits for them, and re-layouts, on_device(): jnp.stack([key_vecs.reshape(rows, width, channels), value_vecs.reshape(ro...  5.6 us
    concatenate x1, other arithmetic, on_device(): jnp.concatenate([kv_rows[:, :, width - mf:], kv_rows, kv_rows[:, :, :mf]]...  4.97 us
  transfers between devices with their start and end apart: 5, of which 3 were waited for; matrix products, arithmetic and copies ran while one was open for 6% of the time, Pallas kernels for 0%

profile of v1, /device:TPU:1, one launch (start us, length us, event | category | flops | bytes accessed | tf_op | source)
XLA Modules:
  0.0 185.9 jit_solution(6113789058428904584)
XLA Ops:
  0.6 0.0 copy-start.1
  0.6 0.0 copy-start.3
  0.7 0.0 copy-start.2
  0.7 2.4 %stack_reshape.6 = bf16[1,4,64,1536]{3,2,1,0:T(8,128)(2,1)S(1)} reshape(bf16[4,32,2,1536]{3,2,1,0:T(2,128)(2,1)} %param.7) | data formatting | bytes 1572864 | tf_op jit(solution)/shard_map/stack;reshape | solution.py:128
  3.1 1.0 constant_dynamic-update-slice_fusion.1
  4.0 2.3 %stack_reshape.7 = bf16[1,4,64,1536]{3,2,1,0:T(8,128)(2,1)S(1)} reshape(bf16[4,32,2,1536]{3,2,1,0:T(2,128)(2,1)} %param.8) | data formatting | bytes 1572864 | tf_op jit(solution)/shard_map/stack;reshape | solution.py:128
  6.3 0.9 constant_dynamic-update-slice_fusion
  7.2 2.6 %collective-permute-start.1 = (bf16[2,4,64,1536]{3,2,1,0:T(8,128)(2,1)}, bf16[2,4,64,1536]{3,2,1,0:T(8,128)(2,1)}, u32[]{:S(2)}, u32[]{:S(2)}) collective-permute-start(bf16[2,4,64,1536]{3,2,1,0:T(8,128)(2,1)} %constant_dynamic-update-slice_fusion), channel_id=1, source_target_pairs={{0,15},{1,2},{2,1},{3,4},{4,3},{5,6},{6,5},{7,8},{8,7},{9,10},{10,... | collective-permute-start | bytes 4718600 | tf_op jit(solution)/shard_map/ppermute | solution.py:20
  9.9 2.9 %collective-permute-start = (bf16[2,4,64,1536]{3,2,1,0:T(8,128)(2,1)}, bf16[2,4,64,1536]{3,2,1,0:T(8,128)(2,1)}, u32[]{:S(2)}, u32[]{:S(2)}) collective-permute-start(bf16[2,4,64,1536]{3,2,1,0:T(8,128)(2,1)} %constant_dynamic-update-slice_fusion), channel_id=1, source_target_pairs={{0,1},{1,0},{2,3},{3,2},{4,5},{5,4},{6,7},{7,6},{8,9},{9,8},{10,11... | collective-permute-start | bytes 4718600 | tf_op jit(solution)/shard_map/ppermute | solution.py:20
  12.7 32.4 %collective-permute-done.1 = bf16[2,4,64,1536]{3,2,1,0:T(8,128)(2,1)} collective-permute-done((bf16[2,4,64,1536]{3,2,1,0:T(8,128)(2,1)}, bf16[2,4,64,1536]{3,2,1,0:T(8,128)(2,1)}, u32[]{:S(2)}, u32[]{:S(2)}) %collective-permute-start.1) | collective-permute-done | bytes 1572896 | tf_op jit(solution)/shard_map/ppermute | solution.py:20
  45.1 0.0 collective-permute-start.2
  45.1 0.0 copy-done.1
  45.1 1.2 reshape.44.do_ref
  46.3 0.5 reshape.46
  46.8 0.0 copy-done.3
  46.9 0.1 copy.12
  47.0 0.2 copy.13
  47.2 0.7 reshape.45.lse_ref
  47.9 3.0 %reshape.43.q_ref = bf16[4,64,1536]{2,1,0:T(8,128)(2,1)} reshape(bf16[4,32,2,1536]{3,2,1,0:T(2,128)(2,1)} %param.6) | data formatting | bytes 1572864 | tf_op jit(solution)/shard_map/reshape | solution.py:117
  50.9 0.0 copy-done.2
  50.9 0.5 reshape.47
  51.4 0.6 fusion.11
  52.0 0.2 copy.25
  52.2 0.7 reshape.49.delta_ref
  52.9 0.0 collective-permute-done
  52.9 0.0 collective-permute-done.2
  52.9 5.0 %fusion = bf16[2,16,80,1536]{3,2,1,0:T(8,128)(2,1)S(1)} fusion(bf16[2,4,64,1536]{3,2,1,0:T(8,128)(2,1)} %collective-permute-done.2, bf16[2,4,64,1536]{3,2,1,0:T(8,128)(2,1)} %collective-permute-done.1, bf16[2,4,64,1536]{3,2,1,0:T(8,128)(2,1)} %collective-permute-done, bf16[2,4,64,1536]{3,2,1,0:T(8,128)(2,1)} %constant_dynamic-update-slice_fusion), kind=kLoop, calls=%fused_computation.6 | loop fusion | flops 94371840 | bytes 14155776 | tf_op jit(solution)/shard_map/concatenate | solution.py:133
  57.9 3.3 %slice_bitcast_fusion = (bf16[16,80,1536]{2,1,0:T(8,128)(2,1)}, bf16[16,80,1536]{2,1,0:T(8,128)(2,1)}) fusion(bf16[2,16,80,1536]{3,2,1,0:T(8,128)(2,1)S(1)} %fusion), kind=kLoop, calls=%fused_computation.13 | loop fusion | bytes 15728640 | tf_op jit(solution)/shard_map/squeeze | solution.py:135
  61.2 18.6 %shard_map.85 = (bf16[4,64,1536]{2,1,0:T(8,128)(2,1)}, f32[16,64,1536]{2,1,0:T(8,128)}, f32[16,64,1536]{2,1,0:T(8,128)}) custom-call(bf16[4,64,1536]{2,1,0:T(8,128)(2,1)} %reshape.43.q_ref, bf16[4,64,1536]{2,1,0:T(8,128)(2,1)} %reshape.44.do_ref, f32[12,4,1,64]{3,2,1,0:T(1,128)} %reshape.45.lse_ref, f32[12,4,1,64]{3,2,1,0:T(1,128)} %reshape.49.delta_ref, ...), custom_call_target="tpu_custom_call" | custom-call | flops 2013265920 | bytes 22806528 | tf_op jit(solution)/shard_map/pallas_call | solution.py:88
  79.8 11.2 %pad_maximum_fusion = f32[2,4,4,64,1536]{4,3,2,1,0:T(8,128)} fusion(f32[1,4,4,64,1536]{4,3,2,1,0:T(8,128)} %bitcast.43, f32[1,4,4,64,1536]{4,3,2,1,0:T(8,128)} %bitcast.38), kind=kLoop, calls=%fused_computation.2 | loop fusion | flops 3145728 | bytes 25165824 | tf_op jit(solution)/shard_map/stack | solution.py:137
  91.0 0.0 slice-start
  91.0 0.0 slice-start.2
  91.0 3.4 %slice.40 = f32[2,2,4,64,1536]{4,3,2,1,0:T(8,128)S(1)} slice(f32[2,4,4,64,1536]{4,3,2,1,0:T(8,128)} %pad_maximum_fusion), slice={[0:2:1], [1:4:2], [0:4:1], [0:64:1], [0:1536:1]} | slice | bytes 12582912 | tf_op jit(solution)/shard_map/slice | solution.py:138
  94.4 0.0 slice-start.1
  94.4 0.0 slice-start.3
  94.4 0.6 copy.27
  95.0 0.6 collective-permute-start.3
  95.6 9.8 %collective-permute-done.3 = f32[2,2,4,64,1536]{4,3,2,0,1:T(8,128)S(1)} collective-permute-done((f32[2,2,4,64,1536]{4,3,2,0,1:T(8,128)S(1)}, f32[2,2,4,64,1536]{4,3,2,0,1:T(8,128)S(1)}, u32[]{:S(2)}, u32[]{:S(2)}) %collective-permute-start.3) | collective-permute-done | bytes 6291488 | tf_op jit(solution)/shard_map/ppermute | solution.py:20
  105.4 0.0 slice-done
  105.4 0.0 slice-done.2
  105.4 0.0 slice-done.1
  105.4 0.0 slice-done.3
  105.5 0.0 copy-start
  105.5 2.6 %fusion.10 = f32[2,4,64,1536]{3,2,1,0:T(8,128)} fusion(f32[1,4,4,64,1536]{4,3,2,1,0:T(8,128)S(1)} %bitcast.42, f32[1,4,4,64,1536]{4,3,2,1,0:T(8,128)S(1)} %bitcast.47, f32[2,2,4,64,1536]{4,3,2,0,1:T(8,128)S(1)} %collective-permute-done.3), kind=kLoop, calls=%fused_computation.23 | loop fusion | flops 1572864 | bytes 18874368 | tf_op jit(solution)/shard_map/add | solution.py:140
  108.1 1.1 copy-done
  109.2 1.7 collective-permute-start.4
  110.9 2.8 %reshape.50 = bf16[4,32,2,1536]{3,2,1,0:T(2,128)(2,1)} reshape(bf16[4,64,1536]{2,1,0:T(8,128)(2,1)} %get-tuple-element.6) | data formatting | bytes 1572864 | tf_op jit(solution)/shard_map/reshape | solution.py:145
  113.8 66.0 %collective-permute-done.4 = f32[2,4,64,1536]{3,2,1,0:T(8,128)S(1)} collective-permute-done((f32[2,4,64,1536]{3,2,1,0:T(8,128)}, f32[2,4,64,1536]{3,2,1,0:T(8,128)S(1)}, u32[]{:S(2)}, u32[]{:S(2)}) %collective-permute-start.4) | collective-permute-done | bytes 3145760 | tf_op jit(solution)/shard_map/ppermute | solution.py:20
  179.8 3.6 %fusion.7 = bf16[2,4,64,1536]{3,2,1,0:T(8,128)(2,1)S(1)} fusion(f32[2,4,64,1536]{3,2,1,0:T(8,128)S(1)} %collective-permute-done.4, f32[1,4,4,64,1536]{4,3,2,1,0:T(8,128)} %bitcast.39, f32[1,4,4,64,1536]{4,3,2,1,0:T(8,128)} %bitcast.44, f32[2,2,4,64,1536]{4,3,2,0,1:T(8,128)} %copy-done), kind=kLoop, calls=%fused_computation.20 | loop fusion | flops 3145728 | bytes 20447232 | tf_op jit(solution)/shard_map/convert.1
  183.4 0.1 fusion.12
  183.6 1.2 convert_element_type.11
  184.8 1.2 convert_element_type.10
  (2 shorter events, 0.0 us)
Async XLA Ops:
  0.6 44.5 %copy-start.1 = (bf16[4,32,2,1536]{3,2,1,0:T(2,128)(2,1)S(1)}, bf16[4,32,2,1536]{3,2,1,0:T(2,128)(2,1)}, u32[]{:S(2)}) copy-start(bf16[4,32,2,1536]{3,2,1,0:T(2,128)(2,1)} %param.10) | copy-start | bytes 2359300
  0.6 46.2 %copy-start.3 = (f32[4,32,2,12]{1,2,3,0:T(2,128)S(1)}, f32[4,32,2,12]{1,2,3,0:T(2,128)}, u32[]{:S(2)}) copy-start(f32[4,32,2,12]{1,2,3,0:T(2,128)} %param.11) | copy-start | bytes 36868
  0.7 50.2 %copy-start.2 = (bf16[4,32,2,1536]{3,2,1,0:T(2,128)(2,1)S(1)}, bf16[4,32,2,1536]{3,2,1,0:T(2,128)(2,1)}, u32[]{:S(2)}) copy-start(bf16[4,32,2,1536]{3,2,1,0:T(2,128)(2,1)} %param.9) | copy-start | bytes 2359300
  7.2 37.9 %collective-permute-start.1 = (bf16[2,4,64,1536]{3,2,1,0:T(8,128)(2,1)}, bf16[2,4,64,1536]{3,2,1,0:T(8,128)(2,1)}, u32[]{:S(2)}, u32[]{:S(2)}) collective-permute-start(bf16[2,4,64,1536]{3,2,1,0:T(8,128)(2,1)} %constant_dynamic-update-slice_fusion), channel_id=1, source_target_pairs={{0,15},{1,2},{2,1},{3,4},{4,3},{5,6},{6,5},{7,8},{8,7},{9,10},{10,... | collective-permute-start | bytes 4718600 | tf_op jit(solution)/shard_map/ppermute | solution.py:20
  9.9 43.1 %collective-permute-start = (bf16[2,4,64,1536]{3,2,1,0:T(8,128)(2,1)}, bf16[2,4,64,1536]{3,2,1,0:T(8,128)(2,1)}, u32[]{:S(2)}, u32[]{:S(2)}) collective-permute-start(bf16[2,4,64,1536]{3,2,1,0:T(8,128)(2,1)} %constant_dynamic-update-slice_fusion), channel_id=1, source_target_pairs={{0,1},{1,0},{2,3},{3,2},{4,5},{5,4},{6,7},{7,6},{8,9},{9,8},{10,11... | collective-permute-start | bytes 4718600 | tf_op jit(solution)/shard_map/ppermute | solution.py:20
  45.1 7.8 %collective-permute-start.2 = (bf16[2,4,64,1536]{3,2,1,0:T(8,128)(2,1)}, bf16[2,4,64,1536]{3,2,1,0:T(8,128)(2,1)}, u32[]{:S(2)}, u32[]{:S(2)}) collective-permute-start(bf16[2,4,64,1536]{3,2,1,0:T(8,128)(2,1)} %collective-permute-done.1), channel_id=1, source_target_pairs={{0,1},{1,0},{2,3},{3,2},{4,5},{5,4},{6,7},{7,6},{8,9},{9,8},{10,11... | collective-permute-start | bytes 4718600 | tf_op jit(solution)/shard_map/ppermute | solution.py:20
  91.0 14.4 %slice-start = ((s8[6291456]{0:T(1024)(128)(4,1)}), s8[4194304]{0:T(1024)(128)(4,1)S(1)}, s32[]{:S(2)}) async-start(s8[6291456]{0:T(1024)(128)(4,1)} %bitcast.40), calls=%async_computation | async-start | bytes 8388608
  91.0 14.4 %slice-start.2 = ((s8[6291456]{0:T(1024)(128)(4,1)}), s8[4194304]{0:T(1024)(128)(4,1)S(1)}, s32[]{:S(2)}) async-start(s8[6291456]{0:T(1024)(128)(4,1)} %bitcast.45), calls=%async_computation.2 | async-start | bytes 8388608
  94.4 11.0 %slice-start.1 = ((s8[6291456]{0:T(1024)(128)(4,1)}), s8[2097152]{0:T(1024)(128)(4,1)S(1)}, s32[]{:S(2)}) async-start(s8[6291456]{0:T(1024)(128)(4,1)} %bitcast.40), calls=%async_computation.1 | async-start | bytes 4194304
  94.4 11.0 %slice-start.3 = ((s8[6291456]{0:T(1024)(128)(4,1)}), s8[2097152]{0:T(1024)(128)(4,1)S(1)}, s32[]{:S(2)}) async-start(s8[6291456]{0:T(1024)(128)(4,1)} %bitcast.45), calls=%async_computation.3 | async-start | bytes 4194304
  95.0 10.4 %collective-permute-start.3 = (f32[2,2,4,64,1536]{4,3,2,0,1:T(8,128)S(1)}, f32[2,2,4,64,1536]{4,3,2,0,1:T(8,128)S(1)}, u32[]{:S(2)}, u32[]{:S(2)}) collective-permute-start(f32[2,2,4,64,1536]{4,3,2,0,1:T(8,128)S(1)} %copy.27), channel_id=1, source_target_pairs={{0,1},{1,0},{2,3},{3,2},{4,5},{5,4},{6,7},{7,6},{8,9},{9,8},{10,11... | collective-permute-start | bytes 18874376 | tf_op jit(solution)/shard_map/ppermute | solution.py:20
  105.5 3.7 %copy-start = (f32[2,2,4,64,1536]{4,3,2,0,1:T(8,128)}, f32[2,2,4,64,1536]{4,3,2,0,1:T(8,128)S(1)}, u32[]{:S(2)}) copy-start(f32[2,2,4,64,1536]{4,3,2,0,1:T(8,128)S(1)} %collective-permute-done.3) | copy-start | bytes 18874372
  109.2 70.6 %collective-permute-start.4 = (f32[2,4,64,1536]{3,2,1,0:T(8,128)}, f32[2,4,64,1536]{3,2,1,0:T(8,128)S(1)}, u32[]{:S(2)}, u32[]{:S(2)}) collective-permute-start(f32[2,4,64,1536]{3,2,1,0:T(8,128)} %fusion.10), channel_id=1, source_target_pairs={{0,15},{1,2},{2,1},{3,4},{4,3},{5,6},{6,5},{7,8},{8,7},{9,10},{10,... | collective-permute-start | bytes 9437192 | tf_op jit(solution)/shard_map/ppermute | solution.py:20

commit v2 on v1

--- a/solution.py
+++ b/solution.py
@@ -28,14 +28,19 @@
     return (i + 1) % n if i % 2 else (i - 1) % n
 
 
-def window_kernel(q_ref, do_ref, lse_ref, delta_ref, k_ref, v_ref, dq_ref, dk_ref, dv_ref, *, tiles, tf, mf):
+def window_kernel(
+    q_ref, do_ref, lse_ref, delta_ref, k_ref, v_ref, dq_ref, own_ref, intra_ref, cross_ref, *, tiles, tf, mf
+):
     scaling = HEAD_DIM ** (-0.5)
     rows = q_ref.shape[0]
     krows = k_ref.shape[0]
-    width = dk_ref.shape[1]
+    width = own_ref.shape[2]
     span = tf + 2 * mf
-    dk_ref[...] = jnp.zeros_like(dk_ref)
-    dv_ref[...] = jnp.zeros_like(dv_ref)
+    own_ref[...] = jnp.zeros_like(own_ref)
+    intra_ref[...] = jnp.zeros_like(intra_ref)
+    cross_ref[...] = jnp.zeros_like(cross_ref)
+    targets = [own_ref, intra_ref.at[0], cross_ref, intra_ref.at[1]]
+    blocks = krows // rows
     for b in range(tiles):
         kw = k_ref[:, b * tf : b * tf + span, :].reshape(krows * span, HEAD_DIM)
         vw = v_ref[:, b * tf : b * tf + span, :].reshape(krows * span, HEAD_DIM)
@@ -48,12 +53,10 @@
         grad_scores = (attention * (grad_attention - delta_ref[b])).astype(jnp.bfloat16)
         grad_v = jnp.dot(attention.astype(jnp.bfloat16), dob, preferred_element_type=jnp.float32)
         grad_k = jnp.dot(grad_scores, qb, preferred_element_type=jnp.float32) * scaling
-        grad_q = (
-            jnp.dot(grad_scores.T, kw, preferred_element_type=jnp.float32) * scaling
-        )
+        grad_q = jnp.dot(grad_scores.T, kw, preferred_element_type=jnp.float32) * scaling
         dq_ref[:, b * tf : (b + 1) * tf, :] = grad_q.reshape(rows, tf, HEAD_DIM).astype(dq_ref.dtype)
-        grad_k = grad_k.reshape(krows, span, HEAD_DIM)
-        grad_v = grad_v.reshape(krows, span, HEAD_DIM)
+        grad_k = grad_k.reshape(blocks, rows, span, HEAD_DIM)
+        grad_v = grad_v.reshape(blocks, rows, span, HEAD_DIM)
         start = b * tf - mf
         pieces = []
         if start < 0:
@@ -64,9 +67,10 @@
             pieces.append((width - start, 0, start + span - width))
         else:
             pieces.append((0, start, span))
-        for src, dst, size in pieces:
-            dk_ref[:, dst : dst + size, :] += grad_k[:, src : src + size, :]
-            dv_ref[:, dst : dst + size, :] += grad_v[:, src : src + size, :]
+        for block, target in enumerate(targets):
+            for src, dst, size in pieces:
+                target[0, :, dst : dst + size, :] += grad_k[block, :, src : src + size, :]
+                target[1, :, dst : dst + size, :] += grad_v[block, :, src : src + size, :]
 
 
 def window_pass(q, do, lse_t, delta_t, k_ext, v_ext, tiles, tf, mf):
@@ -78,22 +82,25 @@
     qspec = pl.BlockSpec((rows, width, HEAD_DIM), lambda h: (0, 0, h))
     kspec = pl.BlockSpec((krows, ext, HEAD_DIM), lambda h: (0, 0, h))
     sspec = pl.BlockSpec((None, tiles, 1, rows * tf), lambda h: (h, 0, 0, 0))
-    ospec = pl.BlockSpec((krows, width, HEAD_DIM), lambda h: (0, 0, h))
+    pspec = pl.BlockSpec((2, rows, width, HEAD_DIM), lambda h: (0, 0, 0, h))
+    ispec = pl.BlockSpec((2, 2, rows, width, HEAD_DIM), lambda h: (0, 0, 0, 0, h))
     pairs = tiles * rows * tf * krows * (tf + 2 * mf) * heads
     cost = pl.CostEstimate(
         flops=10 * pairs * HEAD_DIM,
         transcendentals=pairs,
         bytes_accessed=2 * (2 * q.size + 2 * k_ext.size + q.size) + 8 * krows * width * channels,
     )
+    part = jax.ShapeDtypeStruct((2, rows, width, channels), jnp.float32)
     return pl.pallas_call(
         kernel,
         grid=(heads,),
         in_specs=[qspec, qspec, sspec, sspec, kspec, kspec],
-        out_specs=[qspec, ospec, ospec],
+        out_specs=[qspec, pspec, ispec, pspec],
         out_shape=[
             jax.ShapeDtypeStruct((rows, width, channels), jnp.bfloat16),
-            jax.ShapeDtypeStruct((krows, width, channels), jnp.float32),
-            jax.ShapeDtypeStruct((krows, width, channels), jnp.float32),
+            part,
+            jax.ShapeDtypeStruct((2, 2, rows, width, channels), jnp.float32),
+            part,
         ],
         cost_estimate=cost,
     )(q, do, lse_t, delta_t, k_ext, v_ext)
@@ -125,21 +132,24 @@
     lse_t = stats_tiles(log_norm.reshape(rows, width, heads), tiles, tf)
     delta_t = stats_tiles(row_delta, tiles, tf)
 
-    kv_own = jnp.stack([key_vecs.reshape(rows, width, channels), value_vecs.reshape(rows, width, channels)])
+    kv_own = (key_vecs.reshape(rows, width, channels), value_vecs.reshape(rows, width, channels))
     kv_partner = swap(kv_own, core_partner)
     kv_cross = swap(kv_own, chip_neighbour)
     kv_forward = swap(kv_cross, core_partner)
-    kv_rows = jnp.concatenate([kv_own, kv_partner, kv_cross, kv_forward], axis=1)
-    kv_ext = jnp.concatenate([kv_rows[:, :, width - mf :], kv_rows, kv_rows[:, :, :mf]], axis=2)
 
-    dq, dk, dv = window_pass(q, do, lse_t, delta_t, kv_ext[0], kv_ext[1], tiles, tf, mf)
+    def extended(member):
+        joined = jnp.concatenate(
+            [kv_own[member], kv_partner[member], kv_cross[member], kv_forward[member]], axis=0
+        )
+        return jnp.concatenate([joined[:, width - mf :], joined, joined[:, :mf]], axis=1)
 
-    parts = jnp.stack([dk, dv]).reshape(2, 4, rows, width, channels)
-    back = swap(parts[:, 1:4:2], core_partner)
-    own_total = parts[:, 0] + back[:, 0]
-    cross_total = parts[:, 2] + back[:, 1]
+    dq, own, intra, cross = window_pass(q, do, lse_t, delta_t, extended(0), extended(1), tiles, tf, mf)
+
+    back = swap(intra, core_partner)
+    own_total = own + back[0]
+    cross_total = (cross + back[1]).astype(jnp.bfloat16)
     arrived = swap(cross_total, chip_neighbour)
-    total = own_total + arrived
+    total = own_total + arrived.astype(jnp.float32)
     grad_keys = total[0].astype(jnp.bfloat16).reshape(rows, width_cells, frames, channels)
     grad_values = total[1].astype(jnp.bfloat16).reshape(rows, width_cells, frames, channels)
     grad_queries = dq.reshape(rows, width_cells, frames, channels)

time: 187 us -> 129 us (0.69)
  waiting for transfers between devices: 108 us -> 56.4 us
  other arithmetic: 23 us -> 15.6 us
  local copies, waits for them, and re-layouts: 27.5 us -> 29.6 us
    ppermute x5 -> x8, waiting for transfers between devices: 108 us -> 56.4 us  [swap(): return lax.ppermute(block, 'sy', route)]
    another operation x2 -> x1, other arithmetic: 14.8 us -> 3.18 us  [the longest x1 11.2 us: on_device(): parts = jnp.stack([dk, dv]).reshape(2, 4, rows, width, channels)]
    reshape x0 -> x2, local copies, waits for them, and re-layouts: none -> 6.03 us  [the longest x1 3.08 us: on_device(): value_vecs.reshape(rows, width, channels)]
    convert_element_type x0 -> x1, other arithmetic: none -> 5.89 us  [on_device(): cross_total = (cross + back[1]).astype(jnp.bfloat16)]
    another operation x3 -> x0, local copies, waits for them, and re-layouts: 5.6 us -> none  [on_device(): jnp.stack([key_vecs.reshape(rows, width, channels), value_vecs.reshape(ro...]
    unnamed x19 -> x17, local copies, waits for them, and re-layouts: 2.82 us -> 7.27 us
    squeeze x1 -> x0, local copies, waits for them, and re-layouts: 3.32 us -> none  [on_device(): kv_ext[1]]
    slice x1 -> x2, local copies, waits for them, and re-layouts: 3.39 us -> 0.11 us  [extended(): joined[:, width - mf:]]
  transfers between devices with their start and end apart: 5 -> 8, of which waited for: 3 -> 4; matrix products, arithmetic and copies ran while one was open for 6% -> 20% of each run, Pallas kernels for 0% -> 0%
where the time goes in v2:
time: 129 us; the launch traced here: 128 us
  waiting for transfers between devices  56.4 us (44%)
  local copies, waits for them, and re-layouts  29.6 us (23%)
  Pallas kernels  18.1 us (14%)
  other arithmetic  15.6 us (12%)
  starting transfers between devices  7.88 us (6%)
    ppermute x8, waiting for transfers between devices, swap(): return lax.ppermute(block, 'sy', route)  56.4 us
    pallas_call x1, Pallas kernels, window_pass(): pl.pallas_call(kernel, grid=(heads,), in_specs=[qspec, qspec, sspec, sspe...  18.1 us
    ppermute x8, starting transfers between devices, swap(): return lax.ppermute(block, 'sy', route)  7.88 us
    unnamed x17, local copies, waits for them, and re-layouts  7.27 us
    convert_element_type x1, other arithmetic, on_device(): cross_total = (cross + back[1]).astype(jnp.bfloat16)  5.89 us
    concatenate x2, other arithmetic, extended(): jnp.concatenate([joined[:, width - mf:], joined, joined[:, :mf]], axis=1)  4.34 us
    another operation x1, other arithmetic  3.18 us
    reshape x1, local copies, waits for them, and re-layouts, on_device(): value_vecs.reshape(rows, width, channels)  3.08 us
  transfers between devices with their start and end apart: 8, of which 4 were waited for; matrix products, arithmetic and copies ran while one was open for 20% of the time, Pallas kernels for 0%

profile of v2, /device:TPU:1, one launch (start us, length us, event | category | flops | bytes accessed | tf_op | source)
XLA Modules:
  0.0 128.3 jit_solution(595957270575986134)
XLA Ops:
  0.6 0.0 copy-start.3
  0.6 0.0 copy-start.1
  0.7 3.1 %reshape.50 = bf16[4,64,1536]{2,1,0:T(8,128)(2,1)} reshape(bf16[4,32,2,1536]{3,2,1,0:T(2,128)(2,1)} %param.8) | data formatting | bytes 1572864 | tf_op jit(solution)/shard_map/reshape | solution.py:135
  3.7 2.6 %collective-permute-start.4 = (bf16[4,64,1536]{2,1,0:T(8,128)(2,1)}, bf16[4,64,1536]{2,1,0:T(8,128)(2,1)}, u32[]{:S(2)}, u32[]{:S(2)}) collective-permute-start(bf16[4,64,1536]{2,1,0:T(8,128)(2,1)} %reshape.50), channel_id=1, source_target_pairs={{0,15},{1,2},{2,1},{3,4},{4,3},{5,6},{6,5},{7,8},{8,7},{9,10},{10,... | collective-permute-start | bytes 2359304 | tf_op jit(solution)/shard_map/ppermute | solution.py:20
  6.4 3.0 %reshape.49 = bf16[4,64,1536]{2,1,0:T(8,128)(2,1)} reshape(bf16[4,32,2,1536]{3,2,1,0:T(2,128)(2,1)} %param.7) | data formatting | bytes 1572864 | tf_op jit(solution)/shard_map/reshape | solution.py:135
  9.3 0.0 collective-permute-start.1
  9.3 2.9 %collective-permute-start.3 = (bf16[4,64,1536]{2,1,0:T(8,128)(2,1)}, bf16[4,64,1536]{2,1,0:T(8,128)(2,1)}, u32[]{:S(2)}, u32[]{:S(2)}) collective-permute-start(bf16[4,64,1536]{2,1,0:T(8,128)(2,1)} %reshape.50), channel_id=1, source_target_pairs={{0,1},{1,0},{2,3},{3,2},{4,5},{5,4},{6,7},{7,6},{8,9},{9,8},{10,11... | collective-permute-start | bytes 2359304 | tf_op jit(solution)/shard_map/ppermute | solution.py:20
  12.2 0.1 collective-permute-start
  12.3 0.0 copy-done.3
  12.3 1.5 %reshape.46 = bf16[4,64,12,128]{3,2,1,0:T(8,128)(2,1)} reshape(bf16[4,32,2,1536]{3,2,1,0:T(2,128)(2,1)S(1)} %copy-done.3) | data formatting | bytes 1572864 | tf_op jit(solution)/shard_map/reshape | solution.py:129
  13.8 0.0 copy-done.1
  13.8 0.0 copy-start.4
  13.8 1.5 %reshape.45 = bf16[4,64,12,128]{3,2,1,0:T(8,128)(2,1)} reshape(bf16[4,32,2,1536]{3,2,1,0:T(2,128)(2,1)S(1)} %copy-done.1) | data formatting | bytes 1572864 | tf_op jit(solution)/shard_map/reshape | solution.py:128
  15.3 1.2 constant_dynamic-update-slice_fusion.7
  16.5 2.2 %fusion.5 = f32[4,64,12]{2,1,0:T(8,128)S(1)} fusion(bf16[4,64,12,128]{3,2,1,0:T(8,128)(2,1)} %reshape.45, bf16[4,64,12,128]{3,2,1,0:T(8,128)(2,1)} %reshape.46), kind=kLoop, calls=%fused_computation.10 | loop fusion | flops 1569792 | bytes 1585152
  18.6 3.0 %reshape.43.do_ref = bf16[4,64,1536]{2,1,0:T(8,128)(2,1)} reshape(bf16[4,32,2,1536]{3,2,1,0:T(2,128)(2,1)} %param.10) | data formatting | bytes 1572864 | tf_op jit(solution)/shard_map/reshape | solution.py:125
  21.6 0.0 copy-done.4
  21.6 0.1 copy.9
  21.7 0.2 copy.10
  21.9 0.7 reshape.44.lse_ref
  22.7 3.0 %reshape.42.q_ref = bf16[4,64,1536]{2,1,0:T(8,128)(2,1)} reshape(bf16[4,32,2,1536]{3,2,1,0:T(2,128)(2,1)} %param.6) | data formatting | bytes 1572864 | tf_op jit(solution)/shard_map/reshape | solution.py:124
  25.6 0.2 copy.19
  25.8 0.7 reshape.48.delta_ref
  26.5 1.2 constant_dynamic-update-slice_fusion.3
  27.7 5.5 %collective-permute-done.4 = bf16[4,64,1536]{2,1,0:T(8,128)(2,1)} collective-permute-done((bf16[4,64,1536]{2,1,0:T(8,128)(2,1)}, bf16[4,64,1536]{2,1,0:T(8,128)(2,1)}, u32[]{:S(2)}, u32[]{:S(2)}) %collective-permute-start.4) | collective-permute-done | bytes 786464 | tf_op jit(solution)/shard_map/ppermute | solution.py:20
  33.2 0.0 collective-permute-start.5
  33.2 8.4 %collective-permute-done.1 = bf16[4,64,1536]{2,1,0:T(8,128)(2,1)} collective-permute-done((bf16[4,64,1536]{2,1,0:T(8,128)(2,1)}, bf16[4,64,1536]{2,1,0:T(8,128)(2,1)}, u32[]{:S(2)}, u32[]{:S(2)}) %collective-permute-start.1) | collective-permute-done | bytes 786464 | tf_op jit(solution)/shard_map/ppermute | solution.py:20
  41.6 0.0 collective-permute-start.2
  41.6 0.0 collective-permute-done.3
  41.6 1.2 constant_dynamic-update-slice_fusion.6
  42.8 1.2 constant_dynamic-update-slice_fusion.5
  44.0 0.0 collective-permute-done
  44.0 1.2 constant_dynamic-update-slice_fusion.2
  45.2 1.2 constant_dynamic-update-slice_fusion.1
  46.4 0.0 collective-permute-done.5
  46.4 0.1 constant_dynamic-update-slice_fusion.4
  46.5 0.1 fusion.6
  46.5 0.0 collective-permute-done.2
  46.5 0.1 constant_dynamic-update-slice_fusion
  46.6 0.1 fusion.7
  46.7 2.2 %pad_maximum_fusion.1.v_ref = bf16[16,80,1536]{2,1,0:T(8,128)(2,1)} fusion(bf16[16,8,1536]{2,1,0:T(8,128)(2,1)S(1)} %get-tuple-element.12, bf16[16,64,1536]{2,1,0:T(8,128)(2,1)S(1)} %constant_dynamic-update-slice_fusion.4, bf16[16,8,1536]{2,1,0:T(8,128)(2,1)S(1)} %get-tuple-element.11), kind=kLoop, calls=%fused_computation.1 | loop fusion | flops 11796480 | bytes 7864320 | tf_op jit(solution)/shard_map/concatenate | solution.py:144
  48.9 2.1 %pad_maximum_fusion.k_ref = bf16[16,80,1536]{2,1,0:T(8,128)(2,1)} fusion(bf16[16,8,1536]{2,1,0:T(8,128)(2,1)S(1)} %get-tuple-element.14, bf16[16,64,1536]{2,1,0:T(8,128)(2,1)S(1)} %constant_dynamic-update-slice_fusion, bf16[16,8,1536]{2,1,0:T(8,128)(2,1)S(1)} %get-tuple-element.13), kind=kLoop, calls=%fused_computation | loop fusion | flops 11796480 | bytes 7864320 | tf_op jit(solution)/shard_map/concatenate | solution.py:144
  51.0 18.1 %shard_map.85 = (bf16[4,64,1536]{2,1,0:T(8,128)(2,1)}, f32[2,4,64,1536]{3,2,1,0:T(8,128)}, f32[2,2,4,64,1536]{4,3,2,1,0:T(8,128)}, f32[2,4,64,1536]{3,2,1,0:T(8,128)}) custom-call(bf16[4,64,1536]{2,1,0:T(8,128)(2,1)} %reshape.42.q_ref, bf16[4,64,1536]{2,1,0:T(8,128)(2,1)} %reshape.43.do_ref, f32[12,4,1,64]{3,2,1,0:T(1,128)} %reshape.44.lse_ref, ...), custom_call_target="tpu_custom_call" | custom-call | flops 2013265920 | bytes 22806528 | tf_op jit(solution)/shard_map/pallas_call | solution.py:94
  69.2 0.6 collective-permute-start.6
  69.7 10.0 %collective-permute-done.6 = f32[2,2,4,64,1536]{4,3,2,1,0:T(8,128)S(1)} collective-permute-done((f32[2,2,4,64,1536]{4,3,2,1,0:T(8,128)}, f32[2,2,4,64,1536]{4,3,2,1,0:T(8,128)S(1)}, u32[]{:S(2)}, u32[]{:S(2)}) %collective-permute-start.6) | collective-permute-done | bytes 6291488 | tf_op jit(solution)/shard_map/ppermute | solution.py:20
  79.7 0.0 copy-start
  79.7 0.0 copy-start.2
  79.7 5.9 %fusion.1 = bf16[2,4,64,1536]{3,2,1,0:T(8,128)(2,1)} fusion(f32[2,4,64,1536]{3,2,1,0:T(8,128)} %get-tuple-element.10, f32[2,2,4,64,1536]{4,3,2,1,0:T(8,128)S(1)} %collective-permute-done.6), kind=kLoop, calls=%fused_computation.4 | loop fusion | flops 1572864 | bytes 7864320 | tf_op jit(solution)/shard_map/convert_element_type | solution.py:150
  85.6 0.0 copy-done
  85.6 1.7 %collective-permute-start.7 = (bf16[2,4,64,1536]{3,2,1,0:T(8,128)(2,1)}, bf16[2,4,64,1536]{3,2,1,0:T(8,128)(2,1)}, u32[]{:S(2)}, u32[]{:S(2)}) collective-permute-start(bf16[2,4,64,1536]{3,2,1,0:T(8,128)(2,1)} %fusion.1), channel_id=1, source_target_pairs={{0,15},{1,2},{2,1},{3,4},{4,3},{5,6},{6,5},{7,8},{8,7},{9,10},{10,... | collective-permute-start | bytes 4718600 | tf_op jit(solution)/shard_map/ppermute | solution.py:20
  87.4 2.8 %reshape.51 = bf16[4,32,2,1536]{3,2,1,0:T(2,128)(2,1)} reshape(bf16[4,64,1536]{2,1,0:T(8,128)(2,1)} %get-tuple-element.7) | data formatting | bytes 1572864 | tf_op jit(solution)/shard_map/reshape | solution.py:155
  90.2 32.4 %collective-permute-done.7 = bf16[2,4,64,1536]{3,2,1,0:T(8,128)(2,1)} collective-permute-done((bf16[2,4,64,1536]{3,2,1,0:T(8,128)(2,1)}, bf16[2,4,64,1536]{3,2,1,0:T(8,128)(2,1)}, u32[]{:S(2)}, u32[]{:S(2)}) %collective-permute-start.7) | collective-permute-done | bytes 1572896 | tf_op jit(solution)/shard_map/ppermute | solution.py:20
  122.6 0.0 copy-done.2
  122.6 3.2 %fusion.4 = bf16[2,4,64,1536]{3,2,1,0:T(8,128)(2,1)S(1)} fusion(f32[2,4,64,1536]{3,2,1,0:T(8,128)S(1)} %copy-done.2, f32[2,2,4,64,1536]{4,3,2,1,0:T(8,128)} %copy-done, bf16[2,4,64,1536]{3,2,1,0:T(8,128)(2,1)} %collective-permute-done.7), kind=kLoop, calls=%fused_computation.8 | loop fusion | flops 3145728 | bytes 9437184 | tf_op jit(solution)/shard_map/convert.1
  125.8 0.1 fusion.8
  125.9 1.2 convert_element_type.19
  127.1 1.2 convert_element_type.18
Async XLA Ops:
  0.6 11.6 %copy-start.3 = (bf16[4,32,2,1536]{3,2,1,0:T(2,128)(2,1)S(1)}, bf16[4,32,2,1536]{3,2,1,0:T(2,128)(2,1)}, u32[]{:S(2)}) copy-start(bf16[4,32,2,1536]{3,2,1,0:T(2,128)(2,1)} %param.9) | copy-start | bytes 2359300
  0.6 13.1 %copy-start.1 = (bf16[4,32,2,1536]{3,2,1,0:T(2,128)(2,1)S(1)}, bf16[4,32,2,1536]{3,2,1,0:T(2,128)(2,1)}, u32[]{:S(2)}) copy-start(bf16[4,32,2,1536]{3,2,1,0:T(2,128)(2,1)} %param.10) | copy-start | bytes 2359300
  3.7 29.5 %collective-permute-start.4 = (bf16[4,64,1536]{2,1,0:T(8,128)(2,1)}, bf16[4,64,1536]{2,1,0:T(8,128)(2,1)}, u32[]{:S(2)}, u32[]{:S(2)}) collective-permute-start(bf16[4,64,1536]{2,1,0:T(8,128)(2,1)} %reshape.50), channel_id=1, source_target_pairs={{0,15},{1,2},{2,1},{3,4},{4,3},{5,6},{6,5},{7,8},{8,7},{9,10},{10,... | collective-permute-start | bytes 2359304 | tf_op jit(solution)/shard_map/ppermute | solution.py:20
  9.3 32.3 %collective-permute-start.1 = (bf16[4,64,1536]{2,1,0:T(8,128)(2,1)}, bf16[4,64,1536]{2,1,0:T(8,128)(2,1)}, u32[]{:S(2)}, u32[]{:S(2)}) collective-permute-start(bf16[4,64,1536]{2,1,0:T(8,128)(2,1)} %reshape.49), channel_id=1, source_target_pairs={{0,15},{1,2},{2,1},{3,4},{4,3},{5,6},{6,5},{7,8},{8,7},{9,10},{10,... | collective-permute-start | bytes 2359304 | tf_op jit(solution)/shard_map/ppermute | solution.py:20
  9.3 32.3 %collective-permute-start.3 = (bf16[4,64,1536]{2,1,0:T(8,128)(2,1)}, bf16[4,64,1536]{2,1,0:T(8,128)(2,1)}, u32[]{:S(2)}, u32[]{:S(2)}) collective-permute-start(bf16[4,64,1536]{2,1,0:T(8,128)(2,1)} %reshape.50), channel_id=1, source_target_pairs={{0,1},{1,0},{2,3},{3,2},{4,5},{5,4},{6,7},{7,6},{8,9},{9,8},{10,11... | collective-permute-start | bytes 2359304 | tf_op jit(solution)/shard_map/ppermute | solution.py:20
  12.2 31.8 %collective-permute-start = (bf16[4,64,1536]{2,1,0:T(8,128)(2,1)}, bf16[4,64,1536]{2,1,0:T(8,128)(2,1)}, u32[]{:S(2)}, u32[]{:S(2)}) collective-permute-start(bf16[4,64,1536]{2,1,0:T(8,128)(2,1)} %reshape.49), channel_id=1, source_target_pairs={{0,1},{1,0},{2,3},{3,2},{4,5},{5,4},{6,7},{7,6},{8,9},{9,8},{10,11... | collective-permute-start | bytes 2359304 | tf_op jit(solution)/shard_map/ppermute | solution.py:20
  13.8 7.8 %copy-start.4 = (f32[4,32,2,12]{1,2,3,0:T(2,128)S(1)}, f32[4,32,2,12]{1,2,3,0:T(2,128)}, u32[]{:S(2)}) copy-start(f32[4,32,2,12]{1,2,3,0:T(2,128)} %param.11) | copy-start | bytes 36868
  33.2 13.2 %collective-permute-start.5 = (bf16[4,64,1536]{2,1,0:T(8,128)(2,1)}, bf16[4,64,1536]{2,1,0:T(8,128)(2,1)S(1)}, u32[]{:S(2)}, u32[]{:S(2)}) collective-permute-start(bf16[4,64,1536]{2,1,0:T(8,128)(2,1)} %collective-permute-done.4), channel_id=1, source_target_pairs={{0,1},{1,0},{2,3},{3,2},{4,5},{5,4},{6,7},{7,6},{8,9},{9,8},{10,11... | collective-permute-start | bytes 2359304 | tf_op jit(solution)/shard_map/ppermute | solution.py:20
  41.6 4.9 %collective-permute-start.2 = (bf16[4,64,1536]{2,1,0:T(8,128)(2,1)}, bf16[4,64,1536]{2,1,0:T(8,128)(2,1)S(1)}, u32[]{:S(2)}, u32[]{:S(2)}) collective-permute-start(bf16[4,64,1536]{2,1,0:T(8,128)(2,1)} %collective-permute-done.1), channel_id=1, source_target_pairs={{0,1},{1,0},{2,3},{3,2},{4,5},{5,4},{6,7},{7,6},{8,9},{9,8},{10,11... | collective-permute-start | bytes 2359304 | tf_op jit(solution)/shard_map/ppermute | solution.py:20
  69.2 10.6 %collective-permute-start.6 = (f32[2,2,4,64,1536]{4,3,2,1,0:T(8,128)}, f32[2,2,4,64,1536]{4,3,2,1,0:T(8,128)S(1)}, u32[]{:S(2)}, u32[]{:S(2)}) collective-permute-start(f32[2,2,4,64,1536]{4,3,2,1,0:T(8,128)} %get-tuple-element.9), channel_id=1, source_target_pairs={{0,1},{1,0},{2,3},{3,2},{4,5},{5,4},{6,7},{7,6},{8,9},{9,8},{10,11... | collective-permute-start | bytes 18874376 | tf_op jit(solution)/shard_map/ppermute | solution.py:20
  79.7 5.9 %copy-start = (f32[2,2,4,64,1536]{4,3,2,1,0:T(8,128)}, f32[2,2,4,64,1536]{4,3,2,1,0:T(8,128)S(1)}, u32[]{:S(2)}) copy-start(f32[2,2,4,64,1536]{4,3,2,1,0:T(8,128)S(1)} %collective-permute-done.6) | copy-start | bytes 18874372
  79.7 42.9 %copy-start.2 = (f32[2,4,64,1536]{3,2,1,0:T(8,128)S(1)}, f32[2,4,64,1536]{3,2,1,0:T(8,128)}, u32[]{:S(2)}) copy-start(f32[2,4,64,1536]{3,2,1,0:T(8,128)} %get-tuple-element.8) | copy-start | bytes 9437188
  85.6 37.0 %collective-permute-start.7 = (bf16[2,4,64,1536]{3,2,1,0:T(8,128)(2,1)}, bf16[2,4,64,1536]{3,2,1,0:T(8,128)(2,1)}, u32[]{:S(2)}, u32[]{:S(2)}) collective-permute-start(bf16[2,4,64,1536]{3,2,1,0:T(8,128)(2,1)} %fusion.1), channel_id=1, source_target_pairs={{0,15},{1,2},{2,1},{3,4},{4,3},{5,6},{6,5},{7,8},{8,7},{9,10},{10,... | collective-permute-start | bytes 4718600 | tf_op jit(solution)/shard_map/ppermute | solution.py:20

commit v3 on v2

--- a/solution.py
+++ b/solution.py
@@ -73,29 +73,31 @@
                 target[1, :, dst : dst + size, :] += grad_v[block, :, src : src + size, :]
 
 
-def window_pass(q, do, lse_t, delta_t, k_ext, v_ext, tiles, tf, mf):
-    rows, width, channels = q.shape
+def window_pass(q, do, lse_t, delta_t, k_ext, v_ext, tiles, tf, mf, first):
+    rows, width, _ = q.shape
     krows = k_ext.shape[0]
     ext = k_ext.shape[1]
+    channels = k_ext.shape[2]
     heads = channels // HEAD_DIM
     kernel = functools.partial(window_kernel, tiles=tiles, tf=tf, mf=mf)
-    qspec = pl.BlockSpec((rows, width, HEAD_DIM), lambda h: (0, 0, h))
+    qspec = pl.BlockSpec((rows, width, HEAD_DIM), lambda h: (0, 0, h + first))
+    dqspec = pl.BlockSpec((rows, width, HEAD_DIM), lambda h: (0, 0, h))
     kspec = pl.BlockSpec((krows, ext, HEAD_DIM), lambda h: (0, 0, h))
-    sspec = pl.BlockSpec((None, tiles, 1, rows * tf), lambda h: (h, 0, 0, 0))
+    sspec = pl.BlockSpec((None, tiles, 1, rows * tf), lambda h: (h + first, 0, 0, 0))
     pspec = pl.BlockSpec((2, rows, width, HEAD_DIM), lambda h: (0, 0, 0, h))
     ispec = pl.BlockSpec((2, 2, rows, width, HEAD_DIM), lambda h: (0, 0, 0, 0, h))
     pairs = tiles * rows * tf * krows * (tf + 2 * mf) * heads
     cost = pl.CostEstimate(
         flops=10 * pairs * HEAD_DIM,
         transcendentals=pairs,
-        bytes_accessed=2 * (2 * q.size + 2 * k_ext.size + q.size) + 8 * krows * width * channels,
+        bytes_accessed=2 * (3 * rows * width * channels + 2 * k_ext.size) + 8 * krows * width * channels,
     )
     part = jax.ShapeDtypeStruct((2, rows, width, channels), jnp.float32)
     return pl.pallas_call(
         kernel,
         grid=(heads,),
         in_specs=[qspec, qspec, sspec, sspec, kspec, kspec],
-        out_specs=[qspec, pspec, ispec, pspec],
+        out_specs=[dqspec, pspec, ispec, pspec],
         out_shape=[
             jax.ShapeDtypeStruct((rows, width, channels), jnp.bfloat16),
             part,
@@ -132,24 +134,38 @@
     lse_t = stats_tiles(log_norm.reshape(rows, width, heads), tiles, tf)
     delta_t = stats_tiles(row_delta, tiles, tf)
 
-    kv_own = (key_vecs.reshape(rows, width, channels), value_vecs.reshape(rows, width, channels))
-    kv_partner = swap(kv_own, core_partner)
-    kv_cross = swap(kv_own, chip_neighbour)
-    kv_forward = swap(kv_cross, core_partner)
+    chunks = 2 if heads % 2 == 0 else 1
+    size = channels // chunks
+    dq_parts = []
+    total_parts = []
+    for chunk in range(chunks):
+        columns = slice(chunk * size, (chunk + 1) * size)
+        kv_own = (
+            key_vecs[..., columns].reshape(rows, width, size),
+            value_vecs[..., columns].reshape(rows, width, size),
+        )
+        kv_partner = swap(kv_own, core_partner)
+        kv_cross = swap(kv_own, chip_neighbour)
+        kv_forward = swap(kv_cross, core_partner)
 
-    def extended(member):
-        joined = jnp.concatenate(
-            [kv_own[member], kv_partner[member], kv_cross[member], kv_forward[member]], axis=0
+        def extended(member):
+            joined = jnp.concatenate(
+                [kv_own[member], kv_partner[member], kv_cross[member], kv_forward[member]], axis=0
+            )
+            return jnp.concatenate([joined[:, width - mf :], joined, joined[:, :mf]], axis=1)
+
+        first = chunk * (heads // chunks)
+        dq, own, intra, cross = window_pass(
+            q, do, lse_t, delta_t, extended(0), extended(1), tiles, tf, mf, first
         )
-        return jnp.concatenate([joined[:, width - mf :], joined, joined[:, :mf]], axis=1)
-
-    dq, own, intra, cross = window_pass(q, do, lse_t, delta_t, extended(0), extended(1), tiles, tf, mf)
-
-    back = swap(intra, core_partner)
-    own_total = own + back[0]
-    cross_total = (cross + back[1]).astype(jnp.bfloat16)
-    arrived = swap(cross_total, chip_neighbour)
-    total = own_total + arrived.astype(jnp.float32)
+        back = swap(intra, core_partner)
+        own_total = own + back[0]
+        cross_total = (cross + back[1]).astype(jnp.bfloat16)
+        arrived = swap(cross_total, chip_neighbour)
+        dq_parts.append(dq)
+        total_parts.append(own_total + arrived.astype(jnp.float32))
+    total = jnp.concatenate(total_parts, axis=-1)
+    dq = jnp.concatenate(dq_parts, axis=-1)
     grad_keys = total[0].astype(jnp.bfloat16).reshape(rows, width_cells, frames, channels)
     grad_values = total[1].astype(jnp.bfloat16).reshape(rows, width_cells, frames, channels)
     grad_queries = dq.reshape(rows, width_cells, frames, channels)

time: 129 us -> 134 us (1.039)
  waiting for transfers between devices: 56.4 us -> 37.6 us
  local copies, waits for them, and re-layouts: 29.6 us -> 45.1 us
  starting transfers between devices: 7.88 us -> 14.6 us
  Pallas kernels: 18.1 us -> 20.1 us
    ppermute x8 -> x16, waiting for transfers between devices: 56.4 us -> 37.6 us  [swap(): return lax.ppermute(block, 'sy', route)]
    unnamed x17 -> x37, local copies, waits for them, and re-layouts: 7.27 us -> 17.7 us
    ppermute x8 -> x16, starting transfers between devices: 7.88 us -> 14.6 us  [swap(): return lax.ppermute(block, 'sy', route)]
    add x0 -> x2, other arithmetic: none -> 3.53 us  [on_device(): total_parts.append(own_total + arrived.astype(jnp.float32))]
    reshape x2 -> x4, local copies, waits for them, and re-layouts: 6.03 us -> 2.87 us  [the longest x2 1.82 us: on_device(): value_vecs[..., columns].reshape(rows, width, size)]
    transpose x2, local copies, waits for them, and re-layouts: 0.35 us -> 3.43 us  [stats_tiles(): tiled = jnp.transpose(tiled, (3, 1, 0, 2))]
    another operation x1, other arithmetic: 3.18 us -> 0.13 us
    slice x0 -> x2, local copies, waits for them, and re-layouts: none -> 3.02 us  [the longest x1 2.47 us: on_device(): key_vecs[..., columns].reshape(rows, width, size)]
  transfers between devices with their start and end apart: 8 -> 16, of which waited for: 4 -> 5; matrix products, arithmetic and copies ran while one was open for 20% -> 39% of each run, Pallas kernels for 0% -> 15%
where the time goes in v3:
time: 134 us; the launch traced here: 133 us
  local copies, waits for them, and re-layouts  45.1 us (34%)
  waiting for transfers between devices  37.6 us (28%)
  Pallas kernels  20.1 us (15%)
  other arithmetic  15 us (11%)
  starting transfers between devices  14.6 us (11%)
    ppermute x16, waiting for transfers between devices, swap(): return lax.ppermute(block, 'sy', route)  37.6 us
    pallas_call x2, Pallas kernels, window_pass(): pl.pallas_call(kernel, grid=(heads,), in_specs=[qspec, qspec, sspec, sspe...  20.1 us
    unnamed x37, local copies, waits for them, and re-layouts  17.7 us
    ppermute x16, starting transfers between devices, swap(): return lax.ppermute(block, 'sy', route)  14.6 us
    concatenate x4, other arithmetic, extended(): jnp.concatenate([joined[:, width - mf:], joined, joined[:, :mf]], axis=1)  5.88 us
    convert_element_type x2, other arithmetic, on_device(): cross_total = (cross + back[1]).astype(jnp.bfloat16)  4.1 us
    add x2, other arithmetic, on_device(): total_parts.append(own_total + arrived.astype(jnp.float32))  3.53 us
    transpose x2, local copies, waits for them, and re-layouts, stats_tiles(): tiled = jnp.transpose(tiled, (3, 1, 0, 2))  3.43 us
  transfers between devices with their start and end apart: 16, of which 5 were waited for; matrix products, arithmetic and copies ran while one was open for 39% of the time, Pallas kernels for 15%

profile of v3, /device:TPU:1, one launch (start us, length us, event | category | flops | bytes accessed | tf_op | source)
XLA Modules:
  0.0 133.3 jit_solution(15137218108841565909)
XLA Ops:
  0.6 2.5 %fusion.15 = (bf16[4,32,2,768]{3,2,1,0:T(2,128)(2,1)S(1)}, bf16[4,32,2,768]{3,2,1,0:T(2,128)(2,1)}) fusion(bf16[4,32,2,1536]{3,2,1,0:T(2,128)(2,1)} %param.7), kind=kLoop, calls=%fused_computation.42 | loop fusion | bytes 1572864 | tf_op jit(solution)/shard_map/slice | solution.py:144
  3.1 0.9 reshape.55
  4.0 0.1 collective-permute-start
  4.1 2.6 %collective-permute-start.1 = (bf16[4,64,768]{2,1,0:T(8,128)(2,1)}, bf16[4,64,768]{2,1,0:T(8,128)(2,1)}, u32[]{:S(2)}, u32[]{:S(2)}) collective-permute-start(bf16[4,64,768]{2,1,0:T(8,128)(2,1)} %reshape.55), channel_id=1, source_target_pairs={{0,15},{1,2},{2,1},{3,4},{4,3},{5,6},{6,5},{7,8},{8,7},{9,10},{10,... | collective-permute-start | bytes 1179656 | tf_op jit(solution)/shard_map/ppermute | solution.py:20
  6.7 0.5 fusion.14
  7.2 0.9 reshape.56
  8.1 3.5 %collective-permute-start.3 = (bf16[4,64,768]{2,1,0:T(8,128)(2,1)}, bf16[4,64,768]{2,1,0:T(8,128)(2,1)}, u32[]{:S(2)}, u32[]{:S(2)}) collective-permute-start(bf16[4,64,768]{2,1,0:T(8,128)(2,1)} %reshape.56), channel_id=1, source_target_pairs={{0,1},{1,0},{2,3},{3,2},{4,5},{5,4},{6,7},{7,6},{8,9},{9,8},{10,11... | collective-permute-start | bytes 1179656 | tf_op jit(solution)/shard_map/ppermute | solution.py:20
  11.7 0.9 reshape.58
  12.6 0.6 collective-permute-start.9
  13.2 0.5 reshape.51
  13.7 2.6 %reshape.52 = bf16[4,64,12,128]{3,2,1,0:T(8,128)(2,1)S(1)} reshape(bf16[4,32,2,1536]{3,2,1,0:T(2,128)(2,1)} %param.9) | data formatting | bytes 1572864 | tf_op jit(solution)/shard_map/reshape | solution.py:131
  16.4 1.3 fusion
  17.6 1.8 %constant_dynamic-update-slice_fusion.3 = bf16[16,64,768]{2,1,0:T(8,128)(2,1)} fusion(bf16[4,64,768]{2,1,0:T(8,128)(2,1)} %reshape.55), kind=kLoop, calls=%fused_computation.23 | loop fusion | bytes 786432
  19.4 1.8 %constant_dynamic-update-slice_fusion.7 = bf16[16,64,768]{2,1,0:T(8,128)(2,1)} fusion(bf16[4,64,768]{2,1,0:T(8,128)(2,1)} %reshape.56), kind=kLoop, calls=%fused_computation.27 | loop fusion | bytes 786432
  21.2 1.0 constant_dynamic-update-slice_fusion.15
  22.2 0.1 reshape.57
  22.4 3.0 %reshape.49.do_ref = bf16[4,64,1536]{2,1,0:T(8,128)(2,1)} reshape(bf16[4,32,2,1536]{3,2,1,0:T(2,128)(2,1)} %param.10) | data formatting | bytes 1572864 | tf_op jit(solution)/shard_map/reshape | solution.py:127
  25.4 1.7 %copy.19 = f32[4,4,16,12]{2,0,1,3:T(4,128)} copy(f32[4,4,16,12]{3,2,1,0:T(8,128)} %bitcast.34) | data formatting | bytes 24576 | tf_op jit(solution)/shard_map/transpose | solution.py:114
  27.1 1.6 %reshape.54.delta_ref = f32[12,4,1,64]{3,2,1,0:T(1,128)} reshape(f32[12,4,4,16]{3,2,1,0:T(4,128)} %bitcast.36) | data formatting | bytes 24576 | tf_op jit(solution)/shard_map/reshape | solution.py:115
  28.7 3.0 %reshape.48.q_ref = bf16[4,64,1536]{2,1,0:T(8,128)(2,1)} reshape(bf16[4,32,2,1536]{3,2,1,0:T(2,128)(2,1)} %param.6) | data formatting | bytes 1572864 | tf_op jit(solution)/shard_map/reshape | solution.py:126
  31.7 1.6 %copy.9 = f32[4,32,2,12]{3,2,1,0:T(2,128)} copy(f32[4,32,2,12]{1,2,3,0:T(2,128)} %param.11) | data formatting | bytes 24576 | tf_op args[5]
  33.2 1.7 %copy.10 = f32[12,4,4,16]{3,2,1,0:T(4,128)} copy(f32[12,4,4,16]{0,3,1,2:T(8,128)} %bitcast.35) | data formatting | bytes 24576 | tf_op jit(solution)/shard_map/transpose | solution.py:114
  35.0 1.6 %reshape.50.lse_ref = f32[12,4,1,64]{3,2,1,0:T(1,128)} reshape(f32[12,4,4,16]{3,2,1,0:T(4,128)} %copy.10) | data formatting | bytes 24576 | tf_op jit(solution)/shard_map/reshape | solution.py:115
  36.6 1.1 collective-permute-start.10
  37.7 0.6 collective-permute-start.7
  38.3 1.8 %constant_dynamic-update-slice_fusion.2 = bf16[16,64,768]{2,1,0:T(8,128)(2,1)} fusion(bf16[16,64,768]{2,1,0:T(8,128)(2,1)} %constant_dynamic-update-slice_fusion.3, bf16[4,64,768]{2,1,0:T(8,128)(2,1)} %collective-permute-done), kind=kLoop, calls=%fused_computation.22 | loop fusion | bytes 786432
  40.1 1.8 %constant_dynamic-update-slice_fusion.1 = bf16[16,64,768]{2,1,0:T(8,128)(2,1)} fusion(bf16[16,64,768]{2,1,0:T(8,128)(2,1)} %constant_dynamic-update-slice_fusion.2, bf16[4,64,768]{2,1,0:T(8,128)(2,1)} %collective-permute-done.1), kind=kLoop, calls=%fused_computation.21 | loop fusion | bytes 786432
  41.9 2.7 %collective-permute-start.6 = (bf16[4,64,768]{2,1,0:T(8,128)(2,1)S(1)}, bf16[4,64,768]{2,1,0:T(8,128)(2,1)S(1)}, u32[]{:S(2)}, u32[]{:S(2)}) collective-permute-start(bf16[4,64,768]{2,1,0:T(8,128)(2,1)S(1)} %reshape.57), channel_id=1, source_target_pairs={{0,1},{1,0},{2,3},{3,2},{4,5},{5,4},{6,7},{7,6},{8,9},{9,8},{10,11... | collective-permute-start | bytes 1179656 | tf_op jit(solution)/shard_map/ppermute | solution.py:20
  44.6 1.8 %constant_dynamic-update-slice_fusion.6 = bf16[16,64,768]{2,1,0:T(8,128)(2,1)} fusion(bf16[16,64,768]{2,1,0:T(8,128)(2,1)} %constant_dynamic-update-slice_fusion.7, bf16[4,64,768]{2,1,0:T(8,128)(2,1)} %collective-permute-done.3), kind=kLoop, calls=%fused_computation.26 | loop fusion | bytes 786432
  46.4 0.0 collective-permute-start.2
  46.4 1.8 %constant_dynamic-update-slice_fusion.5 = bf16[16,64,768]{2,1,0:T(8,128)(2,1)} fusion(bf16[16,64,768]{2,1,0:T(8,128)(2,1)} %constant_dynamic-update-slice_fusion.6, bf16[4,64,768]{2,1,0:T(8,128)(2,1)} %collective-permute-done.4), kind=kLoop, calls=%fused_computation.25 | loop fusion | bytes 786432
  48.2 0.5 collective-permute-start.5
  48.7 3.8 %collective-permute-done.10 = bf16[4,64,768]{2,1,0:T(8,128)(2,1)} collective-permute-done((bf16[4,64,768]{2,1,0:T(8,128)(2,1)}, bf16[4,64,768]{2,1,0:T(8,128)(2,1)}, u32[]{:S(2)}, u32[]{:S(2)}) %collective-permute-start.10) | collective-permute-done | bytes 393248 | tf_op jit(solution)/shard_map/ppermute | solution.py:20
  52.5 4.2 %collective-permute-done.7 = bf16[4,64,768]{2,1,0:T(8,128)(2,1)} collective-permute-done((bf16[4,64,768]{2,1,0:T(8,128)(2,1)S(1)}, bf16[4,64,768]{2,1,0:T(8,128)(2,1)}, u32[]{:S(2)}, u32[]{:S(2)}) %collective-permute-start.7) | collective-permute-done | bytes 393248 | tf_op jit(solution)/shard_map/ppermute | solution.py:20
  56.7 1.0 constant_dynamic-update-slice_fusion.14
  57.8 1.0 constant_dynamic-update-slice_fusion.13
  58.8 1.1 constant_dynamic-update-slice_fusion.9
  60.1 0.2 copy-done
  60.4 1.4 %pad_maximum_fusion.k_ref = bf16[16,80,768]{2,1,0:T(8,128)(2,1)} fusion(bf16[16,8,768]{2,1,0:T(8,128)(2,1)S(1)} %get-tuple-element.24, bf16[16,64,768]{2,1,0:T(8,128)(2,1)S(1)} %constant_dynamic-update-slice_fusion, bf16[16,8,768]{2,1,0:T(8,128)(2,1)S(1)} %get-tuple-element.23), kind=kLoop, calls=%fused_computation.3 | loop fusion | flops 5898240 | bytes 3932160 | tf_op jit(solution)/shard_map/concatenate | solution.py:155
  61.8 1.5 %pad_maximum_fusion.1.v_ref = bf16[16,80,768]{2,1,0:T(8,128)(2,1)} fusion(bf16[16,8,768]{2,1,0:T(8,128)(2,1)S(1)} %get-tuple-element.22, bf16[16,64,768]{2,1,0:T(8,128)(2,1)S(1)} %constant_dynamic-update-slice_fusion.4, bf16[16,8,768]{2,1,0:T(8,128)(2,1)S(1)} %get-tuple-element.21), kind=kLoop, calls=%fused_computation.4 | loop fusion | flops 5898240 | bytes 3932160 | tf_op jit(solution)/shard_map/concatenate | solution.py:155
  63.3 10.0 %shard_map.85 = (bf16[4,64,768]{2,1,0:T(8,128)(2,1)}, f32[2,4,64,768]{3,2,1,0:T(8,128)}, f32[2,2,4,64,768]{4,3,2,1,0:T(8,128)}, f32[2,4,64,768]{3,2,1,0:T(8,128)}) custom-call(bf16[4,64,1536]{2,1,0:T(8,128)(2,1)} %reshape.48.q_ref, bf16[4,64,1536]{2,1,0:T(8,128)(2,1)} %reshape.49.do_ref, f32[12,4,1,64]{3,2,1,0:T(1,128)} %reshape.50.lse_ref, ...), custom_call_target="tpu_custom_call" | custom-call | flops 1006632960 | bytes 11403264 | tf_op jit(solution)/shard_map/pallas_call | solution.py:96
  73.4 0.6 collective-permute-start.12
  73.9 1.0 constant_dynamic-update-slice_fusion.12
  75.0 1.0 constant_dynamic-update-slice_fusion.8
  76.1 1.5 %pad_maximum_fusion.3.v_ref = bf16[16,80,768]{2,1,0:T(8,128)(2,1)} fusion(bf16[16,8,768]{2,1,0:T(8,128)(2,1)S(1)} %get-tuple-element.26, bf16[16,64,768]{2,1,0:T(8,128)(2,1)S(1)} %constant_dynamic-update-slice_fusion.12, bf16[16,8,768]{2,1,0:T(8,128)(2,1)S(1)} %get-tuple-element.25), kind=kLoop, calls=%fused_computation.6 | loop fusion | flops 5898240 | bytes 3932160 | tf_op jit(solution)/shard_map/concatenate | solution.py:155
  77.6 1.4 %pad_maximum_fusion.2.k_ref = bf16[16,80,768]{2,1,0:T(8,128)(2,1)} fusion(bf16[16,8,768]{2,1,0:T(8,128)(2,1)S(1)} %get-tuple-element.28, bf16[16,64,768]{2,1,0:T(8,128)(2,1)S(1)} %constant_dynamic-update-slice_fusion.8, bf16[16,8,768]{2,1,0:T(8,128)(2,1)S(1)} %get-tuple-element.27), kind=kLoop, calls=%fused_computation.5 | loop fusion | flops 5898240 | bytes 3932160 | tf_op jit(solution)/shard_map/concatenate | solution.py:155
  79.0 10.0 %shard_map.86 = (bf16[4,64,768]{2,1,0:T(8,128)(2,1)}, f32[2,4,64,768]{3,2,1,0:T(8,128)}, f32[2,2,4,64,768]{4,3,2,1,0:T(8,128)}, f32[2,4,64,768]{3,2,1,0:T(8,128)}) custom-call(bf16[4,64,1536]{2,1,0:T(8,128)(2,1)} %reshape.48.q_ref, bf16[4,64,1536]{2,1,0:T(8,128)(2,1)} %reshape.49.do_ref, f32[12,4,1,64]{3,2,1,0:T(1,128)} %reshape.50.lse_ref, ...), custom_call_target="tpu_custom_call" | custom-call | flops 1006632960 | bytes 11403264 | tf_op jit(solution)/shard_map/pallas_call | solution.py:96
  89.1 0.1 collective-permute-start.14
  89.2 3.0 %fusion.6 = bf16[2,4,64,768]{3,2,1,0:T(8,128)(2,1)} fusion(f32[2,4,64,768]{3,2,1,0:T(8,128)} %get-tuple-element.15, f32[2,2,4,64,768]{4,3,2,1,0:T(8,128)} %collective-permute-done.12), kind=kLoop, calls=%fused_computation.15 | loop fusion | flops 786432 | bytes 3932160 | tf_op jit(solution)/shard_map/convert_element_type | solution.py:163
  92.2 1.1 collective-permute-start.13
  93.3 1.7 %collective-permute-done.14 = f32[2,2,4,64,768]{4,3,2,1,0:T(8,128)S(1)} collective-permute-done((f32[2,2,4,64,768]{4,3,2,1,0:T(8,128)}, f32[2,2,4,64,768]{4,3,2,1,0:T(8,128)S(1)}, u32[]{:S(2)}, u32[]{:S(2)}) %collective-permute-start.14) | collective-permute-done | bytes 3145760 | tf_op jit(solution)/shard_map/ppermute | solution.py:20
  95.0 1.1 fusion.2
  96.1 0.9 copy-done.3
  97.0 1.1 collective-permute-start.15
  98.1 0.1 pad_maximum_fusion.4
  98.1 1.2 reshape.59
  99.3 21.5 %collective-permute-done.13 = bf16[2,4,64,768]{3,2,1,0:T(8,128)(2,1)} collective-permute-done((bf16[2,4,64,768]{3,2,1,0:T(8,128)(2,1)}, bf16[2,4,64,768]{3,2,1,0:T(8,128)(2,1)}, u32[]{:S(2)}, u32[]{:S(2)}) %collective-permute-start.13) | collective-permute-done | bytes 786464 | tf_op jit(solution)/shard_map/ppermute | solution.py:20
  120.8 2.0 %fusion.8 = bf16[2,4,64,768]{3,2,1,0:T(8,128)(2,1)S(1)} fusion(f32[2,4,64,768]{3,2,1,0:T(8,128)S(1)} %copy-done.6, f32[2,2,4,64,768]{4,3,2,1,0:T(8,128)} %collective-permute-done.12, bf16[2,4,64,768]{3,2,1,0:T(8,128)(2,1)} %collective-permute-done.13), kind=kLoop, calls=%fused_computation.18 | loop fusion | flops 1572864 | bytes 4718592 | tf_op jit(solution)/shard_map/add | solution.py:166
  122.8 6.4 %collective-permute-done.15 = bf16[2,4,64,768]{3,2,1,0:T(8,128)(2,1)} collective-permute-done((bf16[2,4,64,768]{3,2,1,0:T(8,128)(2,1)}, bf16[2,4,64,768]{3,2,1,0:T(8,128)(2,1)}, u32[]{:S(2)}, u32[]{:S(2)}) %collective-permute-start.15) | collective-permute-done | bytes 786464 | tf_op jit(solution)/shard_map/ppermute | solution.py:20
  129.2 1.5 %fusion.4 = bf16[2,4,64,768]{3,2,1,0:T(8,128)(2,1)S(1)} fusion(f32[2,4,64,768]{3,2,1,0:T(8,128)S(1)} %copy-done.7, f32[2,2,4,64,768]{4,3,2,1,0:T(8,128)S(1)} %copy-done.4, bf16[2,4,64,768]{3,2,1,0:T(8,128)(2,1)} %collective-permute-done.15), kind=kLoop, calls=%fused_computation.12 | loop fusion | flops 1572864 | bytes 4718592 | tf_op jit(solution)/shard_map/add | solution.py:166
  130.7 0.1 maximum_convert_fusion
  130.8 0.1 fusion.9
  131.0 1.2 convert_element_type.26
  132.1 1.2 convert_element_type.27
  (44 shorter events, 0.3 us)
Async XLA Ops:
  0.6 6.0 %copy-start.9 = (bf16[4,32,2,1536]{3,2,1,0:T(2,128)(2,1)S(1)}, bf16[4,32,2,1536]{3,2,1,0:T(2,128)(2,1)}, u32[]{:S(2)}) copy-start(bf16[4,32,2,1536]{3,2,1,0:T(2,128)(2,1)} %param.8) | copy-start | bytes 2359300
  4.0 9.2 %copy-start.2 = (bf16[4,32,2,1536]{3,2,1,0:T(2,128)(2,1)S(1)}, bf16[4,32,2,1536]{3,2,1,0:T(2,128)(2,1)}, u32[]{:S(2)}) copy-start(bf16[4,32,2,1536]{3,2,1,0:T(2,128)(2,1)} %param.10) | copy-start | bytes 2359300
  4.0 32.6 %collective-permute-start = (bf16[4,64,768]{2,1,0:T(8,128)(2,1)}, bf16[4,64,768]{2,1,0:T(8,128)(2,1)}, u32[]{:S(2)}, u32[]{:S(2)}) collective-permute-start(bf16[4,64,768]{2,1,0:T(8,128)(2,1)} %reshape.55), channel_id=1, source_target_pairs={{0,1},{1,0},{2,3},{3,2},{4,5},{5,4},{6,7},{7,6},{8,9},{9,8},{10,11... | collective-permute-start | bytes 1179656 | tf_op jit(solution)/shard_map/ppermute | solution.py:20
  4.1 33.6 %collective-permute-start.1 = (bf16[4,64,768]{2,1,0:T(8,128)(2,1)}, bf16[4,64,768]{2,1,0:T(8,128)(2,1)}, u32[]{:S(2)}, u32[]{:S(2)}) collective-permute-start(bf16[4,64,768]{2,1,0:T(8,128)(2,1)} %reshape.55), channel_id=1, source_target_pairs={{0,15},{1,2},{2,1},{3,4},{4,3},{5,6},{6,5},{7,8},{8,7},{9,10},{10,... | collective-permute-start | bytes 1179656 | tf_op jit(solution)/shard_map/ppermute | solution.py:20
  8.1 33.8 %collective-permute-start.3 = (bf16[4,64,768]{2,1,0:T(8,128)(2,1)}, bf16[4,64,768]{2,1,0:T(8,128)(2,1)}, u32[]{:S(2)}, u32[]{:S(2)}) collective-permute-start(bf16[4,64,768]{2,1,0:T(8,128)(2,1)} %reshape.56), channel_id=1, source_target_pairs={{0,1},{1,0},{2,3},{3,2},{4,5},{5,4},{6,7},{7,6},{8,9},{9,8},{10,11... | collective-permute-start | bytes 1179656 | tf_op jit(solution)/shard_map/ppermute | solution.py:20
  11.7 34.7 %collective-permute-start.4 = (bf16[4,64,768]{2,1,0:T(8,128)(2,1)}, bf16[4,64,768]{2,1,0:T(8,128)(2,1)}, u32[]{:S(2)}, u32[]{:S(2)}) collective-permute-start(bf16[4,64,768]{2,1,0:T(8,128)(2,1)} %reshape.56), channel_id=1, source_target_pairs={{0,15},{1,2},{2,1},{3,4},{4,3},{5,6},{6,5},{7,8},{8,7},{9,10},{10,... | collective-permute-start | bytes 1179656 | tf_op jit(solution)/shard_map/ppermute | solution.py:20
  12.6 35.6 %collective-permute-start.9 = (bf16[4,64,768]{2,1,0:T(8,128)(2,1)}, bf16[4,64,768]{2,1,0:T(8,128)(2,1)}, u32[]{:S(2)}, u32[]{:S(2)}) collective-permute-start(bf16[4,64,768]{2,1,0:T(8,128)(2,1)} %reshape.58), channel_id=1, source_target_pairs={{0,1},{1,0},{2,3},{3,2},{4,5},{5,4},{6,7},{7,6},{8,9},{9,8},{10,11... | collective-permute-start | bytes 1179656 | tf_op jit(solution)/shard_map/ppermute | solution.py:20
  17.6 4.6 %copy-start.5 = (bf16[4,32,2,768]{3,2,1,0:T(2,128)(2,1)S(1)}, bf16[4,32,2,768]{3,2,1,0:T(2,128)(2,1)}, u32[]{:S(2)}) copy-start(bf16[4,32,2,768]{3,2,1,0:T(2,128)(2,1)} %get-tuple-element.32) | copy-start | bytes 1179652
  36.6 15.9 %collective-permute-start.10 = (bf16[4,64,768]{2,1,0:T(8,128)(2,1)}, bf16[4,64,768]{2,1,0:T(8,128)(2,1)}, u32[]{:S(2)}, u32[]{:S(2)}) collective-permute-start(bf16[4,64,768]{2,1,0:T(8,128)(2,1)} %reshape.58), channel_id=1, source_target_pairs={{0,15},{1,2},{2,1},{3,4},{4,3},{5,6},{6,5},{7,8},{8,7},{9,10},{10,... | collective-permute-start | bytes 1179656 | tf_op jit(solution)/shard_map/ppermute | solution.py:20
  37.7 19.0 %collective-permute-start.7 = (bf16[4,64,768]{2,1,0:T(8,128)(2,1)S(1)}, bf16[4,64,768]{2,1,0:T(8,128)(2,1)}, u32[]{:S(2)}, u32[]{:S(2)}) collective-permute-start(bf16[4,64,768]{2,1,0:T(8,128)(2,1)S(1)} %reshape.57), channel_id=1, source_target_pairs={{0,15},{1,2},{2,1},{3,4},{4,3},{5,6},{6,5},{7,8},{8,7},{9,10},{10,... | collective-permute-start | bytes 1179656 | tf_op jit(solution)/shard_map/ppermute | solution.py:20
  41.9 16.9 %collective-permute-start.6 = (bf16[4,64,768]{2,1,0:T(8,128)(2,1)S(1)}, bf16[4,64,768]{2,1,0:T(8,128)(2,1)S(1)}, u32[]{:S(2)}, u32[]{:S(2)}) collective-permute-start(bf16[4,64,768]{2,1,0:T(8,128)(2,1)S(1)} %reshape.57), channel_id=1, source_target_pairs={{0,1},{1,0},{2,3},{3,2},{4,5},{5,4},{6,7},{7,6},{8,9},{9,8},{10,11... | collective-permute-start | bytes 1179656 | tf_op jit(solution)/shard_map/ppermute | solution.py:20
  46.4 13.6 %collective-permute-start.2 = (bf16[4,64,768]{2,1,0:T(8,128)(2,1)}, bf16[4,64,768]{2,1,0:T(8,128)(2,1)S(1)}, u32[]{:S(2)}, u32[]{:S(2)}) collective-permute-start(bf16[4,64,768]{2,1,0:T(8,128)(2,1)} %collective-permute-done.1), channel_id=1, source_target_pairs={{0,1},{1,0},{2,3},{3,2},{4,5},{5,4},{6,7},{7,6},{8,9},{9,8},{10,11... | collective-permute-start | bytes 1179656 | tf_op jit(solution)/shard_map/ppermute | solution.py:20
  48.2 11.8 %copy-start.1 = (bf16[16,64,768]{2,1,0:T(8,128)(2,1)S(1)}, bf16[16,64,768]{2,1,0:T(8,128)(2,1)}, u32[]{:S(2)}) copy-start(bf16[16,64,768]{2,1,0:T(8,128)(2,1)} %constant_dynamic-update-slice_fusion.1) | copy-start | bytes 4718596
  48.2 11.9 %collective-permute-start.5 = (bf16[4,64,768]{2,1,0:T(8,128)(2,1)}, bf16[4,64,768]{2,1,0:T(8,128)(2,1)S(1)}, u32[]{:S(2)}, u32[]{:S(2)}) collective-permute-start(bf16[4,64,768]{2,1,0:T(8,128)(2,1)} %collective-permute-done.4), channel_id=1, source_target_pairs={{0,1},{1,0},{2,3},{3,2},{4,5},{5,4},{6,7},{7,6},{8,9},{9,8},{10,11... | collective-permute-start | bytes 1179656 | tf_op jit(solution)/shard_map/ppermute | solution.py:20
  52.5 21.4 %collective-permute-start.11 = (bf16[4,64,768]{2,1,0:T(8,128)(2,1)}, bf16[4,64,768]{2,1,0:T(8,128)(2,1)}, u32[]{:S(2)}, u32[]{:S(2)}) collective-permute-start(bf16[4,64,768]{2,1,0:T(8,128)(2,1)} %collective-permute-done.10), channel_id=1, source_target_pairs={{0,1},{1,0},{2,3},{3,2},{4,5},{5,4},{6,7},{7,6},{8,9},{9,8},{10,11... | collective-permute-start | bytes 1179656 | tf_op jit(solution)/shard_map/ppermute | solution.py:20
  56.7 18.3 %collective-permute-start.8 = (bf16[4,64,768]{2,1,0:T(8,128)(2,1)}, bf16[4,64,768]{2,1,0:T(8,128)(2,1)}, u32[]{:S(2)}, u32[]{:S(2)}) collective-permute-start(bf16[4,64,768]{2,1,0:T(8,128)(2,1)} %collective-permute-done.7), channel_id=1, source_target_pairs={{0,1},{1,0},{2,3},{3,2},{4,5},{5,4},{6,7},{7,6},{8,9},{9,8},{10,11... | collective-permute-start | bytes 1179656 | tf_op jit(solution)/shard_map/ppermute | solution.py:20
  58.8 1.5 %copy-start = (bf16[16,64,768]{2,1,0:T(8,128)(2,1)S(1)}, bf16[16,64,768]{2,1,0:T(8,128)(2,1)}, u32[]{:S(2)}) copy-start(bf16[16,64,768]{2,1,0:T(8,128)(2,1)} %constant_dynamic-update-slice_fusion.5) | copy-start | bytes 4718596
  73.4 15.8 %collective-permute-start.12 = (f32[2,2,4,64,768]{4,3,2,1,0:T(8,128)}, f32[2,2,4,64,768]{4,3,2,1,0:T(8,128)}, u32[]{:S(2)}, u32[]{:S(2)}) collective-permute-start(f32[2,2,4,64,768]{4,3,2,1,0:T(8,128)} %get-tuple-element.14), channel_id=1, source_target_pairs={{0,1},{1,0},{2,3},{3,2},{4,5},{5,4},{6,7},{7,6},{8,9},{9,8},{10,11... | collective-permute-start | bytes 9437192 | tf_op jit(solution)/shard_map/ppermute | solution.py:20
  89.1 5.9 %collective-permute-start.14 = (f32[2,2,4,64,768]{4,3,2,1,0:T(8,128)}, f32[2,2,4,64,768]{4,3,2,1,0:T(8,128)S(1)}, u32[]{:S(2)}, u32[]{:S(2)}) collective-permute-start(f32[2,2,4,64,768]{4,3,2,1,0:T(8,128)} %get-tuple-element.17), channel_id=1, source_target_pairs={{0,1},{1,0},{2,3},{3,2},{4,5},{5,4},{6,7},{7,6},{8,9},{9,8},{10,11... | collective-permute-start | bytes 9437192 | tf_op jit(solution)/shard_map/ppermute | solution.py:20
  89.2 5.9 %copy-start.8 = (f32[2,4,64,768]{3,2,1,0:T(8,128)S(1)}, f32[2,4,64,768]{3,2,1,0:T(8,128)}, u32[]{:S(2)}) copy-start(f32[2,4,64,768]{3,2,1,0:T(8,128)} %get-tuple-element.18) | copy-start | bytes 4718596
  92.2 28.6 %collective-permute-start.13 = (bf16[2,4,64,768]{3,2,1,0:T(8,128)(2,1)}, bf16[2,4,64,768]{3,2,1,0:T(8,128)(2,1)}, u32[]{:S(2)}, u32[]{:S(2)}) collective-permute-start(bf16[2,4,64,768]{3,2,1,0:T(8,128)(2,1)} %fusion.6), channel_id=1, source_target_pairs={{0,15},{1,2},{2,1},{3,4},{4,3},{5,6},{6,5},{7,8},{8,7},{9,10},{10,... | collective-permute-start | bytes 2359304 | tf_op jit(solution)/shard_map/ppermute | solution.py:20
  95.0 1.9 %copy-start.3 = (f32[2,2,4,64,768]{4,3,2,1,0:T(8,128)}, f32[2,2,4,64,768]{4,3,2,1,0:T(8,128)S(1)}, u32[]{:S(2)}) copy-start(f32[2,2,4,64,768]{4,3,2,1,0:T(8,128)S(1)} %collective-permute-done.14) | copy-start | bytes 9437188
  95.0 3.1 %copy-start.10 = (bf16[4,64,768]{2,1,0:T(8,128)(2,1)S(1)}, bf16[4,64,768]{2,1,0:T(8,128)(2,1)}, u32[]{:S(2)}) copy-start(bf16[4,64,768]{2,1,0:T(8,128)(2,1)} %get-tuple-element.11) | copy-start | bytes 1179652
  95.0 3.1 %copy-start.11 = (bf16[4,64,768]{2,1,0:T(8,128)(2,1)S(1)}, bf16[4,64,768]{2,1,0:T(8,128)(2,1)}, u32[]{:S(2)}) copy-start(bf16[4,64,768]{2,1,0:T(8,128)(2,1)} %get-tuple-element.12) | copy-start | bytes 1179652
  97.0 32.2 %collective-permute-start.15 = (bf16[2,4,64,768]{3,2,1,0:T(8,128)(2,1)}, bf16[2,4,64,768]{3,2,1,0:T(8,128)(2,1)}, u32[]{:S(2)}, u32[]{:S(2)}) collective-permute-start(bf16[2,4,64,768]{3,2,1,0:T(8,128)(2,1)} %fusion.2), channel_id=1, source_target_pairs={{0,15},{1,2},{2,1},{3,4},{4,3},{5,6},{6,5},{7,8},{8,7},{9,10},{10,... | collective-permute-start | bytes 2359304 | tf_op jit(solution)/shard_map/ppermute | solution.py:20
  98.1 22.7 %copy-start.6 = (f32[2,4,64,768]{3,2,1,0:T(8,128)S(1)}, f32[2,4,64,768]{3,2,1,0:T(8,128)}, u32[]{:S(2)}) copy-start(f32[2,4,64,768]{3,2,1,0:T(8,128)} %get-tuple-element.13) | copy-start | bytes 4718596
  120.8 8.4 %copy-start.4 = (f32[2,2,4,64,768]{4,3,2,1,0:T(8,128)S(1)}, f32[2,2,4,64,768]{4,3,2,1,0:T(8,128)}, u32[]{:S(2)}) copy-start(f32[2,2,4,64,768]{4,3,2,1,0:T(8,128)} %copy-done.3) | copy-start | bytes 9437188
  120.8 8.4 %copy-start.7 = (f32[2,4,64,768]{3,2,1,0:T(8,128)S(1)}, f32[2,4,64,768]{3,2,1,0:T(8,128)}, u32[]{:S(2)}) copy-start(f32[2,4,64,768]{3,2,1,0:T(8,128)} %get-tuple-element.16) | copy-start | bytes 4718596

commit v4 on v2

--- a/solution.py
+++ b/solution.py
@@ -28,18 +28,20 @@
     return (i + 1) % n if i % 2 else (i - 1) % n
 
 
-def window_kernel(
-    q_ref, do_ref, lse_ref, delta_ref, k_ref, v_ref, dq_ref, own_ref, intra_ref, cross_ref, *, tiles, tf, mf
-):
+def window_kernel(*refs, tiles, tf, mf, accumulate):
+    if accumulate:
+        q_ref, do_ref, lse_ref, delta_ref, k_ref, v_ref, dqin_ref, dq_ref, first_ref, second_ref = refs
+    else:
+        q_ref, do_ref, lse_ref, delta_ref, k_ref, v_ref, dq_ref, first_ref, second_ref = refs
+        dqin_ref = None
     scaling = HEAD_DIM ** (-0.5)
     rows = q_ref.shape[0]
     krows = k_ref.shape[0]
-    width = own_ref.shape[2]
+    width = first_ref.shape[2]
     span = tf + 2 * mf
-    own_ref[...] = jnp.zeros_like(own_ref)
-    intra_ref[...] = jnp.zeros_like(intra_ref)
-    cross_ref[...] = jnp.zeros_like(cross_ref)
-    targets = [own_ref, intra_ref.at[0], cross_ref, intra_ref.at[1]]
+    first_ref[...] = jnp.zeros_like(first_ref)
+    second_ref[...] = jnp.zeros_like(second_ref)
+    targets = [first_ref, second_ref]
     blocks = krows // rows
     for b in range(tiles):
         kw = k_ref[:, b * tf : b * tf + span, :].reshape(krows * span, HEAD_DIM)
@@ -54,7 +56,10 @@
         grad_v = jnp.dot(attention.astype(jnp.bfloat16), dob, preferred_element_type=jnp.float32)
         grad_k = jnp.dot(grad_scores, qb, preferred_element_type=jnp.float32) * scaling
         grad_q = jnp.dot(grad_scores.T, kw, preferred_element_type=jnp.float32) * scaling
-        dq_ref[:, b * tf : (b + 1) * tf, :] = grad_q.reshape(rows, tf, HEAD_DIM).astype(dq_ref.dtype)
+        grad_q = grad_q.reshape(rows, tf, HEAD_DIM)
+        if dqin_ref is not None:
+            grad_q = grad_q + dqin_ref[:, b * tf : (b + 1) * tf, :]
+        dq_ref[:, b * tf : (b + 1) * tf, :] = grad_q.astype(dq_ref.dtype)
         grad_k = grad_k.reshape(blocks, rows, span, HEAD_DIM)
         grad_v = grad_v.reshape(blocks, rows, span, HEAD_DIM)
         start = b * tf - mf
@@ -73,37 +78,38 @@
                 target[1, :, dst : dst + size, :] += grad_v[block, :, src : src + size, :]
 
 
-def window_pass(q, do, lse_t, delta_t, k_ext, v_ext, tiles, tf, mf):
+def window_pass(q, do, lse_t, delta_t, k_ext, v_ext, dq_in, tiles, tf, mf):
     rows, width, channels = q.shape
     krows = k_ext.shape[0]
     ext = k_ext.shape[1]
     heads = channels // HEAD_DIM
-    kernel = functools.partial(window_kernel, tiles=tiles, tf=tf, mf=mf)
+    accumulate = dq_in is not None
+    kernel = functools.partial(window_kernel, tiles=tiles, tf=tf, mf=mf, accumulate=accumulate)
     qspec = pl.BlockSpec((rows, width, HEAD_DIM), lambda h: (0, 0, h))
     kspec = pl.BlockSpec((krows, ext, HEAD_DIM), lambda h: (0, 0, h))
     sspec = pl.BlockSpec((None, tiles, 1, rows * tf), lambda h: (h, 0, 0, 0))
     pspec = pl.BlockSpec((2, rows, width, HEAD_DIM), lambda h: (0, 0, 0, h))
-    ispec = pl.BlockSpec((2, 2, rows, width, HEAD_DIM), lambda h: (0, 0, 0, 0, h))
     pairs = tiles * rows * tf * krows * (tf + 2 * mf) * heads
     cost = pl.CostEstimate(
         flops=10 * pairs * HEAD_DIM,
         transcendentals=pairs,
-        bytes_accessed=2 * (2 * q.size + 2 * k_ext.size + q.size) + 8 * krows * width * channels,
+        bytes_accessed=2 * (2 * q.size + 2 * k_ext.size + q.size) + 12 * krows * width * channels,
     )
     part = jax.ShapeDtypeStruct((2, rows, width, channels), jnp.float32)
+    dq_type = jnp.bfloat16 if accumulate else jnp.float32
+    operands = [q, do, lse_t, delta_t, k_ext, v_ext]
+    in_specs = [qspec, qspec, sspec, sspec, kspec, kspec]
+    if accumulate:
+        operands.append(dq_in)
+        in_specs.append(qspec)
     return pl.pallas_call(
         kernel,
         grid=(heads,),
-        in_specs=[qspec, qspec, sspec, sspec, kspec, kspec],
-        out_specs=[qspec, pspec, ispec, pspec],
-        out_shape=[
-            jax.ShapeDtypeStruct((rows, width, channels), jnp.bfloat16),
-            part,
-            jax.ShapeDtypeStruct((2, 2, rows, width, channels), jnp.float32),
-            part,
-        ],
+        in_specs=in_specs,
+        out_specs=[qspec, pspec, pspec],
+        out_shape=[jax.ShapeDtypeStruct((rows, width, channels), dq_type), part, part],
         cost_estimate=cost,
-    )(q, do, lse_t, delta_t, k_ext, v_ext)
+    )(*operands)
 
 
 def stats_tiles(stats, tiles, tf):
@@ -135,19 +141,27 @@
     kv_own = (key_vecs.reshape(rows, width, channels), value_vecs.reshape(rows, width, channels))
     kv_partner = swap(kv_own, core_partner)
     kv_cross = swap(kv_own, chip_neighbour)
-    kv_forward = swap(kv_cross, core_partner)
 
-    def extended(member):
-        joined = jnp.concatenate(
-            [kv_own[member], kv_partner[member], kv_cross[member], kv_forward[member]], axis=0
-        )
+    def extended(upper, lower, member):
+        joined = jnp.concatenate([upper[member], lower[member]], axis=0)
         return jnp.concatenate([joined[:, width - mf :], joined, joined[:, :mf]], axis=1)
 
-    dq, own, intra, cross = window_pass(q, do, lse_t, delta_t, extended(0), extended(1), tiles, tf, mf)
-
-    back = swap(intra, core_partner)
-    own_total = own + back[0]
-    cross_total = (cross + back[1]).astype(jnp.bfloat16)
+    dq_local, part_own, part_partner = window_pass(
+        q, do, lse_t, delta_t,
+        extended(kv_own, kv_partner, 0), extended(kv_own, kv_partner, 1),
+        None, tiles, tf, mf,
+    )
+    kv_cross, dq_local = lax.optimization_barrier((kv_cross, dq_local))
+    kv_forward = swap(kv_cross, core_partner)
+    back_partner = swap(part_partner, core_partner)
+    dq, part_cross, part_forward = window_pass(
+        q, do, lse_t, delta_t,
+        extended(kv_cross, kv_forward, 0), extended(kv_cross, kv_forward, 1),
+        dq_local, tiles, tf, mf,
+    )
+    back_forward = swap(part_forward, core_partner)
+    own_total = part_own + back_partner
+    cross_total = (part_cross + back_forward).astype(jnp.bfloat16)
     arrived = swap(cross_total, chip_neighbour)
     total = own_total + arrived.astype(jnp.float32)
     grad_keys = total[0].astype(jnp.bfloat16).reshape(rows, width_cells, frames, channels)

time: 129 us -> 121 us (0.938)
  waiting for transfers between devices: 56.4 us -> 42.7 us
  Pallas kernels: 18.1 us -> 31 us
  local copies, waits for them, and re-layouts: 29.6 us -> 23.3 us
  other arithmetic: 15.6 us -> 13.4 us
    ppermute x8 -> x9, waiting for transfers between devices: 56.4 us -> 42.7 us  [swap(): return lax.ppermute(block, 'sy', route)]
    pallas_call x1 -> x2, Pallas kernels: 18.1 us -> 31 us  [window_pass(): pl.pallas_call(kernel, grid=(heads,), in_specs=in_specs, out_specs=[qspec...]
    unnamed x17 -> x12, local copies, waits for them, and re-layouts: 7.27 us -> 2.91 us
    concatenate x2 -> x4, local copies, waits for them, and re-layouts: 0.11 us -> 2.47 us  [extended(): joined = jnp.concatenate([upper[member], lower[member]], axis=0)]
    convert_element_type x1, other arithmetic: 5.89 us -> 3.63 us  [on_device(): cross_total = (part_cross + back_forward).astype(jnp.bfloat16)]
    reshape x1, local copies, waits for them, and re-layouts: 2.96 us -> 1.17 us  [on_device(): do = grad_out.reshape(rows, width, channels)]
    reshape x1, local copies, waits for them, and re-layouts: 2.95 us -> 1.17 us  [on_device(): key_vecs.reshape(rows, width, channels)]
    concatenate x2 -> x4, other arithmetic: 4.34 us -> 5.92 us  [extended(): jnp.concatenate([joined[:, width - mf:], joined, joined[:, :mf]], axis=1)]
  transfers between devices with their start and end apart: 8 -> 9, of which waited for: 4 -> 4; matrix products, arithmetic and copies ran while one was open for 20% -> 21% of each run, Pallas kernels for 0% -> 13%
where the time goes in v4:
time: 121 us; the launch traced here: 120 us
  waiting for transfers between devices  42.7 us (35%)
  Pallas kernels  31 us (26%)
  local copies, waits for them, and re-layouts  23.3 us (19%)
  other arithmetic  13.4 us (11%)
  starting transfers between devices  9.07 us (7%)
    ppermute x9, waiting for transfers between devices, swap(): return lax.ppermute(block, 'sy', route)  42.7 us
    pallas_call x2, Pallas kernels, window_pass(): pl.pallas_call(kernel, grid=(heads,), in_specs=in_specs, out_specs=[qspec...  31 us
    ppermute x9, starting transfers between devices, swap(): return lax.ppermute(block, 'sy', route)  9.07 us
    concatenate x4, other arithmetic, extended(): jnp.concatenate([joined[:, width - mf:], joined, joined[:, :mf]], axis=1)  5.92 us
    convert_element_type x1, other arithmetic, on_device(): cross_total = (part_cross + back_forward).astype(jnp.bfloat16)  3.63 us
    another operation x1, other arithmetic  3.19 us
    reshape x1, local copies, waits for them, and re-layouts, on_device(): q = queries.reshape(rows, width, channels)  2.95 us
    unnamed x12, local copies, waits for them, and re-layouts  2.91 us
  transfers between devices with their start and end apart: 9, of which 4 were waited for; matrix products, arithmetic and copies ran while one was open for 21% of the time, Pallas kernels for 13%

profile of v4, /device:TPU:1, one launch (start us, length us, event | category | flops | bytes accessed | tf_op | source)
XLA Modules:
  0.0 120.1 jit_solution(13137457842978131259)
XLA Ops:
  0.6 0.0 copy-start.2
  0.6 0.0 copy-start
  0.7 2.4 %reshape.50 = bf16[4,64,1536]{2,1,0:T(8,128)(2,1)S(1)} reshape(bf16[4,32,2,1536]{3,2,1,0:T(2,128)(2,1)} %param.8) | data formatting | bytes 1572864 | tf_op jit(solution)/shard_map/reshape | solution.py:141
  3.0 0.1 collective-permute-start.3
  3.2 2.7 %collective-permute-start.1 = (bf16[4,64,1536]{2,1,0:T(8,128)(2,1)S(1)}, bf16[4,64,1536]{2,1,0:T(8,128)(2,1)}, u32[]{:S(2)}, u32[]{:S(2)}) collective-permute-start(bf16[4,64,1536]{2,1,0:T(8,128)(2,1)S(1)} %reshape.50), channel_id=1, source_target_pairs={{0,15},{1,2},{2,1},{3,4},{4,3},{5,6},{6,5},{7,8},{8,7},{9,10},{10,... | collective-permute-start | bytes 2359304 | tf_op jit(solution)/shard_map/ppermute | solution.py:20
  5.8 0.0 copy-done.2
  5.8 1.2 reshape.49
  7.0 0.0 copy-start.3
  7.0 3.5 %collective-permute-start.2 = (bf16[4,64,1536]{2,1,0:T(8,128)(2,1)}, bf16[4,64,1536]{2,1,0:T(8,128)(2,1)}, u32[]{:S(2)}, u32[]{:S(2)}) collective-permute-start(bf16[4,64,1536]{2,1,0:T(8,128)(2,1)} %reshape.49), channel_id=1, source_target_pairs={{0,1},{1,0},{2,3},{3,2},{4,5},{5,4},{6,7},{7,6},{8,9},{9,8},{10,11... | collective-permute-start | bytes 2359304 | tf_op jit(solution)/shard_map/ppermute | solution.py:20
  10.5 0.0 collective-permute-start
  10.5 0.0 copy-done
  10.5 1.2 reshape.43.refs_1_
  11.7 0.5 reshape.45
  12.2 0.0 copy-done.3
  12.2 0.1 copy.9
  12.3 0.2 copy.10
  12.5 0.7 reshape.44.refs_2_
  13.2 3.0 %reshape.42.refs_0_ = bf16[4,64,1536]{2,1,0:T(8,128)(2,1)} reshape(bf16[4,32,2,1536]{3,2,1,0:T(2,128)(2,1)} %param.6) | data formatting | bytes 1572864 | tf_op jit(solution)/shard_map/reshape | solution.py:130
  16.2 2.4 %reshape.46 = bf16[4,64,12,128]{3,2,1,0:T(8,128)(2,1)S(1)} reshape(bf16[4,32,2,1536]{3,2,1,0:T(2,128)(2,1)} %param.9) | data formatting | bytes 1572864 | tf_op jit(solution)/shard_map/reshape | solution.py:135
  18.6 0.6 fusion
  19.3 0.2 copy.19
  19.4 0.7 reshape.48.refs_3_
  20.2 0.1 constant_dynamic-update-slice_fusion.3
  20.2 1.2 constant_dynamic-update-slice_fusion.1
  21.4 0.0 collective-permute-done.3
  21.4 1.2 constant_dynamic-update-slice_fusion.2
  22.7 1.5 %pad_maximum_fusion.1.refs_5_ = bf16[8,80,1536]{2,1,0:T(8,128)(2,1)} fusion(bf16[8,8,1536]{2,1,0:T(8,128)(2,1)S(1)} %get-tuple-element.28, bf16[8,64,1536]{2,1,0:T(8,128)(2,1)S(1)} %constant_dynamic-update-slice_fusion.2, bf16[8,8,1536]{2,1,0:T(8,128)(2,1)S(1)} %get-tuple-element.27), kind=kLoop, calls=%fused_computation.5 | loop fusion | flops 5898240 | bytes 3932160 | tf_op jit(solution)/shard_map/concatenate | solution.py:147
  24.1 0.0 collective-permute-done.2
  24.1 1.2 constant_dynamic-update-slice_fusion
  25.4 1.5 %pad_maximum_fusion.refs_4_ = bf16[8,80,1536]{2,1,0:T(8,128)(2,1)} fusion(bf16[8,8,1536]{2,1,0:T(8,128)(2,1)S(1)} %get-tuple-element.30, bf16[8,64,1536]{2,1,0:T(8,128)(2,1)S(1)} %constant_dynamic-update-slice_fusion, bf16[8,8,1536]{2,1,0:T(8,128)(2,1)S(1)} %get-tuple-element.29), kind=kLoop, calls=%fused_computation.4 | loop fusion | flops 5898240 | bytes 3932160 | tf_op jit(solution)/shard_map/concatenate | solution.py:147
  26.9 15.4 %shard_map.85 = (f32[4,64,1536]{2,1,0:T(8,128)}, f32[2,4,64,1536]{3,2,1,0:T(8,128)}, f32[2,4,64,1536]{3,2,1,0:T(8,128)}) custom-call(bf16[4,64,1536]{2,1,0:T(8,128)(2,1)} %reshape.42.refs_0_, bf16[4,64,1536]{2,1,0:T(8,128)(2,1)} %reshape.43.refs_1_, f32[12,4,1,64]{3,2,1,0:T(1,128)} %reshape.44.refs_2_, f32[12,4,1,64]{3,2,1,0:T(1,128)} %reshape.48.refs_3_, ...), custom_call_target="tpu_custom_call" | custom-call | flops 1006632960 | bytes 15728640 | tf_op jit(solution)/shard_map/pallas_call | solution.py:105
  42.2 0.0 collective-permute-done.1
  42.2 0.0 collective-permute-done
  42.3 0.7 collective-permute-start.4
  42.9 0.1 collective-permute-start.5
  43.0 1.5 %constant_dynamic-update-slice_fusion.5 = (bf16[8,64,1536]{2,1,0:T(8,128)(2,1)S(1)}, bf16[8,64,1536]{2,1,0:T(8,128)(2,1)S(1)}) fusion(bf16[4,64,1536]{2,1,0:T(8,128)(2,1)} %collective-permute-done, bf16[4,64,1536]{2,1,0:T(8,128)(2,1)} %collective-permute-done.1), kind=kLoop, calls=%fused_computation.13 | loop fusion | bytes 3145728
  44.5 0.5 collective-permute-done.4
  45.1 0.1 constant_dynamic-update-slice_fusion.4
  45.2 1.0 collective-permute-done.5
  46.2 0.1 constant_dynamic-update-slice_fusion.6
  46.3 1.5 %pad_maximum_fusion.2.refs_4_ = bf16[8,80,1536]{2,1,0:T(8,128)(2,1)} fusion(bf16[8,8,1536]{2,1,0:T(8,128)(2,1)S(1)} %get-tuple-element.26, bf16[8,64,1536]{2,1,0:T(8,128)(2,1)S(1)} %constant_dynamic-update-slice_fusion.4, bf16[8,8,1536]{2,1,0:T(8,128)(2,1)S(1)} %get-tuple-element.25), kind=kLoop, calls=%fused_computation.6 | loop fusion | flops 5898240 | bytes 3932160 | tf_op jit(solution)/shard_map/concatenate | solution.py:147
  47.8 1.5 %pad_maximum_fusion.3.refs_5_ = bf16[8,80,1536]{2,1,0:T(8,128)(2,1)} fusion(bf16[8,8,1536]{2,1,0:T(8,128)(2,1)S(1)} %get-tuple-element.24, bf16[8,64,1536]{2,1,0:T(8,128)(2,1)S(1)} %constant_dynamic-update-slice_fusion.6, bf16[8,8,1536]{2,1,0:T(8,128)(2,1)S(1)} %get-tuple-element.23), kind=kLoop, calls=%fused_computation.7 | loop fusion | flops 5898240 | bytes 3932160 | tf_op jit(solution)/shard_map/concatenate | solution.py:147
  49.2 15.6 %shard_map.86 = (bf16[4,64,1536]{2,1,0:T(8,128)(2,1)}, f32[2,4,64,1536]{3,2,1,0:T(8,128)}, f32[2,4,64,1536]{3,2,1,0:T(8,128)}) custom-call(bf16[4,64,1536]{2,1,0:T(8,128)(2,1)} %reshape.42.refs_0_, bf16[4,64,1536]{2,1,0:T(8,128)(2,1)} %reshape.43.refs_1_, f32[12,4,1,64]{3,2,1,0:T(1,128)} %reshape.44.refs_2_, f32[12,4,1,64]{3,2,1,0:T(1,128)} %reshape.48.refs_3_, ...), custom_call_target="tpu_custom_call" | custom-call | flops 1006632960 | bytes 15728640 | tf_op jit(solution)/shard_map/pallas_call | solution.py:105
  64.8 0.4 collective-permute-start.7
  65.3 0.1 collective-permute-start.6
  65.4 8.5 %collective-permute-done.7 = f32[2,4,64,1536]{3,2,1,0:T(8,128)S(1)} collective-permute-done((f32[2,4,64,1536]{3,2,1,0:T(8,128)}, f32[2,4,64,1536]{3,2,1,0:T(8,128)S(1)}, u32[]{:S(2)}, u32[]{:S(2)}) %collective-permute-start.7) | collective-permute-done | bytes 3145760 | tf_op jit(solution)/shard_map/ppermute | solution.py:20
  73.8 0.0 copy-start.1
  73.8 3.6 %add_convert_fusion.1 = bf16[2,4,64,1536]{3,2,1,0:T(8,128)(2,1)} fusion(f32[2,4,64,1536]{3,2,1,0:T(8,128)} %get-tuple-element.19, f32[2,4,64,1536]{3,2,1,0:T(8,128)S(1)} %collective-permute-done.7), kind=kLoop, calls=%fused_computation.1 | loop fusion | flops 1572864 | bytes 7864320 | tf_op jit(solution)/shard_map/convert_element_type | solution.py:164
  77.5 1.5 %collective-permute-start.8 = (bf16[2,4,64,1536]{3,2,1,0:T(8,128)(2,1)}, bf16[2,4,64,1536]{3,2,1,0:T(8,128)(2,1)}, u32[]{:S(2)}, u32[]{:S(2)}) collective-permute-start(bf16[2,4,64,1536]{3,2,1,0:T(8,128)(2,1)} %add_convert_fusion.1), channel_id=1, source_target_pairs={{0,15},{1,2},{2,1},{3,4},{4,3},{5,6},{6,5},{7,8},{8,7},{9,10},{10,... | collective-permute-start | bytes 4718600 | tf_op jit(solution)/shard_map/ppermute | solution.py:20
  79.0 2.8 %reshape.51 = bf16[4,32,2,1536]{3,2,1,0:T(2,128)(2,1)} reshape(bf16[4,64,1536]{2,1,0:T(8,128)(2,1)} %get-tuple-element.16) | data formatting | bytes 1572864 | tf_op jit(solution)/shard_map/reshape | solution.py:169
  81.8 0.0 collective-permute-done.6
  81.8 32.7 %collective-permute-done.8 = bf16[2,4,64,1536]{3,2,1,0:T(8,128)(2,1)} collective-permute-done((bf16[2,4,64,1536]{3,2,1,0:T(8,128)(2,1)}, bf16[2,4,64,1536]{3,2,1,0:T(8,128)(2,1)}, u32[]{:S(2)}, u32[]{:S(2)}) %collective-permute-start.8) | collective-permute-done | bytes 1572896 | tf_op jit(solution)/shard_map/ppermute | solution.py:20
  114.5 0.0 copy-done.1
  114.5 3.2 %add_convert_fusion = bf16[2,4,64,1536]{3,2,1,0:T(8,128)(2,1)S(1)} fusion(bf16[2,4,64,1536]{3,2,1,0:T(8,128)(2,1)} %collective-permute-done.8, f32[2,4,64,1536]{3,2,1,0:T(8,128)S(1)} %copy-done.1, f32[2,4,64,1536]{3,2,1,0:T(8,128)} %collective-permute-done.6), kind=kLoop, calls=%fused_computation | loop fusion | flops 3145728 | bytes 9437184 | tf_op jit(solution)/shard_map/convert.1
  117.7 0.1 fusion.1
  117.8 1.2 convert_element_type.19
  119.0 1.2 convert_element_type.18
  (4 shorter events, 0.1 us)
Async XLA Ops:
  0.6 5.2 %copy-start.2 = (bf16[4,32,2,1536]{3,2,1,0:T(2,128)(2,1)S(1)}, bf16[4,32,2,1536]{3,2,1,0:T(2,128)(2,1)}, u32[]{:S(2)}) copy-start(bf16[4,32,2,1536]{3,2,1,0:T(2,128)(2,1)} %param.7) | copy-start | bytes 2359300
  0.6 9.8 %copy-start = (bf16[4,32,2,1536]{3,2,1,0:T(2,128)(2,1)S(1)}, bf16[4,32,2,1536]{3,2,1,0:T(2,128)(2,1)}, u32[]{:S(2)}) copy-start(bf16[4,32,2,1536]{3,2,1,0:T(2,128)(2,1)} %param.10) | copy-start | bytes 2359300
  3.0 18.4 %collective-permute-start.3 = (bf16[4,64,1536]{2,1,0:T(8,128)(2,1)S(1)}, bf16[4,64,1536]{2,1,0:T(8,128)(2,1)}, u32[]{:S(2)}, u32[]{:S(2)}) collective-permute-start(bf16[4,64,1536]{2,1,0:T(8,128)(2,1)S(1)} %reshape.50), channel_id=1, source_target_pairs={{0,1},{1,0},{2,3},{3,2},{4,5},{5,4},{6,7},{7,6},{8,9},{9,8},{10,11... | collective-permute-start | bytes 2359304 | tf_op jit(solution)/shard_map/ppermute | solution.py:20
  3.2 39.1 %collective-permute-start.1 = (bf16[4,64,1536]{2,1,0:T(8,128)(2,1)S(1)}, bf16[4,64,1536]{2,1,0:T(8,128)(2,1)}, u32[]{:S(2)}, u32[]{:S(2)}) collective-permute-start(bf16[4,64,1536]{2,1,0:T(8,128)(2,1)S(1)} %reshape.50), channel_id=1, source_target_pairs={{0,15},{1,2},{2,1},{3,4},{4,3},{5,6},{6,5},{7,8},{8,7},{9,10},{10,... | collective-permute-start | bytes 2359304 | tf_op jit(solution)/shard_map/ppermute | solution.py:20
  7.0 5.2 %copy-start.3 = (f32[4,32,2,12]{1,2,3,0:T(2,128)S(1)}, f32[4,32,2,12]{1,2,3,0:T(2,128)}, u32[]{:S(2)}) copy-start(f32[4,32,2,12]{1,2,3,0:T(2,128)} %param.11) | copy-start | bytes 36868
  7.0 17.1 %collective-permute-start.2 = (bf16[4,64,1536]{2,1,0:T(8,128)(2,1)}, bf16[4,64,1536]{2,1,0:T(8,128)(2,1)}, u32[]{:S(2)}, u32[]{:S(2)}) collective-permute-start(bf16[4,64,1536]{2,1,0:T(8,128)(2,1)} %reshape.49), channel_id=1, source_target_pairs={{0,1},{1,0},{2,3},{3,2},{4,5},{5,4},{6,7},{7,6},{8,9},{9,8},{10,11... | collective-permute-start | bytes 2359304 | tf_op jit(solution)/shard_map/ppermute | solution.py:20
  10.5 31.8 %collective-permute-start = (bf16[4,64,1536]{2,1,0:T(8,128)(2,1)}, bf16[4,64,1536]{2,1,0:T(8,128)(2,1)}, u32[]{:S(2)}, u32[]{:S(2)}) collective-permute-start(bf16[4,64,1536]{2,1,0:T(8,128)(2,1)} %reshape.49), channel_id=1, source_target_pairs={{0,15},{1,2},{2,1},{3,4},{4,3},{5,6},{6,5},{7,8},{8,7},{9,10},{10,... | collective-permute-start | bytes 2359304 | tf_op jit(solution)/shard_map/ppermute | solution.py:20
  42.3 2.8 %collective-permute-start.4 = (bf16[4,64,1536]{2,1,0:T(8,128)(2,1)}, bf16[4,64,1536]{2,1,0:T(8,128)(2,1)S(1)}, u32[]{:S(2)}, u32[]{:S(2)}) collective-permute-start(bf16[4,64,1536]{2,1,0:T(8,128)(2,1)} %collective-permute-done), channel_id=1, source_target_pairs={{0,1},{1,0},{2,3},{3,2},{4,5},{5,4},{6,7},{7,6},{8,9},{9,8},{10,11... | collective-permute-start | bytes 2359304 | tf_op jit(solution)/shard_map/ppermute | solution.py:20
  42.9 3.2 %collective-permute-start.5 = (bf16[4,64,1536]{2,1,0:T(8,128)(2,1)}, bf16[4,64,1536]{2,1,0:T(8,128)(2,1)S(1)}, u32[]{:S(2)}, u32[]{:S(2)}) collective-permute-start(bf16[4,64,1536]{2,1,0:T(8,128)(2,1)} %collective-permute-done.1), channel_id=1, source_target_pairs={{0,1},{1,0},{2,3},{3,2},{4,5},{5,4},{6,7},{7,6},{8,9},{9,8},{10,11... | collective-permute-start | bytes 2359304 | tf_op jit(solution)/shard_map/ppermute | solution.py:20
  64.8 9.0 %collective-permute-start.7 = (f32[2,4,64,1536]{3,2,1,0:T(8,128)}, f32[2,4,64,1536]{3,2,1,0:T(8,128)S(1)}, u32[]{:S(2)}, u32[]{:S(2)}) collective-permute-start(f32[2,4,64,1536]{3,2,1,0:T(8,128)} %get-tuple-element.20), channel_id=1, source_target_pairs={{0,1},{1,0},{2,3},{3,2},{4,5},{5,4},{6,7},{7,6},{8,9},{9,8},{10,11... | collective-permute-start | bytes 9437192 | tf_op jit(solution)/shard_map/ppermute | solution.py:20
  65.3 16.6 %collective-permute-start.6 = (f32[2,4,64,1536]{3,2,1,0:T(8,128)}, f32[2,4,64,1536]{3,2,1,0:T(8,128)}, u32[]{:S(2)}, u32[]{:S(2)}) collective-permute-start(f32[2,4,64,1536]{3,2,1,0:T(8,128)} %get-tuple-element.18), channel_id=1, source_target_pairs={{0,1},{1,0},{2,3},{3,2},{4,5},{5,4},{6,7},{7,6},{8,9},{9,8},{10,11... | collective-permute-start | bytes 9437192 | tf_op jit(solution)/shard_map/ppermute | solution.py:20
  73.8 40.6 %copy-start.1 = (f32[2,4,64,1536]{3,2,1,0:T(8,128)S(1)}, f32[2,4,64,1536]{3,2,1,0:T(8,128)}, u32[]{:S(2)}) copy-start(f32[2,4,64,1536]{3,2,1,0:T(8,128)} %get-tuple-element.17) | copy-start | bytes 9437188
  77.5 37.0 %collective-permute-start.8 = (bf16[2,4,64,1536]{3,2,1,0:T(8,128)(2,1)}, bf16[2,4,64,1536]{3,2,1,0:T(8,128)(2,1)}, u32[]{:S(2)}, u32[]{:S(2)}) collective-permute-start(bf16[2,4,64,1536]{3,2,1,0:T(8,128)(2,1)} %add_convert_fusion.1), channel_id=1, source_target_pairs={{0,15},{1,2},{2,1},{3,4},{4,3},{5,6},{6,5},{7,8},{8,7},{9,10},{10,... | collective-permute-start | bytes 4718600 | tf_op jit(solution)/shard_map/ppermute | solution.py:20

commit v5 on v4

--- a/solution.py
+++ b/solution.py
@@ -28,24 +28,38 @@
     return (i + 1) % n if i % 2 else (i - 1) % n
 
 
+def window_pieces(start, span, width):
+    if start + span <= width:
+        return [(0, start, span)]
+    return [(0, start, width - start), (width - start, 0, start + span - width)]
+
+
 def window_kernel(*refs, tiles, tf, mf, accumulate):
     if accumulate:
-        q_ref, do_ref, lse_ref, delta_ref, k_ref, v_ref, dqin_ref, dq_ref, first_ref, second_ref = refs
+        q_ref, do_ref, lse_ref, delta_ref, ka_ref, kb_ref, va_ref, vb_ref, dqin_ref = refs[:9]
     else:
-        q_ref, do_ref, lse_ref, delta_ref, k_ref, v_ref, dq_ref, first_ref, second_ref = refs
+        q_ref, do_ref, lse_ref, delta_ref, ka_ref, kb_ref, va_ref, vb_ref = refs[:8]
         dqin_ref = None
+    dq_ref, first_ref, second_ref = refs[-3:]
     scaling = HEAD_DIM ** (-0.5)
     rows = q_ref.shape[0]
-    krows = k_ref.shape[0]
     width = first_ref.shape[2]
     span = tf + 2 * mf
     first_ref[...] = jnp.zeros_like(first_ref)
     second_ref[...] = jnp.zeros_like(second_ref)
     targets = [first_ref, second_ref]
-    blocks = krows // rows
+
+    def window(refs_pair, pieces):
+        parts = []
+        for ref in refs_pair:
+            slabs = [ref[:, dst : dst + size, :] for _, dst, size in pieces]
+            parts.append(slabs[0] if len(slabs) == 1 else jnp.concatenate(slabs, axis=1))
+        return jnp.concatenate(parts, axis=0).reshape(len(refs_pair) * rows * span, HEAD_DIM)
+
     for b in range(tiles):
-        kw = k_ref[:, b * tf : b * tf + span, :].reshape(krows * span, HEAD_DIM)
-        vw = v_ref[:, b * tf : b * tf + span, :].reshape(krows * span, HEAD_DIM)
+        pieces = window_pieces(b * tf, span, width)
+        kw = window((ka_ref, kb_ref), pieces)
+        vw = window((va_ref, vb_ref), pieces)
         qb = q_ref[:, b * tf : (b + 1) * tf, :].reshape(rows * tf, HEAD_DIM)
         dob = do_ref[:, b * tf : (b + 1) * tf, :].reshape(rows * tf, HEAD_DIM)
         nt = (((1,), (1,)), ((), ()))
@@ -60,45 +74,32 @@
         if dqin_ref is not None:
             grad_q = grad_q + dqin_ref[:, b * tf : (b + 1) * tf, :]
         dq_ref[:, b * tf : (b + 1) * tf, :] = grad_q.astype(dq_ref.dtype)
-        grad_k = grad_k.reshape(blocks, rows, span, HEAD_DIM)
-        grad_v = grad_v.reshape(blocks, rows, span, HEAD_DIM)
-        start = b * tf - mf
-        pieces = []
-        if start < 0:
-            pieces.append((0, width + start, -start))
-            pieces.append((-start, 0, span + start))
-        elif start + span > width:
-            pieces.append((0, start, width - start))
-            pieces.append((width - start, 0, start + span - width))
-        else:
-            pieces.append((0, start, span))
+        grad_k = grad_k.reshape(2, rows, span, HEAD_DIM)
+        grad_v = grad_v.reshape(2, rows, span, HEAD_DIM)
         for block, target in enumerate(targets):
             for src, dst, size in pieces:
                 target[0, :, dst : dst + size, :] += grad_k[block, :, src : src + size, :]
                 target[1, :, dst : dst + size, :] += grad_v[block, :, src : src + size, :]
 
 
-def window_pass(q, do, lse_t, delta_t, k_ext, v_ext, dq_in, tiles, tf, mf):
+def window_pass(q, do, lse_t, delta_t, kv_a, kv_b, dq_in, tiles, tf, mf):
     rows, width, channels = q.shape
-    krows = k_ext.shape[0]
-    ext = k_ext.shape[1]
     heads = channels // HEAD_DIM
     accumulate = dq_in is not None
     kernel = functools.partial(window_kernel, tiles=tiles, tf=tf, mf=mf, accumulate=accumulate)
     qspec = pl.BlockSpec((rows, width, HEAD_DIM), lambda h: (0, 0, h))
-    kspec = pl.BlockSpec((krows, ext, HEAD_DIM), lambda h: (0, 0, h))
     sspec = pl.BlockSpec((None, tiles, 1, rows * tf), lambda h: (h, 0, 0, 0))
     pspec = pl.BlockSpec((2, rows, width, HEAD_DIM), lambda h: (0, 0, 0, h))
-    pairs = tiles * rows * tf * krows * (tf + 2 * mf) * heads
+    pairs = tiles * rows * tf * 2 * rows * (tf + 2 * mf) * heads
     cost = pl.CostEstimate(
         flops=10 * pairs * HEAD_DIM,
         transcendentals=pairs,
-        bytes_accessed=2 * (2 * q.size + 2 * k_ext.size + q.size) + 12 * krows * width * channels,
+        bytes_accessed=2 * 7 * q.size + 24 * q.size,
     )
     part = jax.ShapeDtypeStruct((2, rows, width, channels), jnp.float32)
     dq_type = jnp.bfloat16 if accumulate else jnp.float32
-    operands = [q, do, lse_t, delta_t, k_ext, v_ext]
-    in_specs = [qspec, qspec, sspec, sspec, kspec, kspec]
+    operands = [q, do, lse_t, delta_t, kv_a[0], kv_b[0], kv_a[1], kv_b[1]]
+    in_specs = [qspec, qspec, sspec, sspec, qspec, qspec, qspec, qspec]
     if accumulate:
         operands.append(dq_in)
         in_specs.append(qspec)
@@ -138,32 +139,27 @@
     lse_t = stats_tiles(log_norm.reshape(rows, width, heads), tiles, tf)
     delta_t = stats_tiles(row_delta, tiles, tf)
 
-    kv_own = (key_vecs.reshape(rows, width, channels), value_vecs.reshape(rows, width, channels))
+    kv_own = (
+        jnp.roll(key_vecs.reshape(rows, width, channels), mf, axis=1),
+        jnp.roll(value_vecs.reshape(rows, width, channels), mf, axis=1),
+    )
     kv_partner = swap(kv_own, core_partner)
     kv_cross = swap(kv_own, chip_neighbour)
 
-    def extended(upper, lower, member):
-        joined = jnp.concatenate([upper[member], lower[member]], axis=0)
-        return jnp.concatenate([joined[:, width - mf :], joined, joined[:, :mf]], axis=1)
-
     dq_local, part_own, part_partner = window_pass(
-        q, do, lse_t, delta_t,
-        extended(kv_own, kv_partner, 0), extended(kv_own, kv_partner, 1),
-        None, tiles, tf, mf,
+        q, do, lse_t, delta_t, kv_own, kv_partner, None, tiles, tf, mf
     )
     kv_cross, dq_local = lax.optimization_barrier((kv_cross, dq_local))
     kv_forward = swap(kv_cross, core_partner)
     back_partner = swap(part_partner, core_partner)
     dq, part_cross, part_forward = window_pass(
-        q, do, lse_t, delta_t,
-        extended(kv_cross, kv_forward, 0), extended(kv_cross, kv_forward, 1),
-        dq_local, tiles, tf, mf,
+        q, do, lse_t, delta_t, kv_cross, kv_forward, dq_local, tiles, tf, mf
     )
     back_forward = swap(part_forward, core_partner)
     own_total = part_own + back_partner
     cross_total = (part_cross + back_forward).astype(jnp.bfloat16)
     arrived = swap(cross_total, chip_neighbour)
-    total = own_total + arrived.astype(jnp.float32)
+    total = jnp.roll(own_total + arrived.astype(jnp.float32), -mf, axis=2)
     grad_keys = total[0].astype(jnp.bfloat16).reshape(rows, width_cells, frames, channels)
     grad_values = total[1].astype(jnp.bfloat16).reshape(rows, width_cells, frames, channels)
     grad_queries = dq.reshape(rows, width_cells, frames, channels)

time: 121 us -> 122 us (level)
  waiting for transfers between devices: 42.7 us -> 54.4 us
  other arithmetic: 13.4 us -> 8.57 us
  starting transfers between devices: 9.07 us -> 5.66 us
  local copies, waits for them, and re-layouts: 23.3 us -> 20.4 us
    ppermute x9, waiting for transfers between devices: 42.7 us -> 54.4 us  [swap(): return lax.ppermute(block, 'sy', route)]
    concatenate x4 -> x2, other arithmetic: 5.92 us -> 1 us  [the longest x1 0.94 us: on_device(): jnp.roll(key_vecs.reshape(rows, width, channels), mf, axis=1)]
    ppermute x9, starting transfers between devices: 9.07 us -> 5.66 us  [swap(): return lax.ppermute(block, 'sy', route)]
    add x0 -> x1, other arithmetic: none -> 3.19 us  [on_device(): total = jnp.roll(own_total + arrived.astype(jnp.float32), -mf, axis=2)]
    another operation x1, other arithmetic: 3.19 us -> 0.14 us
    concatenate x4 -> x0, local copies, waits for them, and re-layouts: 2.47 us -> none  [extended(): joined = jnp.concatenate([upper[member], lower[member]], axis=0)]
    unnamed x12 -> x13, local copies, waits for them, and re-layouts: 2.91 us -> 1.04 us
    reshape x1, local copies, waits for them, and re-layouts: 1.17 us -> 2.62 us  [on_device(): key_vecs.reshape(rows, width, channels)]
  transfers between devices with their start and end apart: 9 -> 9, of which waited for: 4 -> 6; matrix products, arithmetic and copies ran while one was open for 21% -> 16% of each run, Pallas kernels for 13% -> 12%
where the time goes in v5:
time: 122 us; the launch traced here: 120 us
  waiting for transfers between devices  54.4 us (45%)
  Pallas kernels  30.3 us (25%)
  local copies, waits for them, and re-layouts  20.4 us (17%)
  other arithmetic  8.57 us (7%)
  starting transfers between devices  5.66 us (5%)
    ppermute x9, waiting for transfers between devices, swap(): return lax.ppermute(block, 'sy', route)  54.4 us
    pallas_call x2, Pallas kernels, window_pass(): pl.pallas_call(kernel, grid=(heads,), in_specs=in_specs, out_specs=[qspec...  30.3 us
    ppermute x9, starting transfers between devices, swap(): return lax.ppermute(block, 'sy', route)  5.66 us
    convert_element_type x1, other arithmetic, on_device(): cross_total = (part_cross + back_forward).astype(jnp.bfloat16)  3.62 us
    add x1, other arithmetic, on_device(): total = jnp.roll(own_total + arrived.astype(jnp.float32), -mf, axis=2)  3.19 us
    reshape x1, local copies, waits for them, and re-layouts, on_device(): q = queries.reshape(rows, width, channels)  2.95 us
    reshape x1, local copies, waits for them, and re-layouts, on_device(): grad_queries = dq.reshape(rows, width_cells, frames, channels)  2.84 us
    reshape x1, local copies, waits for them, and re-layouts, on_device(): key_vecs.reshape(rows, width, channels)  2.62 us
  transfers between devices with their start and end apart: 9, of which 6 were waited for; matrix products, arithmetic and copies ran while one was open for 16% of the time, Pallas kernels for 12%

profile of v5, /device:TPU:1, one launch (start us, length us, event | category | flops | bytes accessed | tf_op | source)
XLA Modules:
  0.0 120.2 jit_solution(17510404512207179506)
XLA Ops:
  0.6 2.3 %reshape.50 = bf16[4,64,1536]{2,1,0:T(8,128)(2,1)S(1)} reshape(bf16[4,32,2,1536]{3,2,1,0:T(2,128)(2,1)} %param.8) | data formatting | bytes 1572864 | tf_op jit(solution)/shard_map/reshape | solution.py:144
  3.0 0.1 pad_maximum_fusion.1.refs_6_
  3.0 0.0 copy-start.1
  3.1 0.0 copy-start
  3.1 0.1 collective-permute-start.3
  3.2 2.6 %reshape.49 = bf16[4,64,1536]{2,1,0:T(8,128)(2,1)S(1)} reshape(bf16[4,32,2,1536]{3,2,1,0:T(2,128)(2,1)} %param.7) | data formatting | bytes 1572864 | tf_op jit(solution)/shard_map/reshape | solution.py:143
  5.9 0.9 pad_maximum_fusion.refs_4_
  6.8 0.0 copy-start.5
  6.8 0.1 collective-permute-start.2
  6.9 0.0 copy-done.1
  6.9 2.6 %collective-permute-start.1 = (bf16[4,64,1536]{2,1,0:T(8,128)(2,1)S(1)}, bf16[4,64,1536]{2,1,0:T(8,128)(2,1)}, u32[]{:S(2)}, u32[]{:S(2)}) collective-permute-start(bf16[4,64,1536]{2,1,0:T(8,128)(2,1)S(1)} %pad_maximum_fusion.1.refs_6_), channel_id=1, source_target_pairs={{0,15},{1,2},{2,1},{3,4},{4,3},{5,6},{6,5},{7,8},{8,7},{9,10},{10,... | collective-permute-start | bytes 2359304 | tf_op jit(solution)/shard_map/ppermute | solution.py:20
  9.6 0.0 collective-permute-start
  9.6 0.0 copy-done
  9.6 1.2 reshape.43.refs_1_
  10.8 0.5 reshape.45
  11.3 0.0 copy-done.5
  11.3 0.1 copy.9
  11.5 0.2 copy.10
  11.6 0.7 reshape.44.refs_2_
  12.4 3.0 %reshape.42.refs_0_ = bf16[4,64,1536]{2,1,0:T(8,128)(2,1)} reshape(bf16[4,32,2,1536]{3,2,1,0:T(2,128)(2,1)} %param.6) | data formatting | bytes 1572864 | tf_op jit(solution)/shard_map/reshape | solution.py:131
  15.3 2.4 %reshape.46 = bf16[4,64,12,128]{3,2,1,0:T(8,128)(2,1)S(1)} reshape(bf16[4,32,2,1536]{3,2,1,0:T(2,128)(2,1)} %param.9) | data formatting | bytes 1572864 | tf_op jit(solution)/shard_map/reshape | solution.py:136
  17.8 0.6 fusion
  18.4 0.2 copy.19
  18.6 0.7 reshape.48.refs_3_
  19.3 0.0 collective-permute-done.3.refs_7_
  19.3 0.0 collective-permute-done.2.refs_5_
  19.3 15.0 %shard_map.85 = (f32[4,64,1536]{2,1,0:T(8,128)}, f32[2,4,64,1536]{3,2,1,0:T(8,128)}, f32[2,4,64,1536]{3,2,1,0:T(8,128)}) custom-call(bf16[4,64,1536]{2,1,0:T(8,128)(2,1)} %reshape.42.refs_0_, bf16[4,64,1536]{2,1,0:T(8,128)(2,1)} %reshape.43.refs_1_, f32[12,4,1,64]{3,2,1,0:T(1,128)} %reshape.44.refs_2_, f32[12,4,1,64]{3,2,1,0:T(1,128)} %reshape.48.refs_3_, ...), custom_call_target="tpu_custom_call" | custom-call | flops 1006632960 | bytes 14942208 | tf_op jit(solution)/shard_map/pallas_call | solution.py:106
  34.3 1.9 %collective-permute-done.1.refs_6_ = bf16[4,64,1536]{2,1,0:T(8,128)(2,1)} collective-permute-done((bf16[4,64,1536]{2,1,0:T(8,128)(2,1)S(1)}, bf16[4,64,1536]{2,1,0:T(8,128)(2,1)}, u32[]{:S(2)}, u32[]{:S(2)}) %collective-permute-start.1) | collective-permute-done | bytes 786464 | tf_op jit(solution)/shard_map/ppermute | solution.py:20
  36.2 8.4 %collective-permute-done.refs_4_ = bf16[4,64,1536]{2,1,0:T(8,128)(2,1)} collective-permute-done((bf16[4,64,1536]{2,1,0:T(8,128)(2,1)}, bf16[4,64,1536]{2,1,0:T(8,128)(2,1)}, u32[]{:S(2)}, u32[]{:S(2)}) %collective-permute-start) | collective-permute-done | bytes 786464 | tf_op jit(solution)/shard_map/ppermute | solution.py:20
  44.6 0.0 collective-permute-start.4
  44.6 0.5 collective-permute-start.5
  45.1 2.0 %collective-permute-done.4.refs_5_ = bf16[4,64,1536]{2,1,0:T(8,128)(2,1)S(1)} collective-permute-done((bf16[4,64,1536]{2,1,0:T(8,128)(2,1)}, bf16[4,64,1536]{2,1,0:T(8,128)(2,1)S(1)}, u32[]{:S(2)}, u32[]{:S(2)}) %collective-permute-start.4) | collective-permute-done | bytes 786464 | tf_op jit(solution)/shard_map/ppermute | solution.py:20
  47.1 0.0 copy-start.3
  47.1 1.1 collective-permute-done.5.refs_7_
  48.2 0.0 copy-done.3
  48.3 0.0 copy-start.4
  48.3 0.9 copy-done.4
  49.1 15.4 %shard_map.86 = (bf16[4,64,1536]{2,1,0:T(8,128)(2,1)}, f32[2,4,64,1536]{3,2,1,0:T(8,128)}, f32[2,4,64,1536]{3,2,1,0:T(8,128)}) custom-call(bf16[4,64,1536]{2,1,0:T(8,128)(2,1)} %reshape.42.refs_0_, bf16[4,64,1536]{2,1,0:T(8,128)(2,1)} %reshape.43.refs_1_, f32[12,4,1,64]{3,2,1,0:T(1,128)} %reshape.44.refs_2_, f32[12,4,1,64]{3,2,1,0:T(1,128)} %reshape.48.refs_3_, ...), custom_call_target="tpu_custom_call" | custom-call | flops 1006632960 | bytes 14942208 | tf_op jit(solution)/shard_map/pallas_call | solution.py:106
  64.5 0.2 collective-permute-start.7
  64.7 0.4 collective-permute-start.6
  65.1 8.5 %collective-permute-done.7 = f32[2,4,64,1536]{3,2,1,0:T(8,128)S(1)} collective-permute-done((f32[2,4,64,1536]{3,2,1,0:T(8,128)}, f32[2,4,64,1536]{3,2,1,0:T(8,128)S(1)}, u32[]{:S(2)}, u32[]{:S(2)}) %collective-permute-start.7) | collective-permute-done | bytes 3145760 | tf_op jit(solution)/shard_map/ppermute | solution.py:20
  73.6 0.0 copy-start.2
  73.6 3.6 %add_convert_fusion = bf16[2,4,64,1536]{3,2,1,0:T(8,128)(2,1)} fusion(f32[2,4,64,1536]{3,2,1,0:T(8,128)} %get-tuple-element.19, f32[2,4,64,1536]{3,2,1,0:T(8,128)S(1)} %collective-permute-done.7), kind=kLoop, calls=%fused_computation.2 | loop fusion | flops 1572864 | bytes 7864320 | tf_op jit(solution)/shard_map/convert_element_type | solution.py:160
  77.2 1.7 %collective-permute-start.8 = (bf16[2,4,64,1536]{3,2,1,0:T(8,128)(2,1)}, bf16[2,4,64,1536]{3,2,1,0:T(8,128)(2,1)}, u32[]{:S(2)}, u32[]{:S(2)}) collective-permute-start(bf16[2,4,64,1536]{3,2,1,0:T(8,128)(2,1)} %add_convert_fusion), channel_id=1, source_target_pairs={{0,15},{1,2},{2,1},{3,4},{4,3},{5,6},{6,5},{7,8},{8,7},{9,10},{10,... | collective-permute-start | bytes 4718600 | tf_op jit(solution)/shard_map/ppermute | solution.py:20
  78.9 2.8 %reshape.51 = bf16[4,32,2,1536]{3,2,1,0:T(2,128)(2,1)} reshape(bf16[4,64,1536]{2,1,0:T(8,128)(2,1)} %get-tuple-element.16) | data formatting | bytes 1572864 | tf_op jit(solution)/shard_map/reshape | solution.py:165
  81.7 0.0 collective-permute-done.6
  81.7 32.5 %collective-permute-done.8 = bf16[2,4,64,1536]{3,2,1,0:T(8,128)(2,1)} collective-permute-done((bf16[2,4,64,1536]{3,2,1,0:T(8,128)(2,1)}, bf16[2,4,64,1536]{3,2,1,0:T(8,128)(2,1)}, u32[]{:S(2)}, u32[]{:S(2)}) %collective-permute-start.8) | collective-permute-done | bytes 1572896 | tf_op jit(solution)/shard_map/ppermute | solution.py:20
  114.2 0.0 copy-done.2
  114.2 3.2 %convert_add_fusion = bf16[2,4,64,1536]{3,2,1,0:T(8,128)(2,1)S(1)} fusion(bf16[2,4,64,1536]{3,2,1,0:T(8,128)(2,1)} %collective-permute-done.8, f32[2,4,64,1536]{3,2,1,0:T(8,128)S(1)} %copy-done.2, f32[2,4,64,1536]{3,2,1,0:T(8,128)} %collective-permute-done.6), kind=kLoop, calls=%fused_computation.1 | loop fusion | flops 3145728 | bytes 9437184 | tf_op jit(solution)/shard_map/add | solution.py:162
  117.4 0.1 slice.42
  117.6 0.1 maximum_convert_fusion
  117.7 0.1 fusion.1
  117.8 1.2 convert_element_type.19
  119.0 1.2 convert_element_type.18
  (5 shorter events, 0.1 us)
Async XLA Ops:
  3.0 3.9 %copy-start.1 = (bf16[4,64,1536]{2,1,0:T(8,128)(2,1)}, bf16[4,64,1536]{2,1,0:T(8,128)(2,1)S(1)}, u32[]{:S(2)}) copy-start(bf16[4,64,1536]{2,1,0:T(8,128)(2,1)S(1)} %pad_maximum_fusion.1.refs_6_) | copy-start | bytes 2359300
  3.1 6.5 %copy-start = (bf16[4,32,2,1536]{3,2,1,0:T(2,128)(2,1)S(1)}, bf16[4,32,2,1536]{3,2,1,0:T(2,128)(2,1)}, u32[]{:S(2)}) copy-start(bf16[4,32,2,1536]{3,2,1,0:T(2,128)(2,1)} %param.10) | copy-start | bytes 2359300
  3.1 16.2 %collective-permute-start.3 = (bf16[4,64,1536]{2,1,0:T(8,128)(2,1)S(1)}, bf16[4,64,1536]{2,1,0:T(8,128)(2,1)}, u32[]{:S(2)}, u32[]{:S(2)}) collective-permute-start(bf16[4,64,1536]{2,1,0:T(8,128)(2,1)S(1)} %pad_maximum_fusion.1.refs_6_), channel_id=1, source_target_pairs={{0,1},{1,0},{2,3},{3,2},{4,5},{5,4},{6,7},{7,6},{8,9},{9,8},{10,11... | collective-permute-start | bytes 2359304 | tf_op jit(solution)/shard_map/ppermute | solution.py:20
  6.8 4.5 %copy-start.5 = (f32[4,32,2,12]{1,2,3,0:T(2,128)S(1)}, f32[4,32,2,12]{1,2,3,0:T(2,128)}, u32[]{:S(2)}) copy-start(f32[4,32,2,12]{1,2,3,0:T(2,128)} %param.11) | copy-start | bytes 36868
  6.8 12.5 %collective-permute-start.2 = (bf16[4,64,1536]{2,1,0:T(8,128)(2,1)}, bf16[4,64,1536]{2,1,0:T(8,128)(2,1)}, u32[]{:S(2)}, u32[]{:S(2)}) collective-permute-start(bf16[4,64,1536]{2,1,0:T(8,128)(2,1)} %pad_maximum_fusion.refs_4_), channel_id=1, source_target_pairs={{0,1},{1,0},{2,3},{3,2},{4,5},{5,4},{6,7},{7,6},{8,9},{9,8},{10,11... | collective-permute-start | bytes 2359304 | tf_op jit(solution)/shard_map/ppermute | solution.py:20
  6.9 29.3 %collective-permute-start.1 = (bf16[4,64,1536]{2,1,0:T(8,128)(2,1)S(1)}, bf16[4,64,1536]{2,1,0:T(8,128)(2,1)}, u32[]{:S(2)}, u32[]{:S(2)}) collective-permute-start(bf16[4,64,1536]{2,1,0:T(8,128)(2,1)S(1)} %pad_maximum_fusion.1.refs_6_), channel_id=1, source_target_pairs={{0,15},{1,2},{2,1},{3,4},{4,3},{5,6},{6,5},{7,8},{8,7},{9,10},{10,... | collective-permute-start | bytes 2359304 | tf_op jit(solution)/shard_map/ppermute | solution.py:20
  9.6 35.1 %collective-permute-start = (bf16[4,64,1536]{2,1,0:T(8,128)(2,1)}, bf16[4,64,1536]{2,1,0:T(8,128)(2,1)}, u32[]{:S(2)}, u32[]{:S(2)}) collective-permute-start(bf16[4,64,1536]{2,1,0:T(8,128)(2,1)} %pad_maximum_fusion.refs_4_), channel_id=1, source_target_pairs={{0,15},{1,2},{2,1},{3,4},{4,3},{5,6},{6,5},{7,8},{8,7},{9,10},{10,... | collective-permute-start | bytes 2359304 | tf_op jit(solution)/shard_map/ppermute | solution.py:20
  44.6 2.5 %collective-permute-start.4 = (bf16[4,64,1536]{2,1,0:T(8,128)(2,1)}, bf16[4,64,1536]{2,1,0:T(8,128)(2,1)S(1)}, u32[]{:S(2)}, u32[]{:S(2)}) collective-permute-start(bf16[4,64,1536]{2,1,0:T(8,128)(2,1)} %collective-permute-done.refs_4_), channel_id=1, source_target_pairs={{0,1},{1,0},{2,3},{3,2},{4,5},{5,4},{6,7},{7,6},{8,9},{9,8},{10,11... | collective-permute-start | bytes 2359304 | tf_op jit(solution)/shard_map/ppermute | solution.py:20
  44.6 3.6 %collective-permute-start.5 = (bf16[4,64,1536]{2,1,0:T(8,128)(2,1)}, bf16[4,64,1536]{2,1,0:T(8,128)(2,1)S(1)}, u32[]{:S(2)}, u32[]{:S(2)}) collective-permute-start(bf16[4,64,1536]{2,1,0:T(8,128)(2,1)} %collective-permute-done.1.refs_6_), channel_id=1, source_target_pairs={{0,1},{1,0},{2,3},{3,2},{4,5},{5,4},{6,7},{7,6},{8,9},{9,8},{10,11... | collective-permute-start | bytes 2359304 | tf_op jit(solution)/shard_map/ppermute | solution.py:20
  47.1 1.1 copy-start.3
  48.3 0.9 copy-start.4
  64.5 9.1 %collective-permute-start.7 = (f32[2,4,64,1536]{3,2,1,0:T(8,128)}, f32[2,4,64,1536]{3,2,1,0:T(8,128)S(1)}, u32[]{:S(2)}, u32[]{:S(2)}) collective-permute-start(f32[2,4,64,1536]{3,2,1,0:T(8,128)} %get-tuple-element.20), channel_id=1, source_target_pairs={{0,1},{1,0},{2,3},{3,2},{4,5},{5,4},{6,7},{7,6},{8,9},{9,8},{10,11... | collective-permute-start | bytes 9437192 | tf_op jit(solution)/shard_map/ppermute | solution.py:20
  64.7 17.0 %collective-permute-start.6 = (f32[2,4,64,1536]{3,2,1,0:T(8,128)}, f32[2,4,64,1536]{3,2,1,0:T(8,128)}, u32[]{:S(2)}, u32[]{:S(2)}) collective-permute-start(f32[2,4,64,1536]{3,2,1,0:T(8,128)} %get-tuple-element.18), channel_id=1, source_target_pairs={{0,1},{1,0},{2,3},{3,2},{4,5},{5,4},{6,7},{7,6},{8,9},{9,8},{10,11... | collective-permute-start | bytes 9437192 | tf_op jit(solution)/shard_map/ppermute | solution.py:20
  73.6 40.6 %copy-start.2 = (f32[2,4,64,1536]{3,2,1,0:T(8,128)S(1)}, f32[2,4,64,1536]{3,2,1,0:T(8,128)}, u32[]{:S(2)}) copy-start(f32[2,4,64,1536]{3,2,1,0:T(8,128)} %get-tuple-element.17) | copy-start | bytes 9437188
  77.2 37.0 %collective-permute-start.8 = (bf16[2,4,64,1536]{3,2,1,0:T(8,128)(2,1)}, bf16[2,4,64,1536]{3,2,1,0:T(8,128)(2,1)}, u32[]{:S(2)}, u32[]{:S(2)}) collective-permute-start(bf16[2,4,64,1536]{3,2,1,0:T(8,128)(2,1)} %add_convert_fusion), channel_id=1, source_target_pairs={{0,15},{1,2},{2,1},{3,4},{4,3},{5,6},{6,5},{7,8},{8,7},{9,10},{10,... | collective-permute-start | bytes 4718600 | tf_op jit(solution)/shard_map/ppermute | solution.py:20

commit v6 on v5

--- a/solution.py
+++ b/solution.py
@@ -82,19 +82,22 @@
                 target[1, :, dst : dst + size, :] += grad_v[block, :, src : src + size, :]
 
 
-def window_pass(q, do, lse_t, delta_t, kv_a, kv_b, dq_in, tiles, tf, mf):
-    rows, width, channels = q.shape
-    heads = channels // HEAD_DIM
+def window_pass(q, do, lse_t, delta_t, kv_a, kv_b, dq_in, tiles, tf, mf, first=0, heads=None):
+    rows, width, all_channels = q.shape
+    if heads is None:
+        heads = all_channels // HEAD_DIM
+    channels = heads * HEAD_DIM
     accumulate = dq_in is not None
     kernel = functools.partial(window_kernel, tiles=tiles, tf=tf, mf=mf, accumulate=accumulate)
-    qspec = pl.BlockSpec((rows, width, HEAD_DIM), lambda h: (0, 0, h))
-    sspec = pl.BlockSpec((None, tiles, 1, rows * tf), lambda h: (h, 0, 0, 0))
+    qspec = pl.BlockSpec((rows, width, HEAD_DIM), lambda h: (0, 0, h + first))
+    dqspec = pl.BlockSpec((rows, width, HEAD_DIM), lambda h: (0, 0, h))
+    sspec = pl.BlockSpec((None, tiles, 1, rows * tf), lambda h: (h + first, 0, 0, 0))
     pspec = pl.BlockSpec((2, rows, width, HEAD_DIM), lambda h: (0, 0, 0, h))
     pairs = tiles * rows * tf * 2 * rows * (tf + 2 * mf) * heads
     cost = pl.CostEstimate(
         flops=10 * pairs * HEAD_DIM,
         transcendentals=pairs,
-        bytes_accessed=2 * 7 * q.size + 24 * q.size,
+        bytes_accessed=38 * rows * width * channels,
     )
     part = jax.ShapeDtypeStruct((2, rows, width, channels), jnp.float32)
     dq_type = jnp.bfloat16 if accumulate else jnp.float32
@@ -107,7 +110,7 @@
         kernel,
         grid=(heads,),
         in_specs=in_specs,
-        out_specs=[qspec, pspec, pspec],
+        out_specs=[dqspec, pspec, pspec],
         out_shape=[jax.ShapeDtypeStruct((rows, width, channels), dq_type), part, part],
         cost_estimate=cost,
     )(*operands)
@@ -152,14 +155,22 @@
     kv_cross, dq_local = lax.optimization_barrier((kv_cross, dq_local))
     kv_forward = swap(kv_cross, core_partner)
     back_partner = swap(part_partner, core_partner)
-    dq, part_cross, part_forward = window_pass(
-        q, do, lse_t, delta_t, kv_cross, kv_forward, dq_local, tiles, tf, mf
-    )
-    back_forward = swap(part_forward, core_partner)
     own_total = part_own + back_partner
-    cross_total = (part_cross + back_forward).astype(jnp.bfloat16)
-    arrived = swap(cross_total, chip_neighbour)
-    total = jnp.roll(own_total + arrived.astype(jnp.float32), -mf, axis=2)
+    halves = 2 if heads % 2 == 0 else 1
+    count = heads // halves
+    dq_parts = []
+    arrived_parts = []
+    for half in range(halves):
+        dq_half, part_cross, part_forward = window_pass(
+            q, do, lse_t, delta_t, kv_cross, kv_forward, dq_local, tiles, tf, mf,
+            first=half * count, heads=count,
+        )
+        back_forward = swap(part_forward, core_partner)
+        cross_total = (part_cross + back_forward).astype(jnp.bfloat16)
+        arrived_parts.append(swap(cross_total, chip_neighbour).astype(jnp.float32))
+        dq_parts.append(dq_half)
+    dq = jnp.concatenate(dq_parts, axis=-1)
+    total = jnp.roll(own_total + jnp.concatenate(arrived_parts, axis=-1), -mf, axis=2)
     grad_keys = total[0].astype(jnp.bfloat16).reshape(rows, width_cells, frames, channels)
     grad_values = total[1].astype(jnp.bfloat16).reshape(rows, width_cells, frames, channels)
     grad_queries = dq.reshape(rows, width_cells, frames, channels)

time: 122 us -> 113 us (0.926)
  waiting for transfers between devices: 54.4 us -> 46.2 us
  local copies, waits for them, and re-layouts: 20.4 us -> 16.6 us
  starting transfers between devices: 5.66 us -> 7.74 us
  Pallas kernels: 30.3 us -> 32.1 us
    ppermute x9 -> x11, waiting for transfers between devices: 54.4 us -> 46.2 us  [swap(): return lax.ppermute(block, 'sy', route)]
    convert_element_type x1 -> x2, other arithmetic: 3.62 us -> 1.25 us  [on_device(): cross_total = (part_cross + back_forward).astype(jnp.bfloat16)]
    ppermute x9 -> x11, starting transfers between devices: 5.66 us -> 7.74 us  [swap(): return lax.ppermute(block, 'sy', route)]
    reshape x1, local copies, waits for them, and re-layouts: 2.27 us -> 0.3 us  [on_device(): value_vecs.reshape(rows, width, channels)]
    pallas_call x2 -> x3, Pallas kernels: 30.3 us -> 32.1 us  [window_pass(): pl.pallas_call(kernel, grid=(heads,), in_specs=in_specs, out_specs=[dqspe...]
    reshape x1, local copies, waits for them, and re-layouts: 2.84 us -> 1.18 us  [on_device(): grad_queries = dq.reshape(rows, width_cells, frames, channels)]
  transfers between devices with their start and end apart: 9 -> 11, of which waited for: 6 -> 7; matrix products, arithmetic and copies ran while one was open for 16% -> 12% of each run, Pallas kernels for 12% -> 29%
where the time goes in v6:
time: 113 us; the launch traced here: 111 us
  waiting for transfers between devices  46.2 us (41%)
  Pallas kernels  32.1 us (28%)
  local copies, waits for them, and re-layouts  16.6 us (15%)
  starting transfers between devices  7.74 us (7%)
  other arithmetic  7.66 us (7%)
    ppermute x11, waiting for transfers between devices, swap(): return lax.ppermute(block, 'sy', route)  46.2 us
    pallas_call x3, Pallas kernels, window_pass(): pl.pallas_call(kernel, grid=(heads,), in_specs=in_specs, out_specs=[dqspe...  32.1 us
    ppermute x11, starting transfers between devices, swap(): return lax.ppermute(block, 'sy', route)  7.74 us
    add x1, other arithmetic, on_device(): own_total + jnp.concatenate(arrived_parts, axis=-1)  3.68 us
    reshape x1, local copies, waits for them, and re-layouts, on_device(): q = queries.reshape(rows, width, channels)  2.95 us
    reshape x1, local copies, waits for them, and re-layouts, on_device(): outputs_fwd.reshape(rows, width, heads, HEAD_DIM)  2.44 us
    reshape x1, local copies, waits for them, and re-layouts, on_device(): key_vecs.reshape(rows, width, channels)  2.27 us
  transfers between devices with their start and end apart: 11, of which 7 were waited for; matrix products, arithmetic and copies ran while one was open for 12% of the time, Pallas kernels for 29%

profile of v6, /device:TPU:1, one launch (start us, length us, event | category | flops | bytes accessed | tf_op | source)
XLA Modules:
  0.0 111.2 jit_solution(15538663204228965177)
XLA Ops:
  0.6 2.3 %reshape.49 = bf16[4,64,1536]{2,1,0:T(8,128)(2,1)S(1)} reshape(bf16[4,32,2,1536]{3,2,1,0:T(2,128)(2,1)} %param.7) | data formatting | bytes 1572864 | tf_op jit(solution)/shard_map/reshape | solution.py:146
  2.9 0.0 copy-start.6
  3.0 0.9 pad_maximum_fusion.refs_4_
  3.9 0.1 collective-permute-start.2
  4.0 0.2 copy-done.6
  4.2 0.3 reshape.50
  4.5 0.0 copy-start.3
  4.6 1.0 pad_maximum_fusion.1.refs_6_
  5.6 0.2 collective-permute-start.3
  5.8 2.6 %collective-permute-start = (bf16[4,64,1536]{2,1,0:T(8,128)(2,1)}, bf16[4,64,1536]{2,1,0:T(8,128)(2,1)S(1)}, u32[]{:S(2)}, u32[]{:S(2)}) collective-permute-start(bf16[4,64,1536]{2,1,0:T(8,128)(2,1)} %pad_maximum_fusion.refs_4_), channel_id=1, source_target_pairs={{0,15},{1,2},{2,1},{3,4},{4,3},{5,6},{6,5},{7,8},{8,7},{9,10},{10,... | collective-permute-start | bytes 2359304 | tf_op jit(solution)/shard_map/ppermute | solution.py:20
  8.4 0.0 collective-permute-start.1
  8.5 0.0 copy-done.3
  8.5 0.5 reshape.45
  9.0 1.2 %reshape.43.refs_1_ = bf16[4,64,1536]{2,1,0:T(8,128)(2,1)} reshape(bf16[4,32,2,1536]{3,2,1,0:T(2,128)(2,1)S(1)} %copy-done.3) | data formatting | bytes 1572864 | tf_op jit(solution)/shard_map/reshape | solution.py:135
  10.2 2.4 %reshape.46 = bf16[4,64,12,128]{3,2,1,0:T(8,128)(2,1)S(1)} reshape(bf16[4,32,2,1536]{3,2,1,0:T(2,128)(2,1)} %param.9) | data formatting | bytes 1572864 | tf_op jit(solution)/shard_map/reshape | solution.py:139
  12.6 0.0 copy-start.9
  12.6 0.6 fusion
  13.3 0.2 copy.19
  13.4 0.7 reshape.48.refs_3_
  14.2 3.0 %reshape.42.refs_0_ = bf16[4,64,1536]{2,1,0:T(8,128)(2,1)} reshape(bf16[4,32,2,1536]{3,2,1,0:T(2,128)(2,1)} %param.6) | data formatting | bytes 1572864 | tf_op jit(solution)/shard_map/reshape | solution.py:134
  17.1 0.0 copy-done.9
  17.1 0.1 copy.9
  17.3 0.2 copy.10
  17.4 0.7 reshape.44.refs_2_
  18.2 0.0 collective-permute-done.2.refs_5_
  18.2 0.0 collective-permute-done.3.refs_7_
  18.2 15.0 %shard_map.85 = (f32[4,64,1536]{2,1,0:T(8,128)}, f32[2,4,64,1536]{3,2,1,0:T(8,128)}, f32[2,4,64,1536]{3,2,1,0:T(8,128)}) custom-call(bf16[4,64,1536]{2,1,0:T(8,128)(2,1)} %reshape.42.refs_0_, bf16[4,64,1536]{2,1,0:T(8,128)(2,1)} %reshape.43.refs_1_, f32[12,4,1,64]{3,2,1,0:T(1,128)} %reshape.44.refs_2_, f32[12,4,1,64]{3,2,1,0:T(1,128)} %reshape.48.refs_3_, ...), custom_call_target="tpu_custom_call" | custom-call | flops 1006632960 | bytes 14942208 | tf_op jit(solution)/shard_map/pallas_call | solution.py:109
  33.2 2.0 %collective-permute-done.refs_4_ = bf16[4,64,1536]{2,1,0:T(8,128)(2,1)S(1)} collective-permute-done((bf16[4,64,1536]{2,1,0:T(8,128)(2,1)}, bf16[4,64,1536]{2,1,0:T(8,128)(2,1)S(1)}, u32[]{:S(2)}, u32[]{:S(2)}) %collective-permute-start) | collective-permute-done | bytes 786464 | tf_op jit(solution)/shard_map/ppermute | solution.py:20
  35.2 0.0 copy-start
  35.2 8.5 %collective-permute-done.1.refs_6_ = bf16[4,64,1536]{2,1,0:T(8,128)(2,1)} collective-permute-done((bf16[4,64,1536]{2,1,0:T(8,128)(2,1)}, bf16[4,64,1536]{2,1,0:T(8,128)(2,1)}, u32[]{:S(2)}, u32[]{:S(2)}) %collective-permute-start.1) | collective-permute-done | bytes 786464 | tf_op jit(solution)/shard_map/ppermute | solution.py:20
  43.7 0.0 collective-permute-start.4
  43.7 0.5 collective-permute-start.5
  44.2 0.0 collective-permute-start.6
  44.2 2.9 %collective-permute-done.4.refs_5_ = bf16[4,64,1536]{2,1,0:T(8,128)(2,1)S(1)} collective-permute-done((bf16[4,64,1536]{2,1,0:T(8,128)(2,1)S(1)}, bf16[4,64,1536]{2,1,0:T(8,128)(2,1)S(1)}, u32[]{:S(2)}, u32[]{:S(2)}) %collective-permute-start.4) | collective-permute-done | bytes 786464 | tf_op jit(solution)/shard_map/ppermute | solution.py:20
  47.1 1.0 collective-permute-done.5.refs_7_
  48.1 0.0 copy-done
  48.1 0.0 copy-done.1
  48.1 0.9 copy-done.2
  49.0 8.5 %shard_map.86 = (bf16[4,64,768]{2,1,0:T(8,128)(2,1)}, f32[2,4,64,768]{3,2,1,0:T(8,128)}, f32[2,4,64,768]{3,2,1,0:T(8,128)}) custom-call(bf16[4,64,1536]{2,1,0:T(8,128)(2,1)} %reshape.42.refs_0_, bf16[4,64,1536]{2,1,0:T(8,128)(2,1)} %reshape.43.refs_1_, f32[12,4,1,64]{3,2,1,0:T(1,128)} %reshape.44.refs_2_, f32[12,4,1,64]{3,2,1,0:T(1,128)} %reshape.48.refs_3_, ...), custom_call_target="tpu_custom_call" | custom-call | flops 503316480 | bytes 7471104 | tf_op jit(solution)/shard_map/pallas_call | solution.py:109
  57.5 0.0 copy-start.5
  57.5 0.4 collective-permute-start.7
  58.0 8.6 %shard_map.87 = (bf16[4,64,768]{2,1,0:T(8,128)(2,1)}, f32[2,4,64,768]{3,2,1,0:T(8,128)}, f32[2,4,64,768]{3,2,1,0:T(8,128)}) custom-call(bf16[4,64,1536]{2,1,0:T(8,128)(2,1)} %reshape.42.refs_0_, bf16[4,64,1536]{2,1,0:T(8,128)(2,1)} %reshape.43.refs_1_, f32[12,4,1,64]{3,2,1,0:T(1,128)} %reshape.44.refs_2_, f32[12,4,1,64]{3,2,1,0:T(1,128)} %reshape.48.refs_3_, ...), custom_call_target="tpu_custom_call" | custom-call | flops 503316480 | bytes 7471104 | tf_op jit(solution)/shard_map/pallas_call | solution.py:109
  66.6 0.3 collective-permute-start.9
  66.8 0.0 collective-permute-done.7
  66.8 0.0 copy-done.5
  66.8 1.0 add_convert_fusion.1
  67.9 1.7 %collective-permute-start.8 = (bf16[2,4,64,768]{3,2,1,0:T(8,128)(2,1)}, bf16[2,4,64,768]{3,2,1,0:T(8,128)(2,1)S(1)}, u32[]{:S(2)}, u32[]{:S(2)}) collective-permute-start(bf16[2,4,64,768]{3,2,1,0:T(8,128)(2,1)} %add_convert_fusion.1), channel_id=1, source_target_pairs={{0,15},{1,2},{2,1},{3,4},{4,3},{5,6},{6,5},{7,8},{8,7},{9,10},{10,... | collective-permute-start | bytes 2359304 | tf_op jit(solution)/shard_map/ppermute | solution.py:20
  69.6 0.6 collective-permute-done.9
  70.2 0.0 copy-done.4
  70.2 0.2 add_convert_fusion
  70.5 1.8 %collective-permute-start.10 = (bf16[2,4,64,768]{3,2,1,0:T(8,128)(2,1)S(1)}, bf16[2,4,64,768]{3,2,1,0:T(8,128)(2,1)S(1)}, u32[]{:S(2)}, u32[]{:S(2)}) collective-permute-start(bf16[2,4,64,768]{3,2,1,0:T(8,128)(2,1)S(1)} %add_convert_fusion), channel_id=1, source_target_pairs={{0,15},{1,2},{2,1},{3,4},{4,3},{5,6},{6,5},{7,8},{8,7},{9,10},{10,... | collective-permute-start | bytes 2359304 | tf_op jit(solution)/shard_map/ppermute | solution.py:20
  72.3 0.0 copy-done.7
  72.3 0.0 copy-done.8
  72.3 0.1 pad_maximum_fusion.2
  72.4 1.2 %reshape.51 = bf16[4,32,2,1536]{3,2,1,0:T(2,128)(2,1)} reshape(bf16[4,64,1536]{2,1,0:T(8,128)(2,1)S(1)} %pad_maximum_fusion.2) | data formatting | bytes 1572864 | tf_op jit(solution)/shard_map/reshape | solution.py:176
  73.5 22.8 %collective-permute-done.8 = bf16[2,4,64,768]{3,2,1,0:T(8,128)(2,1)S(1)} collective-permute-done((bf16[2,4,64,768]{3,2,1,0:T(8,128)(2,1)}, bf16[2,4,64,768]{3,2,1,0:T(8,128)(2,1)S(1)}, u32[]{:S(2)}, u32[]{:S(2)}) %collective-permute-start.8) | collective-permute-done | bytes 786464 | tf_op jit(solution)/shard_map/ppermute | solution.py:20
  96.4 8.4 %collective-permute-done.10 = bf16[2,4,64,768]{3,2,1,0:T(8,128)(2,1)S(1)} collective-permute-done((bf16[2,4,64,768]{3,2,1,0:T(8,128)(2,1)S(1)}, bf16[2,4,64,768]{3,2,1,0:T(8,128)(2,1)S(1)}, u32[]{:S(2)}, u32[]{:S(2)}) %collective-permute-start.10) | collective-permute-done | bytes 786464 | tf_op jit(solution)/shard_map/ppermute | solution.py:20
  104.8 0.0 collective-permute-done.6
  104.8 3.7 %convert_add_fusion = bf16[2,4,64,1536]{3,2,1,0:T(8,128)(2,1)S(1)} fusion(f32[2,4,64,1536]{3,2,1,0:T(8,128)} %get-tuple-element.21, f32[2,4,64,1536]{3,2,1,0:T(8,128)} %collective-permute-done.6, bf16[2,4,64,768]{3,2,1,0:T(8,128)(2,1)S(1)} %collective-permute-done.10, bf16[2,4,64,768]{3,2,1,0:T(8,128)(2,1)S(1)} %collective-permute-done.8), kind=kLoop, calls=%fused_computation.1 | loop fusion | flops 5505024 | bytes 9437184 | tf_op jit(solution)/shard_map/add | solution.py:173
  108.5 0.1 slice.42
  108.6 0.1 maximum_convert_fusion
  108.7 0.1 fusion.1
  108.8 1.2 %convert_element_type.20 = bf16[4,32,2,1536]{3,2,1,0:T(2,128)(2,1)} reshape(bf16[1,4,64,1536]{3,2,1,0:T(8,128)(2,1)S(1)} %get-tuple-element.28) | data formatting | bytes 1572864 | tf_op jit(solution)/shard_map/convert_element_type | solution.py:174
  110.0 1.2 %convert_element_type.21 = bf16[4,32,2,1536]{3,2,1,0:T(2,128)(2,1)} reshape(bf16[1,4,64,1536]{3,2,1,0:T(8,128)(2,1)S(1)} %get-tuple-element.27) | data formatting | bytes 1572864 | tf_op jit(solution)/shard_map/convert_element_type | solution.py:175
  (10 shorter events, 0.1 us)
Async XLA Ops:
  2.9 1.3 %copy-start.6 = (bf16[4,32,2,1536]{3,2,1,0:T(2,128)(2,1)S(1)}, bf16[4,32,2,1536]{3,2,1,0:T(2,128)(2,1)}, u32[]{:S(2)}) copy-start(bf16[4,32,2,1536]{3,2,1,0:T(2,128)(2,1)} %param.8) | copy-start | bytes 2359300
  3.9 14.2 %collective-permute-start.2 = (bf16[4,64,1536]{2,1,0:T(8,128)(2,1)}, bf16[4,64,1536]{2,1,0:T(8,128)(2,1)}, u32[]{:S(2)}, u32[]{:S(2)}) collective-permute-start(bf16[4,64,1536]{2,1,0:T(8,128)(2,1)} %pad_maximum_fusion.refs_4_), channel_id=1, source_target_pairs={{0,1},{1,0},{2,3},{3,2},{4,5},{5,4},{6,7},{7,6},{8,9},{9,8},{10,11... | collective-permute-start | bytes 2359304 | tf_op jit(solution)/shard_map/ppermute | solution.py:20
  4.5 3.9 %copy-start.3 = (bf16[4,32,2,1536]{3,2,1,0:T(2,128)(2,1)S(1)}, bf16[4,32,2,1536]{3,2,1,0:T(2,128)(2,1)}, u32[]{:S(2)}) copy-start(bf16[4,32,2,1536]{3,2,1,0:T(2,128)(2,1)} %param.10) | copy-start | bytes 2359300
  5.6 12.6 %collective-permute-start.3 = (bf16[4,64,1536]{2,1,0:T(8,128)(2,1)}, bf16[4,64,1536]{2,1,0:T(8,128)(2,1)}, u32[]{:S(2)}, u32[]{:S(2)}) collective-permute-start(bf16[4,64,1536]{2,1,0:T(8,128)(2,1)} %pad_maximum_fusion.1.refs_6_), channel_id=1, source_target_pairs={{0,1},{1,0},{2,3},{3,2},{4,5},{5,4},{6,7},{7,6},{8,9},{9,8},{10,11... | collective-permute-start | bytes 2359304 | tf_op jit(solution)/shard_map/ppermute | solution.py:20
  5.8 29.4 %collective-permute-start = (bf16[4,64,1536]{2,1,0:T(8,128)(2,1)}, bf16[4,64,1536]{2,1,0:T(8,128)(2,1)S(1)}, u32[]{:S(2)}, u32[]{:S(2)}) collective-permute-start(bf16[4,64,1536]{2,1,0:T(8,128)(2,1)} %pad_maximum_fusion.refs_4_), channel_id=1, source_target_pairs={{0,15},{1,2},{2,1},{3,4},{4,3},{5,6},{6,5},{7,8},{8,7},{9,10},{10,... | collective-permute-start | bytes 2359304 | tf_op jit(solution)/shard_map/ppermute | solution.py:20
  8.4 35.3 %collective-permute-start.1 = (bf16[4,64,1536]{2,1,0:T(8,128)(2,1)}, bf16[4,64,1536]{2,1,0:T(8,128)(2,1)}, u32[]{:S(2)}, u32[]{:S(2)}) collective-permute-start(bf16[4,64,1536]{2,1,0:T(8,128)(2,1)} %pad_maximum_fusion.1.refs_6_), channel_id=1, source_target_pairs={{0,15},{1,2},{2,1},{3,4},{4,3},{5,6},{6,5},{7,8},{8,7},{9,10},{10,... | collective-permute-start | bytes 2359304 | tf_op jit(solution)/shard_map/ppermute | solution.py:20
  12.6 4.5 %copy-start.9 = (f32[4,32,2,12]{1,2,3,0:T(2,128)S(1)}, f32[4,32,2,12]{1,2,3,0:T(2,128)}, u32[]{:S(2)}) copy-start(f32[4,32,2,12]{1,2,3,0:T(2,128)} %param.11) | copy-start | bytes 36868
  35.2 12.9 %copy-start = (bf16[4,64,1536]{2,1,0:T(8,128)(2,1)}, bf16[4,64,1536]{2,1,0:T(8,128)(2,1)S(1)}, u32[]{:S(2)}) copy-start(bf16[4,64,1536]{2,1,0:T(8,128)(2,1)S(1)} %collective-permute-done.refs_4_) | copy-start | bytes 2359300
  43.7 3.4 %collective-permute-start.4 = (bf16[4,64,1536]{2,1,0:T(8,128)(2,1)S(1)}, bf16[4,64,1536]{2,1,0:T(8,128)(2,1)S(1)}, u32[]{:S(2)}, u32[]{:S(2)}) collective-permute-start(bf16[4,64,1536]{2,1,0:T(8,128)(2,1)S(1)} %collective-permute-done.refs_4_), channel_id=1, source_target_pairs={{0,1},{1,0},{2,3},{3,2},{4,5},{5,4},{6,7},{7,6},{8,9},{9,8},{10,11... | collective-permute-start | bytes 2359304 | tf_op jit(solution)/shard_map/ppermute | solution.py:20
  43.7 4.4 %collective-permute-start.5 = (bf16[4,64,1536]{2,1,0:T(8,128)(2,1)}, bf16[4,64,1536]{2,1,0:T(8,128)(2,1)S(1)}, u32[]{:S(2)}, u32[]{:S(2)}) collective-permute-start(bf16[4,64,1536]{2,1,0:T(8,128)(2,1)} %collective-permute-done.1.refs_6_), channel_id=1, source_target_pairs={{0,1},{1,0},{2,3},{3,2},{4,5},{5,4},{6,7},{7,6},{8,9},{9,8},{10,11... | collective-permute-start | bytes 2359304 | tf_op jit(solution)/shard_map/ppermute | solution.py:20
  44.2 60.6 %collective-permute-start.6 = (f32[2,4,64,1536]{3,2,1,0:T(8,128)}, f32[2,4,64,1536]{3,2,1,0:T(8,128)}, u32[]{:S(2)}, u32[]{:S(2)}) collective-permute-start(f32[2,4,64,1536]{3,2,1,0:T(8,128)} %get-tuple-element.22), channel_id=1, source_target_pairs={{0,1},{1,0},{2,3},{3,2},{4,5},{5,4},{6,7},{7,6},{8,9},{9,8},{10,11... | collective-permute-start | bytes 9437192 | tf_op jit(solution)/shard_map/ppermute | solution.py:20
  47.1 1.0 copy-start.1
  48.1 0.9 copy-start.2
  57.5 9.3 %copy-start.5 = (f32[2,4,64,768]{3,2,1,0:T(8,128)S(1)}, f32[2,4,64,768]{3,2,1,0:T(8,128)}, u32[]{:S(2)}) copy-start(f32[2,4,64,768]{3,2,1,0:T(8,128)} %get-tuple-element.23) | copy-start | bytes 4718596
  57.5 9.3 %collective-permute-start.7 = (f32[2,4,64,768]{3,2,1,0:T(8,128)}, f32[2,4,64,768]{3,2,1,0:T(8,128)S(1)}, u32[]{:S(2)}, u32[]{:S(2)}) collective-permute-start(f32[2,4,64,768]{3,2,1,0:T(8,128)} %get-tuple-element.24), channel_id=1, source_target_pairs={{0,1},{1,0},{2,3},{3,2},{4,5},{5,4},{6,7},{7,6},{8,9},{9,8},{10,11... | collective-permute-start | bytes 4718600 | tf_op jit(solution)/shard_map/ppermute | solution.py:20
  66.6 3.7 %collective-permute-start.9 = (f32[2,4,64,768]{3,2,1,0:T(8,128)}, f32[2,4,64,768]{3,2,1,0:T(8,128)S(1)}, u32[]{:S(2)}, u32[]{:S(2)}) collective-permute-start(f32[2,4,64,768]{3,2,1,0:T(8,128)} %get-tuple-element.26), channel_id=1, source_target_pairs={{0,1},{1,0},{2,3},{3,2},{4,5},{5,4},{6,7},{7,6},{8,9},{9,8},{10,11... | collective-permute-start | bytes 4718600 | tf_op jit(solution)/shard_map/ppermute | solution.py:20
  66.8 3.4 %copy-start.4 = (f32[2,4,64,768]{3,2,1,0:T(8,128)S(1)}, f32[2,4,64,768]{3,2,1,0:T(8,128)}, u32[]{:S(2)}) copy-start(f32[2,4,64,768]{3,2,1,0:T(8,128)} %get-tuple-element.25) | copy-start | bytes 4718596
  67.9 28.5 %collective-permute-start.8 = (bf16[2,4,64,768]{3,2,1,0:T(8,128)(2,1)}, bf16[2,4,64,768]{3,2,1,0:T(8,128)(2,1)S(1)}, u32[]{:S(2)}, u32[]{:S(2)}) collective-permute-start(bf16[2,4,64,768]{3,2,1,0:T(8,128)(2,1)} %add_convert_fusion.1), channel_id=1, source_target_pairs={{0,15},{1,2},{2,1},{3,4},{4,3},{5,6},{6,5},{7,8},{8,7},{9,10},{10,... | collective-permute-start | bytes 2359304 | tf_op jit(solution)/shard_map/ppermute | solution.py:20
  70.2 2.1 %copy-start.7 = (bf16[4,64,768]{2,1,0:T(8,128)(2,1)S(1)}, bf16[4,64,768]{2,1,0:T(8,128)(2,1)}, u32[]{:S(2)}) copy-start(bf16[4,64,768]{2,1,0:T(8,128)(2,1)} %get-tuple-element.19) | copy-start | bytes 1179652
  70.2 2.1 %copy-start.8 = (bf16[4,64,768]{2,1,0:T(8,128)(2,1)S(1)}, bf16[4,64,768]{2,1,0:T(8,128)(2,1)}, u32[]{:S(2)}) copy-start(bf16[4,64,768]{2,1,0:T(8,128)(2,1)} %get-tuple-element.20) | copy-start | bytes 1179652
  70.5 34.3 %collective-permute-start.10 = (bf16[2,4,64,768]{3,2,1,0:T(8,128)(2,1)S(1)}, bf16[2,4,64,768]{3,2,1,0:T(8,128)(2,1)S(1)}, u32[]{:S(2)}, u32[]{:S(2)}) collective-permute-start(bf16[2,4,64,768]{3,2,1,0:T(8,128)(2,1)S(1)} %add_convert_fusion), channel_id=1, source_target_pairs={{0,15},{1,2},{2,1},{3,4},{4,3},{5,6},{6,5},{7,8},{8,7},{9,10},{10,... | collective-permute-start | bytes 2359304 | tf_op jit(solution)/shard_map/ppermute | solution.py:20

commit v7 on v6

--- a/solution.py
+++ b/solution.py
@@ -63,13 +63,16 @@
         qb = q_ref[:, b * tf : (b + 1) * tf, :].reshape(rows * tf, HEAD_DIM)
         dob = do_ref[:, b * tf : (b + 1) * tf, :].reshape(rows * tf, HEAD_DIM)
         nt = (((1,), (1,)), ((), ()))
-        scores = lax.dot_general(kw, qb, nt, preferred_element_type=jnp.float32) * scaling
+        tn = (((0,), (0,)), ((), ()))
+        scores = lax.dot_general(qb, kw, nt, preferred_element_type=jnp.float32) * scaling
         attention = jnp.exp(scores - lse_ref[b])
-        grad_attention = lax.dot_general(vw, dob, nt, preferred_element_type=jnp.float32)
+        grad_attention = lax.dot_general(dob, vw, nt, preferred_element_type=jnp.float32)
         grad_scores = (attention * (grad_attention - delta_ref[b])).astype(jnp.bfloat16)
-        grad_v = jnp.dot(attention.astype(jnp.bfloat16), dob, preferred_element_type=jnp.float32)
-        grad_k = jnp.dot(grad_scores, qb, preferred_element_type=jnp.float32) * scaling
-        grad_q = jnp.dot(grad_scores.T, kw, preferred_element_type=jnp.float32) * scaling
+        grad_v = lax.dot_general(
+            attention.astype(jnp.bfloat16), dob, tn, preferred_element_type=jnp.float32
+        )
+        grad_k = lax.dot_general(grad_scores, qb, tn, preferred_element_type=jnp.float32) * scaling
+        grad_q = jnp.dot(grad_scores, kw, preferred_element_type=jnp.float32) * scaling
         grad_q = grad_q.reshape(rows, tf, HEAD_DIM)
         if dqin_ref is not None:
             grad_q = grad_q + dqin_ref[:, b * tf : (b + 1) * tf, :]
@@ -91,7 +94,7 @@
     kernel = functools.partial(window_kernel, tiles=tiles, tf=tf, mf=mf, accumulate=accumulate)
     qspec = pl.BlockSpec((rows, width, HEAD_DIM), lambda h: (0, 0, h + first))
     dqspec = pl.BlockSpec((rows, width, HEAD_DIM), lambda h: (0, 0, h))
-    sspec = pl.BlockSpec((None, tiles, 1, rows * tf), lambda h: (h + first, 0, 0, 0))
+    sspec = pl.BlockSpec((None, tiles, rows * tf, 1), lambda h: (h + first, 0, 0, 0))
     pspec = pl.BlockSpec((2, rows, width, HEAD_DIM), lambda h: (0, 0, 0, h))
     pairs = tiles * rows * tf * 2 * rows * (tf + 2 * mf) * heads
     cost = pl.CostEstimate(
@@ -120,7 +123,7 @@
     rows, width, heads = stats.shape
     tiled = stats.reshape(rows, tiles, tf, heads)
     tiled = jnp.transpose(tiled, (3, 1, 0, 2))
-    return tiled.reshape(heads, tiles, 1, rows * tf)
+    return tiled.reshape(heads, tiles, rows * tf, 1)
 
 
 def on_device(queries, key_vecs, value_vecs, outputs_fwd, grad_out, log_norm):

time: 113 us -> 114 us (level)
  Pallas kernels: 32.1 us -> 36.2 us
  waiting for transfers between devices: 46.2 us -> 43.4 us
    pallas_call x3, Pallas kernels: 32.1 us -> 36.2 us  [window_pass(): pl.pallas_call(kernel, grid=(heads,), in_specs=in_specs, out_specs=[dqspe...]
    ppermute x11, waiting for transfers between devices: 46.2 us -> 43.4 us  [swap(): return lax.ppermute(block, 'sy', route)]
    reshape x2, local copies, waits for them, and re-layouts: 1.48 us -> 4.02 us  [stats_tiles(): return tiled.reshape(heads, tiles, rows * tf, 1)]
    reshape x1, local copies, waits for them, and re-layouts: 2.95 us -> 1.17 us  [on_device(): q = queries.reshape(rows, width, channels)]
  transfers between devices with their start and end apart: 11 -> 11, of which waited for: 7 -> 6; matrix products, arithmetic and copies ran while one was open for 12% -> 13% of each run, Pallas kernels for 29% -> 32%
where the time goes in v7:
time: 114 us; the launch traced here: 113 us
  waiting for transfers between devices  43.4 us (38%)
  Pallas kernels  36.2 us (32%)
  local copies, waits for them, and re-layouts  17.4 us (15%)
  starting transfers between devices  7.71 us (7%)
  other arithmetic  7.64 us (7%)
    ppermute x11, waiting for transfers between devices, swap(): return lax.ppermute(block, 'sy', route)  43.4 us
    pallas_call x3, Pallas kernels, window_pass(): pl.pallas_call(kernel, grid=(heads,), in_specs=in_specs, out_specs=[dqspe...  36.2 us
    ppermute x11, starting transfers between devices, swap(): return lax.ppermute(block, 'sy', route)  7.71 us
    reshape x2, local copies, waits for them, and re-layouts, stats_tiles(): return tiled.reshape(heads, tiles, rows * tf, 1)  4.02 us
    add x1, other arithmetic, on_device(): own_total + jnp.concatenate(arrived_parts, axis=-1)  3.68 us
    reshape x1, local copies, waits for them, and re-layouts, on_device(): outputs_fwd.reshape(rows, width, heads, HEAD_DIM)  2.44 us
  transfers between devices with their start and end apart: 11, of which 6 were waited for; matrix products, arithmetic and copies ran while one was open for 13% of the time, Pallas kernels for 32%

profile of v7, /device:TPU:1, one launch (start us, length us, event | category | flops | bytes accessed | tf_op | source)
XLA Modules:
  0.0 113.2 jit_solution(8118936912876594352)
XLA Ops:
  0.6 2.3 %reshape.49 = bf16[4,64,1536]{2,1,0:T(8,128)(2,1)S(1)} reshape(bf16[4,32,2,1536]{3,2,1,0:T(2,128)(2,1)} %param.7) | data formatting | bytes 1572864 | tf_op jit(solution)/shard_map/reshape | solution.py:149
  2.9 0.0 copy-start.6
  3.0 0.9 pad_maximum_fusion.refs_4_
  3.9 0.1 collective-permute-start.2
  4.0 0.2 copy-done.6
  4.2 0.3 reshape.50
  4.5 0.0 copy-start.3
  4.6 1.0 pad_maximum_fusion.1.refs_6_
  5.6 0.2 collective-permute-start.3
  5.8 2.6 %collective-permute-start = (bf16[4,64,1536]{2,1,0:T(8,128)(2,1)}, bf16[4,64,1536]{2,1,0:T(8,128)(2,1)S(1)}, u32[]{:S(2)}, u32[]{:S(2)}) collective-permute-start(bf16[4,64,1536]{2,1,0:T(8,128)(2,1)} %pad_maximum_fusion.refs_4_), channel_id=1, source_target_pairs={{0,15},{1,2},{2,1},{3,4},{4,3},{5,6},{6,5},{7,8},{8,7},{9,10},{10,... | collective-permute-start | bytes 2359304 | tf_op jit(solution)/shard_map/ppermute | solution.py:20
  8.4 0.0 collective-permute-start.1
  8.5 0.0 copy-done.3
  8.5 0.5 reshape.45
  9.0 1.2 %reshape.43.refs_1_ = bf16[4,64,1536]{2,1,0:T(8,128)(2,1)} reshape(bf16[4,32,2,1536]{3,2,1,0:T(2,128)(2,1)S(1)} %copy-done.3) | data formatting | bytes 1572864 | tf_op jit(solution)/shard_map/reshape | solution.py:138
  10.2 2.4 %reshape.46 = bf16[4,64,12,128]{3,2,1,0:T(8,128)(2,1)S(1)} reshape(bf16[4,32,2,1536]{3,2,1,0:T(2,128)(2,1)} %param.9) | data formatting | bytes 1572864 | tf_op jit(solution)/shard_map/reshape | solution.py:142
  12.6 0.0 copy-start.10
  12.6 0.6 fusion
  13.2 0.2 copy.25
  13.4 2.0 %reshape.56.refs_3_ = f32[12,4,64,1]{3,2,1,0:T(8,128)} reshape(f32[12,4,4,16]{3,2,1,0:T(4,128)S(1)} %bitcast.12) | data formatting | bytes 24576 | tf_op jit(solution)/shard_map/reshape | solution.py:126
  15.4 0.0 copy-done.10
  15.4 0.1 copy.9
  15.6 0.2 copy.10
  15.8 2.0 %reshape.55.refs_2_ = f32[12,4,64,1]{3,2,1,0:T(8,128)} reshape(f32[12,4,4,16]{3,2,1,0:T(4,128)S(1)} %copy.10) | data formatting | bytes 24576 | tf_op jit(solution)/shard_map/reshape | solution.py:126
  17.7 0.0 copy-done.7
  17.8 1.2 %reshape.42.refs_0_ = bf16[4,64,1536]{2,1,0:T(8,128)(2,1)} reshape(bf16[4,32,2,1536]{3,2,1,0:T(2,128)(2,1)S(1)} %copy-done.7) | data formatting | bytes 1572864 | tf_op jit(solution)/shard_map/reshape | solution.py:137
  18.9 0.0 collective-permute-done.2.refs_5_
  18.9 0.0 collective-permute-done.3.refs_7_
  18.9 17.0 %shard_map.85 = (f32[4,64,1536]{2,1,0:T(8,128)}, f32[2,4,64,1536]{3,2,1,0:T(8,128)}, f32[2,4,64,1536]{3,2,1,0:T(8,128)}) custom-call(bf16[4,64,1536]{2,1,0:T(8,128)(2,1)} %reshape.42.refs_0_, bf16[4,64,1536]{2,1,0:T(8,128)(2,1)} %reshape.43.refs_1_, f32[12,4,64,1]{3,2,1,0:T(8,128)} %reshape.55.refs_2_, f32[12,4,64,1]{3,2,1,0:T(8,128)} %reshape.56.refs_3_, ...), custom_call_target="tpu_custom_call" | custom-call | flops 1006632960 | bytes 14942208 | tf_op jit(solution)/shard_map/pallas_call | solution.py:112
  36.0 0.0 collective-permute-done.refs_4_
  36.0 0.0 copy-start
  36.0 7.7 %collective-permute-done.1.refs_6_ = bf16[4,64,1536]{2,1,0:T(8,128)(2,1)} collective-permute-done((bf16[4,64,1536]{2,1,0:T(8,128)(2,1)}, bf16[4,64,1536]{2,1,0:T(8,128)(2,1)}, u32[]{:S(2)}, u32[]{:S(2)}) %collective-permute-start.1) | collective-permute-done | bytes 786464 | tf_op jit(solution)/shard_map/ppermute | solution.py:20
  43.7 0.0 collective-permute-start.4
  43.7 0.5 collective-permute-start.5
  44.2 0.0 collective-permute-start.6
  44.2 2.9 %collective-permute-done.4.refs_5_ = bf16[4,64,1536]{2,1,0:T(8,128)(2,1)S(1)} collective-permute-done((bf16[4,64,1536]{2,1,0:T(8,128)(2,1)S(1)}, bf16[4,64,1536]{2,1,0:T(8,128)(2,1)S(1)}, u32[]{:S(2)}, u32[]{:S(2)}) %collective-permute-start.4) | collective-permute-done | bytes 786464 | tf_op jit(solution)/shard_map/ppermute | solution.py:20
  47.1 1.0 collective-permute-done.5.refs_7_
  48.1 0.0 copy-done
  48.1 0.0 copy-done.1
  48.1 0.9 copy-done.2
  49.0 9.6 %shard_map.86 = (bf16[4,64,768]{2,1,0:T(8,128)(2,1)}, f32[2,4,64,768]{3,2,1,0:T(8,128)}, f32[2,4,64,768]{3,2,1,0:T(8,128)}) custom-call(bf16[4,64,1536]{2,1,0:T(8,128)(2,1)} %reshape.42.refs_0_, bf16[4,64,1536]{2,1,0:T(8,128)(2,1)} %reshape.43.refs_1_, f32[12,4,64,1]{3,2,1,0:T(8,128)} %reshape.55.refs_2_, f32[12,4,64,1]{3,2,1,0:T(8,128)} %reshape.56.refs_3_, ...), custom_call_target="tpu_custom_call" | custom-call | flops 503316480 | bytes 7471104 | tf_op jit(solution)/shard_map/pallas_call | solution.py:112
  58.5 0.0 copy-start.5
  58.6 0.4 collective-permute-start.7
  59.0 9.6 %shard_map.87 = (bf16[4,64,768]{2,1,0:T(8,128)(2,1)}, f32[2,4,64,768]{3,2,1,0:T(8,128)}, f32[2,4,64,768]{3,2,1,0:T(8,128)}) custom-call(bf16[4,64,1536]{2,1,0:T(8,128)(2,1)} %reshape.42.refs_0_, bf16[4,64,1536]{2,1,0:T(8,128)(2,1)} %reshape.43.refs_1_, f32[12,4,64,1]{3,2,1,0:T(8,128)} %reshape.55.refs_2_, f32[12,4,64,1]{3,2,1,0:T(8,128)} %reshape.56.refs_3_, ...), custom_call_target="tpu_custom_call" | custom-call | flops 503316480 | bytes 7471104 | tf_op jit(solution)/shard_map/pallas_call | solution.py:112
  68.6 0.3 collective-permute-start.9
  68.9 0.0 collective-permute-done.7
  68.9 0.0 copy-done.5
  68.9 1.0 add_convert_fusion.1
  69.9 1.7 %collective-permute-start.8 = (bf16[2,4,64,768]{3,2,1,0:T(8,128)(2,1)}, bf16[2,4,64,768]{3,2,1,0:T(8,128)(2,1)S(1)}, u32[]{:S(2)}, u32[]{:S(2)}) collective-permute-start(bf16[2,4,64,768]{3,2,1,0:T(8,128)(2,1)} %add_convert_fusion.1), channel_id=1, source_target_pairs={{0,15},{1,2},{2,1},{3,4},{4,3},{5,6},{6,5},{7,8},{8,7},{9,10},{10,... | collective-permute-start | bytes 2359304 | tf_op jit(solution)/shard_map/ppermute | solution.py:20
  71.7 0.6 collective-permute-done.9
  72.3 0.0 copy-done.4
  72.3 0.2 add_convert_fusion
  72.5 1.8 %collective-permute-start.10 = (bf16[2,4,64,768]{3,2,1,0:T(8,128)(2,1)S(1)}, bf16[2,4,64,768]{3,2,1,0:T(8,128)(2,1)S(1)}, u32[]{:S(2)}, u32[]{:S(2)}) collective-permute-start(bf16[2,4,64,768]{3,2,1,0:T(8,128)(2,1)S(1)} %add_convert_fusion), channel_id=1, source_target_pairs={{0,15},{1,2},{2,1},{3,4},{4,3},{5,6},{6,5},{7,8},{8,7},{9,10},{10,... | collective-permute-start | bytes 2359304 | tf_op jit(solution)/shard_map/ppermute | solution.py:20
  74.3 0.0 copy-done.8
  74.4 0.1 pad_maximum_fusion.2
  74.4 1.2 %reshape.51 = bf16[4,32,2,1536]{3,2,1,0:T(2,128)(2,1)} reshape(bf16[4,64,1536]{2,1,0:T(8,128)(2,1)S(1)} %pad_maximum_fusion.2) | data formatting | bytes 1572864 | tf_op jit(solution)/shard_map/reshape | solution.py:179
  75.6 22.8 %collective-permute-done.8 = bf16[2,4,64,768]{3,2,1,0:T(8,128)(2,1)S(1)} collective-permute-done((bf16[2,4,64,768]{3,2,1,0:T(8,128)(2,1)}, bf16[2,4,64,768]{3,2,1,0:T(8,128)(2,1)S(1)}, u32[]{:S(2)}, u32[]{:S(2)}) %collective-permute-start.8) | collective-permute-done | bytes 786464 | tf_op jit(solution)/shard_map/ppermute | solution.py:20
  98.4 8.4 %collective-permute-done.10 = bf16[2,4,64,768]{3,2,1,0:T(8,128)(2,1)S(1)} collective-permute-done((bf16[2,4,64,768]{3,2,1,0:T(8,128)(2,1)S(1)}, bf16[2,4,64,768]{3,2,1,0:T(8,128)(2,1)S(1)}, u32[]{:S(2)}, u32[]{:S(2)}) %collective-permute-start.10) | collective-permute-done | bytes 786464 | tf_op jit(solution)/shard_map/ppermute | solution.py:20
  106.8 0.0 collective-permute-done.6
  106.8 3.7 %convert_add_fusion = bf16[2,4,64,1536]{3,2,1,0:T(8,128)(2,1)S(1)} fusion(f32[2,4,64,1536]{3,2,1,0:T(8,128)} %get-tuple-element.21, f32[2,4,64,1536]{3,2,1,0:T(8,128)} %collective-permute-done.6, bf16[2,4,64,768]{3,2,1,0:T(8,128)(2,1)S(1)} %collective-permute-done.10, bf16[2,4,64,768]{3,2,1,0:T(8,128)(2,1)S(1)} %collective-permute-done.8), kind=kLoop, calls=%fused_computation.1 | loop fusion | flops 5505024 | bytes 9437184 | tf_op jit(solution)/shard_map/add | solution.py:176
  110.5 0.1 slice.42
  110.6 0.1 maximum_convert_fusion
  110.8 0.1 fusion.1
  110.9 1.2 %convert_element_type.20 = bf16[4,32,2,1536]{3,2,1,0:T(2,128)(2,1)} reshape(bf16[1,4,64,1536]{3,2,1,0:T(8,128)(2,1)S(1)} %get-tuple-element.28) | data formatting | bytes 1572864 | tf_op jit(solution)/shard_map/convert_element_type | solution.py:177
  112.1 1.2 %convert_element_type.21 = bf16[4,32,2,1536]{3,2,1,0:T(2,128)(2,1)} reshape(bf16[1,4,64,1536]{3,2,1,0:T(8,128)(2,1)S(1)} %get-tuple-element.27) | data formatting | bytes 1572864 | tf_op jit(solution)/shard_map/convert_element_type | solution.py:178
  (12 shorter events, 0.1 us)
Async XLA Ops:
  2.9 1.3 %copy-start.6 = (bf16[4,32,2,1536]{3,2,1,0:T(2,128)(2,1)S(1)}, bf16[4,32,2,1536]{3,2,1,0:T(2,128)(2,1)}, u32[]{:S(2)}) copy-start(bf16[4,32,2,1536]{3,2,1,0:T(2,128)(2,1)} %param.8) | copy-start | bytes 2359300
  3.9 15.0 %collective-permute-start.2 = (bf16[4,64,1536]{2,1,0:T(8,128)(2,1)}, bf16[4,64,1536]{2,1,0:T(8,128)(2,1)}, u32[]{:S(2)}, u32[]{:S(2)}) collective-permute-start(bf16[4,64,1536]{2,1,0:T(8,128)(2,1)} %pad_maximum_fusion.refs_4_), channel_id=1, source_target_pairs={{0,1},{1,0},{2,3},{3,2},{4,5},{5,4},{6,7},{7,6},{8,9},{9,8},{10,11... | collective-permute-start | bytes 2359304 | tf_op jit(solution)/shard_map/ppermute | solution.py:20
  4.5 3.9 %copy-start.3 = (bf16[4,32,2,1536]{3,2,1,0:T(2,128)(2,1)S(1)}, bf16[4,32,2,1536]{3,2,1,0:T(2,128)(2,1)}, u32[]{:S(2)}) copy-start(bf16[4,32,2,1536]{3,2,1,0:T(2,128)(2,1)} %param.10) | copy-start | bytes 2359300
  5.6 13.4 %collective-permute-start.3 = (bf16[4,64,1536]{2,1,0:T(8,128)(2,1)}, bf16[4,64,1536]{2,1,0:T(8,128)(2,1)}, u32[]{:S(2)}, u32[]{:S(2)}) collective-permute-start(bf16[4,64,1536]{2,1,0:T(8,128)(2,1)} %pad_maximum_fusion.1.refs_6_), channel_id=1, source_target_pairs={{0,1},{1,0},{2,3},{3,2},{4,5},{5,4},{6,7},{7,6},{8,9},{9,8},{10,11... | collective-permute-start | bytes 2359304 | tf_op jit(solution)/shard_map/ppermute | solution.py:20
  5.8 30.2 %collective-permute-start = (bf16[4,64,1536]{2,1,0:T(8,128)(2,1)}, bf16[4,64,1536]{2,1,0:T(8,128)(2,1)S(1)}, u32[]{:S(2)}, u32[]{:S(2)}) collective-permute-start(bf16[4,64,1536]{2,1,0:T(8,128)(2,1)} %pad_maximum_fusion.refs_4_), channel_id=1, source_target_pairs={{0,15},{1,2},{2,1},{3,4},{4,3},{5,6},{6,5},{7,8},{8,7},{9,10},{10,... | collective-permute-start | bytes 2359304 | tf_op jit(solution)/shard_map/ppermute | solution.py:20
  8.4 35.3 %collective-permute-start.1 = (bf16[4,64,1536]{2,1,0:T(8,128)(2,1)}, bf16[4,64,1536]{2,1,0:T(8,128)(2,1)}, u32[]{:S(2)}, u32[]{:S(2)}) collective-permute-start(bf16[4,64,1536]{2,1,0:T(8,128)(2,1)} %pad_maximum_fusion.1.refs_6_), channel_id=1, source_target_pairs={{0,15},{1,2},{2,1},{3,4},{4,3},{5,6},{6,5},{7,8},{8,7},{9,10},{10,... | collective-permute-start | bytes 2359304 | tf_op jit(solution)/shard_map/ppermute | solution.py:20
  12.6 2.8 %copy-start.10 = (f32[4,32,2,12]{1,2,3,0:T(2,128)S(1)}, f32[4,32,2,12]{1,2,3,0:T(2,128)}, u32[]{:S(2)}) copy-start(f32[4,32,2,12]{1,2,3,0:T(2,128)} %param.11) | copy-start | bytes 36868
  13.4 4.3 %copy-start.7 = (bf16[4,32,2,1536]{3,2,1,0:T(2,128)(2,1)S(1)}, bf16[4,32,2,1536]{3,2,1,0:T(2,128)(2,1)}, u32[]{:S(2)}) copy-start(bf16[4,32,2,1536]{3,2,1,0:T(2,128)(2,1)} %param.6) | copy-start | bytes 2359300
  36.0 12.1 %copy-start = (bf16[4,64,1536]{2,1,0:T(8,128)(2,1)}, bf16[4,64,1536]{2,1,0:T(8,128)(2,1)S(1)}, u32[]{:S(2)}) copy-start(bf16[4,64,1536]{2,1,0:T(8,128)(2,1)S(1)} %collective-permute-done.refs_4_) | copy-start | bytes 2359300
  43.7 3.4 %collective-permute-start.4 = (bf16[4,64,1536]{2,1,0:T(8,128)(2,1)S(1)}, bf16[4,64,1536]{2,1,0:T(8,128)(2,1)S(1)}, u32[]{:S(2)}, u32[]{:S(2)}) collective-permute-start(bf16[4,64,1536]{2,1,0:T(8,128)(2,1)S(1)} %collective-permute-done.refs_4_), channel_id=1, source_target_pairs={{0,1},{1,0},{2,3},{3,2},{4,5},{5,4},{6,7},{7,6},{8,9},{9,8},{10,11... | collective-permute-start | bytes 2359304 | tf_op jit(solution)/shard_map/ppermute | solution.py:20
  43.7 4.4 %collective-permute-start.5 = (bf16[4,64,1536]{2,1,0:T(8,128)(2,1)}, bf16[4,64,1536]{2,1,0:T(8,128)(2,1)S(1)}, u32[]{:S(2)}, u32[]{:S(2)}) collective-permute-start(bf16[4,64,1536]{2,1,0:T(8,128)(2,1)} %collective-permute-done.1.refs_6_), channel_id=1, source_target_pairs={{0,1},{1,0},{2,3},{3,2},{4,5},{5,4},{6,7},{7,6},{8,9},{9,8},{10,11... | collective-permute-start | bytes 2359304 | tf_op jit(solution)/shard_map/ppermute | solution.py:20
  44.2 62.6 %collective-permute-start.6 = (f32[2,4,64,1536]{3,2,1,0:T(8,128)}, f32[2,4,64,1536]{3,2,1,0:T(8,128)}, u32[]{:S(2)}, u32[]{:S(2)}) collective-permute-start(f32[2,4,64,1536]{3,2,1,0:T(8,128)} %get-tuple-element.22), channel_id=1, source_target_pairs={{0,1},{1,0},{2,3},{3,2},{4,5},{5,4},{6,7},{7,6},{8,9},{9,8},{10,11... | collective-permute-start | bytes 9437192 | tf_op jit(solution)/shard_map/ppermute | solution.py:20
  47.1 1.0 copy-start.1
  48.1 0.9 copy-start.2
  58.5 10.3 %copy-start.5 = (f32[2,4,64,768]{3,2,1,0:T(8,128)S(1)}, f32[2,4,64,768]{3,2,1,0:T(8,128)}, u32[]{:S(2)}) copy-start(f32[2,4,64,768]{3,2,1,0:T(8,128)} %get-tuple-element.23) | copy-start | bytes 4718596
  58.6 10.3 %collective-permute-start.7 = (f32[2,4,64,768]{3,2,1,0:T(8,128)}, f32[2,4,64,768]{3,2,1,0:T(8,128)S(1)}, u32[]{:S(2)}, u32[]{:S(2)}) collective-permute-start(f32[2,4,64,768]{3,2,1,0:T(8,128)} %get-tuple-element.24), channel_id=1, source_target_pairs={{0,1},{1,0},{2,3},{3,2},{4,5},{5,4},{6,7},{7,6},{8,9},{9,8},{10,11... | collective-permute-start | bytes 4718600 | tf_op jit(solution)/shard_map/ppermute | solution.py:20
  68.6 3.7 %collective-permute-start.9 = (f32[2,4,64,768]{3,2,1,0:T(8,128)}, f32[2,4,64,768]{3,2,1,0:T(8,128)S(1)}, u32[]{:S(2)}, u32[]{:S(2)}) collective-permute-start(f32[2,4,64,768]{3,2,1,0:T(8,128)} %get-tuple-element.26), channel_id=1, source_target_pairs={{0,1},{1,0},{2,3},{3,2},{4,5},{5,4},{6,7},{7,6},{8,9},{9,8},{10,11... | collective-permute-start | bytes 4718600 | tf_op jit(solution)/shard_map/ppermute | solution.py:20
  68.9 3.4 %copy-start.4 = (f32[2,4,64,768]{3,2,1,0:T(8,128)S(1)}, f32[2,4,64,768]{3,2,1,0:T(8,128)}, u32[]{:S(2)}) copy-start(f32[2,4,64,768]{3,2,1,0:T(8,128)} %get-tuple-element.25) | copy-start | bytes 4718596
  69.9 28.5 %collective-permute-start.8 = (bf16[2,4,64,768]{3,2,1,0:T(8,128)(2,1)}, bf16[2,4,64,768]{3,2,1,0:T(8,128)(2,1)S(1)}, u32[]{:S(2)}, u32[]{:S(2)}) collective-permute-start(bf16[2,4,64,768]{3,2,1,0:T(8,128)(2,1)} %add_convert_fusion.1), channel_id=1, source_target_pairs={{0,15},{1,2},{2,1},{3,4},{4,3},{5,6},{6,5},{7,8},{8,7},{9,10},{10,... | collective-permute-start | bytes 2359304 | tf_op jit(solution)/shard_map/ppermute | solution.py:20
  72.3 2.0 %copy-start.8 = (bf16[4,64,768]{2,1,0:T(8,128)(2,1)S(1)}, bf16[4,64,768]{2,1,0:T(8,128)(2,1)}, u32[]{:S(2)}) copy-start(bf16[4,64,768]{2,1,0:T(8,128)(2,1)} %get-tuple-element.19) | copy-start | bytes 1179652
  72.3 2.0 %copy-start.9 = (bf16[4,64,768]{2,1,0:T(8,128)(2,1)S(1)}, bf16[4,64,768]{2,1,0:T(8,128)(2,1)}, u32[]{:S(2)}) copy-start(bf16[4,64,768]{2,1,0:T(8,128)(2,1)} %get-tuple-element.20) | copy-start | bytes 1179652
  72.5 34.3 %collective-permute-start.10 = (bf16[2,4,64,768]{3,2,1,0:T(8,128)(2,1)S(1)}, bf16[2,4,64,768]{3,2,1,0:T(8,128)(2,1)S(1)}, u32[]{:S(2)}, u32[]{:S(2)}) collective-permute-start(bf16[2,4,64,768]{3,2,1,0:T(8,128)(2,1)S(1)} %add_convert_fusion), channel_id=1, source_target_pairs={{0,15},{1,2},{2,1},{3,4},{4,3},{5,6},{6,5},{7,8},{8,7},{9,10},{10,... | collective-permute-start | bytes 2359304 | tf_op jit(solution)/shard_map/ppermute | solution.py:20

commit v8 on v5

v8 whole, which is shorter than its diff:
```python
import functools

import jax
import jax.numpy as jnp
from jax import lax
from jax.experimental import pallas as pl
from jax.experimental.pallas import tpu as pltpu
from jax.sharding import PartitionSpec as P

HEAD_DIM = 128
TILE = 8
MARGIN = 4


def swap(block, pairs_of):
    n = lax.axis_size("sy")
    route = []
    for i in range(n):
        route.append((i, pairs_of(i, n)))
    return lax.ppermute(block, "sy", route)


def core_partner(i, n):
    return i ^ 1


def chip_neighbour(i, n):
    return (i + 1) % n if i % 2 else (i - 1) % n


def window_pieces(start, span, width):
    if start + span <= width:
        return [(0, start, span)]
    return [(0, start, width - start), (width - start, 0, start + span - width)]


def window_kernel(*refs, nq, nk, tiles, tf, mf):
    q_refs = refs[0:nq]
    do_refs = refs[nq : 2 * nq]
    lse_ref, delta_ref = refs[2 * nq], refs[2 * nq + 1]
    k_refs = refs[2 * nq + 2 : 2 * nq + 2 + nk]
    v_refs = refs[2 * nq + 2 + nk : 2 * nq + 2 + 2 * nk]
    dq_refs = refs[2 * nq + 2 + 2 * nk : 3 * nq + 2 + 2 * nk]
    targets = refs[3 * nq + 2 + 2 * nk :]
    scaling = HEAD_DIM ** (-0.5)
    rows = q_refs[0].shape[0]
    width = targets[0].shape[2]
    span = tf + 2 * mf
    for target in targets:
        target[...] = jnp.zeros_like(target)

    def window(refs_list, pieces):
        parts = []
        for ref in refs_list:
            slabs = [ref[:, dst : dst + size, :] for _, dst, size in pieces]
            parts.append(slabs[0] if len(slabs) == 1 else jnp.concatenate(slabs, axis=1))
        joined = parts[0] if len(parts) == 1 else jnp.concatenate(parts, axis=0)
        return joined.reshape(len(refs_list) * rows * span, HEAD_DIM)

    def query_rows(refs_list, b):
        parts = [ref[:, b * tf : (b + 1) * tf, :].reshape(rows * tf, HEAD_DIM) for ref in refs_list]
        return parts[0] if len(parts) == 1 else jnp.concatenate(parts, axis=0)

    for b in range(tiles):
        pieces = window_pieces(b * tf, span, width)
        kw = window(k_refs, pieces)
        vw = window(v_refs, pieces)
        qb = query_rows(q_refs, b)
        dob = query_rows(do_refs, b)
        nt = (((1,), (1,)), ((), ()))
        scores = lax.dot_general(kw, qb, nt, preferred_element_type=jnp.float32) * scaling
        attention = jnp.exp(scores - lse_ref[b])
        grad_attention = lax.dot_general(vw, dob, nt, preferred_element_type=jnp.float32)
        grad_scores = (attention * (grad_attention - delta_ref[b])).astype(jnp.bfloat16)
        grad_v = jnp.dot(attention.astype(jnp.bfloat16), dob, preferred_element_type=jnp.float32)
        grad_k = jnp.dot(grad_scores, qb, preferred_element_type=jnp.float32) * scaling
        grad_q = jnp.dot(grad_scores.T, kw, preferred_element_type=jnp.float32) * scaling
        grad_q = grad_q.reshape(nq, rows, tf, HEAD_DIM)
        for source, dq_ref in enumerate(dq_refs):
            dq_ref[:, b * tf : (b + 1) * tf, :] = grad_q[source].astype(dq_ref.dtype)
        grad_k = grad_k.reshape(nk, rows, span, HEAD_DIM)
        grad_v = grad_v.reshape(nk, rows, span, HEAD_DIM)
        for block, target in enumerate(targets):
            for src, dst, size in pieces:
                target[0, :, dst : dst + size, :] += grad_k[block, :, src : src + size, :]
                target[1, :, dst : dst + size, :] += grad_v[block, :, src : src + size, :]


def window_pass(queries, grads, stats, keys, values, tiles, tf, mf):
    _, rows, width, channels = queries[0][0].shape
    heads = channels // HEAD_DIM
    nq, nk = len(queries), len(keys)
    kernel = functools.partial(window_kernel, nq=nq, nk=nk, tiles=tiles, tf=tf, mf=mf)

    def member_spec(member):
        return pl.BlockSpec((None, rows, width, HEAD_DIM), lambda h: (member, 0, 0, h))

    def stats_spec(member):
        return pl.BlockSpec((None, None, tiles, 1, nq * rows * tf), lambda h: (member, h, 0, 0, 0))

    qspec = pl.BlockSpec((rows, width, HEAD_DIM), lambda h: (0, 0, h))
    pspec = pl.BlockSpec((2, rows, width, HEAD_DIM), lambda h: (0, 0, 0, h))
    pairs = tiles * nq * rows * tf * nk * rows * (tf + 2 * mf) * heads
    cost = pl.CostEstimate(
        flops=10 * pairs * HEAD_DIM,
        transcendentals=pairs,
        bytes_accessed=(2 * (2 * nq + 2 * nk) + 4 * nq + 8 * nk) * rows * width * channels,
    )
    part = jax.ShapeDtypeStruct((2, rows, width, channels), jnp.float32)
    dq_shape = jax.ShapeDtypeStruct((rows, width, channels), jnp.float32)
    members = list(queries) + list(grads)
    blocks = list(keys) + list(values)
    operands = [arr for arr, _ in members] + [stats, stats] + [arr for arr, _ in blocks]
    in_specs = (
        [member_spec(m) for _, m in members]
        + [stats_spec(0), stats_spec(1)]
        + [member_spec(m) for _, m in blocks]
    )
    return pl.pallas_call(
        kernel,
        grid=(heads,),
        in_specs=in_specs,
        out_specs=[qspec] * nq + [pspec] * nk,
        out_shape=[dq_shape] * nq + [part] * nk,
        cost_estimate=cost,
    )(*operands)


def stats_tiles(stats, tiles, tf):
    rows, width, heads = stats.shape
    tiled = stats.reshape(rows, tiles, tf, heads)
    tiled = jnp.transpose(tiled, (3, 1, 0, 2))
    return tiled.reshape(heads, tiles, 1, rows * tf)


def on_device(queries, key_vecs, value_vecs, outputs_fwd, grad_out, log_norm):
    rows, width_cells, frames, channels = queries.shape
    heads = log_norm.shape[3]
    width = width_cells * frames
    tiles = width_cells // TILE
    tf = TILE * frames
    mf = MARGIN * frames

    qd = jnp.stack([queries.reshape(rows, width, channels), grad_out.reshape(rows, width, channels)])
    row_delta = jnp.einsum(
        "rwhd,rwhd->rwh",
        grad_out.reshape(rows, width, heads, HEAD_DIM),
        outputs_fwd.reshape(rows, width, heads, HEAD_DIM),
        preferred_element_type=jnp.float32,
    )
    stats = jnp.stack(
        [stats_tiles(log_norm.reshape(rows, width, heads), tiles, tf), stats_tiles(row_delta, tiles, tf)]
    )
    kv_own = jnp.stack(
        [
            jnp.roll(key_vecs.reshape(rows, width, channels), mf, axis=1),
            jnp.roll(value_vecs.reshape(rows, width, channels), mf, axis=1),
        ]
    )
    kv_cross = swap(kv_own, chip_neighbour)
    kv_partner = swap(kv_own, core_partner)
    qd_partner = swap(qd, core_partner)
    stats_partner = swap(stats, core_partner)

    dq_local, part_own, part_partner = window_pass(
        [(qd, 0)], [(qd, 1)], stats,
        [(kv_own, 0), (kv_partner, 0)], [(kv_own, 1), (kv_partner, 1)], tiles, tf, mf,
    )
    back_partner = swap(part_partner, core_partner)
    stats_pair = jnp.concatenate([stats, stats_partner], axis=-1)
    dq_mine, dq_theirs, part_cross = window_pass(
        [(qd, 0), (qd_partner, 0)], [(qd, 1), (qd_partner, 1)], stats_pair,
        [(kv_cross, 0)], [(kv_cross, 1)], tiles, tf, mf,
    )
    arrived = swap(part_cross.astype(jnp.bfloat16), chip_neighbour)
    dq_back = swap(dq_theirs, core_partner)
    dq = (dq_local + dq_mine + dq_back).astype(jnp.bfloat16)
    total = jnp.roll(part_own + back_partner + arrived.astype(jnp.float32), -mf, axis=2)
    grad_keys = total[0].astype(jnp.bfloat16).reshape(rows, width_cells, frames, channels)
    grad_values = total[1].astype(jnp.bfloat16).reshape(rows, width_cells, frames, channels)
    grad_queries = dq.reshape(rows, width_cells, frames, channels)
    return (grad_queries, grad_keys, grad_values)


def solution(mesh):
    spec = P("sy", "groups", None, None)
    return jax.shard_map(
        on_device,
        mesh=mesh,
        in_specs=(spec,) * 6,
        out_specs=(spec,) * 3,
        check_vma=False,
    )
```

time: 122 us -> 113 us (0.926)
  waiting for transfers between devices: 54.4 us -> 37.4 us
  other arithmetic: 8.57 us -> 12 us
  starting transfers between devices: 5.66 us -> 7.6 us
  local copies, waits for them, and re-layouts: 20.4 us -> 22.3 us
    ppermute x9 -> x7, waiting for transfers between devices: 54.4 us -> 37.4 us  [swap(): return lax.ppermute(block, 'sy', route)]
    reshape x4 -> x0, local copies, waits for them, and re-layouts: 5.59 us -> none  [the longest x1 2.95 us: on_device(): q = queries.reshape(rows, width, channels)]
    reshape x1, local copies, waits for them, and re-layouts: 0.52 us -> 3.24 us  [on_device(): grad_out.reshape(rows, width, heads, HEAD_DIM)]
    another operation x0 -> x6, local copies, waits for them, and re-layouts: none -> 2.67 us  [the longest x3 2.4 us: on_device(): jnp.stack([queries.reshape(rows, width, channels), grad_out.reshape(rows,...]
    unnamed x13 -> x27, local copies, waits for them, and re-layouts: 1.04 us -> 3.66 us
    reshape x1, local copies, waits for them, and re-layouts: 2.27 us -> 0.3 us  [on_device(): value_vecs.reshape(rows, width, channels)]
    ppermute x9 -> x7, starting transfers between devices: 5.66 us -> 7.6 us  [swap(): return lax.ppermute(block, 'sy', route)]
    unnamed x1, other arithmetic: 0.62 us -> 2.16 us
  transfers between devices with their start and end apart: 9 -> 7, of which waited for: 6 -> 2; matrix products, arithmetic and copies ran while one was open for 16% -> 20% of each run, Pallas kernels for 12% -> 27%
where the time goes in v8:
time: 113 us; the launch traced here: 110 us
  waiting for transfers between devices  37.4 us (33%)
  Pallas kernels  30.3 us (27%)
  local copies, waits for them, and re-layouts  22.3 us (20%)
  other arithmetic  12 us (11%)
  starting transfers between devices  7.6 us (7%)
    ppermute x7, waiting for transfers between devices, swap(): return lax.ppermute(block, 'sy', route)  37.4 us
    pallas_call x2, Pallas kernels, window_pass(): pl.pallas_call(kernel, grid=(heads,), in_specs=in_specs, out_specs=[qspec...  30.3 us
    ppermute x7, starting transfers between devices, swap(): return lax.ppermute(block, 'sy', route)  7.6 us
    unnamed x27, local copies, waits for them, and re-layouts  3.66 us
    convert_element_type x1, other arithmetic, on_device(): arrived = swap(part_cross.astype(jnp.bfloat16), chip_neighbour)  3.4 us
    reshape x1, local copies, waits for them, and re-layouts, on_device(): grad_out.reshape(rows, width, heads, HEAD_DIM)  3.24 us
    reshape x1, local copies, waits for them, and re-layouts, on_device(): outputs_fwd.reshape(rows, width, heads, HEAD_DIM)  3.22 us
    add x1, other arithmetic, on_device(): part_own + back_partner + arrived.astype(jnp.float32)  3.2 us
  transfers between devices with their start and end apart: 7, of which 2 were waited for; matrix products, arithmetic and copies ran while one was open for 20% of the time, Pallas kernels for 27%

profile of v8, /device:TPU:1, one launch (start us, length us, event | category | flops | bytes accessed | tf_op | source)
XLA Modules:
  0.0 110.5 jit_solution(8444378661608089511)
XLA Ops:
  0.6 0.0 copy-start.8
  0.6 2.3 %reshape.33 = bf16[4,64,1536]{2,1,0:T(8,128)(2,1)S(1)} reshape(bf16[4,32,2,1536]{3,2,1,0:T(2,128)(2,1)} %param.7) | data formatting | bytes 1572864 | tf_op jit(solution)/shard_map/reshape | solution.py:156
  3.0 0.0 copy-start.4
  3.0 0.0 copy-done.8
  3.0 0.3 reshape.34
  3.3 0.5 copy-done.4
  3.9 0.0 slice-start
  3.9 1.0 slice-done
  5.0 0.1 maximum_bitcast_fusion
  5.1 0.0 copy-start.9
  5.1 0.1 pad_maximum_fusion.refs_4_.refs_6_
  5.3 0.0 copy-start.1
  5.3 0.0 copy-start.2
  5.3 0.1 collective-permute-start
  5.4 1.0 copy-done.9
  6.4 1.2 %stack_reshape.12 = bf16[1,4,64,1536]{3,2,1,0:T(8,128)(2,1)} reshape(bf16[4,32,2,1536]{3,2,1,0:T(2,128)(2,1)S(1)} %copy-done.9) | data formatting | bytes 1572864 | tf_op jit(solution)/shard_map/stack;reshape | solution.py:144
  7.6 0.0 copy-done.2
  7.6 1.2 %stack_reshape.13 = bf16[1,4,64,1536]{3,2,1,0:T(8,128)(2,1)} reshape(bf16[4,32,2,1536]{3,2,1,0:T(2,128)(2,1)S(1)} %copy-done.2) | data formatting | bytes 1572864 | tf_op jit(solution)/shard_map/stack;reshape | solution.py:144
  8.8 1.3 %constant_dynamic-update-slice_fusion.1 = bf16[2,4,64,1536]{3,2,1,0:T(8,128)(2,1)S(1)} fusion(bf16[1,4,64,1536]{3,2,1,0:T(8,128)(2,1)} %stack_reshape.12), kind=kLoop, calls=%fused_computation.10 | loop fusion | bytes 1572864
  10.0 0.1 copy-done.3
  10.1 0.1 constant_dynamic-update-slice_fusion.refs_0_.refs_1_.refs_2_
  10.2 0.0 copy-start
  10.2 0.1 collective-permute-start.1
  10.3 0.0 copy-done.1
  10.3 2.7 %collective-permute-start.3 = (bf16[2,4,64,1536]{3,2,1,0:T(8,128)(2,1)S(1)}, bf16[2,4,64,1536]{3,2,1,0:T(8,128)(2,1)}, u32[]{:S(2)}, u32[]{:S(2)}) collective-permute-start(bf16[2,4,64,1536]{3,2,1,0:T(8,128)(2,1)S(1)} %pad_maximum_fusion.refs_4_.refs_6_), channel_id=1, source_target_pairs={{0,15},{1,2},{2,1},{3,4},{4,3},{5,6},{6,5},{7,8},{8,7},{9,10},{10,... | collective-permute-start | bytes 4718600 | tf_op jit(solution)/shard_map/ppermute | solution.py:20
  13.0 3.2 %reshape.30 = bf16[4,64,12,128]{3,2,1,0:T(8,128)(2,1)} reshape(bf16[4,32,2,1536]{3,2,1,0:T(2,128)(2,1)} %param.10) | data formatting | bytes 1572864 | tf_op jit(solution)/shard_map/reshape | solution.py:147
  16.2 0.0 copy-done.11
  16.2 0.1 copy.9
  16.4 0.2 copy.10
  16.5 0.1 stack_reshape.14
  16.7 3.2 %reshape.31 = bf16[4,64,12,128]{3,2,1,0:T(8,128)(2,1)} reshape(bf16[4,32,2,1536]{3,2,1,0:T(2,128)(2,1)} %param.9) | data formatting | bytes 1572864 | tf_op jit(solution)/shard_map/reshape | solution.py:148
  19.9 0.0 copy-done
  19.9 2.2 %fusion = f32[4,64,12]{2,1,0:T(8,128)S(1)} fusion(bf16[4,64,12,128]{3,2,1,0:T(8,128)(2,1)} %reshape.30, bf16[4,64,12,128]{3,2,1,0:T(8,128)(2,1)} %reshape.31), kind=kLoop, calls=%fused_computation.3 | loop fusion | flops 1569792 | bytes 1585152
  22.1 0.2 copy.19
  22.2 0.1 stack_reshape.15
  22.4 0.0 copy-start.10
  22.4 0.0 collective-permute-done.refs_5_.refs_7_
  22.4 0.6 copy-done.10
  23.0 15.2 %shard_map.85 = (f32[4,64,1536]{2,1,0:T(8,128)}, f32[2,4,64,1536]{3,2,1,0:T(8,128)}, f32[2,4,64,1536]{3,2,1,0:T(8,128)}) custom-call(bf16[2,4,64,1536]{3,2,1,0:T(8,128)(2,1)} %copy-done, bf16[2,4,64,1536]{3,2,1,0:T(8,128)(2,1)} %copy-done, f32[2,12,4,1,64]{4,3,2,1,0:T(1,128)} %copy-done.10, f32[2,12,4,1,64]{4,3,2,1,0:T(1,128)} %copy-done.10, ...), custom_call_target="tpu_custom_call" | custom-call | flops 1006632960 | bytes 12582912 | tf_op jit(solution)/shard_map/pallas_call | solution.py:119
  38.2 3.5 %collective-permute-start.5 = (f32[2,4,64,1536]{3,2,1,0:T(8,128)}, f32[2,4,64,1536]{3,2,1,0:T(8,128)}, u32[]{:S(2)}, u32[]{:S(2)}) collective-permute-start(f32[2,4,64,1536]{3,2,1,0:T(8,128)} %get-tuple-element.13), channel_id=1, source_target_pairs={{0,1},{1,0},{2,3},{3,2},{4,5},{5,4},{6,7},{7,6},{8,9},{9,8},{10,11... | collective-permute-start | bytes 9437192 | tf_op jit(solution)/shard_map/ppermute | solution.py:20
  41.7 0.1 collective-permute-start.2
  41.8 5.4 %collective-permute-done.2 = f32[2,12,4,1,64]{4,3,2,1,0:T(1,128)S(1)} collective-permute-done((f32[2,12,4,1,64]{4,3,2,1,0:T(1,128)}, f32[2,12,4,1,64]{4,3,2,1,0:T(1,128)S(1)}, u32[]{:S(2)}, u32[]{:S(2)}) %collective-permute-start.2) | collective-permute-done | bytes 24608 | tf_op jit(solution)/shard_map/ppermute | solution.py:20
  47.2 1.6 %pad_maximum_fusion.1.refs_4_.refs_5_ = f32[2,12,4,1,128]{4,3,2,1,0:T(1,128)} fusion(f32[2,12,4,1,64]{4,3,2,1,0:T(1,128)S(1)} %collective-permute-done.2, f32[2,12,4,1,64]{4,3,2,1,0:T(1,128)} %copy-done.10), kind=kLoop, calls=%fused_computation.8 | loop fusion | flops 12288 | bytes 98304 | tf_op jit(solution)/shard_map/concatenate | solution.py:170
  48.7 0.0 collective-permute-done.1.refs_1_.refs_3_
  48.7 0.0 collective-permute-done.3.refs_6_.refs_7_
  48.8 15.2 %shard_map.86 = (f32[4,64,1536]{2,1,0:T(8,128)}, f32[4,64,1536]{2,1,0:T(8,128)}, f32[2,4,64,1536]{3,2,1,0:T(8,128)}) custom-call(bf16[2,4,64,1536]{3,2,1,0:T(8,128)(2,1)} %copy-done, bf16[2,4,64,1536]{3,2,1,0:T(8,128)(2,1)} %collective-permute-done.1.refs_1_.refs_3_, bf16[2,4,64,1536]{3,2,1,0:T(8,128)(2,1)} %copy-done, ...), custom_call_target="tpu_custom_call" | custom-call | flops 1006632960 | bytes 11010048 | tf_op jit(solution)/shard_map/pallas_call | solution.py:119
  63.9 0.2 collective-permute-start.4
  64.1 3.4 %convert_element_type.20 = bf16[2,4,64,1536]{3,2,1,0:T(8,128)(2,1)} convert(f32[2,4,64,1536]{3,2,1,0:T(8,128)} %get-tuple-element.14) | non-fusion elementwise | flops 786432 | bytes 4718592 | tf_op jit(solution)/shard_map/convert_element_type | solution.py:175
  67.5 0.9 collective-permute-start.6
  68.4 0.0 collective-permute-done.4
  68.4 0.0 copy-done.6
  68.5 0.0 copy-done.7
  68.5 0.0 copy-start.5
  68.5 1.2 %add_convert_fusion = bf16[4,64,1536]{2,1,0:T(8,128)(2,1)} fusion(f32[4,64,1536]{2,1,0:T(8,128)S(1)} %collective-permute-done.4, f32[4,64,1536]{2,1,0:T(8,128)S(1)} %copy-done.6, f32[4,64,1536]{2,1,0:T(8,128)S(1)} %copy-done.7), kind=kLoop, calls=%fused_computation.5 | loop fusion | flops 1179648 | bytes 5505024 | tf_op jit(solution)/shard_map/convert_element_type | solution.py:177
  69.7 2.9 %reshape.35 = bf16[4,32,2,1536]{3,2,1,0:T(2,128)(2,1)} reshape(bf16[4,64,1536]{2,1,0:T(8,128)(2,1)} %add_convert_fusion) | data formatting | bytes 1572864 | tf_op jit(solution)/shard_map/reshape | solution.py:181
  72.5 32.0 %collective-permute-done.6 = bf16[2,4,64,1536]{3,2,1,0:T(8,128)(2,1)} collective-permute-done((bf16[2,4,64,1536]{3,2,1,0:T(8,128)(2,1)}, bf16[2,4,64,1536]{3,2,1,0:T(8,128)(2,1)}, u32[]{:S(2)}, u32[]{:S(2)}) %collective-permute-start.6) | collective-permute-done | bytes 1572896 | tf_op jit(solution)/shard_map/ppermute | solution.py:20
  104.5 0.0 collective-permute-done.5
  104.5 0.0 copy-done.5
  104.5 3.2 %convert_add_fusion = bf16[2,4,64,1536]{3,2,1,0:T(8,128)(2,1)S(1)} fusion(bf16[2,4,64,1536]{3,2,1,0:T(8,128)(2,1)} %collective-permute-done.6, f32[2,4,64,1536]{3,2,1,0:T(8,128)S(1)} %copy-done.5, f32[2,4,64,1536]{3,2,1,0:T(8,128)} %collective-permute-done.5), kind=kLoop, calls=%fused_computation.1 | loop fusion | flops 3145728 | bytes 9437184 | tf_op jit(solution)/shard_map/add | solution.py:178
  107.8 0.1 slice.42
  107.9 0.1 maximum_convert_fusion
  108.0 0.1 fusion.1
  108.1 1.2 %convert_element_type.23 = bf16[4,32,2,1536]{3,2,1,0:T(2,128)(2,1)} reshape(bf16[1,4,64,1536]{3,2,1,0:T(8,128)(2,1)S(1)} %get-tuple-element.15) | data formatting | bytes 1572864 | tf_op jit(solution)/shard_map/convert_element_type | solution.py:180
  109.3 1.2 %convert_element_type.22 = bf16[4,32,2,1536]{3,2,1,0:T(2,128)(2,1)} reshape(bf16[1,4,64,1536]{3,2,1,0:T(8,128)(2,1)S(1)} %get-tuple-element.16) | data formatting | bytes 1572864 | tf_op jit(solution)/shard_map/convert_element_type | solution.py:179
  (10 shorter events, 0.1 us)
Async XLA Ops:
  0.6 2.4 %copy-start.8 = (bf16[4,32,2,1536]{3,2,1,0:T(2,128)(2,1)S(1)}, bf16[4,32,2,1536]{3,2,1,0:T(2,128)(2,1)}, u32[]{:S(2)}) copy-start(bf16[4,32,2,1536]{3,2,1,0:T(2,128)(2,1)} %param.8) | copy-start | bytes 2359300
  3.0 0.9 copy-start.4
  3.9 1.1 slice-start
  5.1 1.3 %copy-start.9 = (bf16[4,32,2,1536]{3,2,1,0:T(2,128)(2,1)S(1)}, bf16[4,32,2,1536]{3,2,1,0:T(2,128)(2,1)}, u32[]{:S(2)}) copy-start(bf16[4,32,2,1536]{3,2,1,0:T(2,128)(2,1)} %param.6) | copy-start | bytes 2359300
  5.3 5.0 %copy-start.1 = (bf16[2,4,64,1536]{3,2,1,0:T(8,128)(2,1)}, bf16[2,4,64,1536]{3,2,1,0:T(8,128)(2,1)S(1)}, u32[]{:S(2)}) copy-start(bf16[2,4,64,1536]{3,2,1,0:T(8,128)(2,1)S(1)} %pad_maximum_fusion.refs_4_.refs_6_) | copy-start | bytes 4718596
  5.3 2.3 %copy-start.2 = (bf16[4,32,2,1536]{3,2,1,0:T(2,128)(2,1)S(1)}, bf16[4,32,2,1536]{3,2,1,0:T(2,128)(2,1)}, u32[]{:S(2)}) copy-start(bf16[4,32,2,1536]{3,2,1,0:T(2,128)(2,1)} %param.10) | copy-start | bytes 2359300
  5.3 17.1 %collective-permute-start = (bf16[2,4,64,1536]{3,2,1,0:T(8,128)(2,1)S(1)}, bf16[2,4,64,1536]{3,2,1,0:T(8,128)(2,1)}, u32[]{:S(2)}, u32[]{:S(2)}) collective-permute-start(bf16[2,4,64,1536]{3,2,1,0:T(8,128)(2,1)S(1)} %pad_maximum_fusion.refs_4_.refs_6_), channel_id=1, source_target_pairs={{0,1},{1,0},{2,3},{3,2},{4,5},{5,4},{6,7},{7,6},{8,9},{9,8},{10,11... | collective-permute-start | bytes 4718600 | tf_op jit(solution)/shard_map/ppermute | solution.py:20
  8.8 1.4 %copy-start.3 = (bf16[1,4,64,1536]{3,2,1,0:T(8,128)(2,1)S(1)}, bf16[1,4,64,1536]{3,2,1,0:T(8,128)(2,1)}, u32[]{:S(2)}) copy-start(bf16[1,4,64,1536]{3,2,1,0:T(8,128)(2,1)} %stack_reshape.13) | copy-start | bytes 2359300
  10.1 6.1 %copy-start.11 = (f32[4,32,2,12]{1,2,3,0:T(2,128)S(1)}, f32[4,32,2,12]{1,2,3,0:T(2,128)}, u32[]{:S(2)}) copy-start(f32[4,32,2,12]{1,2,3,0:T(2,128)} %param.11) | copy-start | bytes 36868
  10.2 9.7 %copy-start = (bf16[2,4,64,1536]{3,2,1,0:T(8,128)(2,1)}, bf16[2,4,64,1536]{3,2,1,0:T(8,128)(2,1)S(1)}, u32[]{:S(2)}) copy-start(bf16[2,4,64,1536]{3,2,1,0:T(8,128)(2,1)S(1)} %constant_dynamic-update-slice_fusion.refs_0_.refs_1_.refs_2_) | copy-start | bytes 4718596
  10.2 38.6 %collective-permute-start.1 = (bf16[2,4,64,1536]{3,2,1,0:T(8,128)(2,1)S(1)}, bf16[2,4,64,1536]{3,2,1,0:T(8,128)(2,1)}, u32[]{:S(2)}, u32[]{:S(2)}) collective-permute-start(bf16[2,4,64,1536]{3,2,1,0:T(8,128)(2,1)S(1)} %constant_dynamic-update-slice_fusion.refs_0_.refs_1_.refs_2_), channel_id=1, source_target_pairs={{0,1},{1,0},{2,3},{3,2},{4,5},{5,4},{6,7},{7,6},{8,9},{9,8},{10,11... | collective-permute-start | bytes 4718600 | tf_op jit(solution)/shard_map/ppermute | solution.py:20
  10.3 38.4 %collective-permute-start.3 = (bf16[2,4,64,1536]{3,2,1,0:T(8,128)(2,1)S(1)}, bf16[2,4,64,1536]{3,2,1,0:T(8,128)(2,1)}, u32[]{:S(2)}, u32[]{:S(2)}) collective-permute-start(bf16[2,4,64,1536]{3,2,1,0:T(8,128)(2,1)S(1)} %pad_maximum_fusion.refs_4_.refs_6_), channel_id=1, source_target_pairs={{0,15},{1,2},{2,1},{3,4},{4,3},{5,6},{6,5},{7,8},{8,7},{9,10},{10,... | collective-permute-start | bytes 4718600 | tf_op jit(solution)/shard_map/ppermute | solution.py:20
  22.4 0.6 copy-start.10
  38.2 66.3 %collective-permute-start.5 = (f32[2,4,64,1536]{3,2,1,0:T(8,128)}, f32[2,4,64,1536]{3,2,1,0:T(8,128)}, u32[]{:S(2)}, u32[]{:S(2)}) collective-permute-start(f32[2,4,64,1536]{3,2,1,0:T(8,128)} %get-tuple-element.13), channel_id=1, source_target_pairs={{0,1},{1,0},{2,3},{3,2},{4,5},{5,4},{6,7},{7,6},{8,9},{9,8},{10,11... | collective-permute-start | bytes 9437192 | tf_op jit(solution)/shard_map/ppermute | solution.py:20
  41.7 5.4 %collective-permute-start.2 = (f32[2,12,4,1,64]{4,3,2,1,0:T(1,128)}, f32[2,12,4,1,64]{4,3,2,1,0:T(1,128)S(1)}, u32[]{:S(2)}, u32[]{:S(2)}) collective-permute-start(f32[2,12,4,1,64]{4,3,2,1,0:T(1,128)} %copy-done.10), channel_id=1, source_target_pairs={{0,1},{1,0},{2,3},{3,2},{4,5},{5,4},{6,7},{7,6},{8,9},{9,8},{10,11... | collective-permute-start | bytes 73736 | tf_op jit(solution)/shard_map/ppermute | solution.py:20
  63.9 4.5 %collective-permute-start.4 = (f32[4,64,1536]{2,1,0:T(8,128)}, f32[4,64,1536]{2,1,0:T(8,128)S(1)}, u32[]{:S(2)}, u32[]{:S(2)}) collective-permute-start(f32[4,64,1536]{2,1,0:T(8,128)} %get-tuple-element.11), channel_id=1, source_target_pairs={{0,1},{1,0},{2,3},{3,2},{4,5},{5,4},{6,7},{7,6},{8,9},{9,8},{10,11... | collective-permute-start | bytes 4718600 | tf_op jit(solution)/shard_map/ppermute | solution.py:20
  64.1 4.3 %copy-start.6 = (f32[4,64,1536]{2,1,0:T(8,128)S(1)}, f32[4,64,1536]{2,1,0:T(8,128)}, u32[]{:S(2)}) copy-start(f32[4,64,1536]{2,1,0:T(8,128)} %get-tuple-element.9) | copy-start | bytes 4718596
  64.1 4.3 %copy-start.7 = (f32[4,64,1536]{2,1,0:T(8,128)S(1)}, f32[4,64,1536]{2,1,0:T(8,128)}, u32[]{:S(2)}) copy-start(f32[4,64,1536]{2,1,0:T(8,128)} %get-tuple-element.10) | copy-start | bytes 4718596
  67.5 37.0 %collective-permute-start.6 = (bf16[2,4,64,1536]{3,2,1,0:T(8,128)(2,1)}, bf16[2,4,64,1536]{3,2,1,0:T(8,128)(2,1)}, u32[]{:S(2)}, u32[]{:S(2)}) collective-permute-start(bf16[2,4,64,1536]{3,2,1,0:T(8,128)(2,1)} %convert_element_type.20), channel_id=1, source_target_pairs={{0,15},{1,2},{2,1},{3,4},{4,3},{5,6},{6,5},{7,8},{8,7},{9,10},{10,... | collective-permute-start | bytes 4718600 | tf_op jit(solution)/shard_map/ppermute | solution.py:20
  68.5 36.1 %copy-start.5 = (f32[2,4,64,1536]{3,2,1,0:T(8,128)S(1)}, f32[2,4,64,1536]{3,2,1,0:T(8,128)}, u32[]{:S(2)}) copy-start(f32[2,4,64,1536]{3,2,1,0:T(8,128)} %get-tuple-element.12) | copy-start | bytes 9437188

commit v9 on v8

--- a/solution.py
+++ b/solution.py
@@ -34,14 +34,15 @@
     return [(0, start, width - start), (width - start, 0, start + span - width)]
 
 
-def window_kernel(*refs, nq, nk, tiles, tf, mf):
+def window_kernel(*refs, nq, nk, tiles, tf, mf, narrow):
     q_refs = refs[0:nq]
     do_refs = refs[nq : 2 * nq]
     lse_ref, delta_ref = refs[2 * nq], refs[2 * nq + 1]
     k_refs = refs[2 * nq + 2 : 2 * nq + 2 + nk]
     v_refs = refs[2 * nq + 2 + nk : 2 * nq + 2 + 2 * nk]
     dq_refs = refs[2 * nq + 2 + 2 * nk : 3 * nq + 2 + 2 * nk]
-    targets = refs[3 * nq + 2 + 2 * nk :]
+    outs = refs[3 * nq + 2 + 2 * nk : 3 * nq + 2 + 2 * nk + nk]
+    targets = refs[3 * nq + 2 + 2 * nk + nk :] if narrow else outs
     scaling = HEAD_DIM ** (-0.5)
     rows = q_refs[0].shape[0]
     width = targets[0].shape[2]
@@ -84,19 +85,26 @@
             for src, dst, size in pieces:
                 target[0, :, dst : dst + size, :] += grad_k[block, :, src : src + size, :]
                 target[1, :, dst : dst + size, :] += grad_v[block, :, src : src + size, :]
-
-
-def window_pass(queries, grads, stats, keys, values, tiles, tf, mf):
-    _, rows, width, channels = queries[0][0].shape
-    heads = channels // HEAD_DIM
+    if narrow:
+        for out, target in zip(outs, targets):
+            out[...] = target[...].astype(out.dtype)
+
+
+def window_pass(queries, grads, stats, keys, values, tiles, tf, mf, first=0, heads=None, narrow=False):
+    _, rows, width, all_channels = queries[0][0].shape
+    if heads is None:
+        heads = all_channels // HEAD_DIM
+    channels = heads * HEAD_DIM
     nq, nk = len(queries), len(keys)
-    kernel = functools.partial(window_kernel, nq=nq, nk=nk, tiles=tiles, tf=tf, mf=mf)
+    kernel = functools.partial(window_kernel, nq=nq, nk=nk, tiles=tiles, tf=tf, mf=mf, narrow=narrow)
 
     def member_spec(member):
-        return pl.BlockSpec((None, rows, width, HEAD_DIM), lambda h: (member, 0, 0, h))
+        return pl.BlockSpec((None, rows, width, HEAD_DIM), lambda h: (member, 0, 0, h + first))
 
     def stats_spec(member):
-        return pl.BlockSpec((None, None, tiles, 1, nq * rows * tf), lambda h: (member, h, 0, 0, 0))
+        return pl.BlockSpec(
+            (None, None, tiles, 1, nq * rows * tf), lambda h: (member, h + first, 0, 0, 0)
+        )
 
     qspec = pl.BlockSpec((rows, width, HEAD_DIM), lambda h: (0, 0, h))
     pspec = pl.BlockSpec((2, rows, width, HEAD_DIM), lambda h: (0, 0, 0, h))
@@ -106,7 +114,8 @@
         transcendentals=pairs,
         bytes_accessed=(2 * (2 * nq + 2 * nk) + 4 * nq + 8 * nk) * rows * width * channels,
     )
-    part = jax.ShapeDtypeStruct((2, rows, width, channels), jnp.float32)
+    part = jax.ShapeDtypeStruct((2, rows, width, channels), jnp.bfloat16 if narrow else jnp.float32)
+    scratch = [pltpu.VMEM((2, rows, width, HEAD_DIM), jnp.float32)] * nk if narrow else []
     dq_shape = jax.ShapeDtypeStruct((rows, width, channels), jnp.float32)
     members = list(queries) + list(grads)
     blocks = list(keys) + list(values)
@@ -122,6 +131,7 @@
         in_specs=in_specs,
         out_specs=[qspec] * nq + [pspec] * nk,
         out_shape=[dq_shape] * nq + [part] * nk,
+        scratch_shapes=scratch,
         cost_estimate=cost,
     )(*operands)
 
@@ -168,12 +178,21 @@
     )
     back_partner = swap(part_partner, core_partner)
     stats_pair = jnp.concatenate([stats, stats_partner], axis=-1)
-    dq_mine, dq_theirs, part_cross = window_pass(
-        [(qd, 0), (qd_partner, 0)], [(qd, 1), (qd_partner, 1)], stats_pair,
-        [(kv_cross, 0)], [(kv_cross, 1)], tiles, tf, mf,
-    )
-    arrived = swap(part_cross.astype(jnp.bfloat16), chip_neighbour)
-    dq_back = swap(dq_theirs, core_partner)
+    halves = 1
+    count = heads // halves
+    mine_parts, back_parts, arrived_parts = [], [], []
+    for half in range(halves):
+        dq_mine, dq_theirs, part_cross = window_pass(
+            [(qd, 0), (qd_partner, 0)], [(qd, 1), (qd_partner, 1)], stats_pair,
+            [(kv_cross, 0)], [(kv_cross, 1)], tiles, tf, mf,
+            first=half * count, heads=count, narrow=True,
+        )
+        arrived_parts.append(swap(part_cross, chip_neighbour))
+        back_parts.append(swap(dq_theirs, core_partner))
+        mine_parts.append(dq_mine)
+    dq_mine = jnp.concatenate(mine_parts, axis=-1)
+    dq_back = jnp.concatenate(back_parts, axis=-1)
+    arrived = jnp.concatenate(arrived_parts, axis=-1)
     dq = (dq_local + dq_mine + dq_back).astype(jnp.bfloat16)
     total = jnp.roll(part_own + back_partner + arrived.astype(jnp.float32), -mf, axis=2)
     grad_keys = total[0].astype(jnp.bfloat16).reshape(rows, width_cells, frames, channels)

time: 113 us -> 109 us (0.965)
  waiting for transfers between devices: 37.4 us -> 35.3 us
  other arithmetic: 12 us -> 10.6 us
    convert_element_type x1 -> x0, other arithmetic: 3.4 us -> none  [on_device(): arrived = swap(part_cross.astype(jnp.bfloat16), chip_neighbour)]
    ppermute x7, waiting for transfers between devices: 37.4 us -> 35.3 us  [swap(): return lax.ppermute(block, 'sy', route)]
    convert_element_type x1, other arithmetic: 1.2 us -> 3.23 us  [on_device(): dq = (dq_local + dq_mine + dq_back).astype(jnp.bfloat16)]
    unnamed x27 -> x23, local copies, waits for them, and re-layouts: 3.66 us -> 3.65 us
  transfers between devices with their start and end apart: 7 -> 7, of which waited for: 2 -> 3; matrix products, arithmetic and copies ran while one was open for 20% -> 19% of each run, Pallas kernels for 27% -> 28%
where the time goes in v9:
time: 109 us; the launch traced here: 107 us
  waiting for transfers between devices  35.3 us (32%)
  Pallas kernels  30 us (28%)
  local copies, waits for them, and re-layouts  22.3 us (20%)
  other arithmetic  10.6 us (10%)
  starting transfers between devices  7.72 us (7%)
    ppermute x7, waiting for transfers between devices, swap(): return lax.ppermute(block, 'sy', route)  35.3 us
    pallas_call x2, Pallas kernels, window_pass(): pl.pallas_call(kernel, grid=(heads,), in_specs=in_specs, out_specs=[qspec...  30 us
    ppermute x7, starting transfers between devices, swap(): return lax.ppermute(block, 'sy', route)  7.72 us
    unnamed x23, local copies, waits for them, and re-layouts  3.65 us
    reshape x1, local copies, waits for them, and re-layouts, on_device(): outputs_fwd.reshape(rows, width, heads, HEAD_DIM)  3.24 us
    convert_element_type x1, other arithmetic, on_device(): dq = (dq_local + dq_mine + dq_back).astype(jnp.bfloat16)  3.23 us
    reshape x1, local copies, waits for them, and re-layouts, on_device(): grad_out.reshape(rows, width, heads, HEAD_DIM)  3.2 us
    add x1, other arithmetic, on_device(): part_own + back_partner + arrived.astype(jnp.float32)  3.2 us
  transfers between devices with their start and end apart: 7, of which 3 were waited for; matrix products, arithmetic and copies ran while one was open for 19% of the time, Pallas kernels for 28%

profile of v9, /device:TPU:1, one launch (start us, length us, event | category | flops | bytes accessed | tf_op | source)
XLA Modules:
  0.0 106.7 jit_solution(18012628849078900120)
XLA Ops:
  0.6 0.0 copy-start.6
  0.6 2.3 %reshape.33 = bf16[4,64,1536]{2,1,0:T(8,128)(2,1)S(1)} reshape(bf16[4,32,2,1536]{3,2,1,0:T(2,128)(2,1)} %param.7) | data formatting | bytes 1572864 | tf_op jit(solution)/shard_map/reshape | solution.py:166
  3.0 0.0 copy-start.4
  3.0 0.0 copy-done.6
  3.0 0.3 reshape.34
  3.3 0.5 copy-done.4
  3.9 0.0 slice-start
  3.9 1.0 slice-done
  5.0 0.1 maximum_bitcast_fusion
  5.1 0.0 copy-start.7
  5.1 0.1 pad_maximum_fusion.refs_4_.refs_6_
  5.3 0.0 copy-start.1
  5.3 0.0 copy-start.2
  5.3 0.1 collective-permute-start
  5.4 1.0 copy-done.7
  6.4 1.2 %stack_reshape.12 = bf16[1,4,64,1536]{3,2,1,0:T(8,128)(2,1)} reshape(bf16[4,32,2,1536]{3,2,1,0:T(2,128)(2,1)S(1)} %copy-done.7) | data formatting | bytes 1572864 | tf_op jit(solution)/shard_map/stack;reshape | solution.py:154
  7.6 0.0 copy-done.2
  7.6 1.2 %stack_reshape.13 = bf16[1,4,64,1536]{3,2,1,0:T(8,128)(2,1)} reshape(bf16[4,32,2,1536]{3,2,1,0:T(2,128)(2,1)S(1)} %copy-done.2) | data formatting | bytes 1572864 | tf_op jit(solution)/shard_map/stack;reshape | solution.py:154
  8.8 0.0 copy-start.3
  8.8 1.3 %constant_dynamic-update-slice_fusion.1 = bf16[2,4,64,1536]{3,2,1,0:T(8,128)(2,1)S(1)} fusion(bf16[1,4,64,1536]{3,2,1,0:T(8,128)(2,1)} %stack_reshape.12), kind=kLoop, calls=%fused_computation.10 | loop fusion | bytes 1572864
  10.0 0.1 copy-done.3
  10.1 0.0 copy-start.9
  10.1 0.1 constant_dynamic-update-slice_fusion.refs_0_.refs_1_.refs_2_
  10.2 0.0 copy-start
  10.2 0.1 collective-permute-start.1
  10.3 0.0 copy-done.1
  10.3 2.7 %collective-permute-start.3 = (bf16[2,4,64,1536]{3,2,1,0:T(8,128)(2,1)S(1)}, bf16[2,4,64,1536]{3,2,1,0:T(8,128)(2,1)}, u32[]{:S(2)}, u32[]{:S(2)}) collective-permute-start(bf16[2,4,64,1536]{3,2,1,0:T(8,128)(2,1)S(1)} %pad_maximum_fusion.refs_4_.refs_6_), channel_id=1, source_target_pairs={{0,15},{1,2},{2,1},{3,4},{4,3},{5,6},{6,5},{7,8},{8,7},{9,10},{10,... | collective-permute-start | bytes 4718600 | tf_op jit(solution)/shard_map/ppermute | solution.py:20
  13.0 3.2 %reshape.30 = bf16[4,64,12,128]{3,2,1,0:T(8,128)(2,1)} reshape(bf16[4,32,2,1536]{3,2,1,0:T(2,128)(2,1)} %param.10) | data formatting | bytes 1572864 | tf_op jit(solution)/shard_map/reshape | solution.py:157
  16.2 0.0 copy-done.9
  16.2 0.1 copy.9
  16.3 0.2 copy.10
  16.5 0.1 stack_reshape.14
  16.6 3.2 %reshape.31 = bf16[4,64,12,128]{3,2,1,0:T(8,128)(2,1)} reshape(bf16[4,32,2,1536]{3,2,1,0:T(2,128)(2,1)} %param.9) | data formatting | bytes 1572864 | tf_op jit(solution)/shard_map/reshape | solution.py:158
  19.9 0.0 copy-done
  19.9 2.2 %fusion = f32[4,64,12]{2,1,0:T(8,128)S(1)} fusion(bf16[4,64,12,128]{3,2,1,0:T(8,128)(2,1)} %reshape.30, bf16[4,64,12,128]{3,2,1,0:T(8,128)(2,1)} %reshape.31), kind=kLoop, calls=%fused_computation.3 | loop fusion | flops 1569792 | bytes 1585152
  22.0 0.2 copy.19
  22.2 0.1 stack_reshape.15
  22.4 0.0 copy-start.8
  22.4 0.0 collective-permute-done.refs_5_.refs_7_
  22.4 0.6 copy-done.8
  23.0 15.1 %shard_map.85 = (f32[4,64,1536]{2,1,0:T(8,128)}, f32[2,4,64,1536]{3,2,1,0:T(8,128)}, f32[2,4,64,1536]{3,2,1,0:T(8,128)}) custom-call(bf16[2,4,64,1536]{3,2,1,0:T(8,128)(2,1)} %copy-done, bf16[2,4,64,1536]{3,2,1,0:T(8,128)(2,1)} %copy-done, f32[2,12,4,1,64]{4,3,2,1,0:T(1,128)} %copy-done.8, f32[2,12,4,1,64]{4,3,2,1,0:T(1,128)} %copy-done.8, ...), custom_call_target="tpu_custom_call" | custom-call | flops 1006632960 | bytes 12582912 | tf_op jit(solution)/shard_map/pallas_call | solution.py:128
  38.1 3.5 %collective-permute-start.5 = (f32[2,4,64,1536]{3,2,1,0:T(8,128)}, f32[2,4,64,1536]{3,2,1,0:T(8,128)}, u32[]{:S(2)}, u32[]{:S(2)}) collective-permute-start(f32[2,4,64,1536]{3,2,1,0:T(8,128)} %get-tuple-element.13), channel_id=1, source_target_pairs={{0,1},{1,0},{2,3},{3,2},{4,5},{5,4},{6,7},{7,6},{8,9},{9,8},{10,11... | collective-permute-start | bytes 9437192 | tf_op jit(solution)/shard_map/ppermute | solution.py:20
  41.6 0.1 collective-permute-start.2
  41.7 5.4 %collective-permute-done.2 = f32[2,12,4,1,64]{4,3,2,1,0:T(1,128)S(1)} collective-permute-done((f32[2,12,4,1,64]{4,3,2,1,0:T(1,128)}, f32[2,12,4,1,64]{4,3,2,1,0:T(1,128)S(1)}, u32[]{:S(2)}, u32[]{:S(2)}) %collective-permute-start.2) | collective-permute-done | bytes 24608 | tf_op jit(solution)/shard_map/ppermute | solution.py:20
  47.1 1.6 %pad_maximum_fusion.1.refs_4_.refs_5_ = f32[2,12,4,1,128]{4,3,2,1,0:T(1,128)} fusion(f32[2,12,4,1,64]{4,3,2,1,0:T(1,128)S(1)} %collective-permute-done.2, f32[2,12,4,1,64]{4,3,2,1,0:T(1,128)} %copy-done.8), kind=kLoop, calls=%fused_computation.8 | loop fusion | flops 12288 | bytes 98304 | tf_op jit(solution)/shard_map/concatenate | solution.py:180
  48.7 0.0 collective-permute-done.1.refs_1_.refs_3_
  48.7 0.0 collective-permute-done.3.refs_6_.refs_7_
  48.7 14.9 %shard_map.86 = (f32[4,64,1536]{2,1,0:T(8,128)}, f32[4,64,1536]{2,1,0:T(8,128)}, bf16[2,4,64,1536]{3,2,1,0:T(8,128)(2,1)}) custom-call(bf16[2,4,64,1536]{3,2,1,0:T(8,128)(2,1)} %copy-done, bf16[2,4,64,1536]{3,2,1,0:T(8,128)(2,1)} %collective-permute-done.1.refs_1_.refs_3_, bf16[2,4,64,1536]{3,2,1,0:T(8,128)(2,1)} %copy-done, ...), custom_call_target="tpu_custom_call" | custom-call | flops 1006632960 | bytes 11010048 | tf_op jit(solution)/shard_map/pallas_call | solution.py:128
  63.6 0.2 collective-permute-start.4
  63.8 1.0 collective-permute-start.6
  64.8 2.4 %collective-permute-done.4 = f32[4,64,1536]{2,1,0:T(8,128)S(1)} collective-permute-done((f32[4,64,1536]{2,1,0:T(8,128)}, f32[4,64,1536]{2,1,0:T(8,128)S(1)}, u32[]{:S(2)}, u32[]{:S(2)}) %collective-permute-start.4) | collective-permute-done | bytes 1572896 | tf_op jit(solution)/shard_map/ppermute | solution.py:20
  67.2 0.0 copy-start.5
  67.2 3.2 %add_convert_fusion = bf16[4,64,1536]{2,1,0:T(8,128)(2,1)} fusion(f32[4,64,1536]{2,1,0:T(8,128)S(1)} %collective-permute-done.4, f32[4,64,1536]{2,1,0:T(8,128)} %get-tuple-element.9, f32[4,64,1536]{2,1,0:T(8,128)} %get-tuple-element.10), kind=kLoop, calls=%fused_computation.5 | loop fusion | flops 1179648 | bytes 5505024 | tf_op jit(solution)/shard_map/convert_element_type | solution.py:196
  70.5 2.8 %reshape.35 = bf16[4,32,2,1536]{3,2,1,0:T(2,128)(2,1)} reshape(bf16[4,64,1536]{2,1,0:T(8,128)(2,1)} %add_convert_fusion) | data formatting | bytes 1572864 | tf_op jit(solution)/shard_map/reshape | solution.py:200
  73.3 27.4 %collective-permute-done.6 = bf16[2,4,64,1536]{3,2,1,0:T(8,128)(2,1)} collective-permute-done((bf16[2,4,64,1536]{3,2,1,0:T(8,128)(2,1)}, bf16[2,4,64,1536]{3,2,1,0:T(8,128)(2,1)}, u32[]{:S(2)}, u32[]{:S(2)}) %collective-permute-start.6) | collective-permute-done | bytes 1572896 | tf_op jit(solution)/shard_map/ppermute | solution.py:20
  100.8 0.0 collective-permute-done.5
  100.8 0.0 copy-done.5
  100.8 3.2 %convert_add_fusion = bf16[2,4,64,1536]{3,2,1,0:T(8,128)(2,1)S(1)} fusion(bf16[2,4,64,1536]{3,2,1,0:T(8,128)(2,1)} %collective-permute-done.6, f32[2,4,64,1536]{3,2,1,0:T(8,128)S(1)} %copy-done.5, f32[2,4,64,1536]{3,2,1,0:T(8,128)} %collective-permute-done.5), kind=kLoop, calls=%fused_computation.1 | loop fusion | flops 3145728 | bytes 9437184 | tf_op jit(solution)/shard_map/add | solution.py:197
  104.0 0.1 slice.42
  104.1 0.1 maximum_convert_fusion
  104.3 0.1 fusion.1
  104.4 1.2 %convert_element_type.19 = bf16[4,32,2,1536]{3,2,1,0:T(2,128)(2,1)} reshape(bf16[1,4,64,1536]{3,2,1,0:T(8,128)(2,1)S(1)} %get-tuple-element.15) | data formatting | bytes 1572864 | tf_op jit(solution)/shard_map/convert_element_type | solution.py:199
  105.5 1.2 %convert_element_type.18 = bf16[4,32,2,1536]{3,2,1,0:T(2,128)(2,1)} reshape(bf16[1,4,64,1536]{3,2,1,0:T(8,128)(2,1)S(1)} %get-tuple-element.16) | data formatting | bytes 1572864 | tf_op jit(solution)/shard_map/convert_element_type | solution.py:198
  (6 shorter events, 0.1 us)
Async XLA Ops:
  0.6 2.4 %copy-start.6 = (bf16[4,32,2,1536]{3,2,1,0:T(2,128)(2,1)S(1)}, bf16[4,32,2,1536]{3,2,1,0:T(2,128)(2,1)}, u32[]{:S(2)}) copy-start(bf16[4,32,2,1536]{3,2,1,0:T(2,128)(2,1)} %param.8) | copy-start | bytes 2359300
  3.0 0.9 copy-start.4
  3.9 1.1 %slice-start = ((bf16[4,64,1536]{2,1,0:T(8,128)(2,1)}), bf16[4,56,1536]{2,1,0:T(8,128)(2,1)S(1)}, s32[]{:S(2)}) async-start(bf16[4,64,1536]{2,1,0:T(8,128)(2,1)} %copy-done.4), calls=%async_computation | async-start | bytes 1376256 | tf_op jit(solution)/shard_map/jit(_roll_static)/slice | solution.py:166
  5.1 1.3 %copy-start.7 = (bf16[4,32,2,1536]{3,2,1,0:T(2,128)(2,1)S(1)}, bf16[4,32,2,1536]{3,2,1,0:T(2,128)(2,1)}, u32[]{:S(2)}) copy-start(bf16[4,32,2,1536]{3,2,1,0:T(2,128)(2,1)} %param.6) | copy-start | bytes 2359300
  5.3 5.0 %copy-start.1 = (bf16[2,4,64,1536]{3,2,1,0:T(8,128)(2,1)}, bf16[2,4,64,1536]{3,2,1,0:T(8,128)(2,1)S(1)}, u32[]{:S(2)}) copy-start(bf16[2,4,64,1536]{3,2,1,0:T(8,128)(2,1)S(1)} %pad_maximum_fusion.refs_4_.refs_6_) | copy-start | bytes 4718596
  5.3 2.3 %copy-start.2 = (bf16[4,32,2,1536]{3,2,1,0:T(2,128)(2,1)S(1)}, bf16[4,32,2,1536]{3,2,1,0:T(2,128)(2,1)}, u32[]{:S(2)}) copy-start(bf16[4,32,2,1536]{3,2,1,0:T(2,128)(2,1)} %param.10) | copy-start | bytes 2359300
  5.3 17.1 %collective-permute-start = (bf16[2,4,64,1536]{3,2,1,0:T(8,128)(2,1)S(1)}, bf16[2,4,64,1536]{3,2,1,0:T(8,128)(2,1)}, u32[]{:S(2)}, u32[]{:S(2)}) collective-permute-start(bf16[2,4,64,1536]{3,2,1,0:T(8,128)(2,1)S(1)} %pad_maximum_fusion.refs_4_.refs_6_), channel_id=1, source_target_pairs={{0,1},{1,0},{2,3},{3,2},{4,5},{5,4},{6,7},{7,6},{8,9},{9,8},{10,11... | collective-permute-start | bytes 4718600 | tf_op jit(solution)/shard_map/ppermute | solution.py:20
  8.8 1.4 %copy-start.3 = (bf16[1,4,64,1536]{3,2,1,0:T(8,128)(2,1)S(1)}, bf16[1,4,64,1536]{3,2,1,0:T(8,128)(2,1)}, u32[]{:S(2)}) copy-start(bf16[1,4,64,1536]{3,2,1,0:T(8,128)(2,1)} %stack_reshape.13) | copy-start | bytes 2359300
  10.1 6.1 %copy-start.9 = (f32[4,32,2,12]{1,2,3,0:T(2,128)S(1)}, f32[4,32,2,12]{1,2,3,0:T(2,128)}, u32[]{:S(2)}) copy-start(f32[4,32,2,12]{1,2,3,0:T(2,128)} %param.11) | copy-start | bytes 36868
  10.2 9.7 %copy-start = (bf16[2,4,64,1536]{3,2,1,0:T(8,128)(2,1)}, bf16[2,4,64,1536]{3,2,1,0:T(8,128)(2,1)S(1)}, u32[]{:S(2)}) copy-start(bf16[2,4,64,1536]{3,2,1,0:T(8,128)(2,1)S(1)} %constant_dynamic-update-slice_fusion.refs_0_.refs_1_.refs_2_) | copy-start | bytes 4718596
  10.2 38.5 %collective-permute-start.1 = (bf16[2,4,64,1536]{3,2,1,0:T(8,128)(2,1)S(1)}, bf16[2,4,64,1536]{3,2,1,0:T(8,128)(2,1)}, u32[]{:S(2)}, u32[]{:S(2)}) collective-permute-start(bf16[2,4,64,1536]{3,2,1,0:T(8,128)(2,1)S(1)} %constant_dynamic-update-slice_fusion.refs_0_.refs_1_.refs_2_), channel_id=1, source_target_pairs={{0,1},{1,0},{2,3},{3,2},{4,5},{5,4},{6,7},{7,6},{8,9},{9,8},{10,11... | collective-permute-start | bytes 4718600 | tf_op jit(solution)/shard_map/ppermute | solution.py:20
  10.3 38.4 %collective-permute-start.3 = (bf16[2,4,64,1536]{3,2,1,0:T(8,128)(2,1)S(1)}, bf16[2,4,64,1536]{3,2,1,0:T(8,128)(2,1)}, u32[]{:S(2)}, u32[]{:S(2)}) collective-permute-start(bf16[2,4,64,1536]{3,2,1,0:T(8,128)(2,1)S(1)} %pad_maximum_fusion.refs_4_.refs_6_), channel_id=1, source_target_pairs={{0,15},{1,2},{2,1},{3,4},{4,3},{5,6},{6,5},{7,8},{8,7},{9,10},{10,... | collective-permute-start | bytes 4718600 | tf_op jit(solution)/shard_map/ppermute | solution.py:20
  22.4 0.6 copy-start.8
  38.1 62.6 %collective-permute-start.5 = (f32[2,4,64,1536]{3,2,1,0:T(8,128)}, f32[2,4,64,1536]{3,2,1,0:T(8,128)}, u32[]{:S(2)}, u32[]{:S(2)}) collective-permute-start(f32[2,4,64,1536]{3,2,1,0:T(8,128)} %get-tuple-element.13), channel_id=1, source_target_pairs={{0,1},{1,0},{2,3},{3,2},{4,5},{5,4},{6,7},{7,6},{8,9},{9,8},{10,11... | collective-permute-start | bytes 9437192 | tf_op jit(solution)/shard_map/ppermute | solution.py:20
  41.6 5.4 %collective-permute-start.2 = (f32[2,12,4,1,64]{4,3,2,1,0:T(1,128)}, f32[2,12,4,1,64]{4,3,2,1,0:T(1,128)S(1)}, u32[]{:S(2)}, u32[]{:S(2)}) collective-permute-start(f32[2,12,4,1,64]{4,3,2,1,0:T(1,128)} %copy-done.8), channel_id=1, source_target_pairs={{0,1},{1,0},{2,3},{3,2},{4,5},{5,4},{6,7},{7,6},{8,9},{9,8},{10,11... | collective-permute-start | bytes 73736 | tf_op jit(solution)/shard_map/ppermute | solution.py:20
  63.6 3.7 %collective-permute-start.4 = (f32[4,64,1536]{2,1,0:T(8,128)}, f32[4,64,1536]{2,1,0:T(8,128)S(1)}, u32[]{:S(2)}, u32[]{:S(2)}) collective-permute-start(f32[4,64,1536]{2,1,0:T(8,128)} %get-tuple-element.11), channel_id=1, source_target_pairs={{0,1},{1,0},{2,3},{3,2},{4,5},{5,4},{6,7},{7,6},{8,9},{9,8},{10,11... | collective-permute-start | bytes 4718600 | tf_op jit(solution)/shard_map/ppermute | solution.py:20
  63.8 37.0 %collective-permute-start.6 = (bf16[2,4,64,1536]{3,2,1,0:T(8,128)(2,1)}, bf16[2,4,64,1536]{3,2,1,0:T(8,128)(2,1)}, u32[]{:S(2)}, u32[]{:S(2)}) collective-permute-start(bf16[2,4,64,1536]{3,2,1,0:T(8,128)(2,1)} %get-tuple-element.14), channel_id=1, source_target_pairs={{0,15},{1,2},{2,1},{3,4},{4,3},{5,6},{6,5},{7,8},{8,7},{9,10},{10,... | collective-permute-start | bytes 4718600 | tf_op jit(solution)/shard_map/ppermute | solution.py:20
  67.2 33.5 %copy-start.5 = (f32[2,4,64,1536]{3,2,1,0:T(8,128)S(1)}, f32[2,4,64,1536]{3,2,1,0:T(8,128)}, u32[]{:S(2)}) copy-start(f32[2,4,64,1536]{3,2,1,0:T(8,128)} %get-tuple-element.12) | copy-start | bytes 9437188

commit v10 on v9

--- a/solution.py
+++ b/solution.py
@@ -163,8 +163,8 @@
     )
     kv_own = jnp.stack(
         [
-            jnp.roll(key_vecs.reshape(rows, width, channels), mf, axis=1),
-            jnp.roll(value_vecs.reshape(rows, width, channels), mf, axis=1),
+            jnp.roll(key_vecs, MARGIN, axis=1).reshape(rows, width, channels),
+            jnp.roll(value_vecs, MARGIN, axis=1).reshape(rows, width, channels),
         ]
     )
     kv_cross = swap(kv_own, chip_neighbour)
@@ -194,9 +194,9 @@
     dq_back = jnp.concatenate(back_parts, axis=-1)
     arrived = jnp.concatenate(arrived_parts, axis=-1)
     dq = (dq_local + dq_mine + dq_back).astype(jnp.bfloat16)
-    total = jnp.roll(part_own + back_partner + arrived.astype(jnp.float32), -mf, axis=2)
-    grad_keys = total[0].astype(jnp.bfloat16).reshape(rows, width_cells, frames, channels)
-    grad_values = total[1].astype(jnp.bfloat16).reshape(rows, width_cells, frames, channels)
+    total = (part_own + back_partner + arrived.astype(jnp.float32)).astype(jnp.bfloat16)
+    grad_keys = jnp.roll(total[0].reshape(rows, width_cells, frames, channels), -MARGIN, axis=1)
+    grad_values = jnp.roll(total[1].reshape(rows, width_cells, frames, channels), -MARGIN, axis=1)
     grad_queries = dq.reshape(rows, width_cells, frames, channels)
     return (grad_queries, grad_keys, grad_values)
 

time: 109 us -> 112 us (1.028)
  other arithmetic: 10.6 us -> 15.1 us
  local copies, waits for them, and re-layouts: 22.3 us -> 21.1 us
    concatenate x0 -> x3, other arithmetic: none -> 4.96 us  [the longest x1 2.92 us: on_device(): jnp.roll(total[0].reshape(rows, width_cells, frames, channels), -MARGIN,...]
    add x1 -> x0, other arithmetic: 3.2 us -> none  [on_device(): part_own + back_partner + arrived.astype(jnp.float32)]
    convert_element_type x0 -> x1, other arithmetic: none -> 3.2 us  [on_device(): (part_own + back_partner + arrived.astype(jnp.float32)).astype(jnp.bfloat16)]
    reshape x2 -> x0, local copies, waits for them, and re-layouts: 2.64 us -> none  [the longest x1 2.34 us: on_device(): key_vecs.reshape(rows, width, channels)]
    another operation x3, local copies, waits for them, and re-layouts: 2.4 us -> 4.78 us  [on_device(): jnp.stack([queries.reshape(rows, width, channels), grad_out.reshape(rows,...]
    convert_element_type x2 -> x0, local copies, waits for them, and re-layouts: 2.35 us -> none  [the longest x1 1.17 us: on_device(): total[1].astype(jnp.bfloat16).reshape(rows, width_cells, frames, channels)]
    another operation x0 -> x5, local copies, waits for them, and re-layouts: none -> 1.24 us  [the longest x3 0.65 us: on_device(): jnp.stack([jnp.roll(key_vecs, MARGIN, axis=1).reshape(rows, width, channe...]
    slice x8 -> x14, local copies, waits for them, and re-layouts: 1.33 us -> 2.48 us  [the longest x4 1.14 us: on_device(): jnp.roll(key_vecs, MARGIN, axis=1).reshape(rows, width, channels)]
  transfers between devices with their start and end apart: 7 -> 7, of which waited for: 3 -> 3; matrix products, arithmetic and copies ran while one was open for 19% -> 21% of each run, Pallas kernels for 28% -> 27%
where the time goes in v10:
time: 112 us; the launch traced here: 110 us
  waiting for transfers between devices  35.2 us (31%)
  Pallas kernels  30 us (27%)
  local copies, waits for them, and re-layouts  21.1 us (19%)
  other arithmetic  15.1 us (13%)
  starting transfers between devices  7.75 us (7%)
    ppermute x7, waiting for transfers between devices, swap(): return lax.ppermute(block, 'sy', route)  35.2 us
    pallas_call x2, Pallas kernels, window_pass(): pl.pallas_call(kernel, grid=(heads,), in_specs=in_specs, out_specs=[qspec...  30 us
    ppermute x7, starting transfers between devices, swap(): return lax.ppermute(block, 'sy', route)  7.75 us
    another operation x3, local copies, waits for them, and re-layouts, on_device(): jnp.stack([queries.reshape(rows, width, channels), grad_out.reshape(rows,...  4.78 us
    convert_element_type x1, other arithmetic, on_device(): dq = (dq_local + dq_mine + dq_back).astype(jnp.bfloat16)  3.23 us
    reshape x1, local copies, waits for them, and re-layouts, on_device(): grad_out.reshape(rows, width, heads, HEAD_DIM)  3.22 us
    reshape x1, local copies, waits for them, and re-layouts, on_device(): outputs_fwd.reshape(rows, width, heads, HEAD_DIM)  3.21 us
    convert_element_type x1, other arithmetic, on_device(): (part_own + back_partner + arrived.astype(jnp.float32)).astype(jnp.bfloat16)  3.2 us
  transfers between devices with their start and end apart: 7, of which 3 were waited for; matrix products, arithmetic and copies ran while one was open for 21% of the time, Pallas kernels for 27%

profile of v10, /device:TPU:1, one launch (start us, length us, event | category | flops | bytes accessed | tf_op | source)
XLA Modules:
  0.0 110.0 jit_solution(13291219005206647491)
XLA Ops:
  0.6 0.0 slice-start.3
  0.6 0.0 slice-start.4
  0.7 0.9 slice-done.3
  1.5 0.3 slice-done.4
  1.8 1.0 pad_maximum_fusion
  2.8 0.3 stack_reshape.22
  3.1 0.0 slice-done.1
  3.1 0.0 slice-done.2
  3.1 1.0 pad_maximum_fusion.1
  4.2 0.3 stack_reshape.23
  4.5 0.1 constant_dynamic-update-slice_fusion.5
  4.5 0.0 copy-start.2
  4.5 0.1 constant_dynamic-update-slice_fusion.4.refs_4_.refs_6_
  4.6 0.0 copy-start.1
  4.6 0.1 collective-permute-start
  4.7 3.5 %stack_reshape.18 = bf16[1,4,64,1536]{3,2,1,0:T(8,128)(2,1)} reshape(bf16[4,32,2,1536]{3,2,1,0:T(2,128)(2,1)} %param.6) | data formatting | bytes 1572864 | tf_op jit(solution)/shard_map/stack;reshape | solution.py:154
  8.3 0.0 copy-done.2
  8.3 1.2 %stack_reshape.19 = bf16[1,4,64,1536]{3,2,1,0:T(8,128)(2,1)} reshape(bf16[4,32,2,1536]{3,2,1,0:T(2,128)(2,1)S(1)} %copy-done.2) | data formatting | bytes 1572864 | tf_op jit(solution)/shard_map/stack;reshape | solution.py:154
  9.5 1.3 %constant_dynamic-update-slice_fusion.1 = bf16[2,4,64,1536]{3,2,1,0:T(8,128)(2,1)S(1)} fusion(bf16[1,4,64,1536]{3,2,1,0:T(8,128)(2,1)} %stack_reshape.18), kind=kLoop, calls=%fused_computation.10 | loop fusion | bytes 1572864
  10.7 0.1 copy-done.3
  10.8 0.1 constant_dynamic-update-slice_fusion.refs_0_.refs_1_.refs_2_
  10.9 0.0 copy-start
  10.9 0.1 collective-permute-start.1
  11.0 0.0 copy-done.1
  11.0 2.7 %collective-permute-start.3 = (bf16[2,4,64,1536]{3,2,1,0:T(8,128)(2,1)S(1)}, bf16[2,4,64,1536]{3,2,1,0:T(8,128)(2,1)}, u32[]{:S(2)}, u32[]{:S(2)}) collective-permute-start(bf16[2,4,64,1536]{3,2,1,0:T(8,128)(2,1)S(1)} %constant_dynamic-update-slice_fusion.4.refs_4_.refs_6_), channel_id=1, source_target_pairs={{0,15},{1,2},{2,1},{3,4},{4,3},{5,6},{6,5},{7,8},{8,7},{9,10},{10,... | collective-permute-start | bytes 4718600 | tf_op jit(solution)/shard_map/ppermute | solution.py:20
  13.7 3.2 %reshape.18 = bf16[4,64,12,128]{3,2,1,0:T(8,128)(2,1)} reshape(bf16[4,32,2,1536]{3,2,1,0:T(2,128)(2,1)} %param.10) | data formatting | bytes 1572864 | tf_op jit(solution)/shard_map/reshape | solution.py:157
  16.9 0.0 copy-done.7
  16.9 0.1 copy.9
  17.0 0.2 copy.10
  17.2 0.1 stack_reshape.20
  17.4 3.2 %reshape.19 = bf16[4,64,12,128]{3,2,1,0:T(8,128)(2,1)} reshape(bf16[4,32,2,1536]{3,2,1,0:T(2,128)(2,1)} %param.9) | data formatting | bytes 1572864 | tf_op jit(solution)/shard_map/reshape | solution.py:158
  20.6 2.2 %fusion = f32[4,64,12]{2,1,0:T(8,128)S(1)} fusion(bf16[4,64,12,128]{3,2,1,0:T(8,128)(2,1)} %reshape.18, bf16[4,64,12,128]{3,2,1,0:T(8,128)(2,1)} %reshape.19), kind=kLoop, calls=%fused_computation.2 | loop fusion | flops 1569792 | bytes 1585152
  22.7 0.2 copy.19
  22.9 0.1 stack_reshape.21
  23.1 0.0 copy-start.6
  23.1 0.0 collective-permute-done.refs_5_.refs_7_
  23.1 0.6 copy-done.6
  23.7 15.1 %shard_map.85 = (f32[4,64,1536]{2,1,0:T(8,128)}, f32[2,4,64,1536]{3,2,1,0:T(8,128)}, f32[2,4,64,1536]{3,2,1,0:T(8,128)}) custom-call(bf16[2,4,64,1536]{3,2,1,0:T(8,128)(2,1)} %copy-done, bf16[2,4,64,1536]{3,2,1,0:T(8,128)(2,1)} %copy-done, f32[2,12,4,1,64]{4,3,2,1,0:T(1,128)} %copy-done.6, f32[2,12,4,1,64]{4,3,2,1,0:T(1,128)} %copy-done.6, ...), custom_call_target="tpu_custom_call" | custom-call | flops 1006632960 | bytes 12582912 | tf_op jit(solution)/shard_map/pallas_call | solution.py:128
  38.8 3.5 %collective-permute-start.5 = (f32[2,4,64,1536]{3,2,1,0:T(8,128)}, f32[2,4,64,1536]{3,2,1,0:T(8,128)}, u32[]{:S(2)}, u32[]{:S(2)}) collective-permute-start(f32[2,4,64,1536]{3,2,1,0:T(8,128)} %get-tuple-element.13), channel_id=1, source_target_pairs={{0,1},{1,0},{2,3},{3,2},{4,5},{5,4},{6,7},{7,6},{8,9},{9,8},{10,11... | collective-permute-start | bytes 9437192 | tf_op jit(solution)/shard_map/ppermute | solution.py:20
  42.3 0.1 collective-permute-start.2
  42.4 5.4 %collective-permute-done.2 = f32[2,12,4,1,64]{4,3,2,1,0:T(1,128)S(1)} collective-permute-done((f32[2,12,4,1,64]{4,3,2,1,0:T(1,128)}, f32[2,12,4,1,64]{4,3,2,1,0:T(1,128)S(1)}, u32[]{:S(2)}, u32[]{:S(2)}) %collective-permute-start.2) | collective-permute-done | bytes 24608 | tf_op jit(solution)/shard_map/ppermute | solution.py:20
  47.8 1.6 %pad_maximum_fusion.4.refs_4_.refs_5_ = f32[2,12,4,1,128]{4,3,2,1,0:T(1,128)} fusion(f32[2,12,4,1,64]{4,3,2,1,0:T(1,128)S(1)} %collective-permute-done.2, f32[2,12,4,1,64]{4,3,2,1,0:T(1,128)} %copy-done.6), kind=kLoop, calls=%fused_computation.8 | loop fusion | flops 12288 | bytes 98304 | tf_op jit(solution)/shard_map/concatenate | solution.py:180
  49.4 0.0 collective-permute-done.1.refs_1_.refs_3_
  49.4 0.0 collective-permute-done.3.refs_6_.refs_7_
  49.4 14.9 %shard_map.86 = (f32[4,64,1536]{2,1,0:T(8,128)}, f32[4,64,1536]{2,1,0:T(8,128)}, bf16[2,4,64,1536]{3,2,1,0:T(8,128)(2,1)}) custom-call(bf16[2,4,64,1536]{3,2,1,0:T(8,128)(2,1)} %copy-done, bf16[2,4,64,1536]{3,2,1,0:T(8,128)(2,1)} %collective-permute-done.1.refs_1_.refs_3_, bf16[2,4,64,1536]{3,2,1,0:T(8,128)(2,1)} %copy-done, ...), custom_call_target="tpu_custom_call" | custom-call | flops 1006632960 | bytes 11010048 | tf_op jit(solution)/shard_map/pallas_call | solution.py:128
  64.2 0.2 collective-permute-start.4
  64.4 1.1 collective-permute-start.6
  65.5 2.4 %collective-permute-done.4 = f32[4,64,1536]{2,1,0:T(8,128)S(1)} collective-permute-done((f32[4,64,1536]{2,1,0:T(8,128)}, f32[4,64,1536]{2,1,0:T(8,128)S(1)}, u32[]{:S(2)}, u32[]{:S(2)}) %collective-permute-start.4) | collective-permute-done | bytes 1572896 | tf_op jit(solution)/shard_map/ppermute | solution.py:20
  67.9 3.2 %add_convert_fusion.1 = bf16[4,64,1536]{2,1,0:T(8,128)(2,1)} fusion(f32[4,64,1536]{2,1,0:T(8,128)S(1)} %collective-permute-done.4, f32[4,64,1536]{2,1,0:T(8,128)} %get-tuple-element.9, f32[4,64,1536]{2,1,0:T(8,128)} %get-tuple-element.10), kind=kLoop, calls=%fused_computation.3 | loop fusion | flops 1179648 | bytes 5505024 | tf_op jit(solution)/shard_map/convert_element_type | solution.py:196
  71.1 2.8 %reshape.21 = bf16[4,32,2,1536]{3,2,1,0:T(2,128)(2,1)} reshape(bf16[4,64,1536]{2,1,0:T(8,128)(2,1)} %add_convert_fusion.1) | data formatting | bytes 1572864 | tf_op jit(solution)/shard_map/reshape | solution.py:200
  74.0 27.4 %collective-permute-done.6 = bf16[2,4,64,1536]{3,2,1,0:T(8,128)(2,1)} collective-permute-done((bf16[2,4,64,1536]{3,2,1,0:T(8,128)(2,1)}, bf16[2,4,64,1536]{3,2,1,0:T(8,128)(2,1)}, u32[]{:S(2)}, u32[]{:S(2)}) %collective-permute-start.6) | collective-permute-done | bytes 1572896 | tf_op jit(solution)/shard_map/ppermute | solution.py:20
  101.4 0.0 collective-permute-done.5
  101.4 3.2 %add_convert_fusion = bf16[2,4,64,1536]{3,2,1,0:T(8,128)(2,1)S(1)} fusion(bf16[2,4,64,1536]{3,2,1,0:T(8,128)(2,1)} %collective-permute-done.6, f32[2,4,64,1536]{3,2,1,0:T(8,128)S(1)} %copy-done.5, f32[2,4,64,1536]{3,2,1,0:T(8,128)} %collective-permute-done.5), kind=kLoop, calls=%fused_computation | loop fusion | flops 3145728 | bytes 9437184 | tf_op jit(solution)/shard_map/convert_element_type | solution.py:197
  104.6 0.1 fusion.1
  104.7 0.3 reshape_squeeze.7
  105.0 0.0 copy-start.4
  105.1 0.1 slice.49
  105.1 0.3 reshape_squeeze.6
  105.4 0.5 copy-done.4
  105.9 0.1 slice.46
  106.0 0.0 slice-start
  106.0 0.5 slice.45
  106.5 0.6 slice-done
  107.1 2.9 %pad_maximum_fusion.2 = (bf16[4,32,2,1536]{3,2,1,0:T(2,128)(2,1)}, bf16[4,32,2,1536]{3,2,1,0:T(2,128)(2,1)}) fusion(bf16[4,4,2,1536]{3,2,1,0:T(2,128)(2,1)S(1)} %slice.46, bf16[4,28,2,1536]{3,2,1,0:T(2,128)(2,1)S(1)} %slice.45, bf16[4,4,2,1536]{3,2,1,0:T(2,128)(2,1)S(1)} %slice.49, bf16[4,28,2,1536]{3,2,1,0:T(2,128)(2,1)S(1)} %slice-done), kind=kLoop, calls=%fused_computation.6 | loop fusion | flops 786432 | bytes 3145728 | tf_op jit(solution)/shard_map/jit(_roll_static)/concatenate | solution.py:198
  (9 shorter events, 0.0 us)
Async XLA Ops:
  0.6 0.9 slice-start.3
  0.6 1.1 %slice-start.4 = ((bf16[4,32,2,1536]{3,2,1,0:T(2,128)(2,1)}), bf16[4,28,2,1536]{3,2,1,0:T(2,128)(2,1)S(1)}, s32[]{:S(2)}) async-start(bf16[4,32,2,1536]{3,2,1,0:T(2,128)(2,1)} %param.7), calls=%async_computation.4 | async-start | bytes 1376256 | tf_op jit(solution)/shard_map/jit(_roll_static)/slice | solution.py:166
  1.8 1.3 %slice-start.1 = ((bf16[4,32,2,1536]{3,2,1,0:T(2,128)(2,1)}), bf16[4,4,2,1536]{3,2,1,0:T(2,128)(2,1)S(1)}, s32[]{:S(2)}) async-start(bf16[4,32,2,1536]{3,2,1,0:T(2,128)(2,1)} %param.8), calls=%async_computation.1 | async-start | bytes 196608 | tf_op jit(solution)/shard_map/jit(_roll_static)/slice | solution.py:167
  1.8 1.3 %slice-start.2 = ((bf16[4,32,2,1536]{3,2,1,0:T(2,128)(2,1)}), bf16[4,28,2,1536]{3,2,1,0:T(2,128)(2,1)S(1)}, s32[]{:S(2)}) async-start(bf16[4,32,2,1536]{3,2,1,0:T(2,128)(2,1)} %param.8), calls=%async_computation.2 | async-start | bytes 1376256 | tf_op jit(solution)/shard_map/jit(_roll_static)/slice | solution.py:167
  4.5 3.8 %copy-start.2 = (bf16[4,32,2,1536]{3,2,1,0:T(2,128)(2,1)S(1)}, bf16[4,32,2,1536]{3,2,1,0:T(2,128)(2,1)}, u32[]{:S(2)}) copy-start(bf16[4,32,2,1536]{3,2,1,0:T(2,128)(2,1)} %param.10) | copy-start | bytes 2359300
  4.6 6.4 %copy-start.1 = (bf16[2,4,64,1536]{3,2,1,0:T(8,128)(2,1)}, bf16[2,4,64,1536]{3,2,1,0:T(8,128)(2,1)S(1)}, u32[]{:S(2)}) copy-start(bf16[2,4,64,1536]{3,2,1,0:T(8,128)(2,1)S(1)} %constant_dynamic-update-slice_fusion.4.refs_4_.refs_6_) | copy-start | bytes 4718596
  4.6 18.5 %collective-permute-start = (bf16[2,4,64,1536]{3,2,1,0:T(8,128)(2,1)S(1)}, bf16[2,4,64,1536]{3,2,1,0:T(8,128)(2,1)}, u32[]{:S(2)}, u32[]{:S(2)}) collective-permute-start(bf16[2,4,64,1536]{3,2,1,0:T(8,128)(2,1)S(1)} %constant_dynamic-update-slice_fusion.4.refs_4_.refs_6_), channel_id=1, source_target_pairs={{0,1},{1,0},{2,3},{3,2},{4,5},{5,4},{6,7},{7,6},{8,9},{9,8},{10,11... | collective-permute-start | bytes 4718600 | tf_op jit(solution)/shard_map/ppermute | solution.py:20
  9.5 1.4 %copy-start.3 = (bf16[1,4,64,1536]{3,2,1,0:T(8,128)(2,1)S(1)}, bf16[1,4,64,1536]{3,2,1,0:T(8,128)(2,1)}, u32[]{:S(2)}) copy-start(bf16[1,4,64,1536]{3,2,1,0:T(8,128)(2,1)} %stack_reshape.19) | copy-start | bytes 2359300
  10.8 6.1 %copy-start.7 = (f32[4,32,2,12]{1,2,3,0:T(2,128)S(1)}, f32[4,32,2,12]{1,2,3,0:T(2,128)}, u32[]{:S(2)}) copy-start(f32[4,32,2,12]{1,2,3,0:T(2,128)} %param.11) | copy-start | bytes 36868
  10.9 9.7 %copy-start = (bf16[2,4,64,1536]{3,2,1,0:T(8,128)(2,1)}, bf16[2,4,64,1536]{3,2,1,0:T(8,128)(2,1)S(1)}, u32[]{:S(2)}) copy-start(bf16[2,4,64,1536]{3,2,1,0:T(8,128)(2,1)S(1)} %constant_dynamic-update-slice_fusion.refs_0_.refs_1_.refs_2_) | copy-start | bytes 4718596
  10.9 38.5 %collective-permute-start.1 = (bf16[2,4,64,1536]{3,2,1,0:T(8,128)(2,1)S(1)}, bf16[2,4,64,1536]{3,2,1,0:T(8,128)(2,1)}, u32[]{:S(2)}, u32[]{:S(2)}) collective-permute-start(bf16[2,4,64,1536]{3,2,1,0:T(8,128)(2,1)S(1)} %constant_dynamic-update-slice_fusion.refs_0_.refs_1_.refs_2_), channel_id=1, source_target_pairs={{0,1},{1,0},{2,3},{3,2},{4,5},{5,4},{6,7},{7,6},{8,9},{9,8},{10,11... | collective-permute-start | bytes 4718600 | tf_op jit(solution)/shard_map/ppermute | solution.py:20
  11.0 38.3 %collective-permute-start.3 = (bf16[2,4,64,1536]{3,2,1,0:T(8,128)(2,1)S(1)}, bf16[2,4,64,1536]{3,2,1,0:T(8,128)(2,1)}, u32[]{:S(2)}, u32[]{:S(2)}) collective-permute-start(bf16[2,4,64,1536]{3,2,1,0:T(8,128)(2,1)S(1)} %constant_dynamic-update-slice_fusion.4.refs_4_.refs_6_), channel_id=1, source_target_pairs={{0,15},{1,2},{2,1},{3,4},{4,3},{5,6},{6,5},{7,8},{8,7},{9,10},{10,... | collective-permute-start | bytes 4718600 | tf_op jit(solution)/shard_map/ppermute | solution.py:20
  23.1 0.6 copy-start.6
  38.8 62.6 %collective-permute-start.5 = (f32[2,4,64,1536]{3,2,1,0:T(8,128)}, f32[2,4,64,1536]{3,2,1,0:T(8,128)}, u32[]{:S(2)}, u32[]{:S(2)}) collective-permute-start(f32[2,4,64,1536]{3,2,1,0:T(8,128)} %get-tuple-element.13), channel_id=1, source_target_pairs={{0,1},{1,0},{2,3},{3,2},{4,5},{5,4},{6,7},{7,6},{8,9},{9,8},{10,11... | collective-permute-start | bytes 9437192 | tf_op jit(solution)/shard_map/ppermute | solution.py:20
  42.3 5.4 %collective-permute-start.2 = (f32[2,12,4,1,64]{4,3,2,1,0:T(1,128)}, f32[2,12,4,1,64]{4,3,2,1,0:T(1,128)S(1)}, u32[]{:S(2)}, u32[]{:S(2)}) collective-permute-start(f32[2,12,4,1,64]{4,3,2,1,0:T(1,128)} %copy-done.6), channel_id=1, source_target_pairs={{0,1},{1,0},{2,3},{3,2},{4,5},{5,4},{6,7},{7,6},{8,9},{9,8},{10,11... | collective-permute-start | bytes 73736 | tf_op jit(solution)/shard_map/ppermute | solution.py:20
  64.2 3.7 %collective-permute-start.4 = (f32[4,64,1536]{2,1,0:T(8,128)}, f32[4,64,1536]{2,1,0:T(8,128)S(1)}, u32[]{:S(2)}, u32[]{:S(2)}) collective-permute-start(f32[4,64,1536]{2,1,0:T(8,128)} %get-tuple-element.11), channel_id=1, source_target_pairs={{0,1},{1,0},{2,3},{3,2},{4,5},{5,4},{6,7},{7,6},{8,9},{9,8},{10,11... | collective-permute-start | bytes 4718600 | tf_op jit(solution)/shard_map/ppermute | solution.py:20
  64.4 37.0 %collective-permute-start.6 = (bf16[2,4,64,1536]{3,2,1,0:T(8,128)(2,1)}, bf16[2,4,64,1536]{3,2,1,0:T(8,128)(2,1)}, u32[]{:S(2)}, u32[]{:S(2)}) collective-permute-start(bf16[2,4,64,1536]{3,2,1,0:T(8,128)(2,1)} %get-tuple-element.14), channel_id=1, source_target_pairs={{0,15},{1,2},{2,1},{3,4},{4,3},{5,6},{6,5},{7,8},{8,7},{9,10},{10,... | collective-permute-start | bytes 4718600 | tf_op jit(solution)/shard_map/ppermute | solution.py:20
  67.9 33.5 %copy-start.5 = (f32[2,4,64,1536]{3,2,1,0:T(8,128)S(1)}, f32[2,4,64,1536]{3,2,1,0:T(8,128)}, u32[]{:S(2)}) copy-start(f32[2,4,64,1536]{3,2,1,0:T(8,128)} %get-tuple-element.12) | copy-start | bytes 9437188
  105.0 0.9 copy-start.4
  106.0 1.1 %slice-start = ((bf16[4,32,2,1536]{3,2,1,0:T(2,128)(2,1)}), bf16[4,28,2,1536]{3,2,1,0:T(2,128)(2,1)S(1)}, s32[]{:S(2)}) async-start(bf16[4,32,2,1536]{3,2,1,0:T(2,128)(2,1)} %copy-done.4), calls=%async_computation | async-start | bytes 1376256 | tf_op jit(solution)/shard_map/jit(_roll_static)/slice | solution.py:199

commit v11 on v9

--- a/solution.py
+++ b/solution.py
@@ -34,7 +34,7 @@
     return [(0, start, width - start), (width - start, 0, start + span - width)]
 
 
-def window_kernel(*refs, nq, nk, tiles, tf, mf, narrow):
+def window_kernel(*refs, nq, nk, tiles, tf, mf, narrow, group):
     q_refs = refs[0:nq]
     do_refs = refs[nq : 2 * nq]
     lse_ref, delta_ref = refs[2 * nq], refs[2 * nq + 1]
@@ -62,29 +62,30 @@
         parts = [ref[:, b * tf : (b + 1) * tf, :].reshape(rows * tf, HEAD_DIM) for ref in refs_list]
         return parts[0] if len(parts) == 1 else jnp.concatenate(parts, axis=0)
 
-    for b in range(tiles):
+    for j, b in [(j, b) for j in range(group) for b in range(tiles)]:
+        lanes = slice(j * HEAD_DIM, (j + 1) * HEAD_DIM)
         pieces = window_pieces(b * tf, span, width)
-        kw = window(k_refs, pieces)
-        vw = window(v_refs, pieces)
-        qb = query_rows(q_refs, b)
-        dob = query_rows(do_refs, b)
+        kw = window([ref.at[:, :, lanes] for ref in k_refs], pieces)
+        vw = window([ref.at[:, :, lanes] for ref in v_refs], pieces)
+        qb = query_rows([ref.at[:, :, lanes] for ref in q_refs], b)
+        dob = query_rows([ref.at[:, :, lanes] for ref in do_refs], b)
         nt = (((1,), (1,)), ((), ()))
         scores = lax.dot_general(kw, qb, nt, preferred_element_type=jnp.float32) * scaling
-        attention = jnp.exp(scores - lse_ref[b])
+        attention = jnp.exp(scores - lse_ref[j, b])
         grad_attention = lax.dot_general(vw, dob, nt, preferred_element_type=jnp.float32)
-        grad_scores = (attention * (grad_attention - delta_ref[b])).astype(jnp.bfloat16)
+        grad_scores = (attention * (grad_attention - delta_ref[j, b])).astype(jnp.bfloat16)
         grad_v = jnp.dot(attention.astype(jnp.bfloat16), dob, preferred_element_type=jnp.float32)
         grad_k = jnp.dot(grad_scores, qb, preferred_element_type=jnp.float32) * scaling
         grad_q = jnp.dot(grad_scores.T, kw, preferred_element_type=jnp.float32) * scaling
         grad_q = grad_q.reshape(nq, rows, tf, HEAD_DIM)
         for source, dq_ref in enumerate(dq_refs):
-            dq_ref[:, b * tf : (b + 1) * tf, :] = grad_q[source].astype(dq_ref.dtype)
+            dq_ref[:, b * tf : (b + 1) * tf, lanes] = grad_q[source].astype(dq_ref.dtype)
         grad_k = grad_k.reshape(nk, rows, span, HEAD_DIM)
         grad_v = grad_v.reshape(nk, rows, span, HEAD_DIM)
         for block, target in enumerate(targets):
             for src, dst, size in pieces:
-                target[0, :, dst : dst + size, :] += grad_k[block, :, src : src + size, :]
-                target[1, :, dst : dst + size, :] += grad_v[block, :, src : src + size, :]
+                target[0, :, dst : dst + size, lanes] += grad_k[block, :, src : src + size, :]
+                target[1, :, dst : dst + size, lanes] += grad_v[block, :, src : src + size, :]
     if narrow:
         for out, target in zip(outs, targets):
             out[...] = target[...].astype(out.dtype)
@@ -96,18 +97,22 @@
         heads = all_channels // HEAD_DIM
     channels = heads * HEAD_DIM
     nq, nk = len(queries), len(keys)
-    kernel = functools.partial(window_kernel, nq=nq, nk=nk, tiles=tiles, tf=tf, mf=mf, narrow=narrow)
+    group = 2 if heads % 2 == 0 else 1
+    kernel = functools.partial(
+        window_kernel, nq=nq, nk=nk, tiles=tiles, tf=tf, mf=mf, narrow=narrow, group=group
+    )
+    lanes = group * HEAD_DIM
 
     def member_spec(member):
-        return pl.BlockSpec((None, rows, width, HEAD_DIM), lambda h: (member, 0, 0, h + first))
+        return pl.BlockSpec((None, rows, width, lanes), lambda h: (member, 0, 0, h + first // group))
 
     def stats_spec(member):
         return pl.BlockSpec(
-            (None, None, tiles, 1, nq * rows * tf), lambda h: (member, h + first, 0, 0, 0)
+            (None, group, tiles, 1, nq * rows * tf), lambda h: (member, h + first // group, 0, 0, 0)
         )
 
-    qspec = pl.BlockSpec((rows, width, HEAD_DIM), lambda h: (0, 0, h))
-    pspec = pl.BlockSpec((2, rows, width, HEAD_DIM), lambda h: (0, 0, 0, h))
+    qspec = pl.BlockSpec((rows, width, lanes), lambda h: (0, 0, h))
+    pspec = pl.BlockSpec((2, rows, width, lanes), lambda h: (0, 0, 0, h))
     pairs = tiles * nq * rows * tf * nk * rows * (tf + 2 * mf) * heads
     cost = pl.CostEstimate(
         flops=10 * pairs * HEAD_DIM,
@@ -115,7 +120,7 @@
         bytes_accessed=(2 * (2 * nq + 2 * nk) + 4 * nq + 8 * nk) * rows * width * channels,
     )
     part = jax.ShapeDtypeStruct((2, rows, width, channels), jnp.bfloat16 if narrow else jnp.float32)
-    scratch = [pltpu.VMEM((2, rows, width, HEAD_DIM), jnp.float32)] * nk if narrow else []
+    scratch = [pltpu.VMEM((2, rows, width, lanes), jnp.float32)] * nk if narrow else []
     dq_shape = jax.ShapeDtypeStruct((rows, width, channels), jnp.float32)
     members = list(queries) + list(grads)
     blocks = list(keys) + list(values)
@@ -127,7 +132,7 @@
     )
     return pl.pallas_call(
         kernel,
-        grid=(heads,),
+        grid=(heads // group,),
         in_specs=in_specs,
         out_specs=[qspec] * nq + [pspec] * nk,
         out_shape=[dq_shape] * nq + [part] * nk,

time: 109 us -> 105 us (0.963); the launches traced: 107 us -> 105 us
  Pallas kernels: 30 us -> 27.1 us
    pallas_call x2, Pallas kernels: 30 us -> 27.1 us  [window_pass(): pl.pallas_call(kernel, grid=(heads // group,), in_specs=in_specs, out_spe...]
  transfers between devices with their start and end apart: 7 -> 7, of which waited for: 3 -> 4; matrix products, arithmetic and copies ran while one was open for 19% -> 20% of each run, Pallas kernels for 28% -> 26%
where the time goes in v11:
time: 105 us
  waiting for transfers between devices  35.4 us (34%)
  Pallas kernels  27.1 us (26%)
  local copies, waits for them, and re-layouts  22.3 us (21%)
  other arithmetic  10.6 us (10%)
  starting transfers between devices  8.33 us (8%)
    ppermute x7, waiting for transfers between devices, swap(): return lax.ppermute(block, 'sy', route)  35.4 us
    pallas_call x2, Pallas kernels, window_pass(): pl.pallas_call(kernel, grid=(heads // group,), in_specs=in_specs, out_spe...  27.1 us
    ppermute x7, starting transfers between devices, swap(): return lax.ppermute(block, 'sy', route)  8.33 us
    unnamed x23, local copies, waits for them, and re-layouts  3.65 us
    reshape x1, local copies, waits for them, and re-layouts, on_device(): outputs_fwd.reshape(rows, width, heads, HEAD_DIM)  3.24 us
    convert_element_type x1, other arithmetic, on_device(): dq = (dq_local + dq_mine + dq_back).astype(jnp.bfloat16)  3.23 us
    reshape x1, local copies, waits for them, and re-layouts, on_device(): grad_out.reshape(rows, width, heads, HEAD_DIM)  3.2 us
    add x1, other arithmetic, on_device(): part_own + back_partner + arrived.astype(jnp.float32)  3.2 us
  transfers between devices with their start and end apart: 7, of which 4 were waited for; matrix products, arithmetic and copies ran while one was open for 20% of the time, Pallas kernels for 26%

profile of v11, /device:TPU:1, one launch (start us, length us, event | category | flops | bytes accessed | tf_op | source)
XLA Modules:
  0.0 104.6 jit_solution(9545614944248538164)
XLA Ops:
  0.6 0.0 copy-start.6
  0.6 2.3 %reshape.33 = bf16[4,64,1536]{2,1,0:T(8,128)(2,1)S(1)} reshape(bf16[4,32,2,1536]{3,2,1,0:T(2,128)(2,1)} %param.7) | data formatting | bytes 1572864 | tf_op jit(solution)/shard_map/reshape | solution.py:171
  3.0 0.0 copy-start.4
  3.0 0.0 copy-done.6
  3.0 0.3 reshape.34
  3.3 0.5 copy-done.4
  3.9 0.0 slice-start
  3.9 1.0 slice-done
  5.0 0.1 maximum_bitcast_fusion
  5.1 0.0 copy-start.7
  5.1 0.1 pad_maximum_fusion.refs_4_.refs_6_
  5.3 0.0 copy-start.1
  5.3 0.0 copy-start.2
  5.3 0.1 collective-permute-start
  5.4 1.0 copy-done.7
  6.4 1.2 %stack_reshape.12 = bf16[1,4,64,1536]{3,2,1,0:T(8,128)(2,1)} reshape(bf16[4,32,2,1536]{3,2,1,0:T(2,128)(2,1)S(1)} %copy-done.7) | data formatting | bytes 1572864 | tf_op jit(solution)/shard_map/stack;reshape | solution.py:159
  7.6 0.0 copy-done.2
  7.6 1.2 %stack_reshape.13 = bf16[1,4,64,1536]{3,2,1,0:T(8,128)(2,1)} reshape(bf16[4,32,2,1536]{3,2,1,0:T(2,128)(2,1)S(1)} %copy-done.2) | data formatting | bytes 1572864 | tf_op jit(solution)/shard_map/stack;reshape | solution.py:159
  8.8 0.0 copy-start.3
  8.8 1.3 %constant_dynamic-update-slice_fusion.1 = bf16[2,4,64,1536]{3,2,1,0:T(8,128)(2,1)S(1)} fusion(bf16[1,4,64,1536]{3,2,1,0:T(8,128)(2,1)} %stack_reshape.12), kind=kLoop, calls=%fused_computation.10 | loop fusion | bytes 1572864
  10.0 0.1 copy-done.3
  10.1 0.0 copy-start.9
  10.1 0.1 constant_dynamic-update-slice_fusion.refs_0_.refs_1_.refs_2_
  10.2 0.0 copy-start
  10.2 0.1 collective-permute-start.1
  10.3 0.0 copy-done.1
  10.3 2.7 %collective-permute-start.3 = (bf16[2,4,64,1536]{3,2,1,0:T(8,128)(2,1)S(1)}, bf16[2,4,64,1536]{3,2,1,0:T(8,128)(2,1)}, u32[]{:S(2)}, u32[]{:S(2)}) collective-permute-start(bf16[2,4,64,1536]{3,2,1,0:T(8,128)(2,1)S(1)} %pad_maximum_fusion.refs_4_.refs_6_), channel_id=1, source_target_pairs={{0,15},{1,2},{2,1},{3,4},{4,3},{5,6},{6,5},{7,8},{8,7},{9,10},{10,... | collective-permute-start | bytes 4718600 | tf_op jit(solution)/shard_map/ppermute | solution.py:20
  13.0 3.2 %reshape.30 = bf16[4,64,12,128]{3,2,1,0:T(8,128)(2,1)} reshape(bf16[4,32,2,1536]{3,2,1,0:T(2,128)(2,1)} %param.10) | data formatting | bytes 1572864 | tf_op jit(solution)/shard_map/reshape | solution.py:162
  16.2 0.0 copy-done.9
  16.2 0.1 copy.9
  16.3 0.2 copy.10
  16.5 0.1 stack_reshape.14
  16.6 3.2 %reshape.31 = bf16[4,64,12,128]{3,2,1,0:T(8,128)(2,1)} reshape(bf16[4,32,2,1536]{3,2,1,0:T(2,128)(2,1)} %param.9) | data formatting | bytes 1572864 | tf_op jit(solution)/shard_map/reshape | solution.py:163
  19.9 0.0 copy-done
  19.9 2.2 %fusion = f32[4,64,12]{2,1,0:T(8,128)S(1)} fusion(bf16[4,64,12,128]{3,2,1,0:T(8,128)(2,1)} %reshape.30, bf16[4,64,12,128]{3,2,1,0:T(8,128)(2,1)} %reshape.31), kind=kLoop, calls=%fused_computation.3 | loop fusion | flops 1569792 | bytes 1585152
  22.0 0.2 copy.19
  22.2 0.1 stack_reshape.15
  22.4 0.0 copy-start.8
  22.4 0.0 collective-permute-done.refs_5_.refs_7_
  22.4 0.6 copy-done.8
  23.0 13.6 %shard_map.85 = (f32[4,64,1536]{2,1,0:T(8,128)}, f32[2,4,64,1536]{3,2,1,0:T(8,128)}, f32[2,4,64,1536]{3,2,1,0:T(8,128)}) custom-call(bf16[2,4,64,1536]{3,2,1,0:T(8,128)(2,1)} %copy-done, bf16[2,4,64,1536]{3,2,1,0:T(8,128)(2,1)} %copy-done, f32[2,12,4,1,64]{4,3,2,1,0:T(1,128)} %copy-done.8, f32[2,12,4,1,64]{4,3,2,1,0:T(1,128)} %copy-done.8, ...), custom_call_target="tpu_custom_call" | custom-call | flops 1006632960 | bytes 12582912 | tf_op jit(solution)/shard_map/pallas_call | solution.py:133
  36.6 3.5 %collective-permute-start.5 = (f32[2,4,64,1536]{3,2,1,0:T(8,128)}, f32[2,4,64,1536]{3,2,1,0:T(8,128)}, u32[]{:S(2)}, u32[]{:S(2)}) collective-permute-start(f32[2,4,64,1536]{3,2,1,0:T(8,128)} %get-tuple-element.13), channel_id=1, source_target_pairs={{0,1},{1,0},{2,3},{3,2},{4,5},{5,4},{6,7},{7,6},{8,9},{9,8},{10,11... | collective-permute-start | bytes 9437192 | tf_op jit(solution)/shard_map/ppermute | solution.py:20
  40.2 0.1 collective-permute-start.2
  40.2 5.4 %collective-permute-done.2 = f32[2,12,4,1,64]{4,3,2,1,0:T(1,128)S(1)} collective-permute-done((f32[2,12,4,1,64]{4,3,2,1,0:T(1,128)}, f32[2,12,4,1,64]{4,3,2,1,0:T(1,128)S(1)}, u32[]{:S(2)}, u32[]{:S(2)}) %collective-permute-start.2) | collective-permute-done | bytes 24608 | tf_op jit(solution)/shard_map/ppermute | solution.py:20
  45.6 1.6 %pad_maximum_fusion.1.refs_4_.refs_5_ = f32[2,12,4,1,128]{4,3,2,1,0:T(1,128)} fusion(f32[2,12,4,1,64]{4,3,2,1,0:T(1,128)S(1)} %collective-permute-done.2, f32[2,12,4,1,64]{4,3,2,1,0:T(1,128)} %copy-done.8), kind=kLoop, calls=%fused_computation.8 | loop fusion | flops 12288 | bytes 98304 | tf_op jit(solution)/shard_map/concatenate | solution.py:185
  47.2 0.0 collective-permute-done.1.refs_1_.refs_3_
  47.2 0.8 collective-permute-done.3.refs_6_.refs_7_
  48.0 13.5 %shard_map.86 = (f32[4,64,1536]{2,1,0:T(8,128)}, f32[4,64,1536]{2,1,0:T(8,128)}, bf16[2,4,64,1536]{3,2,1,0:T(8,128)(2,1)}) custom-call(bf16[2,4,64,1536]{3,2,1,0:T(8,128)(2,1)} %copy-done, bf16[2,4,64,1536]{3,2,1,0:T(8,128)(2,1)} %collective-permute-done.1.refs_1_.refs_3_, bf16[2,4,64,1536]{3,2,1,0:T(8,128)(2,1)} %copy-done, ...), custom_call_target="tpu_custom_call" | custom-call | flops 1006632960 | bytes 11010048 | tf_op jit(solution)/shard_map/pallas_call | solution.py:133
  61.5 0.0 collective-permute-start.4
  61.6 1.8 %collective-permute-start.6 = (bf16[2,4,64,1536]{3,2,1,0:T(8,128)(2,1)}, bf16[2,4,64,1536]{3,2,1,0:T(8,128)(2,1)}, u32[]{:S(2)}, u32[]{:S(2)}) collective-permute-start(bf16[2,4,64,1536]{3,2,1,0:T(8,128)(2,1)} %get-tuple-element.14), channel_id=1, source_target_pairs={{0,15},{1,2},{2,1},{3,4},{4,3},{5,6},{6,5},{7,8},{8,7},{9,10},{10,... | collective-permute-start | bytes 4718600 | tf_op jit(solution)/shard_map/ppermute | solution.py:20
  63.4 1.8 %collective-permute-done.4 = f32[4,64,1536]{2,1,0:T(8,128)S(1)} collective-permute-done((f32[4,64,1536]{2,1,0:T(8,128)}, f32[4,64,1536]{2,1,0:T(8,128)S(1)}, u32[]{:S(2)}, u32[]{:S(2)}) %collective-permute-start.4) | collective-permute-done | bytes 1572896 | tf_op jit(solution)/shard_map/ppermute | solution.py:20
  65.2 0.0 copy-start.5
  65.2 3.2 %add_convert_fusion = bf16[4,64,1536]{2,1,0:T(8,128)(2,1)} fusion(f32[4,64,1536]{2,1,0:T(8,128)S(1)} %collective-permute-done.4, f32[4,64,1536]{2,1,0:T(8,128)} %get-tuple-element.9, f32[4,64,1536]{2,1,0:T(8,128)} %get-tuple-element.10), kind=kLoop, calls=%fused_computation.5 | loop fusion | flops 1179648 | bytes 5505024 | tf_op jit(solution)/shard_map/convert_element_type | solution.py:201
  68.4 2.8 %reshape.35 = bf16[4,32,2,1536]{3,2,1,0:T(2,128)(2,1)} reshape(bf16[4,64,1536]{2,1,0:T(8,128)(2,1)} %add_convert_fusion) | data formatting | bytes 1572864 | tf_op jit(solution)/shard_map/reshape | solution.py:205
  71.2 27.4 %collective-permute-done.6 = bf16[2,4,64,1536]{3,2,1,0:T(8,128)(2,1)} collective-permute-done((bf16[2,4,64,1536]{3,2,1,0:T(8,128)(2,1)}, bf16[2,4,64,1536]{3,2,1,0:T(8,128)(2,1)}, u32[]{:S(2)}, u32[]{:S(2)}) %collective-permute-start.6) | collective-permute-done | bytes 1572896 | tf_op jit(solution)/shard_map/ppermute | solution.py:20
  98.6 0.0 collective-permute-done.5
  98.6 0.0 copy-done.5
  98.6 3.2 %convert_add_fusion = bf16[2,4,64,1536]{3,2,1,0:T(8,128)(2,1)S(1)} fusion(bf16[2,4,64,1536]{3,2,1,0:T(8,128)(2,1)} %collective-permute-done.6, f32[2,4,64,1536]{3,2,1,0:T(8,128)S(1)} %copy-done.5, f32[2,4,64,1536]{3,2,1,0:T(8,128)} %collective-permute-done.5), kind=kLoop, calls=%fused_computation.1 | loop fusion | flops 3145728 | bytes 9437184 | tf_op jit(solution)/shard_map/add | solution.py:202
  101.9 0.1 slice.42
  102.0 0.1 maximum_convert_fusion
  102.1 0.1 fusion.1
  102.2 1.2 %convert_element_type.19 = bf16[4,32,2,1536]{3,2,1,0:T(2,128)(2,1)} reshape(bf16[1,4,64,1536]{3,2,1,0:T(8,128)(2,1)S(1)} %get-tuple-element.15) | data formatting | bytes 1572864 | tf_op jit(solution)/shard_map/convert_element_type | solution.py:204
  103.4 1.2 %convert_element_type.18 = bf16[4,32,2,1536]{3,2,1,0:T(2,128)(2,1)} reshape(bf16[1,4,64,1536]{3,2,1,0:T(8,128)(2,1)S(1)} %get-tuple-element.16) | data formatting | bytes 1572864 | tf_op jit(solution)/shard_map/convert_element_type | solution.py:203
  (6 shorter events, 0.1 us)
Async XLA Ops:
  0.6 2.4 %copy-start.6 = (bf16[4,32,2,1536]{3,2,1,0:T(2,128)(2,1)S(1)}, bf16[4,32,2,1536]{3,2,1,0:T(2,128)(2,1)}, u32[]{:S(2)}) copy-start(bf16[4,32,2,1536]{3,2,1,0:T(2,128)(2,1)} %param.8) | copy-start | bytes 2359300
  3.0 0.9 copy-start.4
  3.9 1.1 %slice-start = ((bf16[4,64,1536]{2,1,0:T(8,128)(2,1)}), bf16[4,56,1536]{2,1,0:T(8,128)(2,1)S(1)}, s32[]{:S(2)}) async-start(bf16[4,64,1536]{2,1,0:T(8,128)(2,1)} %copy-done.4), calls=%async_computation | async-start | bytes 1376256 | tf_op jit(solution)/shard_map/jit(_roll_static)/slice | solution.py:171
  5.1 1.3 %copy-start.7 = (bf16[4,32,2,1536]{3,2,1,0:T(2,128)(2,1)S(1)}, bf16[4,32,2,1536]{3,2,1,0:T(2,128)(2,1)}, u32[]{:S(2)}) copy-start(bf16[4,32,2,1536]{3,2,1,0:T(2,128)(2,1)} %param.6) | copy-start | bytes 2359300
  5.3 5.0 %copy-start.1 = (bf16[2,4,64,1536]{3,2,1,0:T(8,128)(2,1)}, bf16[2,4,64,1536]{3,2,1,0:T(8,128)(2,1)S(1)}, u32[]{:S(2)}) copy-start(bf16[2,4,64,1536]{3,2,1,0:T(8,128)(2,1)S(1)} %pad_maximum_fusion.refs_4_.refs_6_) | copy-start | bytes 4718596
  5.3 2.3 %copy-start.2 = (bf16[4,32,2,1536]{3,2,1,0:T(2,128)(2,1)S(1)}, bf16[4,32,2,1536]{3,2,1,0:T(2,128)(2,1)}, u32[]{:S(2)}) copy-start(bf16[4,32,2,1536]{3,2,1,0:T(2,128)(2,1)} %param.10) | copy-start | bytes 2359300
  5.3 17.1 %collective-permute-start = (bf16[2,4,64,1536]{3,2,1,0:T(8,128)(2,1)S(1)}, bf16[2,4,64,1536]{3,2,1,0:T(8,128)(2,1)}, u32[]{:S(2)}, u32[]{:S(2)}) collective-permute-start(bf16[2,4,64,1536]{3,2,1,0:T(8,128)(2,1)S(1)} %pad_maximum_fusion.refs_4_.refs_6_), channel_id=1, source_target_pairs={{0,1},{1,0},{2,3},{3,2},{4,5},{5,4},{6,7},{7,6},{8,9},{9,8},{10,11... | collective-permute-start | bytes 4718600 | tf_op jit(solution)/shard_map/ppermute | solution.py:20
  8.8 1.4 %copy-start.3 = (bf16[1,4,64,1536]{3,2,1,0:T(8,128)(2,1)S(1)}, bf16[1,4,64,1536]{3,2,1,0:T(8,128)(2,1)}, u32[]{:S(2)}) copy-start(bf16[1,4,64,1536]{3,2,1,0:T(8,128)(2,1)} %stack_reshape.13) | copy-start | bytes 2359300
  10.1 6.1 %copy-start.9 = (f32[4,32,2,12]{1,2,3,0:T(2,128)S(1)}, f32[4,32,2,12]{1,2,3,0:T(2,128)}, u32[]{:S(2)}) copy-start(f32[4,32,2,12]{1,2,3,0:T(2,128)} %param.11) | copy-start | bytes 36868
  10.2 9.7 %copy-start = (bf16[2,4,64,1536]{3,2,1,0:T(8,128)(2,1)}, bf16[2,4,64,1536]{3,2,1,0:T(8,128)(2,1)S(1)}, u32[]{:S(2)}) copy-start(bf16[2,4,64,1536]{3,2,1,0:T(8,128)(2,1)S(1)} %constant_dynamic-update-slice_fusion.refs_0_.refs_1_.refs_2_) | copy-start | bytes 4718596
  10.2 37.0 %collective-permute-start.1 = (bf16[2,4,64,1536]{3,2,1,0:T(8,128)(2,1)S(1)}, bf16[2,4,64,1536]{3,2,1,0:T(8,128)(2,1)}, u32[]{:S(2)}, u32[]{:S(2)}) collective-permute-start(bf16[2,4,64,1536]{3,2,1,0:T(8,128)(2,1)S(1)} %constant_dynamic-update-slice_fusion.refs_0_.refs_1_.refs_2_), channel_id=1, source_target_pairs={{0,1},{1,0},{2,3},{3,2},{4,5},{5,4},{6,7},{7,6},{8,9},{9,8},{10,11... | collective-permute-start | bytes 4718600 | tf_op jit(solution)/shard_map/ppermute | solution.py:20
  10.3 37.7 %collective-permute-start.3 = (bf16[2,4,64,1536]{3,2,1,0:T(8,128)(2,1)S(1)}, bf16[2,4,64,1536]{3,2,1,0:T(8,128)(2,1)}, u32[]{:S(2)}, u32[]{:S(2)}) collective-permute-start(bf16[2,4,64,1536]{3,2,1,0:T(8,128)(2,1)S(1)} %pad_maximum_fusion.refs_4_.refs_6_), channel_id=1, source_target_pairs={{0,15},{1,2},{2,1},{3,4},{4,3},{5,6},{6,5},{7,8},{8,7},{9,10},{10,... | collective-permute-start | bytes 4718600 | tf_op jit(solution)/shard_map/ppermute | solution.py:20
  22.4 0.6 copy-start.8
  36.6 62.0 %collective-permute-start.5 = (f32[2,4,64,1536]{3,2,1,0:T(8,128)}, f32[2,4,64,1536]{3,2,1,0:T(8,128)}, u32[]{:S(2)}, u32[]{:S(2)}) collective-permute-start(f32[2,4,64,1536]{3,2,1,0:T(8,128)} %get-tuple-element.13), channel_id=1, source_target_pairs={{0,1},{1,0},{2,3},{3,2},{4,5},{5,4},{6,7},{7,6},{8,9},{9,8},{10,11... | collective-permute-start | bytes 9437192 | tf_op jit(solution)/shard_map/ppermute | solution.py:20
  40.2 5.4 %collective-permute-start.2 = (f32[2,12,4,1,64]{4,3,2,1,0:T(1,128)}, f32[2,12,4,1,64]{4,3,2,1,0:T(1,128)S(1)}, u32[]{:S(2)}, u32[]{:S(2)}) collective-permute-start(f32[2,12,4,1,64]{4,3,2,1,0:T(1,128)} %copy-done.8), channel_id=1, source_target_pairs={{0,1},{1,0},{2,3},{3,2},{4,5},{5,4},{6,7},{7,6},{8,9},{9,8},{10,11... | collective-permute-start | bytes 73736 | tf_op jit(solution)/shard_map/ppermute | solution.py:20
  61.5 3.6 %collective-permute-start.4 = (f32[4,64,1536]{2,1,0:T(8,128)}, f32[4,64,1536]{2,1,0:T(8,128)S(1)}, u32[]{:S(2)}, u32[]{:S(2)}) collective-permute-start(f32[4,64,1536]{2,1,0:T(8,128)} %get-tuple-element.11), channel_id=1, source_target_pairs={{0,1},{1,0},{2,3},{3,2},{4,5},{5,4},{6,7},{7,6},{8,9},{9,8},{10,11... | collective-permute-start | bytes 4718600 | tf_op jit(solution)/shard_map/ppermute | solution.py:20
  61.6 37.1 %collective-permute-start.6 = (bf16[2,4,64,1536]{3,2,1,0:T(8,128)(2,1)}, bf16[2,4,64,1536]{3,2,1,0:T(8,128)(2,1)}, u32[]{:S(2)}, u32[]{:S(2)}) collective-permute-start(bf16[2,4,64,1536]{3,2,1,0:T(8,128)(2,1)} %get-tuple-element.14), channel_id=1, source_target_pairs={{0,15},{1,2},{2,1},{3,4},{4,3},{5,6},{6,5},{7,8},{8,7},{9,10},{10,... | collective-permute-start | bytes 4718600 | tf_op jit(solution)/shard_map/ppermute | solution.py:20
  65.2 33.5 %copy-start.5 = (f32[2,4,64,1536]{3,2,1,0:T(8,128)S(1)}, f32[2,4,64,1536]{3,2,1,0:T(8,128)}, u32[]{:S(2)}) copy-start(f32[2,4,64,1536]{3,2,1,0:T(8,128)} %get-tuple-element.12) | copy-start | bytes 9437188

commit v12 on v11

--- a/solution.py
+++ b/solution.py
@@ -97,7 +97,7 @@
         heads = all_channels // HEAD_DIM
     channels = heads * HEAD_DIM
     nq, nk = len(queries), len(keys)
-    group = 2 if heads % 2 == 0 else 1
+    group = 4 if heads % 4 == 0 else (2 if heads % 2 == 0 else 1)
     kernel = functools.partial(
         window_kernel, nq=nq, nk=nk, tiles=tiles, tf=tf, mf=mf, narrow=narrow, group=group
     )

time: 105 us -> 105 us (level)
  no operation moved by 1% of the time
where the time goes in v12:
time: 105 us
  waiting for transfers between devices  35.5 us (34%)
  Pallas kernels  27 us (26%)
  local copies, waits for them, and re-layouts  22.3 us (21%)
  other arithmetic  10.6 us (10%)
  starting transfers between devices  8.32 us (8%)
    ppermute x7, waiting for transfers between devices, swap(): return lax.ppermute(block, 'sy', route)  35.5 us
    pallas_call x2, Pallas kernels, window_pass(): pl.pallas_call(kernel, grid=(heads // group,), in_specs=in_specs, out_spe...  27 us
    ppermute x7, starting transfers between devices, swap(): return lax.ppermute(block, 'sy', route)  8.32 us
    unnamed x23, local copies, waits for them, and re-layouts  3.65 us
    reshape x1, local copies, waits for them, and re-layouts, on_device(): outputs_fwd.reshape(rows, width, heads, HEAD_DIM)  3.24 us
    convert_element_type x1, other arithmetic, on_device(): dq = (dq_local + dq_mine + dq_back).astype(jnp.bfloat16)  3.23 us
    reshape x1, local copies, waits for them, and re-layouts, on_device(): grad_out.reshape(rows, width, heads, HEAD_DIM)  3.2 us
    add x1, other arithmetic, on_device(): part_own + back_partner + arrived.astype(jnp.float32)  3.2 us
  transfers between devices with their start and end apart: 7, of which 4 were waited for; matrix products, arithmetic and copies ran while one was open for 20% of the time, Pallas kernels for 26%

profile of v12, /device:TPU:1, one launch (start us, length us, event | category | flops | bytes accessed | tf_op | source)
XLA Modules:
  0.0 104.5 jit_solution(18372037584445027991)
XLA Ops:
  0.6 0.0 copy-start.6
  0.6 2.3 %reshape.33 = bf16[4,64,1536]{2,1,0:T(8,128)(2,1)S(1)} reshape(bf16[4,32,2,1536]{3,2,1,0:T(2,128)(2,1)} %param.7) | data formatting | bytes 1572864 | tf_op jit(solution)/shard_map/reshape | solution.py:171
  3.0 0.0 copy-start.4
  3.0 0.0 copy-done.6
  3.0 0.3 reshape.34
  3.3 0.5 copy-done.4
  3.9 0.0 slice-start
  3.9 1.0 slice-done
  5.0 0.1 maximum_bitcast_fusion
  5.1 0.0 copy-start.7
  5.1 0.1 pad_maximum_fusion.refs_4_.refs_6_
  5.3 0.0 copy-start.1
  5.3 0.0 copy-start.2
  5.3 0.1 collective-permute-start
  5.4 1.0 copy-done.7
  6.4 1.2 %stack_reshape.12 = bf16[1,4,64,1536]{3,2,1,0:T(8,128)(2,1)} reshape(bf16[4,32,2,1536]{3,2,1,0:T(2,128)(2,1)S(1)} %copy-done.7) | data formatting | bytes 1572864 | tf_op jit(solution)/shard_map/stack;reshape | solution.py:159
  7.6 0.0 copy-done.2
  7.6 1.2 %stack_reshape.13 = bf16[1,4,64,1536]{3,2,1,0:T(8,128)(2,1)} reshape(bf16[4,32,2,1536]{3,2,1,0:T(2,128)(2,1)S(1)} %copy-done.2) | data formatting | bytes 1572864 | tf_op jit(solution)/shard_map/stack;reshape | solution.py:159
  8.8 0.0 copy-start.3
  8.8 1.3 %constant_dynamic-update-slice_fusion.1 = bf16[2,4,64,1536]{3,2,1,0:T(8,128)(2,1)S(1)} fusion(bf16[1,4,64,1536]{3,2,1,0:T(8,128)(2,1)} %stack_reshape.12), kind=kLoop, calls=%fused_computation.10 | loop fusion | bytes 1572864
  10.0 0.1 copy-done.3
  10.1 0.0 copy-start.9
  10.1 0.1 constant_dynamic-update-slice_fusion.refs_0_.refs_1_.refs_2_
  10.2 0.0 copy-start
  10.2 0.1 collective-permute-start.1
  10.3 0.0 copy-done.1
  10.3 2.7 %collective-permute-start.3 = (bf16[2,4,64,1536]{3,2,1,0:T(8,128)(2,1)S(1)}, bf16[2,4,64,1536]{3,2,1,0:T(8,128)(2,1)}, u32[]{:S(2)}, u32[]{:S(2)}) collective-permute-start(bf16[2,4,64,1536]{3,2,1,0:T(8,128)(2,1)S(1)} %pad_maximum_fusion.refs_4_.refs_6_), channel_id=1, source_target_pairs={{0,15},{1,2},{2,1},{3,4},{4,3},{5,6},{6,5},{7,8},{8,7},{9,10},{10,... | collective-permute-start | bytes 4718600 | tf_op jit(solution)/shard_map/ppermute | solution.py:20
  13.0 3.2 %reshape.30 = bf16[4,64,12,128]{3,2,1,0:T(8,128)(2,1)} reshape(bf16[4,32,2,1536]{3,2,1,0:T(2,128)(2,1)} %param.10) | data formatting | bytes 1572864 | tf_op jit(solution)/shard_map/reshape | solution.py:162
  16.2 0.0 copy-done.9
  16.2 0.1 copy.9
  16.3 0.2 copy.10
  16.5 0.1 stack_reshape.14
  16.6 3.2 %reshape.31 = bf16[4,64,12,128]{3,2,1,0:T(8,128)(2,1)} reshape(bf16[4,32,2,1536]{3,2,1,0:T(2,128)(2,1)} %param.9) | data formatting | bytes 1572864 | tf_op jit(solution)/shard_map/reshape | solution.py:163
  19.9 0.0 copy-done
  19.9 2.2 %fusion = f32[4,64,12]{2,1,0:T(8,128)S(1)} fusion(bf16[4,64,12,128]{3,2,1,0:T(8,128)(2,1)} %reshape.30, bf16[4,64,12,128]{3,2,1,0:T(8,128)(2,1)} %reshape.31), kind=kLoop, calls=%fused_computation.3 | loop fusion | flops 1569792 | bytes 1585152
  22.0 0.2 copy.19
  22.2 0.1 stack_reshape.15
  22.4 0.0 copy-start.8
  22.4 0.0 collective-permute-done.refs_5_.refs_7_
  22.4 0.6 copy-done.8
  23.0 13.6 %shard_map.85 = (f32[4,64,1536]{2,1,0:T(8,128)}, f32[2,4,64,1536]{3,2,1,0:T(8,128)}, f32[2,4,64,1536]{3,2,1,0:T(8,128)}) custom-call(bf16[2,4,64,1536]{3,2,1,0:T(8,128)(2,1)} %copy-done, bf16[2,4,64,1536]{3,2,1,0:T(8,128)(2,1)} %copy-done, f32[2,12,4,1,64]{4,3,2,1,0:T(1,128)} %copy-done.8, f32[2,12,4,1,64]{4,3,2,1,0:T(1,128)} %copy-done.8, ...), custom_call_target="tpu_custom_call" | custom-call | flops 1006632960 | bytes 12582912 | tf_op jit(solution)/shard_map/pallas_call | solution.py:133
  36.6 3.5 %collective-permute-start.5 = (f32[2,4,64,1536]{3,2,1,0:T(8,128)}, f32[2,4,64,1536]{3,2,1,0:T(8,128)}, u32[]{:S(2)}, u32[]{:S(2)}) collective-permute-start(f32[2,4,64,1536]{3,2,1,0:T(8,128)} %get-tuple-element.13), channel_id=1, source_target_pairs={{0,1},{1,0},{2,3},{3,2},{4,5},{5,4},{6,7},{7,6},{8,9},{9,8},{10,11... | collective-permute-start | bytes 9437192 | tf_op jit(solution)/shard_map/ppermute | solution.py:20
  40.1 0.1 collective-permute-start.2
  40.2 5.4 %collective-permute-done.2 = f32[2,12,4,1,64]{4,3,2,1,0:T(1,128)S(1)} collective-permute-done((f32[2,12,4,1,64]{4,3,2,1,0:T(1,128)}, f32[2,12,4,1,64]{4,3,2,1,0:T(1,128)S(1)}, u32[]{:S(2)}, u32[]{:S(2)}) %collective-permute-start.2) | collective-permute-done | bytes 24608 | tf_op jit(solution)/shard_map/ppermute | solution.py:20
  45.5 1.6 %pad_maximum_fusion.1.refs_4_.refs_5_ = f32[2,12,4,1,128]{4,3,2,1,0:T(1,128)} fusion(f32[2,12,4,1,64]{4,3,2,1,0:T(1,128)S(1)} %collective-permute-done.2, f32[2,12,4,1,64]{4,3,2,1,0:T(1,128)} %copy-done.8), kind=kLoop, calls=%fused_computation.8 | loop fusion | flops 12288 | bytes 98304 | tf_op jit(solution)/shard_map/concatenate | solution.py:185
  47.1 0.0 collective-permute-done.1.refs_1_.refs_3_
  47.1 0.9 collective-permute-done.3.refs_6_.refs_7_
  48.0 13.4 %shard_map.86 = (f32[4,64,1536]{2,1,0:T(8,128)}, f32[4,64,1536]{2,1,0:T(8,128)}, bf16[2,4,64,1536]{3,2,1,0:T(8,128)(2,1)}) custom-call(bf16[2,4,64,1536]{3,2,1,0:T(8,128)(2,1)} %copy-done, bf16[2,4,64,1536]{3,2,1,0:T(8,128)(2,1)} %collective-permute-done.1.refs_1_.refs_3_, bf16[2,4,64,1536]{3,2,1,0:T(8,128)(2,1)} %copy-done, ...), custom_call_target="tpu_custom_call" | custom-call | flops 1006632960 | bytes 11010048 | tf_op jit(solution)/shard_map/pallas_call | solution.py:133
  61.5 0.0 collective-permute-start.4
  61.5 1.8 %collective-permute-start.6 = (bf16[2,4,64,1536]{3,2,1,0:T(8,128)(2,1)}, bf16[2,4,64,1536]{3,2,1,0:T(8,128)(2,1)}, u32[]{:S(2)}, u32[]{:S(2)}) collective-permute-start(bf16[2,4,64,1536]{3,2,1,0:T(8,128)(2,1)} %get-tuple-element.14), channel_id=1, source_target_pairs={{0,15},{1,2},{2,1},{3,4},{4,3},{5,6},{6,5},{7,8},{8,7},{9,10},{10,... | collective-permute-start | bytes 4718600 | tf_op jit(solution)/shard_map/ppermute | solution.py:20
  63.3 1.8 %collective-permute-done.4 = f32[4,64,1536]{2,1,0:T(8,128)S(1)} collective-permute-done((f32[4,64,1536]{2,1,0:T(8,128)}, f32[4,64,1536]{2,1,0:T(8,128)S(1)}, u32[]{:S(2)}, u32[]{:S(2)}) %collective-permute-start.4) | collective-permute-done | bytes 1572896 | tf_op jit(solution)/shard_map/ppermute | solution.py:20
  65.1 0.0 copy-start.5
  65.1 3.2 %add_convert_fusion = bf16[4,64,1536]{2,1,0:T(8,128)(2,1)} fusion(f32[4,64,1536]{2,1,0:T(8,128)S(1)} %collective-permute-done.4, f32[4,64,1536]{2,1,0:T(8,128)} %get-tuple-element.9, f32[4,64,1536]{2,1,0:T(8,128)} %get-tuple-element.10), kind=kLoop, calls=%fused_computation.5 | loop fusion | flops 1179648 | bytes 5505024 | tf_op jit(solution)/shard_map/convert_element_type | solution.py:201
  68.3 2.8 %reshape.35 = bf16[4,32,2,1536]{3,2,1,0:T(2,128)(2,1)} reshape(bf16[4,64,1536]{2,1,0:T(8,128)(2,1)} %add_convert_fusion) | data formatting | bytes 1572864 | tf_op jit(solution)/shard_map/reshape | solution.py:205
  71.2 27.4 %collective-permute-done.6 = bf16[2,4,64,1536]{3,2,1,0:T(8,128)(2,1)} collective-permute-done((bf16[2,4,64,1536]{3,2,1,0:T(8,128)(2,1)}, bf16[2,4,64,1536]{3,2,1,0:T(8,128)(2,1)}, u32[]{:S(2)}, u32[]{:S(2)}) %collective-permute-start.6) | collective-permute-done | bytes 1572896 | tf_op jit(solution)/shard_map/ppermute | solution.py:20
  98.6 0.0 collective-permute-done.5
  98.6 0.0 copy-done.5
  98.6 3.2 %convert_add_fusion = bf16[2,4,64,1536]{3,2,1,0:T(8,128)(2,1)S(1)} fusion(bf16[2,4,64,1536]{3,2,1,0:T(8,128)(2,1)} %collective-permute-done.6, f32[2,4,64,1536]{3,2,1,0:T(8,128)S(1)} %copy-done.5, f32[2,4,64,1536]{3,2,1,0:T(8,128)} %collective-permute-done.5), kind=kLoop, calls=%fused_computation.1 | loop fusion | flops 3145728 | bytes 9437184 | tf_op jit(solution)/shard_map/add | solution.py:202
  101.8 0.1 slice.42
  101.9 0.1 maximum_convert_fusion
  102.0 0.1 fusion.1
  102.2 1.2 %convert_element_type.19 = bf16[4,32,2,1536]{3,2,1,0:T(2,128)(2,1)} reshape(bf16[1,4,64,1536]{3,2,1,0:T(8,128)(2,1)S(1)} %get-tuple-element.15) | data formatting | bytes 1572864 | tf_op jit(solution)/shard_map/convert_element_type | solution.py:204
  103.3 1.2 %convert_element_type.18 = bf16[4,32,2,1536]{3,2,1,0:T(2,128)(2,1)} reshape(bf16[1,4,64,1536]{3,2,1,0:T(8,128)(2,1)S(1)} %get-tuple-element.16) | data formatting | bytes 1572864 | tf_op jit(solution)/shard_map/convert_element_type | solution.py:203
  (6 shorter events, 0.1 us)
Async XLA Ops:
  0.6 2.4 %copy-start.6 = (bf16[4,32,2,1536]{3,2,1,0:T(2,128)(2,1)S(1)}, bf16[4,32,2,1536]{3,2,1,0:T(2,128)(2,1)}, u32[]{:S(2)}) copy-start(bf16[4,32,2,1536]{3,2,1,0:T(2,128)(2,1)} %param.8) | copy-start | bytes 2359300
  3.0 0.9 copy-start.4
  3.9 1.1 %slice-start = ((bf16[4,64,1536]{2,1,0:T(8,128)(2,1)}), bf16[4,56,1536]{2,1,0:T(8,128)(2,1)S(1)}, s32[]{:S(2)}) async-start(bf16[4,64,1536]{2,1,0:T(8,128)(2,1)} %copy-done.4), calls=%async_computation | async-start | bytes 1376256 | tf_op jit(solution)/shard_map/jit(_roll_static)/slice | solution.py:171
  5.1 1.3 %copy-start.7 = (bf16[4,32,2,1536]{3,2,1,0:T(2,128)(2,1)S(1)}, bf16[4,32,2,1536]{3,2,1,0:T(2,128)(2,1)}, u32[]{:S(2)}) copy-start(bf16[4,32,2,1536]{3,2,1,0:T(2,128)(2,1)} %param.6) | copy-start | bytes 2359300
  5.3 5.0 %copy-start.1 = (bf16[2,4,64,1536]{3,2,1,0:T(8,128)(2,1)}, bf16[2,4,64,1536]{3,2,1,0:T(8,128)(2,1)S(1)}, u32[]{:S(2)}) copy-start(bf16[2,4,64,1536]{3,2,1,0:T(8,128)(2,1)S(1)} %pad_maximum_fusion.refs_4_.refs_6_) | copy-start | bytes 4718596
  5.3 2.3 %copy-start.2 = (bf16[4,32,2,1536]{3,2,1,0:T(2,128)(2,1)S(1)}, bf16[4,32,2,1536]{3,2,1,0:T(2,128)(2,1)}, u32[]{:S(2)}) copy-start(bf16[4,32,2,1536]{3,2,1,0:T(2,128)(2,1)} %param.10) | copy-start | bytes 2359300
  5.3 17.1 %collective-permute-start = (bf16[2,4,64,1536]{3,2,1,0:T(8,128)(2,1)S(1)}, bf16[2,4,64,1536]{3,2,1,0:T(8,128)(2,1)}, u32[]{:S(2)}, u32[]{:S(2)}) collective-permute-start(bf16[2,4,64,1536]{3,2,1,0:T(8,128)(2,1)S(1)} %pad_maximum_fusion.refs_4_.refs_6_), channel_id=1, source_target_pairs={{0,1},{1,0},{2,3},{3,2},{4,5},{5,4},{6,7},{7,6},{8,9},{9,8},{10,11... | collective-permute-start | bytes 4718600 | tf_op jit(solution)/shard_map/ppermute | solution.py:20
  8.8 1.4 %copy-start.3 = (bf16[1,4,64,1536]{3,2,1,0:T(8,128)(2,1)S(1)}, bf16[1,4,64,1536]{3,2,1,0:T(8,128)(2,1)}, u32[]{:S(2)}) copy-start(bf16[1,4,64,1536]{3,2,1,0:T(8,128)(2,1)} %stack_reshape.13) | copy-start | bytes 2359300
  10.1 6.1 %copy-start.9 = (f32[4,32,2,12]{1,2,3,0:T(2,128)S(1)}, f32[4,32,2,12]{1,2,3,0:T(2,128)}, u32[]{:S(2)}) copy-start(f32[4,32,2,12]{1,2,3,0:T(2,128)} %param.11) | copy-start | bytes 36868
  10.2 9.7 %copy-start = (bf16[2,4,64,1536]{3,2,1,0:T(8,128)(2,1)}, bf16[2,4,64,1536]{3,2,1,0:T(8,128)(2,1)S(1)}, u32[]{:S(2)}) copy-start(bf16[2,4,64,1536]{3,2,1,0:T(8,128)(2,1)S(1)} %constant_dynamic-update-slice_fusion.refs_0_.refs_1_.refs_2_) | copy-start | bytes 4718596
  10.2 36.9 %collective-permute-start.1 = (bf16[2,4,64,1536]{3,2,1,0:T(8,128)(2,1)S(1)}, bf16[2,4,64,1536]{3,2,1,0:T(8,128)(2,1)}, u32[]{:S(2)}, u32[]{:S(2)}) collective-permute-start(bf16[2,4,64,1536]{3,2,1,0:T(8,128)(2,1)S(1)} %constant_dynamic-update-slice_fusion.refs_0_.refs_1_.refs_2_), channel_id=1, source_target_pairs={{0,1},{1,0},{2,3},{3,2},{4,5},{5,4},{6,7},{7,6},{8,9},{9,8},{10,11... | collective-permute-start | bytes 4718600 | tf_op jit(solution)/shard_map/ppermute | solution.py:20
  10.3 37.7 %collective-permute-start.3 = (bf16[2,4,64,1536]{3,2,1,0:T(8,128)(2,1)S(1)}, bf16[2,4,64,1536]{3,2,1,0:T(8,128)(2,1)}, u32[]{:S(2)}, u32[]{:S(2)}) collective-permute-start(bf16[2,4,64,1536]{3,2,1,0:T(8,128)(2,1)S(1)} %pad_maximum_fusion.refs_4_.refs_6_), channel_id=1, source_target_pairs={{0,15},{1,2},{2,1},{3,4},{4,3},{5,6},{6,5},{7,8},{8,7},{9,10},{10,... | collective-permute-start | bytes 4718600 | tf_op jit(solution)/shard_map/ppermute | solution.py:20
  22.4 0.6 copy-start.8
  36.6 62.0 %collective-permute-start.5 = (f32[2,4,64,1536]{3,2,1,0:T(8,128)}, f32[2,4,64,1536]{3,2,1,0:T(8,128)}, u32[]{:S(2)}, u32[]{:S(2)}) collective-permute-start(f32[2,4,64,1536]{3,2,1,0:T(8,128)} %get-tuple-element.13), channel_id=1, source_target_pairs={{0,1},{1,0},{2,3},{3,2},{4,5},{5,4},{6,7},{7,6},{8,9},{9,8},{10,11... | collective-permute-start | bytes 9437192 | tf_op jit(solution)/shard_map/ppermute | solution.py:20
  40.1 5.4 %collective-permute-start.2 = (f32[2,12,4,1,64]{4,3,2,1,0:T(1,128)}, f32[2,12,4,1,64]{4,3,2,1,0:T(1,128)S(1)}, u32[]{:S(2)}, u32[]{:S(2)}) collective-permute-start(f32[2,12,4,1,64]{4,3,2,1,0:T(1,128)} %copy-done.8), channel_id=1, source_target_pairs={{0,1},{1,0},{2,3},{3,2},{4,5},{5,4},{6,7},{7,6},{8,9},{9,8},{10,11... | collective-permute-start | bytes 73736 | tf_op jit(solution)/shard_map/ppermute | solution.py:20
  61.5 3.6 %collective-permute-start.4 = (f32[4,64,1536]{2,1,0:T(8,128)}, f32[4,64,1536]{2,1,0:T(8,128)S(1)}, u32[]{:S(2)}, u32[]{:S(2)}) collective-permute-start(f32[4,64,1536]{2,1,0:T(8,128)} %get-tuple-element.11), channel_id=1, source_target_pairs={{0,1},{1,0},{2,3},{3,2},{4,5},{5,4},{6,7},{7,6},{8,9},{9,8},{10,11... | collective-permute-start | bytes 4718600 | tf_op jit(solution)/shard_map/ppermute | solution.py:20
  61.5 37.1 %collective-permute-start.6 = (bf16[2,4,64,1536]{3,2,1,0:T(8,128)(2,1)}, bf16[2,4,64,1536]{3,2,1,0:T(8,128)(2,1)}, u32[]{:S(2)}, u32[]{:S(2)}) collective-permute-start(bf16[2,4,64,1536]{3,2,1,0:T(8,128)(2,1)} %get-tuple-element.14), channel_id=1, source_target_pairs={{0,15},{1,2},{2,1},{3,4},{4,3},{5,6},{6,5},{7,8},{8,7},{9,10},{10,... | collective-permute-start | bytes 4718600 | tf_op jit(solution)/shard_map/ppermute | solution.py:20
  65.1 33.5 %copy-start.5 = (f32[2,4,64,1536]{3,2,1,0:T(8,128)S(1)}, f32[2,4,64,1536]{3,2,1,0:T(8,128)}, u32[]{:S(2)}) copy-start(f32[2,4,64,1536]{3,2,1,0:T(8,128)} %get-tuple-element.12) | copy-start | bytes 9437188

commit v13 on v12

--- a/solution.py
+++ b/solution.py
@@ -82,8 +82,9 @@
             dq_ref[:, b * tf : (b + 1) * tf, lanes] = grad_q[source].astype(dq_ref.dtype)
         grad_k = grad_k.reshape(nk, rows, span, HEAD_DIM)
         grad_v = grad_v.reshape(nk, rows, span, HEAD_DIM)
+        stores = window_pieces((b * tf - mf) % width, span, width)
         for block, target in enumerate(targets):
-            for src, dst, size in pieces:
+            for src, dst, size in stores:
                 target[0, :, dst : dst + size, lanes] += grad_k[block, :, src : src + size, :]
                 target[1, :, dst : dst + size, lanes] += grad_v[block, :, src : src + size, :]
     if narrow:
@@ -199,7 +200,7 @@
     dq_back = jnp.concatenate(back_parts, axis=-1)
     arrived = jnp.concatenate(arrived_parts, axis=-1)
     dq = (dq_local + dq_mine + dq_back).astype(jnp.bfloat16)
-    total = jnp.roll(part_own + back_partner + arrived.astype(jnp.float32), -mf, axis=2)
+    total = part_own + back_partner + arrived.astype(jnp.float32)
     grad_keys = total[0].astype(jnp.bfloat16).reshape(rows, width_cells, frames, channels)
     grad_values = total[1].astype(jnp.bfloat16).reshape(rows, width_cells, frames, channels)
     grad_queries = dq.reshape(rows, width_cells, frames, channels)

time: 105 us -> 105 us (level)
    add x1 -> x0, other arithmetic: 3.2 us -> none  [on_device(): part_own + back_partner + arrived.astype(jnp.float32)]
    another operation x1, other arithmetic: 0.14 us -> 3.2 us
where the time goes in v13:
time: 105 us; the launch traced here: 104 us
  waiting for transfers between devices  35.5 us (34%)
  Pallas kernels  27 us (26%)
  local copies, waits for them, and re-layouts  22.2 us (21%)
  other arithmetic  10.5 us (10%)
  starting transfers between devices  8.32 us (8%)
    ppermute x7, waiting for transfers between devices, swap(): return lax.ppermute(block, 'sy', route)  35.5 us
    pallas_call x2, Pallas kernels, window_pass(): pl.pallas_call(kernel, grid=(heads // group,), in_specs=in_specs, out_spe...  27 us
    ppermute x7, starting transfers between devices, swap(): return lax.ppermute(block, 'sy', route)  8.32 us
    unnamed x23, local copies, waits for them, and re-layouts  3.65 us
    reshape x1, local copies, waits for them, and re-layouts, on_device(): outputs_fwd.reshape(rows, width, heads, HEAD_DIM)  3.24 us
    convert_element_type x1, other arithmetic, on_device(): dq = (dq_local + dq_mine + dq_back).astype(jnp.bfloat16)  3.23 us
    reshape x1, local copies, waits for them, and re-layouts, on_device(): grad_out.reshape(rows, width, heads, HEAD_DIM)  3.2 us
    another operation x1, other arithmetic  3.2 us
  transfers between devices with their start and end apart: 7, of which 4 were waited for; matrix products, arithmetic and copies ran while one was open for 20% of the time, Pallas kernels for 26%

profile of v13, /device:TPU:1, one launch (start us, length us, event | category | flops | bytes accessed | tf_op | source)
XLA Modules:
  0.0 104.2 jit_solution(13441526275913184628)
XLA Ops:
  0.6 0.0 copy-start.6
  0.6 2.3 %reshape.33 = bf16[4,64,1536]{2,1,0:T(8,128)(2,1)S(1)} reshape(bf16[4,32,2,1536]{3,2,1,0:T(2,128)(2,1)} %param.7) | data formatting | bytes 1572864 | tf_op jit(solution)/shard_map/reshape | solution.py:172
  3.0 0.0 copy-start.4
  3.0 0.0 copy-done.6
  3.0 0.3 reshape.34
  3.3 0.5 copy-done.4
  3.9 0.0 slice-start
  3.9 1.0 slice-done
  5.0 0.1 maximum_bitcast_fusion
  5.1 0.0 copy-start.7
  5.1 0.1 pad_maximum_fusion.refs_4_.refs_6_
  5.3 0.0 copy-start.1
  5.3 0.0 copy-start.2
  5.3 0.1 collective-permute-start
  5.4 1.0 copy-done.7
  6.4 1.2 %stack_reshape.12 = bf16[1,4,64,1536]{3,2,1,0:T(8,128)(2,1)} reshape(bf16[4,32,2,1536]{3,2,1,0:T(2,128)(2,1)S(1)} %copy-done.7) | data formatting | bytes 1572864 | tf_op jit(solution)/shard_map/stack;reshape | solution.py:160
  7.6 0.0 copy-done.2
  7.6 1.2 %stack_reshape.13 = bf16[1,4,64,1536]{3,2,1,0:T(8,128)(2,1)} reshape(bf16[4,32,2,1536]{3,2,1,0:T(2,128)(2,1)S(1)} %copy-done.2) | data formatting | bytes 1572864 | tf_op jit(solution)/shard_map/stack;reshape | solution.py:160
  8.8 0.0 copy-start.3
  8.8 1.3 %constant_dynamic-update-slice_fusion.1 = bf16[2,4,64,1536]{3,2,1,0:T(8,128)(2,1)S(1)} fusion(bf16[1,4,64,1536]{3,2,1,0:T(8,128)(2,1)} %stack_reshape.12), kind=kLoop, calls=%fused_computation.9 | loop fusion | bytes 1572864
  10.0 0.1 copy-done.3
  10.1 0.0 copy-start.9
  10.1 0.1 constant_dynamic-update-slice_fusion.refs_0_.refs_1_.refs_2_
  10.2 0.0 copy-start
  10.2 0.1 collective-permute-start.1
  10.3 0.0 copy-done.1
  10.3 2.7 %collective-permute-start.3 = (bf16[2,4,64,1536]{3,2,1,0:T(8,128)(2,1)S(1)}, bf16[2,4,64,1536]{3,2,1,0:T(8,128)(2,1)}, u32[]{:S(2)}, u32[]{:S(2)}) collective-permute-start(bf16[2,4,64,1536]{3,2,1,0:T(8,128)(2,1)S(1)} %pad_maximum_fusion.refs_4_.refs_6_), channel_id=1, source_target_pairs={{0,15},{1,2},{2,1},{3,4},{4,3},{5,6},{6,5},{7,8},{8,7},{9,10},{10,... | collective-permute-start | bytes 4718600 | tf_op jit(solution)/shard_map/ppermute | solution.py:20
  13.0 3.2 %reshape.30 = bf16[4,64,12,128]{3,2,1,0:T(8,128)(2,1)} reshape(bf16[4,32,2,1536]{3,2,1,0:T(2,128)(2,1)} %param.10) | data formatting | bytes 1572864 | tf_op jit(solution)/shard_map/reshape | solution.py:163
  16.2 0.0 copy-done.9
  16.2 0.1 copy.9
  16.3 0.2 copy.10
  16.5 0.1 stack_reshape.14
  16.6 3.2 %reshape.31 = bf16[4,64,12,128]{3,2,1,0:T(8,128)(2,1)} reshape(bf16[4,32,2,1536]{3,2,1,0:T(2,128)(2,1)} %param.9) | data formatting | bytes 1572864 | tf_op jit(solution)/shard_map/reshape | solution.py:164
  19.9 0.0 copy-done
  19.9 2.2 %fusion = f32[4,64,12]{2,1,0:T(8,128)S(1)} fusion(bf16[4,64,12,128]{3,2,1,0:T(8,128)(2,1)} %reshape.30, bf16[4,64,12,128]{3,2,1,0:T(8,128)(2,1)} %reshape.31), kind=kLoop, calls=%fused_computation.2 | loop fusion | flops 1569792 | bytes 1585152
  22.0 0.2 copy.19
  22.2 0.1 stack_reshape.15
  22.4 0.0 copy-start.8
  22.4 0.0 collective-permute-done.refs_5_.refs_7_
  22.4 0.6 copy-done.8
  23.0 13.6 %shard_map.85 = (f32[4,64,1536]{2,1,0:T(8,128)}, f32[2,4,64,1536]{3,2,1,0:T(8,128)}, f32[2,4,64,1536]{3,2,1,0:T(8,128)}) custom-call(bf16[2,4,64,1536]{3,2,1,0:T(8,128)(2,1)} %copy-done, bf16[2,4,64,1536]{3,2,1,0:T(8,128)(2,1)} %copy-done, f32[2,12,4,1,64]{4,3,2,1,0:T(1,128)} %copy-done.8, f32[2,12,4,1,64]{4,3,2,1,0:T(1,128)} %copy-done.8, ...), custom_call_target="tpu_custom_call" | custom-call | flops 1006632960 | bytes 12582912 | tf_op jit(solution)/shard_map/pallas_call | solution.py:134
  36.6 3.5 %collective-permute-start.5 = (f32[2,4,64,1536]{3,2,1,0:T(8,128)}, f32[2,4,64,1536]{3,2,1,0:T(8,128)}, u32[]{:S(2)}, u32[]{:S(2)}) collective-permute-start(f32[2,4,64,1536]{3,2,1,0:T(8,128)} %get-tuple-element.13), channel_id=1, source_target_pairs={{0,1},{1,0},{2,3},{3,2},{4,5},{5,4},{6,7},{7,6},{8,9},{9,8},{10,11... | collective-permute-start | bytes 9437192 | tf_op jit(solution)/shard_map/ppermute | solution.py:20
  40.1 0.1 collective-permute-start.2
  40.2 5.4 %collective-permute-done.2 = f32[2,12,4,1,64]{4,3,2,1,0:T(1,128)S(1)} collective-permute-done((f32[2,12,4,1,64]{4,3,2,1,0:T(1,128)}, f32[2,12,4,1,64]{4,3,2,1,0:T(1,128)S(1)}, u32[]{:S(2)}, u32[]{:S(2)}) %collective-permute-start.2) | collective-permute-done | bytes 24608 | tf_op jit(solution)/shard_map/ppermute | solution.py:20
  45.5 1.6 %pad_maximum_fusion.1.refs_4_.refs_5_ = f32[2,12,4,1,128]{4,3,2,1,0:T(1,128)} fusion(f32[2,12,4,1,64]{4,3,2,1,0:T(1,128)S(1)} %collective-permute-done.2, f32[2,12,4,1,64]{4,3,2,1,0:T(1,128)} %copy-done.8), kind=kLoop, calls=%fused_computation.7 | loop fusion | flops 12288 | bytes 98304 | tf_op jit(solution)/shard_map/concatenate | solution.py:186
  47.1 0.0 collective-permute-done.1.refs_1_.refs_3_
  47.1 0.9 collective-permute-done.3.refs_6_.refs_7_
  48.0 13.4 %shard_map.86 = (f32[4,64,1536]{2,1,0:T(8,128)}, f32[4,64,1536]{2,1,0:T(8,128)}, bf16[2,4,64,1536]{3,2,1,0:T(8,128)(2,1)}) custom-call(bf16[2,4,64,1536]{3,2,1,0:T(8,128)(2,1)} %copy-done, bf16[2,4,64,1536]{3,2,1,0:T(8,128)(2,1)} %collective-permute-done.1.refs_1_.refs_3_, bf16[2,4,64,1536]{3,2,1,0:T(8,128)(2,1)} %copy-done, ...), custom_call_target="tpu_custom_call" | custom-call | flops 1006632960 | bytes 11010048 | tf_op jit(solution)/shard_map/pallas_call | solution.py:134
  61.5 0.0 collective-permute-start.4
  61.5 1.8 %collective-permute-start.6 = (bf16[2,4,64,1536]{3,2,1,0:T(8,128)(2,1)}, bf16[2,4,64,1536]{3,2,1,0:T(8,128)(2,1)}, u32[]{:S(2)}, u32[]{:S(2)}) collective-permute-start(bf16[2,4,64,1536]{3,2,1,0:T(8,128)(2,1)} %get-tuple-element.14), channel_id=1, source_target_pairs={{0,15},{1,2},{2,1},{3,4},{4,3},{5,6},{6,5},{7,8},{8,7},{9,10},{10,... | collective-permute-start | bytes 4718600 | tf_op jit(solution)/shard_map/ppermute | solution.py:20
  63.3 1.8 %collective-permute-done.4 = f32[4,64,1536]{2,1,0:T(8,128)S(1)} collective-permute-done((f32[4,64,1536]{2,1,0:T(8,128)}, f32[4,64,1536]{2,1,0:T(8,128)S(1)}, u32[]{:S(2)}, u32[]{:S(2)}) %collective-permute-start.4) | collective-permute-done | bytes 1572896 | tf_op jit(solution)/shard_map/ppermute | solution.py:20
  65.1 0.0 copy-start.5
  65.1 3.2 %add_convert_fusion.1 = bf16[4,64,1536]{2,1,0:T(8,128)(2,1)} fusion(f32[4,64,1536]{2,1,0:T(8,128)S(1)} %collective-permute-done.4, f32[4,64,1536]{2,1,0:T(8,128)} %get-tuple-element.9, f32[4,64,1536]{2,1,0:T(8,128)} %get-tuple-element.10), kind=kLoop, calls=%fused_computation.4 | loop fusion | flops 1179648 | bytes 5505024 | tf_op jit(solution)/shard_map/convert_element_type | solution.py:202
  68.3 2.8 %reshape.35 = bf16[4,32,2,1536]{3,2,1,0:T(2,128)(2,1)} reshape(bf16[4,64,1536]{2,1,0:T(8,128)(2,1)} %add_convert_fusion.1) | data formatting | bytes 1572864 | tf_op jit(solution)/shard_map/reshape | solution.py:206
  71.2 27.4 %collective-permute-done.6 = bf16[2,4,64,1536]{3,2,1,0:T(8,128)(2,1)} collective-permute-done((bf16[2,4,64,1536]{3,2,1,0:T(8,128)(2,1)}, bf16[2,4,64,1536]{3,2,1,0:T(8,128)(2,1)}, u32[]{:S(2)}, u32[]{:S(2)}) %collective-permute-start.6) | collective-permute-done | bytes 1572896 | tf_op jit(solution)/shard_map/ppermute | solution.py:20
  98.6 0.0 collective-permute-done.5
  98.6 0.0 copy-done.5
  98.6 3.2 %add_convert_fusion = bf16[2,4,64,1536]{3,2,1,0:T(8,128)(2,1)S(1)} fusion(bf16[2,4,64,1536]{3,2,1,0:T(8,128)(2,1)} %collective-permute-done.6, f32[2,4,64,1536]{3,2,1,0:T(8,128)S(1)} %copy-done.5, f32[2,4,64,1536]{3,2,1,0:T(8,128)} %collective-permute-done.5), kind=kLoop, calls=%fused_computation | loop fusion | flops 3145728 | bytes 9437184 | tf_op jit(solution)/shard_map/convert.1
  101.8 0.1 fusion.1
  101.9 1.2 %convert_element_type.19 = bf16[4,32,2,1536]{3,2,1,0:T(2,128)(2,1)} reshape(bf16[1,4,64,1536]{3,2,1,0:T(8,128)(2,1)S(1)} %get-tuple-element.15) | data formatting | bytes 1572864 | tf_op jit(solution)/shard_map/convert_element_type | solution.py:205
  103.0 1.2 %convert_element_type.18 = bf16[4,32,2,1536]{3,2,1,0:T(2,128)(2,1)} reshape(bf16[1,4,64,1536]{3,2,1,0:T(8,128)(2,1)S(1)} %get-tuple-element.16) | data formatting | bytes 1572864 | tf_op jit(solution)/shard_map/convert_element_type | solution.py:204
  (5 shorter events, 0.1 us)
Async XLA Ops:
  0.6 2.4 %copy-start.6 = (bf16[4,32,2,1536]{3,2,1,0:T(2,128)(2,1)S(1)}, bf16[4,32,2,1536]{3,2,1,0:T(2,128)(2,1)}, u32[]{:S(2)}) copy-start(bf16[4,32,2,1536]{3,2,1,0:T(2,128)(2,1)} %param.8) | copy-start | bytes 2359300
  3.0 0.9 copy-start.4
  3.9 1.1 %slice-start = ((bf16[4,64,1536]{2,1,0:T(8,128)(2,1)}), bf16[4,56,1536]{2,1,0:T(8,128)(2,1)S(1)}, s32[]{:S(2)}) async-start(bf16[4,64,1536]{2,1,0:T(8,128)(2,1)} %copy-done.4), calls=%async_computation | async-start | bytes 1376256 | tf_op jit(solution)/shard_map/jit(_roll_static)/slice | solution.py:172
  5.1 1.3 %copy-start.7 = (bf16[4,32,2,1536]{3,2,1,0:T(2,128)(2,1)S(1)}, bf16[4,32,2,1536]{3,2,1,0:T(2,128)(2,1)}, u32[]{:S(2)}) copy-start(bf16[4,32,2,1536]{3,2,1,0:T(2,128)(2,1)} %param.6) | copy-start | bytes 2359300
  5.3 5.0 %copy-start.1 = (bf16[2,4,64,1536]{3,2,1,0:T(8,128)(2,1)}, bf16[2,4,64,1536]{3,2,1,0:T(8,128)(2,1)S(1)}, u32[]{:S(2)}) copy-start(bf16[2,4,64,1536]{3,2,1,0:T(8,128)(2,1)S(1)} %pad_maximum_fusion.refs_4_.refs_6_) | copy-start | bytes 4718596
  5.3 2.3 %copy-start.2 = (bf16[4,32,2,1536]{3,2,1,0:T(2,128)(2,1)S(1)}, bf16[4,32,2,1536]{3,2,1,0:T(2,128)(2,1)}, u32[]{:S(2)}) copy-start(bf16[4,32,2,1536]{3,2,1,0:T(2,128)(2,1)} %param.10) | copy-start | bytes 2359300
  5.3 17.1 %collective-permute-start = (bf16[2,4,64,1536]{3,2,1,0:T(8,128)(2,1)S(1)}, bf16[2,4,64,1536]{3,2,1,0:T(8,128)(2,1)}, u32[]{:S(2)}, u32[]{:S(2)}) collective-permute-start(bf16[2,4,64,1536]{3,2,1,0:T(8,128)(2,1)S(1)} %pad_maximum_fusion.refs_4_.refs_6_), channel_id=1, source_target_pairs={{0,1},{1,0},{2,3},{3,2},{4,5},{5,4},{6,7},{7,6},{8,9},{9,8},{10,11... | collective-permute-start | bytes 4718600 | tf_op jit(solution)/shard_map/ppermute | solution.py:20
  8.8 1.4 %copy-start.3 = (bf16[1,4,64,1536]{3,2,1,0:T(8,128)(2,1)S(1)}, bf16[1,4,64,1536]{3,2,1,0:T(8,128)(2,1)}, u32[]{:S(2)}) copy-start(bf16[1,4,64,1536]{3,2,1,0:T(8,128)(2,1)} %stack_reshape.13) | copy-start | bytes 2359300
  10.1 6.1 %copy-start.9 = (f32[4,32,2,12]{1,2,3,0:T(2,128)S(1)}, f32[4,32,2,12]{1,2,3,0:T(2,128)}, u32[]{:S(2)}) copy-start(f32[4,32,2,12]{1,2,3,0:T(2,128)} %param.11) | copy-start | bytes 36868
  10.2 9.7 %copy-start = (bf16[2,4,64,1536]{3,2,1,0:T(8,128)(2,1)}, bf16[2,4,64,1536]{3,2,1,0:T(8,128)(2,1)S(1)}, u32[]{:S(2)}) copy-start(bf16[2,4,64,1536]{3,2,1,0:T(8,128)(2,1)S(1)} %constant_dynamic-update-slice_fusion.refs_0_.refs_1_.refs_2_) | copy-start | bytes 4718596
  10.2 36.9 %collective-permute-start.1 = (bf16[2,4,64,1536]{3,2,1,0:T(8,128)(2,1)S(1)}, bf16[2,4,64,1536]{3,2,1,0:T(8,128)(2,1)}, u32[]{:S(2)}, u32[]{:S(2)}) collective-permute-start(bf16[2,4,64,1536]{3,2,1,0:T(8,128)(2,1)S(1)} %constant_dynamic-update-slice_fusion.refs_0_.refs_1_.refs_2_), channel_id=1, source_target_pairs={{0,1},{1,0},{2,3},{3,2},{4,5},{5,4},{6,7},{7,6},{8,9},{9,8},{10,11... | collective-permute-start | bytes 4718600 | tf_op jit(solution)/shard_map/ppermute | solution.py:20
  10.3 37.7 %collective-permute-start.3 = (bf16[2,4,64,1536]{3,2,1,0:T(8,128)(2,1)S(1)}, bf16[2,4,64,1536]{3,2,1,0:T(8,128)(2,1)}, u32[]{:S(2)}, u32[]{:S(2)}) collective-permute-start(bf16[2,4,64,1536]{3,2,1,0:T(8,128)(2,1)S(1)} %pad_maximum_fusion.refs_4_.refs_6_), channel_id=1, source_target_pairs={{0,15},{1,2},{2,1},{3,4},{4,3},{5,6},{6,5},{7,8},{8,7},{9,10},{10,... | collective-permute-start | bytes 4718600 | tf_op jit(solution)/shard_map/ppermute | solution.py:20
  22.4 0.6 copy-start.8
  36.6 62.0 %collective-permute-start.5 = (f32[2,4,64,1536]{3,2,1,0:T(8,128)}, f32[2,4,64,1536]{3,2,1,0:T(8,128)}, u32[]{:S(2)}, u32[]{:S(2)}) collective-permute-start(f32[2,4,64,1536]{3,2,1,0:T(8,128)} %get-tuple-element.13), channel_id=1, source_target_pairs={{0,1},{1,0},{2,3},{3,2},{4,5},{5,4},{6,7},{7,6},{8,9},{9,8},{10,11... | collective-permute-start | bytes 9437192 | tf_op jit(solution)/shard_map/ppermute | solution.py:20
  40.1 5.4 %collective-permute-start.2 = (f32[2,12,4,1,64]{4,3,2,1,0:T(1,128)}, f32[2,12,4,1,64]{4,3,2,1,0:T(1,128)S(1)}, u32[]{:S(2)}, u32[]{:S(2)}) collective-permute-start(f32[2,12,4,1,64]{4,3,2,1,0:T(1,128)} %copy-done.8), channel_id=1, source_target_pairs={{0,1},{1,0},{2,3},{3,2},{4,5},{5,4},{6,7},{7,6},{8,9},{9,8},{10,11... | collective-permute-start | bytes 73736 | tf_op jit(solution)/shard_map/ppermute | solution.py:20
  61.5 3.6 %collective-permute-start.4 = (f32[4,64,1536]{2,1,0:T(8,128)}, f32[4,64,1536]{2,1,0:T(8,128)S(1)}, u32[]{:S(2)}, u32[]{:S(2)}) collective-permute-start(f32[4,64,1536]{2,1,0:T(8,128)} %get-tuple-element.11), channel_id=1, source_target_pairs={{0,1},{1,0},{2,3},{3,2},{4,5},{5,4},{6,7},{7,6},{8,9},{9,8},{10,11... | collective-permute-start | bytes 4718600 | tf_op jit(solution)/shard_map/ppermute | solution.py:20
  61.5 37.1 %collective-permute-start.6 = (bf16[2,4,64,1536]{3,2,1,0:T(8,128)(2,1)}, bf16[2,4,64,1536]{3,2,1,0:T(8,128)(2,1)}, u32[]{:S(2)}, u32[]{:S(2)}) collective-permute-start(bf16[2,4,64,1536]{3,2,1,0:T(8,128)(2,1)} %get-tuple-element.14), channel_id=1, source_target_pairs={{0,15},{1,2},{2,1},{3,4},{4,3},{5,6},{6,5},{7,8},{8,7},{9,10},{10,... | collective-permute-start | bytes 4718600 | tf_op jit(solution)/shard_map/ppermute | solution.py:20
  65.1 33.5 %copy-start.5 = (f32[2,4,64,1536]{3,2,1,0:T(8,128)S(1)}, f32[2,4,64,1536]{3,2,1,0:T(8,128)}, u32[]{:S(2)}) copy-start(f32[2,4,64,1536]{3,2,1,0:T(8,128)} %get-tuple-element.12) | copy-start | bytes 9437188

commit v14 on v13

--- a/solution.py
+++ b/solution.py
@@ -64,7 +64,7 @@
 
     for j, b in [(j, b) for j in range(group) for b in range(tiles)]:
         lanes = slice(j * HEAD_DIM, (j + 1) * HEAD_DIM)
-        pieces = window_pieces(b * tf, span, width)
+        pieces = window_pieces((b * tf - mf) % width, span, width)
         kw = window([ref.at[:, :, lanes] for ref in k_refs], pieces)
         vw = window([ref.at[:, :, lanes] for ref in v_refs], pieces)
         qb = query_rows([ref.at[:, :, lanes] for ref in q_refs], b)
@@ -169,8 +169,8 @@
     )
     kv_own = jnp.stack(
         [
-            jnp.roll(key_vecs.reshape(rows, width, channels), mf, axis=1),
-            jnp.roll(value_vecs.reshape(rows, width, channels), mf, axis=1),
+            key_vecs.reshape(rows, width, channels),
+            value_vecs.reshape(rows, width, channels),
         ]
     )
     kv_cross = swap(kv_own, chip_neighbour)

time: 105 us -> 106 us (level)
  waiting for transfers between devices: 35.5 us -> 38 us
    another operation x0 -> x3, local copies, waits for them, and re-layouts: none -> 4.6 us  [on_device(): jnp.stack([key_vecs.reshape(rows, width, channels), value_vecs.reshape(ro...]
    reshape x2 -> x0, local copies, waits for them, and re-layouts: 2.64 us -> none  [the longest x1 2.34 us: on_device(): key_vecs.reshape(rows, width, channels)]
    ppermute x7, waiting for transfers between devices: 35.5 us -> 38 us  [swap(): return lax.ppermute(block, 'sy', route)]
    another operation x3, local copies, waits for them, and re-layouts: 2.4 us -> 4.78 us  [on_device(): jnp.stack([queries.reshape(rows, width, channels), grad_out.reshape(rows,...]
    reshape x1, local copies, waits for them, and re-layouts: 2.84 us -> 1.17 us  [on_device(): grad_queries = dq.reshape(rows, width_cells, frames, channels)]
    unnamed x23 -> x16, local copies, waits for them, and re-layouts: 3.65 us -> 2.18 us
    slice x5 -> x0, local copies, waits for them, and re-layouts: 1.1 us -> none  [the longest x3 1.05 us: on_device(): jnp.roll(key_vecs.reshape(rows, width, channels), mf, axis=1)]
    another operation x3 -> x1, other arithmetic: 3.48 us -> 3.68 us
  transfers between devices with their start and end apart: 7 -> 7, of which waited for: 4 -> 4; matrix products, arithmetic and copies ran while one was open for 20% -> 19% of each run, Pallas kernels for 26% -> 26%
where the time goes in v14:
time: 106 us
  waiting for transfers between devices  38 us (36%)
  Pallas kernels  27.1 us (26%)
  local copies, waits for them, and re-layouts  22.3 us (21%)
  other arithmetic  9.63 us (9%)
  starting transfers between devices  8.32 us (8%)
    ppermute x7, waiting for transfers between devices, swap(): return lax.ppermute(block, 'sy', route)  38 us
    pallas_call x2, Pallas kernels, window_pass(): pl.pallas_call(kernel, grid=(heads // group,), in_specs=in_specs, out_spe...  27.1 us
    ppermute x7, starting transfers between devices, swap(): return lax.ppermute(block, 'sy', route)  8.32 us
    another operation x3, local copies, waits for them, and re-layouts, on_device(): jnp.stack([queries.reshape(rows, width, channels), grad_out.reshape(rows,...  4.78 us
    another operation x3, local copies, waits for them, and re-layouts, on_device(): jnp.stack([key_vecs.reshape(rows, width, channels), value_vecs.reshape(ro...  4.6 us
    another operation x1, other arithmetic  3.68 us
    reshape x1, local copies, waits for them, and re-layouts, on_device(): outputs_fwd.reshape(rows, width, heads, HEAD_DIM)  3.22 us
    reshape x1, local copies, waits for them, and re-layouts, on_device(): grad_out.reshape(rows, width, heads, HEAD_DIM)  3.2 us
  transfers between devices with their start and end apart: 7, of which 4 were waited for; matrix products, arithmetic and copies ran while one was open for 19% of the time, Pallas kernels for 26%

profile of v14, /device:TPU:1, one launch (start us, length us, event | category | flops | bytes accessed | tf_op | source)
XLA Modules:
  0.0 106.1 jit_solution(17502220776695052989)
XLA Ops:
  0.6 2.3 %stack_reshape.22 = bf16[1,4,64,1536]{3,2,1,0:T(8,128)(2,1)S(1)} reshape(bf16[4,32,2,1536]{3,2,1,0:T(2,128)(2,1)} %param.7) | data formatting | bytes 1572864 | tf_op jit(solution)/shard_map/stack;reshape | solution.py:170
  2.9 0.1 constant_dynamic-update-slice_fusion.5
  3.0 2.3 %stack_reshape.23 = bf16[1,4,64,1536]{3,2,1,0:T(8,128)(2,1)S(1)} reshape(bf16[4,32,2,1536]{3,2,1,0:T(2,128)(2,1)} %param.8) | data formatting | bytes 1572864 | tf_op jit(solution)/shard_map/stack;reshape | solution.py:170
  5.3 0.0 copy-start.2
  5.3 0.1 constant_dynamic-update-slice_fusion.4.refs_4_.refs_6_
  5.3 0.0 copy-start.1
  5.3 0.1 collective-permute-start
  5.5 3.6 %stack_reshape.18 = bf16[1,4,64,1536]{3,2,1,0:T(8,128)(2,1)} reshape(bf16[4,32,2,1536]{3,2,1,0:T(2,128)(2,1)} %param.6) | data formatting | bytes 1572864 | tf_op jit(solution)/shard_map/stack;reshape | solution.py:160
  9.0 0.0 copy-done.2
  9.0 1.2 %stack_reshape.19 = bf16[1,4,64,1536]{3,2,1,0:T(8,128)(2,1)} reshape(bf16[4,32,2,1536]{3,2,1,0:T(2,128)(2,1)S(1)} %copy-done.2) | data formatting | bytes 1572864 | tf_op jit(solution)/shard_map/stack;reshape | solution.py:160
  10.2 0.0 copy-start.3
  10.2 1.3 %constant_dynamic-update-slice_fusion.1 = bf16[2,4,64,1536]{3,2,1,0:T(8,128)(2,1)S(1)} fusion(bf16[1,4,64,1536]{3,2,1,0:T(8,128)(2,1)} %stack_reshape.18), kind=kLoop, calls=%fused_computation.6 | loop fusion | bytes 1572864
  11.5 0.1 copy-done.3
  11.6 0.0 copy-start.5
  11.6 0.1 constant_dynamic-update-slice_fusion.refs_0_.refs_1_.refs_2_
  11.6 0.0 copy-start
  11.6 0.1 collective-permute-start.1
  11.8 0.0 copy-done.1
  11.8 2.7 %collective-permute-start.3 = (bf16[2,4,64,1536]{3,2,1,0:T(8,128)(2,1)S(1)}, bf16[2,4,64,1536]{3,2,1,0:T(8,128)(2,1)}, u32[]{:S(2)}, u32[]{:S(2)}) collective-permute-start(bf16[2,4,64,1536]{3,2,1,0:T(8,128)(2,1)S(1)} %constant_dynamic-update-slice_fusion.4.refs_4_.refs_6_), channel_id=1, source_target_pairs={{0,15},{1,2},{2,1},{3,4},{4,3},{5,6},{6,5},{7,8},{8,7},{9,10},{10,... | collective-permute-start | bytes 4718600 | tf_op jit(solution)/shard_map/ppermute | solution.py:20
  14.4 3.2 %reshape.24 = bf16[4,64,12,128]{3,2,1,0:T(8,128)(2,1)} reshape(bf16[4,32,2,1536]{3,2,1,0:T(2,128)(2,1)} %param.10) | data formatting | bytes 1572864 | tf_op jit(solution)/shard_map/reshape | solution.py:163
  17.6 0.0 copy-done.5
  17.6 0.1 copy.9
  17.8 0.2 copy.10
  17.9 0.1 stack_reshape.20
  18.1 3.2 %reshape.25 = bf16[4,64,12,128]{3,2,1,0:T(8,128)(2,1)} reshape(bf16[4,32,2,1536]{3,2,1,0:T(2,128)(2,1)} %param.9) | data formatting | bytes 1572864 | tf_op jit(solution)/shard_map/reshape | solution.py:164
  21.3 0.0 copy-done
  21.3 2.2 %fusion = f32[4,64,12]{2,1,0:T(8,128)S(1)} fusion(bf16[4,64,12,128]{3,2,1,0:T(8,128)(2,1)} %reshape.24, bf16[4,64,12,128]{3,2,1,0:T(8,128)(2,1)} %reshape.25), kind=kLoop, calls=%fused_computation.2 | loop fusion | flops 1569792 | bytes 1585152
  23.5 0.2 copy.19
  23.6 0.1 stack_reshape.21
  23.8 0.0 copy-start.4
  23.8 0.0 collective-permute-done.refs_5_.refs_7_
  23.8 0.6 copy-done.4
  24.4 13.6 %shard_map.85 = (f32[4,64,1536]{2,1,0:T(8,128)}, f32[2,4,64,1536]{3,2,1,0:T(8,128)}, f32[2,4,64,1536]{3,2,1,0:T(8,128)}) custom-call(bf16[2,4,64,1536]{3,2,1,0:T(8,128)(2,1)} %copy-done, bf16[2,4,64,1536]{3,2,1,0:T(8,128)(2,1)} %copy-done, f32[2,12,4,1,64]{4,3,2,1,0:T(1,128)} %copy-done.4, f32[2,12,4,1,64]{4,3,2,1,0:T(1,128)} %copy-done.4, ...), custom_call_target="tpu_custom_call" | custom-call | flops 1006632960 | bytes 12582912 | tf_op jit(solution)/shard_map/pallas_call | solution.py:134
  38.1 3.5 %collective-permute-start.5 = (f32[2,4,64,1536]{3,2,1,0:T(8,128)}, f32[2,4,64,1536]{3,2,1,0:T(8,128)}, u32[]{:S(2)}, u32[]{:S(2)}) collective-permute-start(f32[2,4,64,1536]{3,2,1,0:T(8,128)} %get-tuple-element.13), channel_id=1, source_target_pairs={{0,1},{1,0},{2,3},{3,2},{4,5},{5,4},{6,7},{7,6},{8,9},{9,8},{10,11... | collective-permute-start | bytes 9437192 | tf_op jit(solution)/shard_map/ppermute | solution.py:20
  41.6 0.1 collective-permute-start.2
  41.7 5.4 %collective-permute-done.2 = f32[2,12,4,1,64]{4,3,2,1,0:T(1,128)S(1)} collective-permute-done((f32[2,12,4,1,64]{4,3,2,1,0:T(1,128)}, f32[2,12,4,1,64]{4,3,2,1,0:T(1,128)S(1)}, u32[]{:S(2)}, u32[]{:S(2)}) %collective-permute-start.2) | collective-permute-done | bytes 24608 | tf_op jit(solution)/shard_map/ppermute | solution.py:20
  47.0 1.6 %pad_maximum_fusion.refs_4_.refs_5_ = f32[2,12,4,1,128]{4,3,2,1,0:T(1,128)} fusion(f32[2,12,4,1,64]{4,3,2,1,0:T(1,128)S(1)} %collective-permute-done.2, f32[2,12,4,1,64]{4,3,2,1,0:T(1,128)} %copy-done.4), kind=kLoop, calls=%fused_computation.4 | loop fusion | flops 12288 | bytes 98304 | tf_op jit(solution)/shard_map/concatenate | solution.py:186
  48.6 0.0 collective-permute-done.1.refs_1_.refs_3_
  48.6 0.9 collective-permute-done.3.refs_6_.refs_7_
  49.5 13.5 %shard_map.86 = (f32[4,64,1536]{2,1,0:T(8,128)}, f32[4,64,1536]{2,1,0:T(8,128)}, bf16[2,4,64,1536]{3,2,1,0:T(8,128)(2,1)}) custom-call(bf16[2,4,64,1536]{3,2,1,0:T(8,128)(2,1)} %copy-done, bf16[2,4,64,1536]{3,2,1,0:T(8,128)(2,1)} %collective-permute-done.1.refs_1_.refs_3_, bf16[2,4,64,1536]{3,2,1,0:T(8,128)(2,1)} %copy-done, ...), custom_call_target="tpu_custom_call" | custom-call | flops 1006632960 | bytes 11010048 | tf_op jit(solution)/shard_map/pallas_call | solution.py:134
  62.9 0.0 collective-permute-start.4
  62.9 1.8 %collective-permute-start.6 = (bf16[2,4,64,1536]{3,2,1,0:T(8,128)(2,1)}, bf16[2,4,64,1536]{3,2,1,0:T(8,128)(2,1)S(1)}, u32[]{:S(2)}, u32[]{:S(2)}) collective-permute-start(bf16[2,4,64,1536]{3,2,1,0:T(8,128)(2,1)} %get-tuple-element.14), channel_id=1, source_target_pairs={{0,15},{1,2},{2,1},{3,4},{4,3},{5,6},{6,5},{7,8},{8,7},{9,10},{10,... | collective-permute-start | bytes 4718600 | tf_op jit(solution)/shard_map/ppermute | solution.py:20
  64.7 1.8 %collective-permute-done.4 = f32[4,64,1536]{2,1,0:T(8,128)S(1)} collective-permute-done((f32[4,64,1536]{2,1,0:T(8,128)}, f32[4,64,1536]{2,1,0:T(8,128)S(1)}, u32[]{:S(2)}, u32[]{:S(2)}) %collective-permute-start.4) | collective-permute-done | bytes 1572896 | tf_op jit(solution)/shard_map/ppermute | solution.py:20
  66.6 2.2 %add_convert_fusion.1 = bf16[4,64,1536]{2,1,0:T(8,128)(2,1)S(1)} fusion(f32[4,64,1536]{2,1,0:T(8,128)S(1)} %collective-permute-done.4, f32[4,64,1536]{2,1,0:T(8,128)} %get-tuple-element.9, f32[4,64,1536]{2,1,0:T(8,128)} %get-tuple-element.10), kind=kLoop, calls=%fused_computation.3 | loop fusion | flops 1179648 | bytes 5505024 | tf_op jit(solution)/shard_map/convert_element_type | solution.py:202
  68.8 1.2 %reshape.27 = bf16[4,32,2,1536]{3,2,1,0:T(2,128)(2,1)} reshape(bf16[4,64,1536]{2,1,0:T(8,128)(2,1)S(1)} %add_convert_fusion.1) | data formatting | bytes 1572864 | tf_op jit(solution)/shard_map/reshape | solution.py:206
  69.9 30.0 %collective-permute-done.6 = bf16[2,4,64,1536]{3,2,1,0:T(8,128)(2,1)S(1)} collective-permute-done((bf16[2,4,64,1536]{3,2,1,0:T(8,128)(2,1)}, bf16[2,4,64,1536]{3,2,1,0:T(8,128)(2,1)S(1)}, u32[]{:S(2)}, u32[]{:S(2)}) %collective-permute-start.6) | collective-permute-done | bytes 1572896 | tf_op jit(solution)/shard_map/ppermute | solution.py:20
  99.9 0.0 collective-permute-done.5
  99.9 3.7 %add_convert_fusion = bf16[2,4,64,1536]{3,2,1,0:T(8,128)(2,1)S(1)} fusion(bf16[2,4,64,1536]{3,2,1,0:T(8,128)(2,1)S(1)} %collective-permute-done.6, f32[2,4,64,1536]{3,2,1,0:T(8,128)} %get-tuple-element.12, f32[2,4,64,1536]{3,2,1,0:T(8,128)} %collective-permute-done.5), kind=kLoop, calls=%fused_computation | loop fusion | flops 3145728 | bytes 9437184 | tf_op jit(solution)/shard_map/convert.1
  103.6 0.1 fusion.1
  103.8 1.2 %convert_element_type.19 = bf16[4,32,2,1536]{3,2,1,0:T(2,128)(2,1)} reshape(bf16[1,4,64,1536]{3,2,1,0:T(8,128)(2,1)S(1)} %get-tuple-element.15) | data formatting | bytes 1572864 | tf_op jit(solution)/shard_map/convert_element_type | solution.py:205
  104.9 1.2 %convert_element_type.18 = bf16[4,32,2,1536]{3,2,1,0:T(2,128)(2,1)} reshape(bf16[1,4,64,1536]{3,2,1,0:T(8,128)(2,1)S(1)} %get-tuple-element.16) | data formatting | bytes 1572864 | tf_op jit(solution)/shard_map/convert_element_type | solution.py:204
  (2 shorter events, 0.0 us)
Async XLA Ops:
  5.3 3.8 %copy-start.2 = (bf16[4,32,2,1536]{3,2,1,0:T(2,128)(2,1)S(1)}, bf16[4,32,2,1536]{3,2,1,0:T(2,128)(2,1)}, u32[]{:S(2)}) copy-start(bf16[4,32,2,1536]{3,2,1,0:T(2,128)(2,1)} %param.10) | copy-start | bytes 2359300
  5.3 6.4 %copy-start.1 = (bf16[2,4,64,1536]{3,2,1,0:T(8,128)(2,1)}, bf16[2,4,64,1536]{3,2,1,0:T(8,128)(2,1)S(1)}, u32[]{:S(2)}) copy-start(bf16[2,4,64,1536]{3,2,1,0:T(8,128)(2,1)S(1)} %constant_dynamic-update-slice_fusion.4.refs_4_.refs_6_) | copy-start | bytes 4718596
  5.3 18.5 %collective-permute-start = (bf16[2,4,64,1536]{3,2,1,0:T(8,128)(2,1)S(1)}, bf16[2,4,64,1536]{3,2,1,0:T(8,128)(2,1)}, u32[]{:S(2)}, u32[]{:S(2)}) collective-permute-start(bf16[2,4,64,1536]{3,2,1,0:T(8,128)(2,1)S(1)} %constant_dynamic-update-slice_fusion.4.refs_4_.refs_6_), channel_id=1, source_target_pairs={{0,1},{1,0},{2,3},{3,2},{4,5},{5,4},{6,7},{7,6},{8,9},{9,8},{10,11... | collective-permute-start | bytes 4718600 | tf_op jit(solution)/shard_map/ppermute | solution.py:20
  10.2 1.4 %copy-start.3 = (bf16[1,4,64,1536]{3,2,1,0:T(8,128)(2,1)S(1)}, bf16[1,4,64,1536]{3,2,1,0:T(8,128)(2,1)}, u32[]{:S(2)}) copy-start(bf16[1,4,64,1536]{3,2,1,0:T(8,128)(2,1)} %stack_reshape.19) | copy-start | bytes 2359300
  11.6 6.1 %copy-start.5 = (f32[4,32,2,12]{1,2,3,0:T(2,128)S(1)}, f32[4,32,2,12]{1,2,3,0:T(2,128)}, u32[]{:S(2)}) copy-start(f32[4,32,2,12]{1,2,3,0:T(2,128)} %param.11) | copy-start | bytes 36868
  11.6 9.7 %copy-start = (bf16[2,4,64,1536]{3,2,1,0:T(8,128)(2,1)}, bf16[2,4,64,1536]{3,2,1,0:T(8,128)(2,1)S(1)}, u32[]{:S(2)}) copy-start(bf16[2,4,64,1536]{3,2,1,0:T(8,128)(2,1)S(1)} %constant_dynamic-update-slice_fusion.refs_0_.refs_1_.refs_2_) | copy-start | bytes 4718596
  11.6 37.0 %collective-permute-start.1 = (bf16[2,4,64,1536]{3,2,1,0:T(8,128)(2,1)S(1)}, bf16[2,4,64,1536]{3,2,1,0:T(8,128)(2,1)}, u32[]{:S(2)}, u32[]{:S(2)}) collective-permute-start(bf16[2,4,64,1536]{3,2,1,0:T(8,128)(2,1)S(1)} %constant_dynamic-update-slice_fusion.refs_0_.refs_1_.refs_2_), channel_id=1, source_target_pairs={{0,1},{1,0},{2,3},{3,2},{4,5},{5,4},{6,7},{7,6},{8,9},{9,8},{10,11... | collective-permute-start | bytes 4718600 | tf_op jit(solution)/shard_map/ppermute | solution.py:20
  11.8 37.7 %collective-permute-start.3 = (bf16[2,4,64,1536]{3,2,1,0:T(8,128)(2,1)S(1)}, bf16[2,4,64,1536]{3,2,1,0:T(8,128)(2,1)}, u32[]{:S(2)}, u32[]{:S(2)}) collective-permute-start(bf16[2,4,64,1536]{3,2,1,0:T(8,128)(2,1)S(1)} %constant_dynamic-update-slice_fusion.4.refs_4_.refs_6_), channel_id=1, source_target_pairs={{0,15},{1,2},{2,1},{3,4},{4,3},{5,6},{6,5},{7,8},{8,7},{9,10},{10,... | collective-permute-start | bytes 4718600 | tf_op jit(solution)/shard_map/ppermute | solution.py:20
  23.8 0.6 copy-start.4
  38.1 61.9 %collective-permute-start.5 = (f32[2,4,64,1536]{3,2,1,0:T(8,128)}, f32[2,4,64,1536]{3,2,1,0:T(8,128)}, u32[]{:S(2)}, u32[]{:S(2)}) collective-permute-start(f32[2,4,64,1536]{3,2,1,0:T(8,128)} %get-tuple-element.13), channel_id=1, source_target_pairs={{0,1},{1,0},{2,3},{3,2},{4,5},{5,4},{6,7},{7,6},{8,9},{9,8},{10,11... | collective-permute-start | bytes 9437192 | tf_op jit(solution)/shard_map/ppermute | solution.py:20
  41.6 5.4 %collective-permute-start.2 = (f32[2,12,4,1,64]{4,3,2,1,0:T(1,128)}, f32[2,12,4,1,64]{4,3,2,1,0:T(1,128)S(1)}, u32[]{:S(2)}, u32[]{:S(2)}) collective-permute-start(f32[2,12,4,1,64]{4,3,2,1,0:T(1,128)} %copy-done.4), channel_id=1, source_target_pairs={{0,1},{1,0},{2,3},{3,2},{4,5},{5,4},{6,7},{7,6},{8,9},{9,8},{10,11... | collective-permute-start | bytes 73736 | tf_op jit(solution)/shard_map/ppermute | solution.py:20
  62.9 3.6 %collective-permute-start.4 = (f32[4,64,1536]{2,1,0:T(8,128)}, f32[4,64,1536]{2,1,0:T(8,128)S(1)}, u32[]{:S(2)}, u32[]{:S(2)}) collective-permute-start(f32[4,64,1536]{2,1,0:T(8,128)} %get-tuple-element.11), channel_id=1, source_target_pairs={{0,1},{1,0},{2,3},{3,2},{4,5},{5,4},{6,7},{7,6},{8,9},{9,8},{10,11... | collective-permute-start | bytes 4718600 | tf_op jit(solution)/shard_map/ppermute | solution.py:20
  62.9 37.0 %collective-permute-start.6 = (bf16[2,4,64,1536]{3,2,1,0:T(8,128)(2,1)}, bf16[2,4,64,1536]{3,2,1,0:T(8,128)(2,1)S(1)}, u32[]{:S(2)}, u32[]{:S(2)}) collective-permute-start(bf16[2,4,64,1536]{3,2,1,0:T(8,128)(2,1)} %get-tuple-element.14), channel_id=1, source_target_pairs={{0,15},{1,2},{2,1},{3,4},{4,3},{5,6},{6,5},{7,8},{8,7},{9,10},{10,... | collective-permute-start | bytes 4718600 | tf_op jit(solution)/shard_map/ppermute | solution.py:20

commit v15 on v13

--- a/solution.py
+++ b/solution.py
@@ -98,7 +98,7 @@
         heads = all_channels // HEAD_DIM
     channels = heads * HEAD_DIM
     nq, nk = len(queries), len(keys)
-    group = 4 if heads % 4 == 0 else (2 if heads % 2 == 0 else 1)
+    group = 6 if heads % 6 == 0 else (2 if heads % 2 == 0 else 1)
     kernel = functools.partial(
         window_kernel, nq=nq, nk=nk, tiles=tiles, tf=tf, mf=mf, narrow=narrow, group=group
     )

time: 105 us -> 105 us (level)
  transfers between devices with their start and end apart: 7 -> 7, of which waited for: 4 -> 4; matrix products, arithmetic and copies ran while one was open for 20% -> 20% of each run, Pallas kernels for 26% -> 27%
where the time goes in v15:
time: 105 us
  waiting for transfers between devices  35 us (33%)
  Pallas kernels  27.8 us (26%)
  local copies, waits for them, and re-layouts  22.2 us (21%)
  other arithmetic  10.5 us (10%)
  starting transfers between devices  8.32 us (8%)
    ppermute x7, waiting for transfers between devices, swap(): return lax.ppermute(block, 'sy', route)  35 us
    pallas_call x2, Pallas kernels, window_pass(): pl.pallas_call(kernel, grid=(heads // group,), in_specs=in_specs, out_spe...  27.8 us
    ppermute x7, starting transfers between devices, swap(): return lax.ppermute(block, 'sy', route)  8.32 us
    unnamed x23, local copies, waits for them, and re-layouts  3.65 us
    reshape x1, local copies, waits for them, and re-layouts, on_device(): outputs_fwd.reshape(rows, width, heads, HEAD_DIM)  3.24 us
    convert_element_type x1, other arithmetic, on_device(): dq = (dq_local + dq_mine + dq_back).astype(jnp.bfloat16)  3.23 us
    reshape x1, local copies, waits for them, and re-layouts, on_device(): grad_out.reshape(rows, width, heads, HEAD_DIM)  3.2 us
    another operation x1, other arithmetic  3.2 us
  transfers between devices with their start and end apart: 7, of which 4 were waited for; matrix products, arithmetic and copies ran while one was open for 20% of the time, Pallas kernels for 27%

profile of v15, /device:TPU:1, one launch (start us, length us, event | category | flops | bytes accessed | tf_op | source)
XLA Modules:
  0.0 104.6 jit_solution(11796900835601818819)
XLA Ops:
  0.6 0.0 copy-start.6
  0.6 2.3 %reshape.33 = bf16[4,64,1536]{2,1,0:T(8,128)(2,1)S(1)} reshape(bf16[4,32,2,1536]{3,2,1,0:T(2,128)(2,1)} %param.7) | data formatting | bytes 1572864 | tf_op jit(solution)/shard_map/reshape | solution.py:172
  3.0 0.0 copy-start.4
  3.0 0.0 copy-done.6
  3.0 0.3 reshape.34
  3.3 0.5 copy-done.4
  3.9 0.0 slice-start
  3.9 1.0 slice-done
  5.0 0.1 maximum_bitcast_fusion
  5.1 0.0 copy-start.7
  5.1 0.1 pad_maximum_fusion.refs_4_.refs_6_
  5.3 0.0 copy-start.1
  5.3 0.0 copy-start.2
  5.3 0.1 collective-permute-start
  5.4 1.0 copy-done.7
  6.4 1.2 %stack_reshape.12 = bf16[1,4,64,1536]{3,2,1,0:T(8,128)(2,1)} reshape(bf16[4,32,2,1536]{3,2,1,0:T(2,128)(2,1)S(1)} %copy-done.7) | data formatting | bytes 1572864 | tf_op jit(solution)/shard_map/stack;reshape | solution.py:160
  7.6 0.0 copy-done.2
  7.6 1.2 %stack_reshape.13 = bf16[1,4,64,1536]{3,2,1,0:T(8,128)(2,1)} reshape(bf16[4,32,2,1536]{3,2,1,0:T(2,128)(2,1)S(1)} %copy-done.2) | data formatting | bytes 1572864 | tf_op jit(solution)/shard_map/stack;reshape | solution.py:160
  8.8 0.0 copy-start.3
  8.8 1.3 %constant_dynamic-update-slice_fusion.1 = bf16[2,4,64,1536]{3,2,1,0:T(8,128)(2,1)S(1)} fusion(bf16[1,4,64,1536]{3,2,1,0:T(8,128)(2,1)} %stack_reshape.12), kind=kLoop, calls=%fused_computation.9 | loop fusion | bytes 1572864
  10.0 0.1 copy-done.3
  10.1 0.0 copy-start.9
  10.1 0.1 constant_dynamic-update-slice_fusion.refs_0_.refs_1_.refs_2_
  10.2 0.0 copy-start
  10.2 0.1 collective-permute-start.1
  10.3 0.0 copy-done.1
  10.3 2.7 %collective-permute-start.3 = (bf16[2,4,64,1536]{3,2,1,0:T(8,128)(2,1)S(1)}, bf16[2,4,64,1536]{3,2,1,0:T(8,128)(2,1)}, u32[]{:S(2)}, u32[]{:S(2)}) collective-permute-start(bf16[2,4,64,1536]{3,2,1,0:T(8,128)(2,1)S(1)} %pad_maximum_fusion.refs_4_.refs_6_), channel_id=1, source_target_pairs={{0,15},{1,2},{2,1},{3,4},{4,3},{5,6},{6,5},{7,8},{8,7},{9,10},{10,... | collective-permute-start | bytes 4718600 | tf_op jit(solution)/shard_map/ppermute | solution.py:20
  13.0 3.2 %reshape.30 = bf16[4,64,12,128]{3,2,1,0:T(8,128)(2,1)} reshape(bf16[4,32,2,1536]{3,2,1,0:T(2,128)(2,1)} %param.10) | data formatting | bytes 1572864 | tf_op jit(solution)/shard_map/reshape | solution.py:163
  16.2 0.0 copy-done.9
  16.2 0.1 copy.9
  16.3 0.2 copy.10
  16.5 0.1 stack_reshape.14
  16.6 3.2 %reshape.31 = bf16[4,64,12,128]{3,2,1,0:T(8,128)(2,1)} reshape(bf16[4,32,2,1536]{3,2,1,0:T(2,128)(2,1)} %param.9) | data formatting | bytes 1572864 | tf_op jit(solution)/shard_map/reshape | solution.py:164
  19.9 0.0 copy-done
  19.9 2.2 %fusion = f32[4,64,12]{2,1,0:T(8,128)S(1)} fusion(bf16[4,64,12,128]{3,2,1,0:T(8,128)(2,1)} %reshape.30, bf16[4,64,12,128]{3,2,1,0:T(8,128)(2,1)} %reshape.31), kind=kLoop, calls=%fused_computation.2 | loop fusion | flops 1569792 | bytes 1585152
  22.0 0.2 copy.19
  22.2 0.1 stack_reshape.15
  22.4 0.0 copy-start.8
  22.4 0.0 collective-permute-done.refs_5_.refs_7_
  22.4 0.6 copy-done.8
  23.0 14.0 %shard_map.85 = (f32[4,64,1536]{2,1,0:T(8,128)}, f32[2,4,64,1536]{3,2,1,0:T(8,128)}, f32[2,4,64,1536]{3,2,1,0:T(8,128)}) custom-call(bf16[2,4,64,1536]{3,2,1,0:T(8,128)(2,1)} %copy-done, bf16[2,4,64,1536]{3,2,1,0:T(8,128)(2,1)} %copy-done, f32[2,12,4,1,64]{4,3,2,1,0:T(1,128)} %copy-done.8, f32[2,12,4,1,64]{4,3,2,1,0:T(1,128)} %copy-done.8, ...), custom_call_target="tpu_custom_call" | custom-call | flops 1006632960 | bytes 12582912 | tf_op jit(solution)/shard_map/pallas_call | solution.py:134
  37.1 3.5 %collective-permute-start.5 = (f32[2,4,64,1536]{3,2,1,0:T(8,128)}, f32[2,4,64,1536]{3,2,1,0:T(8,128)}, u32[]{:S(2)}, u32[]{:S(2)}) collective-permute-start(f32[2,4,64,1536]{3,2,1,0:T(8,128)} %get-tuple-element.13), channel_id=1, source_target_pairs={{0,1},{1,0},{2,3},{3,2},{4,5},{5,4},{6,7},{7,6},{8,9},{9,8},{10,11... | collective-permute-start | bytes 9437192 | tf_op jit(solution)/shard_map/ppermute | solution.py:20
  40.6 0.1 collective-permute-start.2
  40.7 5.4 %collective-permute-done.2 = f32[2,12,4,1,64]{4,3,2,1,0:T(1,128)S(1)} collective-permute-done((f32[2,12,4,1,64]{4,3,2,1,0:T(1,128)}, f32[2,12,4,1,64]{4,3,2,1,0:T(1,128)S(1)}, u32[]{:S(2)}, u32[]{:S(2)}) %collective-permute-start.2) | collective-permute-done | bytes 24608 | tf_op jit(solution)/shard_map/ppermute | solution.py:20
  46.0 1.6 %pad_maximum_fusion.1.refs_4_.refs_5_ = f32[2,12,4,1,128]{4,3,2,1,0:T(1,128)} fusion(f32[2,12,4,1,64]{4,3,2,1,0:T(1,128)S(1)} %collective-permute-done.2, f32[2,12,4,1,64]{4,3,2,1,0:T(1,128)} %copy-done.8), kind=kLoop, calls=%fused_computation.7 | loop fusion | flops 12288 | bytes 98304 | tf_op jit(solution)/shard_map/concatenate | solution.py:186
  47.6 0.0 collective-permute-done.1.refs_1_.refs_3_
  47.6 0.4 collective-permute-done.3.refs_6_.refs_7_
  48.0 13.8 %shard_map.86 = (f32[4,64,1536]{2,1,0:T(8,128)}, f32[4,64,1536]{2,1,0:T(8,128)}, bf16[2,4,64,1536]{3,2,1,0:T(8,128)(2,1)}) custom-call(bf16[2,4,64,1536]{3,2,1,0:T(8,128)(2,1)} %copy-done, bf16[2,4,64,1536]{3,2,1,0:T(8,128)(2,1)} %collective-permute-done.1.refs_1_.refs_3_, bf16[2,4,64,1536]{3,2,1,0:T(8,128)(2,1)} %copy-done, ...), custom_call_target="tpu_custom_call" | custom-call | flops 1006632960 | bytes 11010048 | tf_op jit(solution)/shard_map/pallas_call | solution.py:134
  61.8 0.0 collective-permute-start.4
  61.8 1.8 %collective-permute-start.6 = (bf16[2,4,64,1536]{3,2,1,0:T(8,128)(2,1)}, bf16[2,4,64,1536]{3,2,1,0:T(8,128)(2,1)}, u32[]{:S(2)}, u32[]{:S(2)}) collective-permute-start(bf16[2,4,64,1536]{3,2,1,0:T(8,128)(2,1)} %get-tuple-element.14), channel_id=1, source_target_pairs={{0,15},{1,2},{2,1},{3,4},{4,3},{5,6},{6,5},{7,8},{8,7},{9,10},{10,... | collective-permute-start | bytes 4718600 | tf_op jit(solution)/shard_map/ppermute | solution.py:20
  63.6 1.8 %collective-permute-done.4 = f32[4,64,1536]{2,1,0:T(8,128)S(1)} collective-permute-done((f32[4,64,1536]{2,1,0:T(8,128)}, f32[4,64,1536]{2,1,0:T(8,128)S(1)}, u32[]{:S(2)}, u32[]{:S(2)}) %collective-permute-start.4) | collective-permute-done | bytes 1572896 | tf_op jit(solution)/shard_map/ppermute | solution.py:20
  65.4 0.0 copy-start.5
  65.4 3.2 %add_convert_fusion.1 = bf16[4,64,1536]{2,1,0:T(8,128)(2,1)} fusion(f32[4,64,1536]{2,1,0:T(8,128)S(1)} %collective-permute-done.4, f32[4,64,1536]{2,1,0:T(8,128)} %get-tuple-element.9, f32[4,64,1536]{2,1,0:T(8,128)} %get-tuple-element.10), kind=kLoop, calls=%fused_computation.4 | loop fusion | flops 1179648 | bytes 5505024 | tf_op jit(solution)/shard_map/convert_element_type | solution.py:202
  68.7 2.8 %reshape.35 = bf16[4,32,2,1536]{3,2,1,0:T(2,128)(2,1)} reshape(bf16[4,64,1536]{2,1,0:T(8,128)(2,1)} %add_convert_fusion.1) | data formatting | bytes 1572864 | tf_op jit(solution)/shard_map/reshape | solution.py:206
  71.5 27.4 %collective-permute-done.6 = bf16[2,4,64,1536]{3,2,1,0:T(8,128)(2,1)} collective-permute-done((bf16[2,4,64,1536]{3,2,1,0:T(8,128)(2,1)}, bf16[2,4,64,1536]{3,2,1,0:T(8,128)(2,1)}, u32[]{:S(2)}, u32[]{:S(2)}) %collective-permute-start.6) | collective-permute-done | bytes 1572896 | tf_op jit(solution)/shard_map/ppermute | solution.py:20
  98.9 0.0 collective-permute-done.5
  98.9 0.0 copy-done.5
  98.9 3.2 %add_convert_fusion = bf16[2,4,64,1536]{3,2,1,0:T(8,128)(2,1)S(1)} fusion(bf16[2,4,64,1536]{3,2,1,0:T(8,128)(2,1)} %collective-permute-done.6, f32[2,4,64,1536]{3,2,1,0:T(8,128)S(1)} %copy-done.5, f32[2,4,64,1536]{3,2,1,0:T(8,128)} %collective-permute-done.5), kind=kLoop, calls=%fused_computation | loop fusion | flops 3145728 | bytes 9437184 | tf_op jit(solution)/shard_map/convert.1
  102.1 0.1 fusion.1
  102.2 1.2 %convert_element_type.19 = bf16[4,32,2,1536]{3,2,1,0:T(2,128)(2,1)} reshape(bf16[1,4,64,1536]{3,2,1,0:T(8,128)(2,1)S(1)} %get-tuple-element.15) | data formatting | bytes 1572864 | tf_op jit(solution)/shard_map/convert_element_type | solution.py:205
  103.4 1.2 %convert_element_type.18 = bf16[4,32,2,1536]{3,2,1,0:T(2,128)(2,1)} reshape(bf16[1,4,64,1536]{3,2,1,0:T(8,128)(2,1)S(1)} %get-tuple-element.16) | data formatting | bytes 1572864 | tf_op jit(solution)/shard_map/convert_element_type | solution.py:204
  (5 shorter events, 0.1 us)
Async XLA Ops:
  0.6 2.4 %copy-start.6 = (bf16[4,32,2,1536]{3,2,1,0:T(2,128)(2,1)S(1)}, bf16[4,32,2,1536]{3,2,1,0:T(2,128)(2,1)}, u32[]{:S(2)}) copy-start(bf16[4,32,2,1536]{3,2,1,0:T(2,128)(2,1)} %param.8) | copy-start | bytes 2359300
  3.0 0.9 copy-start.4
  3.9 1.1 %slice-start = ((bf16[4,64,1536]{2,1,0:T(8,128)(2,1)}), bf16[4,56,1536]{2,1,0:T(8,128)(2,1)S(1)}, s32[]{:S(2)}) async-start(bf16[4,64,1536]{2,1,0:T(8,128)(2,1)} %copy-done.4), calls=%async_computation | async-start | bytes 1376256 | tf_op jit(solution)/shard_map/jit(_roll_static)/slice | solution.py:172
  5.1 1.3 %copy-start.7 = (bf16[4,32,2,1536]{3,2,1,0:T(2,128)(2,1)S(1)}, bf16[4,32,2,1536]{3,2,1,0:T(2,128)(2,1)}, u32[]{:S(2)}) copy-start(bf16[4,32,2,1536]{3,2,1,0:T(2,128)(2,1)} %param.6) | copy-start | bytes 2359300
  5.3 5.0 %copy-start.1 = (bf16[2,4,64,1536]{3,2,1,0:T(8,128)(2,1)}, bf16[2,4,64,1536]{3,2,1,0:T(8,128)(2,1)S(1)}, u32[]{:S(2)}) copy-start(bf16[2,4,64,1536]{3,2,1,0:T(8,128)(2,1)S(1)} %pad_maximum_fusion.refs_4_.refs_6_) | copy-start | bytes 4718596
  5.3 2.3 %copy-start.2 = (bf16[4,32,2,1536]{3,2,1,0:T(2,128)(2,1)S(1)}, bf16[4,32,2,1536]{3,2,1,0:T(2,128)(2,1)}, u32[]{:S(2)}) copy-start(bf16[4,32,2,1536]{3,2,1,0:T(2,128)(2,1)} %param.10) | copy-start | bytes 2359300
  5.3 17.1 %collective-permute-start = (bf16[2,4,64,1536]{3,2,1,0:T(8,128)(2,1)S(1)}, bf16[2,4,64,1536]{3,2,1,0:T(8,128)(2,1)}, u32[]{:S(2)}, u32[]{:S(2)}) collective-permute-start(bf16[2,4,64,1536]{3,2,1,0:T(8,128)(2,1)S(1)} %pad_maximum_fusion.refs_4_.refs_6_), channel_id=1, source_target_pairs={{0,1},{1,0},{2,3},{3,2},{4,5},{5,4},{6,7},{7,6},{8,9},{9,8},{10,11... | collective-permute-start | bytes 4718600 | tf_op jit(solution)/shard_map/ppermute | solution.py:20
  8.8 1.4 %copy-start.3 = (bf16[1,4,64,1536]{3,2,1,0:T(8,128)(2,1)S(1)}, bf16[1,4,64,1536]{3,2,1,0:T(8,128)(2,1)}, u32[]{:S(2)}) copy-start(bf16[1,4,64,1536]{3,2,1,0:T(8,128)(2,1)} %stack_reshape.13) | copy-start | bytes 2359300
  10.1 6.1 %copy-start.9 = (f32[4,32,2,12]{1,2,3,0:T(2,128)S(1)}, f32[4,32,2,12]{1,2,3,0:T(2,128)}, u32[]{:S(2)}) copy-start(f32[4,32,2,12]{1,2,3,0:T(2,128)} %param.11) | copy-start | bytes 36868
  10.2 9.7 %copy-start = (bf16[2,4,64,1536]{3,2,1,0:T(8,128)(2,1)}, bf16[2,4,64,1536]{3,2,1,0:T(8,128)(2,1)S(1)}, u32[]{:S(2)}) copy-start(bf16[2,4,64,1536]{3,2,1,0:T(8,128)(2,1)S(1)} %constant_dynamic-update-slice_fusion.refs_0_.refs_1_.refs_2_) | copy-start | bytes 4718596
  10.2 37.4 %collective-permute-start.1 = (bf16[2,4,64,1536]{3,2,1,0:T(8,128)(2,1)S(1)}, bf16[2,4,64,1536]{3,2,1,0:T(8,128)(2,1)}, u32[]{:S(2)}, u32[]{:S(2)}) collective-permute-start(bf16[2,4,64,1536]{3,2,1,0:T(8,128)(2,1)S(1)} %constant_dynamic-update-slice_fusion.refs_0_.refs_1_.refs_2_), channel_id=1, source_target_pairs={{0,1},{1,0},{2,3},{3,2},{4,5},{5,4},{6,7},{7,6},{8,9},{9,8},{10,11... | collective-permute-start | bytes 4718600 | tf_op jit(solution)/shard_map/ppermute | solution.py:20
  10.3 37.7 %collective-permute-start.3 = (bf16[2,4,64,1536]{3,2,1,0:T(8,128)(2,1)S(1)}, bf16[2,4,64,1536]{3,2,1,0:T(8,128)(2,1)}, u32[]{:S(2)}, u32[]{:S(2)}) collective-permute-start(bf16[2,4,64,1536]{3,2,1,0:T(8,128)(2,1)S(1)} %pad_maximum_fusion.refs_4_.refs_6_), channel_id=1, source_target_pairs={{0,15},{1,2},{2,1},{3,4},{4,3},{5,6},{6,5},{7,8},{8,7},{9,10},{10,... | collective-permute-start | bytes 4718600 | tf_op jit(solution)/shard_map/ppermute | solution.py:20
  22.4 0.6 copy-start.8
  37.1 61.9 %collective-permute-start.5 = (f32[2,4,64,1536]{3,2,1,0:T(8,128)}, f32[2,4,64,1536]{3,2,1,0:T(8,128)}, u32[]{:S(2)}, u32[]{:S(2)}) collective-permute-start(f32[2,4,64,1536]{3,2,1,0:T(8,128)} %get-tuple-element.13), channel_id=1, source_target_pairs={{0,1},{1,0},{2,3},{3,2},{4,5},{5,4},{6,7},{7,6},{8,9},{9,8},{10,11... | collective-permute-start | bytes 9437192 | tf_op jit(solution)/shard_map/ppermute | solution.py:20
  40.6 5.4 %collective-permute-start.2 = (f32[2,12,4,1,64]{4,3,2,1,0:T(1,128)}, f32[2,12,4,1,64]{4,3,2,1,0:T(1,128)S(1)}, u32[]{:S(2)}, u32[]{:S(2)}) collective-permute-start(f32[2,12,4,1,64]{4,3,2,1,0:T(1,128)} %copy-done.8), channel_id=1, source_target_pairs={{0,1},{1,0},{2,3},{3,2},{4,5},{5,4},{6,7},{7,6},{8,9},{9,8},{10,11... | collective-permute-start | bytes 73736 | tf_op jit(solution)/shard_map/ppermute | solution.py:20
  61.8 3.6 %collective-permute-start.4 = (f32[4,64,1536]{2,1,0:T(8,128)}, f32[4,64,1536]{2,1,0:T(8,128)S(1)}, u32[]{:S(2)}, u32[]{:S(2)}) collective-permute-start(f32[4,64,1536]{2,1,0:T(8,128)} %get-tuple-element.11), channel_id=1, source_target_pairs={{0,1},{1,0},{2,3},{3,2},{4,5},{5,4},{6,7},{7,6},{8,9},{9,8},{10,11... | collective-permute-start | bytes 4718600 | tf_op jit(solution)/shard_map/ppermute | solution.py:20
  61.8 37.1 %collective-permute-start.6 = (bf16[2,4,64,1536]{3,2,1,0:T(8,128)(2,1)}, bf16[2,4,64,1536]{3,2,1,0:T(8,128)(2,1)}, u32[]{:S(2)}, u32[]{:S(2)}) collective-permute-start(bf16[2,4,64,1536]{3,2,1,0:T(8,128)(2,1)} %get-tuple-element.14), channel_id=1, source_target_pairs={{0,15},{1,2},{2,1},{3,4},{4,3},{5,6},{6,5},{7,8},{8,7},{9,10},{10,... | collective-permute-start | bytes 4718600 | tf_op jit(solution)/shard_map/ppermute | solution.py:20
  65.4 33.5 %copy-start.5 = (f32[2,4,64,1536]{3,2,1,0:T(8,128)S(1)}, f32[2,4,64,1536]{3,2,1,0:T(8,128)}, u32[]{:S(2)}) copy-start(f32[2,4,64,1536]{3,2,1,0:T(8,128)} %get-tuple-element.12) | copy-start | bytes 9437188

commit v16 on v13

--- a/solution.py
+++ b/solution.py
@@ -200,9 +200,12 @@
     dq_back = jnp.concatenate(back_parts, axis=-1)
     arrived = jnp.concatenate(arrived_parts, axis=-1)
     dq = (dq_local + dq_mine + dq_back).astype(jnp.bfloat16)
-    total = part_own + back_partner + arrived.astype(jnp.float32)
-    grad_keys = total[0].astype(jnp.bfloat16).reshape(rows, width_cells, frames, channels)
-    grad_values = total[1].astype(jnp.bfloat16).reshape(rows, width_cells, frames, channels)
+    def finished(member):
+        total = part_own[member] + back_partner[member] + arrived[member].astype(jnp.float32)
+        return total.reshape(rows, width_cells, frames, channels).astype(jnp.bfloat16)
+
+    grad_keys = finished(0)
+    grad_values = finished(1)
     grad_queries = dq.reshape(rows, width_cells, frames, channels)
     return (grad_queries, grad_keys, grad_values)
 

time: 105 us -> 105 us (level)
  waiting for transfers between devices: 35.5 us -> 38 us
  local copies, waits for them, and re-layouts: 22.2 us -> 20.4 us
    convert_element_type x0 -> x1, other arithmetic: none -> 3.66 us  [finished(): total.reshape(rows, width_cells, frames, channels).astype(jnp.bfloat16)]
    another operation x1 -> x0, other arithmetic: 3.2 us -> none
    ppermute x7, waiting for transfers between devices: 35.5 us -> 38 us  [swap(): return lax.ppermute(block, 'sy', route)]
    reshape x1, local copies, waits for them, and re-layouts: 2.84 us -> 1.17 us  [on_device(): grad_queries = dq.reshape(rows, width_cells, frames, channels)]
    unnamed x23 -> x21, local copies, waits for them, and re-layouts: 3.65 us -> 3.64 us
  transfers between devices with their start and end apart: 7 -> 7, of which waited for: 4 -> 4; matrix products, arithmetic and copies ran while one was open for 20% -> 17% of each run, Pallas kernels for 26% -> 26%
where the time goes in v16:
time: 105 us
  waiting for transfers between devices  38 us (36%)
  Pallas kernels  27.1 us (26%)
  local copies, waits for them, and re-layouts  20.4 us (19%)
  other arithmetic  9.9 us (9%)
  starting transfers between devices  8.32 us (8%)
    ppermute x7, waiting for transfers between devices, swap(): return lax.ppermute(block, 'sy', route)  38 us
    pallas_call x2, Pallas kernels, window_pass(): pl.pallas_call(kernel, grid=(heads // group,), in_specs=in_specs, out_spe...  27.1 us
    ppermute x7, starting transfers between devices, swap(): return lax.ppermute(block, 'sy', route)  8.32 us
    convert_element_type x1, other arithmetic, finished(): total.reshape(rows, width_cells, frames, channels).astype(jnp.bfloat16)  3.66 us
    unnamed x21, local copies, waits for them, and re-layouts  3.64 us
    reshape x1, local copies, waits for them, and re-layouts, on_device(): outputs_fwd.reshape(rows, width, heads, HEAD_DIM)  3.25 us
    reshape x1, local copies, waits for them, and re-layouts, on_device(): grad_out.reshape(rows, width, heads, HEAD_DIM)  3.21 us
    another operation x3, local copies, waits for them, and re-layouts, on_device(): jnp.stack([queries.reshape(rows, width, channels), grad_out.reshape(rows,...  2.4 us
  transfers between devices with their start and end apart: 7, of which 4 were waited for; matrix products, arithmetic and copies ran while one was open for 17% of the time, Pallas kernels for 26%

profile of v16, /device:TPU:1, one launch (start us, length us, event | category | flops | bytes accessed | tf_op | source)
XLA Modules:
  0.0 104.5 jit_solution(17341903191262727803)
XLA Ops:
  0.6 0.0 copy-start.5
  0.6 2.3 %reshape.43 = bf16[4,64,1536]{2,1,0:T(8,128)(2,1)S(1)} reshape(bf16[4,32,2,1536]{3,2,1,0:T(2,128)(2,1)} %param.7) | data formatting | bytes 1572864 | tf_op jit(solution)/shard_map/reshape | solution.py:172
  3.0 0.0 copy-start.4
  3.0 0.0 copy-done.5
  3.0 0.3 reshape.44
  3.3 0.5 copy-done.4
  3.9 0.0 slice-start
  3.9 1.0 slice-done
  5.0 0.1 maximum_bitcast_fusion
  5.1 0.0 copy-start.6
  5.1 0.1 pad_maximum_fusion.refs_4_.refs_6_
  5.3 0.0 copy-start.1
  5.3 0.0 copy-start.2
  5.3 0.1 collective-permute-start
  5.4 1.0 copy-done.6
  6.4 1.2 %stack_reshape.12 = bf16[1,4,64,1536]{3,2,1,0:T(8,128)(2,1)} reshape(bf16[4,32,2,1536]{3,2,1,0:T(2,128)(2,1)S(1)} %copy-done.6) | data formatting | bytes 1572864 | tf_op jit(solution)/shard_map/stack;reshape | solution.py:160
  7.6 0.0 copy-done.2
  7.6 1.2 %stack_reshape.13 = bf16[1,4,64,1536]{3,2,1,0:T(8,128)(2,1)} reshape(bf16[4,32,2,1536]{3,2,1,0:T(2,128)(2,1)S(1)} %copy-done.2) | data formatting | bytes 1572864 | tf_op jit(solution)/shard_map/stack;reshape | solution.py:160
  8.8 0.0 copy-start.3
  8.8 1.3 %constant_dynamic-update-slice_fusion.1 = bf16[2,4,64,1536]{3,2,1,0:T(8,128)(2,1)S(1)} fusion(bf16[1,4,64,1536]{3,2,1,0:T(8,128)(2,1)} %stack_reshape.12), kind=kLoop, calls=%fused_computation.14 | loop fusion | bytes 1572864
  10.0 0.1 copy-done.3
  10.1 0.0 copy-start.8
  10.1 0.1 constant_dynamic-update-slice_fusion.refs_0_.refs_1_.refs_2_
  10.2 0.0 copy-start
  10.2 0.1 collective-permute-start.1
  10.3 0.0 copy-done.1
  10.3 2.7 %collective-permute-start.3 = (bf16[2,4,64,1536]{3,2,1,0:T(8,128)(2,1)S(1)}, bf16[2,4,64,1536]{3,2,1,0:T(8,128)(2,1)}, u32[]{:S(2)}, u32[]{:S(2)}) collective-permute-start(bf16[2,4,64,1536]{3,2,1,0:T(8,128)(2,1)S(1)} %pad_maximum_fusion.refs_4_.refs_6_), channel_id=1, source_target_pairs={{0,15},{1,2},{2,1},{3,4},{4,3},{5,6},{6,5},{7,8},{8,7},{9,10},{10,... | collective-permute-start | bytes 4718600 | tf_op jit(solution)/shard_map/ppermute | solution.py:20
  13.0 3.2 %reshape.40 = bf16[4,64,12,128]{3,2,1,0:T(8,128)(2,1)} reshape(bf16[4,32,2,1536]{3,2,1,0:T(2,128)(2,1)} %param.10) | data formatting | bytes 1572864 | tf_op jit(solution)/shard_map/reshape | solution.py:163
  16.2 0.0 copy-done.8
  16.2 0.1 copy.9
  16.3 0.2 copy.10
  16.5 0.1 stack_reshape.14
  16.6 3.2 %reshape.41 = bf16[4,64,12,128]{3,2,1,0:T(8,128)(2,1)} reshape(bf16[4,32,2,1536]{3,2,1,0:T(2,128)(2,1)} %param.9) | data formatting | bytes 1572864 | tf_op jit(solution)/shard_map/reshape | solution.py:164
  19.9 0.0 copy-done
  19.9 2.2 %fusion = f32[4,64,12]{2,1,0:T(8,128)S(1)} fusion(bf16[4,64,12,128]{3,2,1,0:T(8,128)(2,1)} %reshape.40, bf16[4,64,12,128]{3,2,1,0:T(8,128)(2,1)} %reshape.41), kind=kLoop, calls=%fused_computation.1 | loop fusion | flops 1569792 | bytes 1585152
  22.1 0.2 copy.19
  22.2 0.1 stack_reshape.15
  22.4 0.0 copy-start.7
  22.4 0.0 collective-permute-done.refs_5_.refs_7_
  22.4 0.6 copy-done.7
  23.0 13.6 %shard_map.85 = (f32[4,64,1536]{2,1,0:T(8,128)}, f32[2,4,64,1536]{3,2,1,0:T(8,128)}, f32[2,4,64,1536]{3,2,1,0:T(8,128)}) custom-call(bf16[2,4,64,1536]{3,2,1,0:T(8,128)(2,1)} %copy-done, bf16[2,4,64,1536]{3,2,1,0:T(8,128)(2,1)} %copy-done, f32[2,12,4,1,64]{4,3,2,1,0:T(1,128)} %copy-done.7, f32[2,12,4,1,64]{4,3,2,1,0:T(1,128)} %copy-done.7, ...), custom_call_target="tpu_custom_call" | custom-call | flops 1006632960 | bytes 12582912 | tf_op jit(solution)/shard_map/pallas_call | solution.py:134
  36.7 3.5 %collective-permute-start.5 = (f32[2,4,64,1536]{3,2,1,0:T(8,128)}, f32[2,4,64,1536]{3,2,1,0:T(8,128)}, u32[]{:S(2)}, u32[]{:S(2)}) collective-permute-start(f32[2,4,64,1536]{3,2,1,0:T(8,128)} %get-tuple-element.13), channel_id=1, source_target_pairs={{0,1},{1,0},{2,3},{3,2},{4,5},{5,4},{6,7},{7,6},{8,9},{9,8},{10,11... | collective-permute-start | bytes 9437192 | tf_op jit(solution)/shard_map/ppermute | solution.py:20
  40.2 0.1 collective-permute-start.2
  40.3 5.4 %collective-permute-done.2 = f32[2,12,4,1,64]{4,3,2,1,0:T(1,128)S(1)} collective-permute-done((f32[2,12,4,1,64]{4,3,2,1,0:T(1,128)}, f32[2,12,4,1,64]{4,3,2,1,0:T(1,128)S(1)}, u32[]{:S(2)}, u32[]{:S(2)}) %collective-permute-start.2) | collective-permute-done | bytes 24608 | tf_op jit(solution)/shard_map/ppermute | solution.py:20
  45.6 1.6 %pad_maximum_fusion.1.refs_4_.refs_5_ = f32[2,12,4,1,128]{4,3,2,1,0:T(1,128)} fusion(f32[2,12,4,1,64]{4,3,2,1,0:T(1,128)S(1)} %collective-permute-done.2, f32[2,12,4,1,64]{4,3,2,1,0:T(1,128)} %copy-done.7), kind=kLoop, calls=%fused_computation.12 | loop fusion | flops 12288 | bytes 98304 | tf_op jit(solution)/shard_map/concatenate | solution.py:186
  47.2 0.0 collective-permute-done.1.refs_1_.refs_3_
  47.2 0.8 collective-permute-done.3.refs_6_.refs_7_
  48.0 13.5 %shard_map.86 = (f32[4,64,1536]{2,1,0:T(8,128)}, f32[4,64,1536]{2,1,0:T(8,128)}, bf16[2,4,64,1536]{3,2,1,0:T(8,128)(2,1)}) custom-call(bf16[2,4,64,1536]{3,2,1,0:T(8,128)(2,1)} %copy-done, bf16[2,4,64,1536]{3,2,1,0:T(8,128)(2,1)} %collective-permute-done.1.refs_1_.refs_3_, bf16[2,4,64,1536]{3,2,1,0:T(8,128)(2,1)} %copy-done, ...), custom_call_target="tpu_custom_call" | custom-call | flops 1006632960 | bytes 11010048 | tf_op jit(solution)/shard_map/pallas_call | solution.py:134
  61.5 0.0 collective-permute-start.4
  61.5 1.8 %collective-permute-start.6 = (bf16[2,4,64,1536]{3,2,1,0:T(8,128)(2,1)}, bf16[2,4,64,1536]{3,2,1,0:T(8,128)(2,1)S(1)}, u32[]{:S(2)}, u32[]{:S(2)}) collective-permute-start(bf16[2,4,64,1536]{3,2,1,0:T(8,128)(2,1)} %get-tuple-element.14), channel_id=1, source_target_pairs={{0,15},{1,2},{2,1},{3,4},{4,3},{5,6},{6,5},{7,8},{8,7},{9,10},{10,... | collective-permute-start | bytes 4718600 | tf_op jit(solution)/shard_map/ppermute | solution.py:20
  63.3 1.8 %collective-permute-done.4 = f32[4,64,1536]{2,1,0:T(8,128)S(1)} collective-permute-done((f32[4,64,1536]{2,1,0:T(8,128)}, f32[4,64,1536]{2,1,0:T(8,128)S(1)}, u32[]{:S(2)}, u32[]{:S(2)}) %collective-permute-start.4) | collective-permute-done | bytes 1572896 | tf_op jit(solution)/shard_map/ppermute | solution.py:20
  65.1 2.2 %add_convert_fusion = bf16[4,64,1536]{2,1,0:T(8,128)(2,1)S(1)} fusion(f32[4,64,1536]{2,1,0:T(8,128)S(1)} %collective-permute-done.4, f32[4,64,1536]{2,1,0:T(8,128)} %get-tuple-element.9, f32[4,64,1536]{2,1,0:T(8,128)} %get-tuple-element.10), kind=kLoop, calls=%fused_computation.9 | loop fusion | flops 1179648 | bytes 5505024 | tf_op jit(solution)/shard_map/convert_element_type | solution.py:202
  67.4 1.2 %reshape.45 = bf16[4,32,2,1536]{3,2,1,0:T(2,128)(2,1)} reshape(bf16[4,64,1536]{2,1,0:T(8,128)(2,1)S(1)} %add_convert_fusion) | data formatting | bytes 1572864 | tf_op jit(solution)/shard_map/reshape | solution.py:209
  68.5 30.0 %collective-permute-done.6 = bf16[2,4,64,1536]{3,2,1,0:T(8,128)(2,1)S(1)} collective-permute-done((bf16[2,4,64,1536]{3,2,1,0:T(8,128)(2,1)}, bf16[2,4,64,1536]{3,2,1,0:T(8,128)(2,1)S(1)}, u32[]{:S(2)}, u32[]{:S(2)}) %collective-permute-start.6) | collective-permute-done | bytes 1572896 | tf_op jit(solution)/shard_map/ppermute | solution.py:20
  98.5 0.0 collective-permute-done.5
  98.5 3.7 %fusion.2 = (bf16[1,4,64,1536]{3,2,1,0:T(8,128)(2,1)S(1)}, bf16[1,4,64,1536]{3,2,1,0:T(8,128)(2,1)S(1)}) fusion(f32[2,4,64,1536]{3,2,1,0:T(8,128)} %collective-permute-done.5, f32[2,4,64,1536]{3,2,1,0:T(8,128)} %get-tuple-element.12, bf16[2,4,64,1536]{3,2,1,0:T(8,128)(2,1)S(1)} %collective-permute-done.6), kind=kLoop, calls=%fused_computation.4 | loop fusion | flops 3145728 | bytes 9437184 | tf_op jit(solution)/shard_map/convert_element_type | solution.py:205
  102.2 1.2 %convert_element_type.31 = bf16[4,32,2,1536]{3,2,1,0:T(2,128)(2,1)} reshape(bf16[1,4,64,1536]{3,2,1,0:T(8,128)(2,1)S(1)} %get-tuple-element.15) | data formatting | bytes 1572864 | tf_op jit(solution)/shard_map/convert_element_type | solution.py:205
  103.3 1.2 %convert_element_type.28 = bf16[4,32,2,1536]{3,2,1,0:T(2,128)(2,1)} reshape(bf16[1,4,64,1536]{3,2,1,0:T(8,128)(2,1)S(1)} %get-tuple-element.16) | data formatting | bytes 1572864 | tf_op jit(solution)/shard_map/convert_element_type | solution.py:205
  (5 shorter events, 0.1 us)
Async XLA Ops:
  0.6 2.4 %copy-start.5 = (bf16[4,32,2,1536]{3,2,1,0:T(2,128)(2,1)S(1)}, bf16[4,32,2,1536]{3,2,1,0:T(2,128)(2,1)}, u32[]{:S(2)}) copy-start(bf16[4,32,2,1536]{3,2,1,0:T(2,128)(2,1)} %param.8) | copy-start | bytes 2359300
  3.0 0.9 copy-start.4
  3.9 1.1 %slice-start = ((bf16[4,64,1536]{2,1,0:T(8,128)(2,1)}), bf16[4,56,1536]{2,1,0:T(8,128)(2,1)S(1)}, s32[]{:S(2)}) async-start(bf16[4,64,1536]{2,1,0:T(8,128)(2,1)} %copy-done.4), calls=%async_computation | async-start | bytes 1376256 | tf_op jit(solution)/shard_map/jit(_roll_static)/slice | solution.py:172
  5.1 1.3 %copy-start.6 = (bf16[4,32,2,1536]{3,2,1,0:T(2,128)(2,1)S(1)}, bf16[4,32,2,1536]{3,2,1,0:T(2,128)(2,1)}, u32[]{:S(2)}) copy-start(bf16[4,32,2,1536]{3,2,1,0:T(2,128)(2,1)} %param.6) | copy-start | bytes 2359300
  5.3 5.0 %copy-start.1 = (bf16[2,4,64,1536]{3,2,1,0:T(8,128)(2,1)}, bf16[2,4,64,1536]{3,2,1,0:T(8,128)(2,1)S(1)}, u32[]{:S(2)}) copy-start(bf16[2,4,64,1536]{3,2,1,0:T(8,128)(2,1)S(1)} %pad_maximum_fusion.refs_4_.refs_6_) | copy-start | bytes 4718596
  5.3 2.3 %copy-start.2 = (bf16[4,32,2,1536]{3,2,1,0:T(2,128)(2,1)S(1)}, bf16[4,32,2,1536]{3,2,1,0:T(2,128)(2,1)}, u32[]{:S(2)}) copy-start(bf16[4,32,2,1536]{3,2,1,0:T(2,128)(2,1)} %param.10) | copy-start | bytes 2359300
  5.3 17.1 %collective-permute-start = (bf16[2,4,64,1536]{3,2,1,0:T(8,128)(2,1)S(1)}, bf16[2,4,64,1536]{3,2,1,0:T(8,128)(2,1)}, u32[]{:S(2)}, u32[]{:S(2)}) collective-permute-start(bf16[2,4,64,1536]{3,2,1,0:T(8,128)(2,1)S(1)} %pad_maximum_fusion.refs_4_.refs_6_), channel_id=1, source_target_pairs={{0,1},{1,0},{2,3},{3,2},{4,5},{5,4},{6,7},{7,6},{8,9},{9,8},{10,11... | collective-permute-start | bytes 4718600 | tf_op jit(solution)/shard_map/ppermute | solution.py:20
  8.8 1.4 %copy-start.3 = (bf16[1,4,64,1536]{3,2,1,0:T(8,128)(2,1)S(1)}, bf16[1,4,64,1536]{3,2,1,0:T(8,128)(2,1)}, u32[]{:S(2)}) copy-start(bf16[1,4,64,1536]{3,2,1,0:T(8,128)(2,1)} %stack_reshape.13) | copy-start | bytes 2359300
  10.1 6.1 %copy-start.8 = (f32[4,32,2,12]{1,2,3,0:T(2,128)S(1)}, f32[4,32,2,12]{1,2,3,0:T(2,128)}, u32[]{:S(2)}) copy-start(f32[4,32,2,12]{1,2,3,0:T(2,128)} %param.11) | copy-start | bytes 36868
  10.2 9.7 %copy-start = (bf16[2,4,64,1536]{3,2,1,0:T(8,128)(2,1)}, bf16[2,4,64,1536]{3,2,1,0:T(8,128)(2,1)S(1)}, u32[]{:S(2)}) copy-start(bf16[2,4,64,1536]{3,2,1,0:T(8,128)(2,1)S(1)} %constant_dynamic-update-slice_fusion.refs_0_.refs_1_.refs_2_) | copy-start | bytes 4718596
  10.2 37.0 %collective-permute-start.1 = (bf16[2,4,64,1536]{3,2,1,0:T(8,128)(2,1)S(1)}, bf16[2,4,64,1536]{3,2,1,0:T(8,128)(2,1)}, u32[]{:S(2)}, u32[]{:S(2)}) collective-permute-start(bf16[2,4,64,1536]{3,2,1,0:T(8,128)(2,1)S(1)} %constant_dynamic-update-slice_fusion.refs_0_.refs_1_.refs_2_), channel_id=1, source_target_pairs={{0,1},{1,0},{2,3},{3,2},{4,5},{5,4},{6,7},{7,6},{8,9},{9,8},{10,11... | collective-permute-start | bytes 4718600 | tf_op jit(solution)/shard_map/ppermute | solution.py:20
  10.3 37.7 %collective-permute-start.3 = (bf16[2,4,64,1536]{3,2,1,0:T(8,128)(2,1)S(1)}, bf16[2,4,64,1536]{3,2,1,0:T(8,128)(2,1)}, u32[]{:S(2)}, u32[]{:S(2)}) collective-permute-start(bf16[2,4,64,1536]{3,2,1,0:T(8,128)(2,1)S(1)} %pad_maximum_fusion.refs_4_.refs_6_), channel_id=1, source_target_pairs={{0,15},{1,2},{2,1},{3,4},{4,3},{5,6},{6,5},{7,8},{8,7},{9,10},{10,... | collective-permute-start | bytes 4718600 | tf_op jit(solution)/shard_map/ppermute | solution.py:20
  22.4 0.6 copy-start.7
  36.7 61.8 %collective-permute-start.5 = (f32[2,4,64,1536]{3,2,1,0:T(8,128)}, f32[2,4,64,1536]{3,2,1,0:T(8,128)}, u32[]{:S(2)}, u32[]{:S(2)}) collective-permute-start(f32[2,4,64,1536]{3,2,1,0:T(8,128)} %get-tuple-element.13), channel_id=1, source_target_pairs={{0,1},{1,0},{2,3},{3,2},{4,5},{5,4},{6,7},{7,6},{8,9},{9,8},{10,11... | collective-permute-start | bytes 9437192 | tf_op jit(solution)/shard_map/ppermute | solution.py:20
  40.2 5.4 %collective-permute-start.2 = (f32[2,12,4,1,64]{4,3,2,1,0:T(1,128)}, f32[2,12,4,1,64]{4,3,2,1,0:T(1,128)S(1)}, u32[]{:S(2)}, u32[]{:S(2)}) collective-permute-start(f32[2,12,4,1,64]{4,3,2,1,0:T(1,128)} %copy-done.7), channel_id=1, source_target_pairs={{0,1},{1,0},{2,3},{3,2},{4,5},{5,4},{6,7},{7,6},{8,9},{9,8},{10,11... | collective-permute-start | bytes 73736 | tf_op jit(solution)/shard_map/ppermute | solution.py:20
  61.5 3.6 %collective-permute-start.4 = (f32[4,64,1536]{2,1,0:T(8,128)}, f32[4,64,1536]{2,1,0:T(8,128)S(1)}, u32[]{:S(2)}, u32[]{:S(2)}) collective-permute-start(f32[4,64,1536]{2,1,0:T(8,128)} %get-tuple-element.11), channel_id=1, source_target_pairs={{0,1},{1,0},{2,3},{3,2},{4,5},{5,4},{6,7},{7,6},{8,9},{9,8},{10,11... | collective-permute-start | bytes 4718600 | tf_op jit(solution)/shard_map/ppermute | solution.py:20
  61.5 37.0 %collective-permute-start.6 = (bf16[2,4,64,1536]{3,2,1,0:T(8,128)(2,1)}, bf16[2,4,64,1536]{3,2,1,0:T(8,128)(2,1)S(1)}, u32[]{:S(2)}, u32[]{:S(2)}) collective-permute-start(bf16[2,4,64,1536]{3,2,1,0:T(8,128)(2,1)} %get-tuple-element.14), channel_id=1, source_target_pairs={{0,15},{1,2},{2,1},{3,4},{4,3},{5,6},{6,5},{7,8},{8,7},{9,10},{10,... | collective-permute-start | bytes 4718600 | tf_op jit(solution)/shard_map/ppermute | solution.py:20

commit v17 on v13

--- a/solution.py
+++ b/solution.py
@@ -99,6 +99,8 @@
     channels = heads * HEAD_DIM
     nq, nk = len(queries), len(keys)
     group = 4 if heads % 4 == 0 else (2 if heads % 2 == 0 else 1)
+    if narrow and heads % 6 == 0:
+        group = 6
     kernel = functools.partial(
         window_kernel, nq=nq, nk=nk, tiles=tiles, tf=tf, mf=mf, narrow=narrow, group=group
     )

time: 105 us -> 105 us (level)
  no operation moved by 1% of the time
where the time goes in v17:
time: 105 us
  waiting for transfers between devices  35.5 us (34%)
  Pallas kernels  27.3 us (26%)
  local copies, waits for them, and re-layouts  22.2 us (21%)
  other arithmetic  10.5 us (10%)
  starting transfers between devices  8.32 us (8%)
    ppermute x7, waiting for transfers between devices, swap(): return lax.ppermute(block, 'sy', route)  35.5 us
    pallas_call x2, Pallas kernels, window_pass(): pl.pallas_call(kernel, grid=(heads // group,), in_specs=in_specs, out_spe...  27.3 us
    ppermute x7, starting transfers between devices, swap(): return lax.ppermute(block, 'sy', route)  8.32 us
    unnamed x23, local copies, waits for them, and re-layouts  3.65 us
    reshape x1, local copies, waits for them, and re-layouts, on_device(): outputs_fwd.reshape(rows, width, heads, HEAD_DIM)  3.24 us
    convert_element_type x1, other arithmetic, on_device(): dq = (dq_local + dq_mine + dq_back).astype(jnp.bfloat16)  3.23 us
    reshape x1, local copies, waits for them, and re-layouts, on_device(): grad_out.reshape(rows, width, heads, HEAD_DIM)  3.2 us
    another operation x1, other arithmetic  3.2 us
  transfers between devices with their start and end apart: 7, of which 4 were waited for; matrix products, arithmetic and copies ran while one was open for 20% of the time, Pallas kernels for 26%

profile of v17, /device:TPU:1, one launch (start us, length us, event | category | flops | bytes accessed | tf_op | source)
XLA Modules:
  0.0 104.6 jit_solution(12403767932568067132)
XLA Ops:
  0.6 0.0 copy-start.6
  0.6 2.3 %reshape.33 = bf16[4,64,1536]{2,1,0:T(8,128)(2,1)S(1)} reshape(bf16[4,32,2,1536]{3,2,1,0:T(2,128)(2,1)} %param.7) | data formatting | bytes 1572864 | tf_op jit(solution)/shard_map/reshape | solution.py:174
  3.0 0.0 copy-start.4
  3.0 0.0 copy-done.6
  3.0 0.3 reshape.34
  3.3 0.5 copy-done.4
  3.9 0.0 slice-start
  3.9 1.0 slice-done
  5.0 0.1 maximum_bitcast_fusion
  5.1 0.0 copy-start.7
  5.1 0.1 pad_maximum_fusion.refs_4_.refs_6_
  5.3 0.0 copy-start.1
  5.3 0.0 copy-start.2
  5.3 0.1 collective-permute-start
  5.4 1.0 copy-done.7
  6.4 1.2 %stack_reshape.12 = bf16[1,4,64,1536]{3,2,1,0:T(8,128)(2,1)} reshape(bf16[4,32,2,1536]{3,2,1,0:T(2,128)(2,1)S(1)} %copy-done.7) | data formatting | bytes 1572864 | tf_op jit(solution)/shard_map/stack;reshape | solution.py:162
  7.6 0.0 copy-done.2
  7.6 1.2 %stack_reshape.13 = bf16[1,4,64,1536]{3,2,1,0:T(8,128)(2,1)} reshape(bf16[4,32,2,1536]{3,2,1,0:T(2,128)(2,1)S(1)} %copy-done.2) | data formatting | bytes 1572864 | tf_op jit(solution)/shard_map/stack;reshape | solution.py:162
  8.8 0.0 copy-start.3
  8.8 1.3 %constant_dynamic-update-slice_fusion.1 = bf16[2,4,64,1536]{3,2,1,0:T(8,128)(2,1)S(1)} fusion(bf16[1,4,64,1536]{3,2,1,0:T(8,128)(2,1)} %stack_reshape.12), kind=kLoop, calls=%fused_computation.9 | loop fusion | bytes 1572864
  10.0 0.1 copy-done.3
  10.1 0.0 copy-start.9
  10.1 0.1 constant_dynamic-update-slice_fusion.refs_0_.refs_1_.refs_2_
  10.2 0.0 copy-start
  10.2 0.1 collective-permute-start.1
  10.3 0.0 copy-done.1
  10.3 2.7 %collective-permute-start.3 = (bf16[2,4,64,1536]{3,2,1,0:T(8,128)(2,1)S(1)}, bf16[2,4,64,1536]{3,2,1,0:T(8,128)(2,1)}, u32[]{:S(2)}, u32[]{:S(2)}) collective-permute-start(bf16[2,4,64,1536]{3,2,1,0:T(8,128)(2,1)S(1)} %pad_maximum_fusion.refs_4_.refs_6_), channel_id=1, source_target_pairs={{0,15},{1,2},{2,1},{3,4},{4,3},{5,6},{6,5},{7,8},{8,7},{9,10},{10,... | collective-permute-start | bytes 4718600 | tf_op jit(solution)/shard_map/ppermute | solution.py:20
  13.0 3.2 %reshape.30 = bf16[4,64,12,128]{3,2,1,0:T(8,128)(2,1)} reshape(bf16[4,32,2,1536]{3,2,1,0:T(2,128)(2,1)} %param.10) | data formatting | bytes 1572864 | tf_op jit(solution)/shard_map/reshape | solution.py:165
  16.2 0.0 copy-done.9
  16.2 0.1 copy.9
  16.3 0.2 copy.10
  16.5 0.1 stack_reshape.14
  16.6 3.2 %reshape.31 = bf16[4,64,12,128]{3,2,1,0:T(8,128)(2,1)} reshape(bf16[4,32,2,1536]{3,2,1,0:T(2,128)(2,1)} %param.9) | data formatting | bytes 1572864 | tf_op jit(solution)/shard_map/reshape | solution.py:166
  19.9 0.0 copy-done
  19.9 2.2 %fusion = f32[4,64,12]{2,1,0:T(8,128)S(1)} fusion(bf16[4,64,12,128]{3,2,1,0:T(8,128)(2,1)} %reshape.30, bf16[4,64,12,128]{3,2,1,0:T(8,128)(2,1)} %reshape.31), kind=kLoop, calls=%fused_computation.2 | loop fusion | flops 1569792 | bytes 1585152
  22.0 0.2 copy.19
  22.2 0.1 stack_reshape.15
  22.4 0.0 copy-start.8
  22.4 0.0 collective-permute-done.refs_5_.refs_7_
  22.4 0.6 copy-done.8
  23.0 13.6 %shard_map.85 = (f32[4,64,1536]{2,1,0:T(8,128)}, f32[2,4,64,1536]{3,2,1,0:T(8,128)}, f32[2,4,64,1536]{3,2,1,0:T(8,128)}) custom-call(bf16[2,4,64,1536]{3,2,1,0:T(8,128)(2,1)} %copy-done, bf16[2,4,64,1536]{3,2,1,0:T(8,128)(2,1)} %copy-done, f32[2,12,4,1,64]{4,3,2,1,0:T(1,128)} %copy-done.8, f32[2,12,4,1,64]{4,3,2,1,0:T(1,128)} %copy-done.8, ...), custom_call_target="tpu_custom_call" | custom-call | flops 1006632960 | bytes 12582912 | tf_op jit(solution)/shard_map/pallas_call | solution.py:136
  36.6 3.5 %collective-permute-start.5 = (f32[2,4,64,1536]{3,2,1,0:T(8,128)}, f32[2,4,64,1536]{3,2,1,0:T(8,128)}, u32[]{:S(2)}, u32[]{:S(2)}) collective-permute-start(f32[2,4,64,1536]{3,2,1,0:T(8,128)} %get-tuple-element.13), channel_id=1, source_target_pairs={{0,1},{1,0},{2,3},{3,2},{4,5},{5,4},{6,7},{7,6},{8,9},{9,8},{10,11... | collective-permute-start | bytes 9437192 | tf_op jit(solution)/shard_map/ppermute | solution.py:20
  40.1 0.1 collective-permute-start.2
  40.2 5.4 %collective-permute-done.2 = f32[2,12,4,1,64]{4,3,2,1,0:T(1,128)S(1)} collective-permute-done((f32[2,12,4,1,64]{4,3,2,1,0:T(1,128)}, f32[2,12,4,1,64]{4,3,2,1,0:T(1,128)S(1)}, u32[]{:S(2)}, u32[]{:S(2)}) %collective-permute-start.2) | collective-permute-done | bytes 24608 | tf_op jit(solution)/shard_map/ppermute | solution.py:20
  45.5 1.6 %pad_maximum_fusion.1.refs_4_.refs_5_ = f32[2,12,4,1,128]{4,3,2,1,0:T(1,128)} fusion(f32[2,12,4,1,64]{4,3,2,1,0:T(1,128)S(1)} %collective-permute-done.2, f32[2,12,4,1,64]{4,3,2,1,0:T(1,128)} %copy-done.8), kind=kLoop, calls=%fused_computation.7 | loop fusion | flops 12288 | bytes 98304 | tf_op jit(solution)/shard_map/concatenate | solution.py:188
  47.1 0.0 collective-permute-done.1.refs_1_.refs_3_
  47.1 0.9 collective-permute-done.3.refs_6_.refs_7_
  48.0 13.8 %shard_map.86 = (f32[4,64,1536]{2,1,0:T(8,128)}, f32[4,64,1536]{2,1,0:T(8,128)}, bf16[2,4,64,1536]{3,2,1,0:T(8,128)(2,1)}) custom-call(bf16[2,4,64,1536]{3,2,1,0:T(8,128)(2,1)} %copy-done, bf16[2,4,64,1536]{3,2,1,0:T(8,128)(2,1)} %collective-permute-done.1.refs_1_.refs_3_, bf16[2,4,64,1536]{3,2,1,0:T(8,128)(2,1)} %copy-done, ...), custom_call_target="tpu_custom_call" | custom-call | flops 1006632960 | bytes 11010048 | tf_op jit(solution)/shard_map/pallas_call | solution.py:136
  61.8 0.0 collective-permute-start.4
  61.8 1.8 %collective-permute-start.6 = (bf16[2,4,64,1536]{3,2,1,0:T(8,128)(2,1)}, bf16[2,4,64,1536]{3,2,1,0:T(8,128)(2,1)}, u32[]{:S(2)}, u32[]{:S(2)}) collective-permute-start(bf16[2,4,64,1536]{3,2,1,0:T(8,128)(2,1)} %get-tuple-element.14), channel_id=1, source_target_pairs={{0,15},{1,2},{2,1},{3,4},{4,3},{5,6},{6,5},{7,8},{8,7},{9,10},{10,... | collective-permute-start | bytes 4718600 | tf_op jit(solution)/shard_map/ppermute | solution.py:20
  63.6 1.8 %collective-permute-done.4 = f32[4,64,1536]{2,1,0:T(8,128)S(1)} collective-permute-done((f32[4,64,1536]{2,1,0:T(8,128)}, f32[4,64,1536]{2,1,0:T(8,128)S(1)}, u32[]{:S(2)}, u32[]{:S(2)}) %collective-permute-start.4) | collective-permute-done | bytes 1572896 | tf_op jit(solution)/shard_map/ppermute | solution.py:20
  65.4 0.0 copy-start.5
  65.4 3.2 %add_convert_fusion.1 = bf16[4,64,1536]{2,1,0:T(8,128)(2,1)} fusion(f32[4,64,1536]{2,1,0:T(8,128)S(1)} %collective-permute-done.4, f32[4,64,1536]{2,1,0:T(8,128)} %get-tuple-element.9, f32[4,64,1536]{2,1,0:T(8,128)} %get-tuple-element.10), kind=kLoop, calls=%fused_computation.4 | loop fusion | flops 1179648 | bytes 5505024 | tf_op jit(solution)/shard_map/convert_element_type | solution.py:204
  68.7 2.8 %reshape.35 = bf16[4,32,2,1536]{3,2,1,0:T(2,128)(2,1)} reshape(bf16[4,64,1536]{2,1,0:T(8,128)(2,1)} %add_convert_fusion.1) | data formatting | bytes 1572864 | tf_op jit(solution)/shard_map/reshape | solution.py:208
  71.5 27.4 %collective-permute-done.6 = bf16[2,4,64,1536]{3,2,1,0:T(8,128)(2,1)} collective-permute-done((bf16[2,4,64,1536]{3,2,1,0:T(8,128)(2,1)}, bf16[2,4,64,1536]{3,2,1,0:T(8,128)(2,1)}, u32[]{:S(2)}, u32[]{:S(2)}) %collective-permute-start.6) | collective-permute-done | bytes 1572896 | tf_op jit(solution)/shard_map/ppermute | solution.py:20
  98.9 0.0 collective-permute-done.5
  98.9 0.0 copy-done.5
  98.9 3.2 %add_convert_fusion = bf16[2,4,64,1536]{3,2,1,0:T(8,128)(2,1)S(1)} fusion(bf16[2,4,64,1536]{3,2,1,0:T(8,128)(2,1)} %collective-permute-done.6, f32[2,4,64,1536]{3,2,1,0:T(8,128)S(1)} %copy-done.5, f32[2,4,64,1536]{3,2,1,0:T(8,128)} %collective-permute-done.5), kind=kLoop, calls=%fused_computation | loop fusion | flops 3145728 | bytes 9437184 | tf_op jit(solution)/shard_map/convert.1
  102.1 0.1 fusion.1
  102.2 1.2 %convert_element_type.19 = bf16[4,32,2,1536]{3,2,1,0:T(2,128)(2,1)} reshape(bf16[1,4,64,1536]{3,2,1,0:T(8,128)(2,1)S(1)} %get-tuple-element.15) | data formatting | bytes 1572864 | tf_op jit(solution)/shard_map/convert_element_type | solution.py:207
  103.4 1.2 %convert_element_type.18 = bf16[4,32,2,1536]{3,2,1,0:T(2,128)(2,1)} reshape(bf16[1,4,64,1536]{3,2,1,0:T(8,128)(2,1)S(1)} %get-tuple-element.16) | data formatting | bytes 1572864 | tf_op jit(solution)/shard_map/convert_element_type | solution.py:206
  (5 shorter events, 0.1 us)
Async XLA Ops:
  0.6 2.4 %copy-start.6 = (bf16[4,32,2,1536]{3,2,1,0:T(2,128)(2,1)S(1)}, bf16[4,32,2,1536]{3,2,1,0:T(2,128)(2,1)}, u32[]{:S(2)}) copy-start(bf16[4,32,2,1536]{3,2,1,0:T(2,128)(2,1)} %param.8) | copy-start | bytes 2359300
  3.0 0.9 copy-start.4
  3.9 1.1 %slice-start = ((bf16[4,64,1536]{2,1,0:T(8,128)(2,1)}), bf16[4,56,1536]{2,1,0:T(8,128)(2,1)S(1)}, s32[]{:S(2)}) async-start(bf16[4,64,1536]{2,1,0:T(8,128)(2,1)} %copy-done.4), calls=%async_computation | async-start | bytes 1376256 | tf_op jit(solution)/shard_map/jit(_roll_static)/slice | solution.py:174
  5.1 1.3 %copy-start.7 = (bf16[4,32,2,1536]{3,2,1,0:T(2,128)(2,1)S(1)}, bf16[4,32,2,1536]{3,2,1,0:T(2,128)(2,1)}, u32[]{:S(2)}) copy-start(bf16[4,32,2,1536]{3,2,1,0:T(2,128)(2,1)} %param.6) | copy-start | bytes 2359300
  5.3 5.0 %copy-start.1 = (bf16[2,4,64,1536]{3,2,1,0:T(8,128)(2,1)}, bf16[2,4,64,1536]{3,2,1,0:T(8,128)(2,1)S(1)}, u32[]{:S(2)}) copy-start(bf16[2,4,64,1536]{3,2,1,0:T(8,128)(2,1)S(1)} %pad_maximum_fusion.refs_4_.refs_6_) | copy-start | bytes 4718596
  5.3 2.3 %copy-start.2 = (bf16[4,32,2,1536]{3,2,1,0:T(2,128)(2,1)S(1)}, bf16[4,32,2,1536]{3,2,1,0:T(2,128)(2,1)}, u32[]{:S(2)}) copy-start(bf16[4,32,2,1536]{3,2,1,0:T(2,128)(2,1)} %param.10) | copy-start | bytes 2359300
  5.3 17.1 %collective-permute-start = (bf16[2,4,64,1536]{3,2,1,0:T(8,128)(2,1)S(1)}, bf16[2,4,64,1536]{3,2,1,0:T(8,128)(2,1)}, u32[]{:S(2)}, u32[]{:S(2)}) collective-permute-start(bf16[2,4,64,1536]{3,2,1,0:T(8,128)(2,1)S(1)} %pad_maximum_fusion.refs_4_.refs_6_), channel_id=1, source_target_pairs={{0,1},{1,0},{2,3},{3,2},{4,5},{5,4},{6,7},{7,6},{8,9},{9,8},{10,11... | collective-permute-start | bytes 4718600 | tf_op jit(solution)/shard_map/ppermute | solution.py:20
  8.8 1.4 %copy-start.3 = (bf16[1,4,64,1536]{3,2,1,0:T(8,128)(2,1)S(1)}, bf16[1,4,64,1536]{3,2,1,0:T(8,128)(2,1)}, u32[]{:S(2)}) copy-start(bf16[1,4,64,1536]{3,2,1,0:T(8,128)(2,1)} %stack_reshape.13) | copy-start | bytes 2359300
  10.1 6.1 %copy-start.9 = (f32[4,32,2,12]{1,2,3,0:T(2,128)S(1)}, f32[4,32,2,12]{1,2,3,0:T(2,128)}, u32[]{:S(2)}) copy-start(f32[4,32,2,12]{1,2,3,0:T(2,128)} %param.11) | copy-start | bytes 36868
  10.2 9.7 %copy-start = (bf16[2,4,64,1536]{3,2,1,0:T(8,128)(2,1)}, bf16[2,4,64,1536]{3,2,1,0:T(8,128)(2,1)S(1)}, u32[]{:S(2)}) copy-start(bf16[2,4,64,1536]{3,2,1,0:T(8,128)(2,1)S(1)} %constant_dynamic-update-slice_fusion.refs_0_.refs_1_.refs_2_) | copy-start | bytes 4718596
  10.2 36.9 %collective-permute-start.1 = (bf16[2,4,64,1536]{3,2,1,0:T(8,128)(2,1)S(1)}, bf16[2,4,64,1536]{3,2,1,0:T(8,128)(2,1)}, u32[]{:S(2)}, u32[]{:S(2)}) collective-permute-start(bf16[2,4,64,1536]{3,2,1,0:T(8,128)(2,1)S(1)} %constant_dynamic-update-slice_fusion.refs_0_.refs_1_.refs_2_), channel_id=1, source_target_pairs={{0,1},{1,0},{2,3},{3,2},{4,5},{5,4},{6,7},{7,6},{8,9},{9,8},{10,11... | collective-permute-start | bytes 4718600 | tf_op jit(solution)/shard_map/ppermute | solution.py:20
  10.3 37.7 %collective-permute-start.3 = (bf16[2,4,64,1536]{3,2,1,0:T(8,128)(2,1)S(1)}, bf16[2,4,64,1536]{3,2,1,0:T(8,128)(2,1)}, u32[]{:S(2)}, u32[]{:S(2)}) collective-permute-start(bf16[2,4,64,1536]{3,2,1,0:T(8,128)(2,1)S(1)} %pad_maximum_fusion.refs_4_.refs_6_), channel_id=1, source_target_pairs={{0,15},{1,2},{2,1},{3,4},{4,3},{5,6},{6,5},{7,8},{8,7},{9,10},{10,... | collective-permute-start | bytes 4718600 | tf_op jit(solution)/shard_map/ppermute | solution.py:20
  22.4 0.6 copy-start.8
  36.6 62.3 %collective-permute-start.5 = (f32[2,4,64,1536]{3,2,1,0:T(8,128)}, f32[2,4,64,1536]{3,2,1,0:T(8,128)}, u32[]{:S(2)}, u32[]{:S(2)}) collective-permute-start(f32[2,4,64,1536]{3,2,1,0:T(8,128)} %get-tuple-element.13), channel_id=1, source_target_pairs={{0,1},{1,0},{2,3},{3,2},{4,5},{5,4},{6,7},{7,6},{8,9},{9,8},{10,11... | collective-permute-start | bytes 9437192 | tf_op jit(solution)/shard_map/ppermute | solution.py:20
  40.1 5.4 %collective-permute-start.2 = (f32[2,12,4,1,64]{4,3,2,1,0:T(1,128)}, f32[2,12,4,1,64]{4,3,2,1,0:T(1,128)S(1)}, u32[]{:S(2)}, u32[]{:S(2)}) collective-permute-start(f32[2,12,4,1,64]{4,3,2,1,0:T(1,128)} %copy-done.8), channel_id=1, source_target_pairs={{0,1},{1,0},{2,3},{3,2},{4,5},{5,4},{6,7},{7,6},{8,9},{9,8},{10,11... | collective-permute-start | bytes 73736 | tf_op jit(solution)/shard_map/ppermute | solution.py:20
  61.8 3.6 %collective-permute-start.4 = (f32[4,64,1536]{2,1,0:T(8,128)}, f32[4,64,1536]{2,1,0:T(8,128)S(1)}, u32[]{:S(2)}, u32[]{:S(2)}) collective-permute-start(f32[4,64,1536]{2,1,0:T(8,128)} %get-tuple-element.11), channel_id=1, source_target_pairs={{0,1},{1,0},{2,3},{3,2},{4,5},{5,4},{6,7},{7,6},{8,9},{9,8},{10,11... | collective-permute-start | bytes 4718600 | tf_op jit(solution)/shard_map/ppermute | solution.py:20
  61.8 37.1 %collective-permute-start.6 = (bf16[2,4,64,1536]{3,2,1,0:T(8,128)(2,1)}, bf16[2,4,64,1536]{3,2,1,0:T(8,128)(2,1)}, u32[]{:S(2)}, u32[]{:S(2)}) collective-permute-start(bf16[2,4,64,1536]{3,2,1,0:T(8,128)(2,1)} %get-tuple-element.14), channel_id=1, source_target_pairs={{0,15},{1,2},{2,1},{3,4},{4,3},{5,6},{6,5},{7,8},{8,7},{9,10},{10,... | collective-permute-start | bytes 4718600 | tf_op jit(solution)/shard_map/ppermute | solution.py:20
  65.4 33.5 %copy-start.5 = (f32[2,4,64,1536]{3,2,1,0:T(8,128)S(1)}, f32[2,4,64,1536]{3,2,1,0:T(8,128)}, u32[]{:S(2)}) copy-start(f32[2,4,64,1536]{3,2,1,0:T(8,128)} %get-tuple-element.12) | copy-start | bytes 9437188
